TPU v7x, 128 devices: a whole 4x4x4 slice. The times are simulated.
128 devices in a mesh: dp: 8 (over z, core), seq: 16 (over y, x).
Axes of the slice: x: 4, y: 4, z: 4, core: 2. Of those that a mesh axis runs over, the one named last changes fastest.
Arguments:
- tokens: bfloat16 [8, 8192, 2048], P('dp', 'seq'), may hold values from -6 to 6
- input_gain: bfloat16 [2048], replicated, may hold values from 0.099609375 to 1.8984375
- qkv_weight: bfloat16 [2048, 6144], P(None, ('dp', 'seq')), may hold values from -0.125 to 0.125
- head_gain: bfloat16 [2048], replicated, may hold values from 0.099609375 to 1.8984375
- prefix_state: float32 [8, 16, 128, 128], P('dp'), may hold values from -256 to 256
Outputs:
- attended: bfloat16 [8, 8192, 2048], P('dp', 'seq')
All inputs are finite; a program needn't handle non-finite values.
Results may differ from a plain program's by a relative error of at most 0.0061.
Values may be sent and summed in bfloat16 or wider, within the bound.
No kernel may reach another device: no remote copies, remote signals or barrier semaphores. Data moves between devices by JAX's collectives and lax.ppermute only.
A program may use at most 128 MiB of HBM per device.

v0:
```python
import jax
import jax.numpy as jnp
from jax import lax
from jax.sharding import PartitionSpec as P

D = 2048
H = 16
DH = 128
BLOCK = 512


epsilon = 1e-05


def feature_map(inputs):
    return jnp.where(inputs > 0, inputs + 1.0, jnp.exp(jnp.minimum(inputs, 0.0)))


def span_attention(queries, key_feats, values, memory, head_gain):
    num_blocks = queries.shape[0] // BLOCK
    causal = jnp.arange(BLOCK)[:, None] >= jnp.arange(BLOCK)[None, :]
    gains = head_gain.astype(jnp.float32).reshape(H, DH)

    def advance(running, blocks):
        query_blk, key_blk, value_blk = blocks
        carried = jnp.einsum(
            "bhd,hde->bhe",
            query_blk,
            running.astype(jnp.bfloat16),
            preferred_element_type=jnp.float32,
        )
        scores = jnp.einsum("bhd,chd->hbc", query_blk, key_blk, preferred_element_type=jnp.float32)
        scores = jnp.where(causal[None], scores, 0.0).astype(jnp.bfloat16)
        within = jnp.einsum("hbc,che->bhe", scores, value_blk, preferred_element_type=jnp.float32)
        numerator = carried + within
        scale = lax.rsqrt(jnp.mean(numerator * numerator, axis=-1, keepdims=True) + epsilon)
        running = running + jnp.einsum(
            "bhd,bhe->hde", key_blk, value_blk, preferred_element_type=jnp.float32
        )
        return (running, (numerator * scale * gains).astype(jnp.bfloat16))

    def shaped(inputs):
        return inputs.reshape(num_blocks, BLOCK, H, DH)

    final_memory, outputs = lax.scan(
        advance, memory, (shaped(queries), shaped(key_feats), shaped(values))
    )
    return outputs.reshape(num_blocks * BLOCK, H * DH)


def body(tokens, input_gain, qkv_weight, head_gain, prefix_state):
    inputs = tokens[0].astype(jnp.float32)
    normed = inputs * lax.rsqrt(jnp.mean(inputs * inputs, axis=-1, keepdims=True) + epsilon)
    normed = (normed * input_gain.astype(jnp.float32)).astype(jnp.bfloat16)
    tok_rows = normed.shape[0]
    projected = jnp.dot(
        normed,
        lax.all_gather(qkv_weight, ("dp", "seq"), axis=1, tiled=True),
        preferred_element_type=jnp.float32,
    )
    queries = feature_map(projected[:, :D]).astype(jnp.bfloat16).reshape(tok_rows, H, DH)
    key_feats = feature_map(projected[:, D : 2 * D]).astype(jnp.bfloat16).reshape(tok_rows, H, DH)
    values = projected[:, 2 * D :].astype(jnp.bfloat16).reshape(tok_rows, H, DH)
    local = jnp.einsum(
        "thd,the->hde", key_feats, values, preferred_element_type=jnp.float32
    ).astype(jnp.bfloat16)
    gathered = lax.all_gather(local[None], "seq", axis=0, tiled=True)
    my_index = lax.axis_index("seq")
    earlier = (jnp.arange(gathered.shape[0]) < my_index).astype(jnp.bfloat16)
    before = jnp.einsum("c,chde->hde", earlier, gathered, preferred_element_type=jnp.float32)
    memory = prefix_state[0] + before
    attended = span_attention(queries, key_feats, values, memory, head_gain)
    return attended[None]


def solution(mesh):
    placed = (P("dp", "seq", None), P(), P(None, ("dp", "seq")), P(), P("dp", None, None, None))
    return jax.shard_map(
        body, mesh=mesh, in_specs=placed, out_specs=P("dp", "seq", None), check_vma=False
    )
```

profile of v0, /device:TPU:1, one launch (start us, length us, event | category | flops | bytes accessed | tf_op | source)
XLA Modules:
  0.0 235.7 jit_solution(6228382882600847953)
XLA Ops:
  6.5 0.0 all-gather.4.cloned.1.call-start
  6.5 0.7 all-gather.4.cloned.1.call-update
  7.3 0.0 all-gather.6.cloned.1.call-start
  7.3 0.7 convert_element_type.38
  8.0 2.1 fusion.2
  10.1 97.0 %all-gather.4.cloned.1.call-done = bf16[2048,6144]{0,1:T(8,128)(2,1)} async-done(((bf16[2048,48]{0,1:T(8,128)(2,1)}), bf16[2048,6144]{0,1:T(8,128)(2,1)}) %all-gather.4.cloned.1.call-update) | async-done | bytes 25165840 | tf_op jit(solution)/shard_map/all_gather | solution.py:58
  107.1 20.0 %fusion.10 = f32[512,6144]{1,0:T(8,128)} fusion(bf16[2048,6144]{0,1:T(8,128)(2,1)} %all-gather.4.cloned.1.call-done, bf16[1,512,2048]{2,1,0:T(8,128)(2,1)} %param.5, f32[2048]{0:T(1024)S(1)} %convert_element_type.38, f32[512]{0:T(512)S(1)} %add_rsqrt_fusion.1), kind=kOutput, calls=%fused_computation.19 | convolution fusion | flops 12889096192 | bytes 39856128 | tf_op jit(solution)/shard_map/dot_general | solution.py:56
  127.1 5.7 %fusion.9 = (bf16[64,16,8,128]{3,2,1,0:T(8,128)(2,1)}, bf16[512,2048]{1,0:T(8,128)(2,1)}) fusion(f32[512,6144]{1,0:T(8,128)} %fusion.10), kind=kLoop, calls=%fused_computation.18 | loop fusion | flops 10485760 | bytes 12582912
  132.8 3.8 %slice.21 = bf16[512,2048]{1,0:T(8,128)(2,1)} slice(f32[512,6144]{1,0:T(8,128)} %fusion.10), slice={[0:512], [4096:6144]} | slice | bytes 4194304 | tf_op jit(solution)/shard_map/slice | solution.py:63
  136.6 2.9 %copy.22 = bf16[512,2048]{0,1:T(8,128)(2,1)S(1)} copy(bf16[512,2048]{1,0:T(8,128)(2,1)} %get-tuple-element.20) | data formatting | bytes 4194304 | tf_op jit(solution)/shard_map/reshape | solution.py:62
  139.5 0.0 copy-start.3
  139.5 4.0 %copy.23 = bf16[512,2048]{0,1:T(8,128)(2,1)} copy(bf16[512,2048]{1,0:T(8,128)(2,1)} %slice.21) | data formatting | bytes 4194304 | tf_op jit(solution)/shard_map/reshape | solution.py:63
  143.5 3.1 %convolution_convert_fusion = bf16[16,128,128]{2,1,0:T(8,128)(2,1)} fusion(bf16[512,16,128]{0,2,1:T(8,128)(2,1)S(1)} %bitcast.53, bf16[512,16,128]{0,2,1:T(8,128)(2,1)} %bitcast.55), kind=kOutput, calls=%fused_computation.27 | convolution fusion | flops 268697600 | bytes 4718592 | tf_op jit(solution)/shard_map/thd,the->hde/dot_general | solution.py:64
  146.6 0.0 all-gather.6.cloned.1.call-update
  146.6 0.1 iota_compare_fusion
  146.7 0.0 copy-done.3
  146.7 9.2 %fusion.8 = f32[16,128,512]{2,1,0:T(8,128)} fusion(bf16[512,16,128]{0,2,1:T(8,128)(2,1)} %bitcast.56, bf16[512,16,128]{0,2,1:T(8,128)(2,1)S(1)} %bitcast.54, pred[512,512]{1,0:T(8,128)(4,1)S(1)} %iota_compare_fusion, bf16[64,16,8,128]{3,2,1,0:T(8,128)(2,1)} %get-tuple-element.19), kind=kOutput, calls=%fused_computation.16 | convolution fusion | flops 2155872256 | bytes 10747904 | tf_op jit(solution)/shard_map/while/body/eval_jaxpr/hbc,che->bhe/dot_general | solution.py:34
  155.9 60.4 %all-gather.6.cloned.1.call-done = bf16[256,128,128]{2,1,0:T(8,128)(2,1)} async-done(((bf16[16,128,128]{2,1,0:T(8,128)(2,1)}), bf16[256,128,128]{2,1,0:T(8,128)(2,1)}) %all-gather.6.cloned.1.call-update) | async-done | bytes 8388624 | tf_op jit(solution)/shard_map/all_gather | solution.py:67
  216.3 8.4 %fusion = f32[1,16,128,128]{3,0,2,1:T(1,128)S(1)} fusion(bf16[16,16,128,128]{3,2,1,0:T(8,128)(2,1)} %bitcast.52, s32[]{:T(128)S(6)} %axis_index.12), kind=kOutput, calls=%fused_computation.1 | convolution fusion | flops 8388624 | bytes 9437188 | tf_op jit(solution)/shard_map/c,chde->hde/dot_general | solution.py:70
  224.8 0.0 copy-done
  224.8 0.0 copy-done.1
  224.8 1.0 fusion.5
  225.9 0.6 fusion.7
  226.5 2.4 %copy.17 = bf16[1,512,2048]{2,1,0:T(8,128)(2,1)} copy(bf16[1,512,2048]{1,2,0:T(8,128)(2,1)S(1)} %bitcast.57) | data formatting | bytes 4194304 | tf_op jit(solution)/shard_map/broadcast_in_dim;reshape | solution.py:73
  (7 shorter events, 0.0 us)
Async XLA Ops:
  6.5 100.6 %all-gather.4.cloned.1.call-start = ((), (), s32[]{:S(2)}) async-start(), calls=%async_computation | async-start | bytes 25362432 | tf_op jit(solution)/shard_map/all_gather | solution.py:58
  7.3 209.1 %all-gather.6.cloned.1.call-start = ((), (), s32[]{:S(2)}) async-start(), calls=%async_computation.1 | async-start | bytes 8912896 | tf_op jit(solution)/shard_map/all_gather | solution.py:67
  139.5 7.2 %copy-start.3 = (bf16[2048]{0:T(1024)(128)(2,1)S(1)}, bf16[2048]{0:T(1024)(128)(2,1)}, u32[]{:S(2)}) copy-start(bf16[2048]{0:T(1024)(128)(2,1)} %param.8) | copy-start | bytes 12292
  216.3 8.5 %copy-start = (bf16[64,16,8,128]{3,2,1,0:T(8,128)(2,1)S(1)}, bf16[64,16,8,128]{3,2,1,0:T(8,128)(2,1)}, u32[]{:S(2)}) copy-start(bf16[64,16,8,128]{3,2,1,0:T(8,128)(2,1)} %get-tuple-element.19) | copy-start | bytes 6291460
  216.3 8.5 %copy-start.1 = (f32[16,128,512]{2,1,0:T(8,128)S(1)}, f32[16,128,512]{2,1,0:T(8,128)}, u32[]{:S(2)}) copy-start(f32[16,128,512]{2,1,0:T(8,128)} %fusion.8) | copy-start | bytes 12582916
  216.3 8.5 %copy-start.2 = (f32[1,16,128,128]{3,2,1,0:T(8,128)S(1)}, f32[1,16,128,128]{3,2,1,0:T(8,128)}, u32[]{:S(2)}) copy-start(f32[1,16,128,128]{3,2,1,0:T(8,128)} %param.9) | copy-start | bytes 3145732
Sparse Core Ops, SparseCore 0:
  10.4 96.6 all-gather.3
  146.7 69.5 all-gather.5
where the time goes:
time: 236 us
  waiting for transfers between devices  158 us (67%)
  matrix products  41.8 us (18%)
  between operations  13.5 us (6%)
  local copies, waits for them, and re-layouts  13 us (6%)
  other arithmetic  9.23 us (4%)
    all_gather x1, waiting for transfers between devices, body(): lax.all_gather(qkv_weight, ('dp', 'seq'), axis=1, tiled=True)  97 us
    all_gather x1, waiting for transfers between devices, body(): gathered = lax.all_gather(local[None], 'seq', axis=0, tiled=True)  60.4 us
    dot_general x1, matrix products, body(): jnp.dot(normed, lax.all_gather(qkv_weight, ('dp', 'seq'), axis=1, tiled=T...  20 us
    dot_general x1, matrix products, advance(): jnp.einsum('hbc,che->bhe', scores, value_blk, preferred_element_type=jnp....  9.24 us
    dot_general x1, matrix products, body(): jnp.einsum('c,chde->hde', earlier, gathered, preferred_element_type=jnp.f...  8.45 us
    unnamed x1, other arithmetic  5.73 us
  transfers between devices with their start and end apart: 2, of which 2 were waited for; matrix products, arithmetic and copies ran while one was open for 5% of the time, Pallas kernels for 0%

commit v1 on v0

--- a/solution.py
+++ b/solution.py
@@ -1,7 +1,7 @@
 import jax
 import jax.numpy as jnp
 from jax import lax
-from jax.sharding import PartitionSpec as P
+from jax.sharding import Mesh, PartitionSpec as P
 
 D = 2048
 H = 16
@@ -49,18 +49,31 @@
 
 
 def body(tokens, input_gain, qkv_weight, head_gain, prefix_state):
+    swap = [(0, 1), (1, 0)]
+    core = lax.axis_index("c")
     inputs = tokens[0].astype(jnp.float32)
     normed = inputs * lax.rsqrt(jnp.mean(inputs * inputs, axis=-1, keepdims=True) + epsilon)
     normed = (normed * input_gain.astype(jnp.float32)).astype(jnp.bfloat16)
     tok_rows = normed.shape[0]
-    projected = jnp.dot(
-        normed,
-        lax.all_gather(qkv_weight, ("dp", "seq"), axis=1, tiled=True),
-        preferred_element_type=jnp.float32,
-    )
-    queries = feature_map(projected[:, :D]).astype(jnp.bfloat16).reshape(tok_rows, H, DH)
-    key_feats = feature_map(projected[:, D : 2 * D]).astype(jnp.bfloat16).reshape(tok_rows, H, DH)
-    values = projected[:, 2 * D :].astype(jnp.bfloat16).reshape(tok_rows, H, DH)
+    partner = lax.ppermute(normed, "c", swap)
+    both = jnp.concatenate([normed, partner], axis=0)
+    half_w = lax.all_gather(qkv_weight, ("z", "seq"), axis=1, tiled=True)
+    n_z = half_w.shape[1] // qkv_weight.shape[1] // lax.axis_size("seq")
+    span = half_w.shape[1] // n_z
+    projected = jnp.dot(both, half_w, preferred_element_type=jnp.float32)
+    col = jnp.arange(half_w.shape[1])
+    global_col = (2 * (col // span) + core) * span + col % span
+    feats = jnp.where(global_col < 2 * D, feature_map(projected), projected).astype(jnp.bfloat16)
+    mine = feats[:tok_rows].reshape(tok_rows, n_z, 1, span)
+    theirs = lax.ppermute(feats[tok_rows:], "c", swap).reshape(tok_rows, n_z, 1, span)
+    full = jnp.where(
+        core == 0,
+        jnp.concatenate([mine, theirs], axis=2),
+        jnp.concatenate([theirs, mine], axis=2),
+    ).reshape(tok_rows, 3 * D)
+    queries = full[:, :D].reshape(tok_rows, H, DH)
+    key_feats = full[:, D : 2 * D].reshape(tok_rows, H, DH)
+    values = full[:, 2 * D :].reshape(tok_rows, H, DH)
     local = jnp.einsum(
         "thd,the->hde", key_feats, values, preferred_element_type=jnp.float32
     ).astype(jnp.bfloat16)
@@ -74,7 +87,10 @@
 
 
 def solution(mesh):
-    placed = (P("dp", "seq", None), P(), P(None, ("dp", "seq")), P(), P("dp", None, None, None))
+    n_dp, n_seq = mesh.devices.shape
+    split = Mesh(mesh.devices.reshape(n_dp // 2, 2, n_seq), ("z", "c", "seq"))
+    rows = ("z", "c")
+    placed = (P(rows, "seq", None), P(), P(None, ("z", "c", "seq")), P(), P(rows, None, None, None))
     return jax.shard_map(
-        body, mesh=mesh, in_specs=placed, out_specs=P("dp", "seq", None), check_vma=False
+        body, mesh=split, in_specs=placed, out_specs=P(rows, "seq", None), check_vma=False
     )

time: 236 us -> 233 us (0.987)
  matrix products: 41.8 us -> 37.8 us
  waiting for transfers between devices: 158 us -> 155 us
    all_gather x1, waiting for transfers between devices: 97 us -> 86.8 us  [body(): half_w = lax.all_gather(qkv_weight, ('z', 'seq'), axis=1, tiled=True)]
    ppermute x0 -> x2, waiting for transfers between devices: none -> 6.72 us  [the longest x1 3.9 us: body(): partner = lax.ppermute(normed, 'c', swap)]
    unnamed x1 -> x0, other arithmetic: 5.73 us -> none
    select_n x0 -> x1, other arithmetic: none -> 4.04 us  [body(): jnp.where(core == 0, jnp.concatenate([mine, theirs], axis=2), jnp.concate...]
  transfers between devices with their start and end apart: 2 -> 4, of which waited for: 2 -> 4; matrix products, arithmetic and copies ran while one was open for 5% -> 7% of each run, Pallas kernels for 0% -> 0%
where the time goes in v1:
time: 233 us
  waiting for transfers between devices  155 us (67%)
  matrix products  37.8 us (16%)
  local copies, waits for them, and re-layouts  15.2 us (7%)
  between operations  13.5 us (6%)
  other arithmetic  9.6 us (4%)
    all_gather x1, waiting for transfers between devices, body(): half_w = lax.all_gather(qkv_weight, ('z', 'seq'), axis=1, tiled=True)  86.8 us
    all_gather x1, waiting for transfers between devices, body(): gathered = lax.all_gather(local[None], 'seq', axis=0, tiled=True)  60.7 us
    dot_general x1, matrix products, body(): projected = jnp.dot(both, half_w, preferred_element_type=jnp.float32)  17.7 us
    dot_general x1, matrix products, advance(): jnp.einsum('hbc,che->bhe', scores, value_blk, preferred_element_type=jnp....  9.27 us
    dot_general x1, matrix products, body(): jnp.einsum('c,chde->hde', earlier, gathered, preferred_element_type=jnp.f...  8.45 us
    reshape x1, local copies, waits for them, and re-layouts, body(): lax.ppermute(feats[tok_rows:], 'c', swap).reshape(tok_rows, n_z, 1, span)  4.77 us
  transfers between devices with their start and end apart: 4, of which 4 were waited for; matrix products, arithmetic and copies ran while one was open for 7% of the time, Pallas kernels for 0%

profile of v1, /device:TPU:1, one launch (start us, length us, event | category | flops | bytes accessed | tf_op | source)
XLA Modules:
  0.0 233.1 jit_solution(4633194310293579864)
XLA Ops:
  6.5 0.7 all-gather.4.cloned.1.call-update
  7.3 0.7 convert_element_type.34
  8.0 2.1 fusion.2
  10.1 2.1 fusion.4
  12.2 1.5 collective-permute-start
  13.7 3.9 %collective-permute-done = bf16[512,2048]{1,0:T(8,128)(2,1)} collective-permute-done((bf16[512,2048]{1,0:T(8,128)(2,1)S(1)}, bf16[512,2048]{1,0:T(8,128)(2,1)}, u32[]{:S(2)}, u32[]{:S(2)}) %collective-permute-start) | collective-permute-done | bytes 2097184 | tf_op jit(solution)/shard_map/ppermute | solution.py:58
  17.6 86.8 %all-gather.4.cloned.1.call-done = bf16[2048,3072]{0,1:T(8,128)(2,1)} async-done(((bf16[2048,48]{0,1:T(8,128)(2,1)}), bf16[2048,3072]{0,1:T(8,128)(2,1)}) %all-gather.4.cloned.1.call-update) | async-done | bytes 12582928 | tf_op jit(solution)/shard_map/all_gather | solution.py:60
  104.4 17.7 %select_convert_fusion.1 = bf16[1024,3072]{1,0:T(8,128)(2,1)S(1)} fusion(pred[3072]{0:T(1024)(128)(4,1)S(1)} %fusion.28, bf16[2048,3072]{0,1:T(8,128)(2,1)} %all-gather.4.cloned.1.call-done, bf16[512,2048]{1,0:T(8,128)(2,1)} %collective-permute-done, bf16[512,2048]{1,0:T(8,128)(2,1)S(1)} %fusion.4), kind=kOutput, calls=%fused_computation.1 | convolution fusion | flops 12912164864 | bytes 23071744 | tf_op jit(solution)/shard_map/dot_general | solution.py:63
  122.2 2.2 fusion.36
  124.3 0.7 collective-permute-start.1
  125.0 2.8 %copy.35 = bf16[512,3072]{0,1:T(8,128)(2,1)} copy(bf16[512,3072]{1,0:T(8,128)(2,1)S(1)} %get-tuple-element.22) | data formatting | bytes 6291456 | tf_op jit(solution)/shard_map/reshape | solution.py:67
  127.8 2.8 %collective-permute-done.1 = bf16[512,3072]{1,0:T(8,128)(2,1)} collective-permute-done((bf16[512,3072]{1,0:T(8,128)(2,1)}, bf16[512,3072]{1,0:T(8,128)(2,1)}, u32[]{:S(2)}, u32[]{:S(2)}) %collective-permute-start.1) | collective-permute-done | bytes 3145760 | tf_op jit(solution)/shard_map/ppermute | solution.py:68
  130.6 4.8 %copy.36 = bf16[512,3072]{0,1:T(8,128)(2,1)} copy(bf16[512,3072]{1,0:T(8,128)(2,1)} %collective-permute-done.1) | data formatting | bytes 6291456 | tf_op jit(solution)/shard_map/reshape | solution.py:68
  135.4 4.0 %maximum_select_fusion = bf16[512,4,2,768]{0,3,2,1:T(8,128)(2,1)S(1)} fusion(bf16[512,4,1,768]{0,3,2,1:T(8,128)(2,1)} %bitcast.47, bf16[512,4,1,768]{0,3,2,1:T(8,128)(2,1)S(1)} %bitcast.46, pred[]{:T(512)S(6)} %eq.5), kind=kLoop, calls=%fused_computation.4 | loop fusion | flops 9437184 | bytes 12582913 | tf_op jit(solution)/shard_map/jit(_where)/select_n | solution.py:69
  139.4 1.7 fusion.35
  141.2 1.3 copy-done.1
  142.5 1.5 convolution_convert_fusion
  144.0 0.1 iota_compare_fusion
  144.1 9.3 %fusion.14 = f32[16,128,512]{2,1,0:T(8,128)} fusion(bf16[512,16,128]{0,2,1:T(8,128)(2,1)} %bitcast.53, bf16[512,16,128]{0,2,1:T(8,128)(2,1)} %bitcast.54, bf16[512,16,128]{0,2,1:T(8,128)(2,1)S(1)} %bitcast.51, pred[512,512]{1,0:T(8,128)(4,1)S(1)} %iota_compare_fusion), kind=kOutput, calls=%fused_computation.19 | convolution fusion | flops 2155872256 | bytes 10747904 | tf_op jit(solution)/shard_map/while/body/eval_jaxpr/hbc,che->bhe/dot_general | solution.py:34
  153.4 60.7 %all-gather.6.cloned.1.call-done = bf16[256,128,128]{2,1,0:T(8,128)(2,1)} async-done(((bf16[16,128,128]{2,1,0:T(8,128)(2,1)}), bf16[256,128,128]{2,1,0:T(8,128)(2,1)}) %all-gather.6.cloned.1.call-update) | async-done | bytes 8388624 | tf_op jit(solution)/shard_map/all_gather | solution.py:80
  214.0 8.4 %fusion = f32[1,16,128,128]{3,0,2,1:T(1,128)S(1)} fusion(bf16[16,16,128,128]{3,2,1,0:T(8,128)(2,1)} %bitcast.48, s32[]{:T(128)S(6)} %axis_index.22), kind=kOutput, calls=%fused_computation.2 | convolution fusion | flops 8388624 | bytes 9437188 | tf_op jit(solution)/shard_map/c,chde->hde/dot_general | solution.py:83
  222.5 0.8 fusion.11
  223.4 0.5 fusion.13
  223.9 2.4 %copy.26 = bf16[1,512,2048]{2,1,0:T(8,128)(2,1)} copy(bf16[1,512,2048]{1,2,0:T(8,128)(2,1)S(1)} %bitcast.49) | data formatting | bytes 4194304 | tf_op jit(solution)/shard_map/broadcast_in_dim;reshape | solution.py:86
  (18 shorter events, 0.1 us)
Async XLA Ops:
  6.5 97.9 %all-gather.4.cloned.1.call-start = ((), (), s32[]{:S(2)}) async-start(), calls=%async_computation | async-start | bytes 12779520 | tf_op jit(solution)/shard_map/all_gather | solution.py:60
  7.3 206.8 %all-gather.6.cloned.1.call-start = ((), (), s32[]{:S(2)}) async-start(), calls=%async_computation.1 | async-start | bytes 8912896 | tf_op jit(solution)/shard_map/all_gather | solution.py:80
  12.2 5.4 %collective-permute-start = (bf16[512,2048]{1,0:T(8,128)(2,1)S(1)}, bf16[512,2048]{1,0:T(8,128)(2,1)}, u32[]{:S(2)}, u32[]{:S(2)}) collective-permute-start(bf16[512,2048]{1,0:T(8,128)(2,1)S(1)} %fusion.4), channel_id=1, source_target_pairs={{0,16},{16,0},{1,17},{17,1},{2,18},{18,2},{3,19},{19,3},{4,20},{20... | collective-permute-start | bytes 6291464 | tf_op jit(solution)/shard_map/ppermute | solution.py:58
  124.3 6.3 %collective-permute-start.1 = (bf16[512,3072]{1,0:T(8,128)(2,1)}, bf16[512,3072]{1,0:T(8,128)(2,1)}, u32[]{:S(2)}, u32[]{:S(2)}) collective-permute-start(bf16[512,3072]{1,0:T(8,128)(2,1)} %get-tuple-element.23), channel_id=1, source_target_pairs={{0,16},{16,0},{1,17},{17,1},{2,18},{18,2},{3,19},{19,3},{4,20},{20... | collective-permute-start | bytes 9437192 | tf_op jit(solution)/shard_map/ppermute | solution.py:68
  127.8 7.6 %copy-start = (bf16[512,3072]{0,1:T(8,128)(2,1)S(1)}, bf16[512,3072]{0,1:T(8,128)(2,1)}, u32[]{:S(2)}) copy-start(bf16[512,3072]{0,1:T(8,128)(2,1)} %copy.35) | copy-start | bytes 9437188
  141.2 1.3 copy-start.1
  141.2 2.9 %copy-start.5 = (bf16[2048]{0:T(1024)(128)(2,1)S(1)}, bf16[2048]{0:T(1024)(128)(2,1)}, u32[]{:S(2)}) copy-start(bf16[2048]{0:T(1024)(128)(2,1)} %param.8) | copy-start | bytes 12292
  214.0 8.5 %copy-start.2 = (bf16[512,2048]{0,1:T(8,128)(2,1)S(1)}, bf16[512,2048]{0,1:T(8,128)(2,1)}, u32[]{:S(2)}) copy-start(bf16[512,2048]{0,1:T(8,128)(2,1)} %get-tuple-element.20) | copy-start | bytes 6291460
  214.0 8.5 %copy-start.3 = (f32[16,128,512]{2,1,0:T(8,128)S(1)}, f32[16,128,512]{2,1,0:T(8,128)}, u32[]{:S(2)}) copy-start(f32[16,128,512]{2,1,0:T(8,128)} %fusion.14) | copy-start | bytes 12582916
  214.0 8.5 %copy-start.4 = (f32[1,16,128,128]{3,2,1,0:T(8,128)S(1)}, f32[1,16,128,128]{3,2,1,0:T(8,128)}, u32[]{:S(2)}) copy-start(f32[1,16,128,128]{3,2,1,0:T(8,128)} %param.9) | copy-start | bytes 3145732
Sparse Core Ops, SparseCore 0:
  10.1 94.2 all-gather.3
  144.1 69.8 all-gather.5

commit v2 on v1

--- a/solution.py
+++ b/solution.py
@@ -48,6 +48,30 @@
     return outputs.reshape(num_blocks * BLOCK, H * DH)
 
 
+def ring_gather(value, axis, size):
+    here = lax.axis_index(axis)
+    out = jnp.zeros((size,) + value.shape, value.dtype)
+    out = lax.dynamic_update_index_in_dim(out, value, here, 0)
+    for shift in range(1, size):
+        got = lax.ppermute(value, axis, [(j, (j + shift) % size) for j in range(size)])
+        out = lax.dynamic_update_index_in_dim(out, got, (here - shift) % size, 0)
+    return out
+
+
+def gather_half_weight(qkv_weight):
+    wt = qkv_weight.T
+    n_part = 3
+    width = wt.shape[0] // n_part
+    orders = (("x", "y", "z"), ("y", "z", "x"), ("z", "x", "y"))
+    parts = []
+    for p in range(n_part):
+        piece = wt[p * width : (p + 1) * width]
+        for axis in orders[p]:
+            piece = ring_gather(piece, axis, lax.axis_size(axis))
+        parts.append(piece)
+    return parts, orders
+
+
 def body(tokens, input_gain, qkv_weight, head_gain, prefix_state):
     swap = [(0, 1), (1, 0)]
     core = lax.axis_index("c")
@@ -57,19 +81,34 @@
     tok_rows = normed.shape[0]
     partner = lax.ppermute(normed, "c", swap)
     both = jnp.concatenate([normed, partner], axis=0)
-    half_w = lax.all_gather(qkv_weight, ("z", "seq"), axis=1, tiled=True)
-    n_z = half_w.shape[1] // qkv_weight.shape[1] // lax.axis_size("seq")
-    span = half_w.shape[1] // n_z
-    projected = jnp.dot(both, half_w, preferred_element_type=jnp.float32)
-    col = jnp.arange(half_w.shape[1])
-    global_col = (2 * (col // span) + core) * span + col % span
-    feats = jnp.where(global_col < 2 * D, feature_map(projected), projected).astype(jnp.bfloat16)
-    mine = feats[:tok_rows].reshape(tok_rows, n_z, 1, span)
-    theirs = lax.ppermute(feats[tok_rows:], "c", swap).reshape(tok_rows, n_z, 1, span)
+    parts, orders = gather_half_weight(qkv_weight)
+    n_c = 2
+    sizes = {a: lax.axis_size(a) for a in ("z", "y", "x")}
+    width = parts[0].shape[-2]
+    per_dev = width * len(parts)
+    mine, theirs = [], []
+    for p, wpart in enumerate(parts):
+        names = orders[p][::-1]
+        dims = [sizes[a] for a in names]
+        proj = jnp.dot(both, wpart.reshape(-1, wpart.shape[-1]).T, preferred_element_type=jnp.float32)
+        proj = proj.reshape([2 * tok_rows] + dims + [width])
+        coord = {}
+        for k, a in enumerate(names):
+            shape = [1] * 5
+            shape[k + 1] = dims[k]
+            coord[a] = jnp.arange(dims[k]).reshape(shape)
+        dev = ((coord["z"] * n_c + core) * sizes["y"] + coord["y"]) * sizes["x"] + coord["x"]
+        global_col = dev * per_dev + p * width + jnp.arange(width).reshape(1, 1, 1, 1, width)
+        feats = jnp.where(global_col < 2 * D, feature_map(proj), proj).astype(jnp.bfloat16)
+        back = [0] + [1 + names.index(a) for a in ("z", "y", "x")] + [4]
+        mine.append(jnp.transpose(feats[:tok_rows], back))
+        theirs.append(jnp.transpose(lax.ppermute(feats[tok_rows:], "c", swap), back))
+    mine = jnp.stack(mine, axis=-2)
+    theirs = jnp.stack(theirs, axis=-2)
     full = jnp.where(
         core == 0,
-        jnp.concatenate([mine, theirs], axis=2),
-        jnp.concatenate([theirs, mine], axis=2),
+        jnp.stack([mine, theirs], axis=2),
+        jnp.stack([theirs, mine], axis=2),
     ).reshape(tok_rows, 3 * D)
     queries = full[:, :D].reshape(tok_rows, H, DH)
     key_feats = full[:, D : 2 * D].reshape(tok_rows, H, DH)
@@ -77,8 +116,8 @@
     local = jnp.einsum(
         "thd,the->hde", key_feats, values, preferred_element_type=jnp.float32
     ).astype(jnp.bfloat16)
-    gathered = lax.all_gather(local[None], "seq", axis=0, tiled=True)
-    my_index = lax.axis_index("seq")
+    gathered = lax.all_gather(local[None], ("y", "x"), axis=0, tiled=True)
+    my_index = lax.axis_index(("y", "x"))
     earlier = (jnp.arange(gathered.shape[0]) < my_index).astype(jnp.bfloat16)
     before = jnp.einsum("c,chde->hde", earlier, gathered, preferred_element_type=jnp.float32)
     memory = prefix_state[0] + before
@@ -88,9 +127,11 @@
 
 def solution(mesh):
     n_dp, n_seq = mesh.devices.shape
-    split = Mesh(mesh.devices.reshape(n_dp // 2, 2, n_seq), ("z", "c", "seq"))
+    n_x = int(round(n_seq ** 0.5))
+    split = Mesh(mesh.devices.reshape(n_dp // 2, 2, n_seq // n_x, n_x), ("z", "c", "y", "x"))
     rows = ("z", "c")
-    placed = (P(rows, "seq", None), P(), P(None, ("z", "c", "seq")), P(), P(rows, None, None, None))
+    cols = ("y", "x")
+    placed = (P(rows, cols, None), P(), P(None, ("z", "c", "y", "x")), P(), P(rows, None, None, None))
     return jax.shard_map(
-        body, mesh=split, in_specs=placed, out_specs=P(rows, "seq", None), check_vma=False
+        body, mesh=split, in_specs=placed, out_specs=P(rows, cols, None), check_vma=False
     )

time: 233 us -> 297 us (1.27)
  starting transfers between devices: 2.21 us -> 51.1 us
  waiting for transfers between devices: 155 us -> 167 us
  matrix products: 37.8 us -> 34.6 us
    ppermute x1 -> x30, waiting for transfers between devices: 2.83 us -> 108 us  [the longest x27 105 us: ring_gather(): lax.ppermute(value, axis, [(j, (j + shift) % size) for j in range(size)])]
    all_gather x2 -> x1, waiting for transfers between devices: 147 us -> 59.9 us  [body(): gathered = lax.all_gather(local[None], ('y', 'x'), axis=0, tiled=True)]
    ppermute x1 -> x30, starting transfers between devices: 0.67 us -> 47.9 us  [the longest x27 33.2 us: ring_gather(): lax.ppermute(value, axis, [(j, (j + shift) % size) for j in range(size)])]
    reshape x2 -> x0, local copies, waits for them, and re-layouts: 7.57 us -> none  [the longest x1 4.77 us: body(): lax.ppermute(feats[tok_rows:], 'c', swap).reshape(tok_rows, n_z, 1, span)]
    another operation x0 -> x12, local copies, waits for them, and re-layouts: none -> 5.72 us  [the longest x3 3.78 us: body(): mine = jnp.stack(mine, axis=-2)]
    ppermute x1, waiting for transfers between devices: 3.9 us -> 0.01 us  [body(): partner = lax.ppermute(normed, 'c', swap)]
    dot_general x1 -> x3, matrix products: 17.7 us -> 14.4 us  [body(): jnp.dot(both, wpart.reshape(-1, wpart.shape[-1]).T, preferred_element_typ...]
    select_n x1, other arithmetic: 4.04 us -> 1.03 us  [body(): jnp.where(core == 0, jnp.stack([mine, theirs], axis=2), jnp.stack([theirs...]
  transfers between devices with their start and end apart: 4 -> 32, of which waited for: 4 -> 13; matrix products, arithmetic and copies ran while one was open for 7% -> 11% of each run, Pallas kernels for 0% -> 0%
where the time goes in v2:
time: 297 us; the launch traced here: 294 us
  waiting for transfers between devices  167 us (56%)
  starting transfers between devices  51.1 us (17%)
  matrix products  34.6 us (12%)
  local copies, waits for them, and re-layouts  16 us (5%)
  between operations  14.5 us (5%)
  other arithmetic  10.6 us (4%)
    ppermute x27, waiting for transfers between devices, ring_gather(): lax.ppermute(value, axis, [(j, (j + shift) % size) for j in range(size)])  105 us
    all_gather x1, waiting for transfers between devices, body(): gathered = lax.all_gather(local[None], ('y', 'x'), axis=0, tiled=True)  59.9 us
    ppermute x27, starting transfers between devices, ring_gather(): lax.ppermute(value, axis, [(j, (j + shift) % size) for j in range(size)])  33.2 us
    ppermute x3, starting transfers between devices, body(): lax.ppermute(feats[tok_rows:], 'c', swap)  14.7 us
    dot_general x3, matrix products, body(): jnp.dot(both, wpart.reshape(-1, wpart.shape[-1]).T, preferred_element_typ...  14.4 us
    dot_general x1, matrix products, advance(): jnp.einsum('hbc,che->bhe', scores, value_blk, preferred_element_type=jnp....  9.33 us
    dot_general x1, matrix products, body(): jnp.einsum('c,chde->hde', earlier, gathered, preferred_element_type=jnp.f...  8.45 us
  transfers between devices with their start and end apart: 32, of which 13 were waited for; matrix products, arithmetic and copies ran while one was open for 11% of the time, Pallas kernels for 0%

profile of v2, /device:TPU:1, one launch (start us, length us, event | category | flops | bytes accessed | tf_op | source)
XLA Modules:
  0.0 294.2 jit_solution(13095927377618866298)
XLA Ops:
  7.6 2.5 collective-permute-start.19
  10.1 3.3 %collective-permute-start.20 = (bf16[16,2048]{1,0:T(8,128)(2,1)S(1)}, bf16[16,2048]{1,0:T(8,128)(2,1)S(1)}, u32[]{:S(2)}, u32[]{:S(2)}) collective-permute-start(bf16[16,2048]{1,0:T(8,128)(2,1)S(1)} %get-tuple-element.39), channel_id=1, source_target_pairs={{0,64},{32,96},{64,0},{96,32},{1,65},{33,97},{65,1},{97,33},{2,66}... | collective-permute-start | bytes 196616 | tf_op jit(solution)/shard_map/ppermute | solution.py:56
  15.4 2.5 collective-permute-start.2
  26.9 2.7 collective-permute-start.11
  30.9 3.3 %collective-permute-start = (bf16[512,2048]{1,0:T(8,128)(2,1)}, bf16[512,2048]{1,0:T(8,128)(2,1)S(1)}, u32[]{:S(2)}, u32[]{:S(2)}) collective-permute-start(bf16[512,2048]{1,0:T(8,128)(2,1)} %fusion.4), channel_id=1, source_target_pairs={{0,16},{16,0},{1,17},{17,1},{2,18},{18,2},{3,19},{19,3},{4,20},{20... | collective-permute-start | bytes 6291464 | tf_op jit(solution)/shard_map/ppermute | solution.py:82
  38.0 11.0 %collective-permute-done.22 = bf16[4,16,2048]{2,1,0:T(8,128)(2,1)S(1)} collective-permute-done((bf16[4,16,2048]{2,1,0:T(8,128)(2,1)S(1)}, bf16[4,16,2048]{2,1,0:T(8,128)(2,1)S(1)}, u32[]{:S(2)}, u32[]{:S(2)}) %collective-permute-start.22) | collective-permute-done | bytes 262176 | tf_op jit(solution)/shard_map/ppermute | solution.py:56
  49.1 2.8 collective-permute-start.6
  53.7 3.8 %collective-permute-done.5 = bf16[4,16,2048]{2,1,0:T(8,128)(2,1)S(1)} collective-permute-done((bf16[4,16,2048]{2,1,0:T(8,128)(2,1)S(1)}, bf16[4,16,2048]{2,1,0:T(8,128)(2,1)S(1)}, u32[]{:S(2)}, u32[]{:S(2)}) %collective-permute-start.5) | collective-permute-done | bytes 262176 | tf_op jit(solution)/shard_map/ppermute | solution.py:56
  57.6 3.2 %collective-permute-done.6 = bf16[4,16,2048]{2,1,0:T(8,128)(2,1)S(1)} collective-permute-done((bf16[4,16,2048]{2,1,0:T(8,128)(2,1)S(1)}, bf16[4,16,2048]{2,1,0:T(8,128)(2,1)S(1)}, u32[]{:S(2)}, u32[]{:S(2)}) %collective-permute-start.6) | collective-permute-done | bytes 262176 | tf_op jit(solution)/shard_map/ppermute | solution.py:56
  60.8 2.7 collective-permute-start.25
  68.8 17.9 %collective-permute-done.25 = bf16[4,4,16,2048]{3,2,1,0:T(8,128)(2,1)S(1)} collective-permute-done((bf16[4,4,16,2048]{3,2,1,0:T(8,128)(2,1)S(1)}, bf16[4,4,16,2048]{3,2,1,0:T(8,128)(2,1)S(1)}, u32[]{:S(2)}, u32[]{:S(2)}) %collective-permute-start.25) | collective-permute-done | bytes 1048608 | tf_op jit(solution)/shard_map/ppermute | solution.py:56
  87.0 23.6 %collective-permute-done.26 = bf16[4,4,16,2048]{3,2,1,0:T(8,128)(2,1)S(1)} collective-permute-done((bf16[4,4,16,2048]{3,2,1,0:T(8,128)(2,1)S(1)}, bf16[4,4,16,2048]{3,2,1,0:T(8,128)(2,1)S(1)}, u32[]{:S(2)}, u32[]{:S(2)}) %collective-permute-start.26) | collective-permute-done | bytes 1048608 | tf_op jit(solution)/shard_map/ppermute | solution.py:56
  113.3 3.9 %collective-permute-done.8 = bf16[4,4,16,2048]{3,2,1,0:T(8,128)(2,1)S(1)} collective-permute-done((bf16[4,4,16,2048]{3,2,1,0:T(8,128)(2,1)S(1)}, bf16[4,4,16,2048]{3,2,1,0:T(8,128)(2,1)S(1)}, u32[]{:S(2)}, u32[]{:S(2)}) %collective-permute-start.8) | collective-permute-done | bytes 1048608 | tf_op jit(solution)/shard_map/ppermute | solution.py:56
  117.6 16.6 %collective-permute-done.9 = bf16[4,4,16,2048]{3,2,1,0:T(8,128)(2,1)S(1)} collective-permute-done((bf16[4,4,16,2048]{3,2,1,0:T(8,128)(2,1)S(1)}, bf16[4,4,16,2048]{3,2,1,0:T(8,128)(2,1)S(1)}, u32[]{:S(2)}, u32[]{:S(2)}) %collective-permute-start.9) | collective-permute-done | bytes 1048608 | tf_op jit(solution)/shard_map/ppermute | solution.py:56
  136.7 20.4 %collective-permute-done.17 = bf16[4,4,16,2048]{3,2,1,0:T(8,128)(2,1)S(1)} collective-permute-done((bf16[4,4,16,2048]{3,2,1,0:T(8,128)(2,1)S(1)}, bf16[4,4,16,2048]{3,2,1,0:T(8,128)(2,1)S(1)}, u32[]{:S(2)}, u32[]{:S(2)}) %collective-permute-start.17) | collective-permute-done | bytes 1048608 | tf_op jit(solution)/shard_map/ppermute | solution.py:56
  157.2 2.4 collective-permute-done.18
  159.8 5.0 %select_convert_fusion.1 = bf16[1024,4,4,4,16]{0,4,2,1,3:T(8,128)(2,1)S(1)} fusion(bf16[4,4,4,16,2048]{4,3,2,1,0:T(8,128)(2,1)S(1)} %bitcast_dynamic-update-slice_fusion, pred[4,4,4,16]{3,1,0,2:T(4,128)(4,1)S(1)} %add_compare_fusion, bf16[512,2048]{1,0:T(8,128)(2,1)S(1)} %collective-permute-done, bf16[512,2048]{1,0:T(8,128)(2,1)S(1)} %copy-done.4), kind=kOutput, calls=%fused_computation.25 | convolution fusion | flops 4309647360 | bytes 10486784 | tf_op jit(solution)/shard_map/dot_general | solution.py:93
  167.5 4.5 %fusion.5 = f32[1024,4,4,4,16]{0,4,3,2,1:T(8,128)S(1)} fusion(bf16[4,4,4,16,2048]{4,3,2,1,0:T(8,128)(2,1)S(1)} %bitcast_dynamic-update-slice_fusion.8, bf16[512,2048]{1,0:T(8,128)(2,1)S(1)} %collective-permute-done, bf16[512,2048]{1,0:T(8,128)(2,1)S(1)} %copy-done.4), kind=kOutput, calls=%fused_computation.10 | convolution fusion | flops 4303355904 | bytes 12582912 | tf_op jit(solution)/shard_map/dot_general | solution.py:93
  174.5 12.7 %collective-permute-start.28 = (bf16[512,4,4,4,16]{0,4,3,2,1:T(8,128)(2,1)}, bf16[512,4,4,4,16]{0,4,3,2,1:T(8,128)(2,1)}, u32[]{:S(2)}, u32[]{:S(2)}) collective-permute-start(bf16[512,4,4,4,16]{0,4,3,2,1:T(8,128)(2,1)} %get-tuple-element.23), channel_id=1, source_target_pairs={{0,16},{16,0},{1,17},{17,1},{2,18},{18,2},{3,19},{19,3},{4,20},{20... | collective-permute-start | bytes 3145736 | tf_op jit(solution)/shard_map/ppermute | solution.py:105
  187.1 5.0 %select_convert_fusion.2 = bf16[1024,4,4,4,16]{0,4,2,1,3:T(8,128)(2,1)S(1)} fusion(bf16[4,4,4,16,2048]{4,3,2,1,0:T(8,128)(2,1)S(1)} %bitcast_dynamic-update-slice_fusion.4, pred[4,4,4,16]{3,1,0,2:T(4,128)(4,1)S(1)} %add_compare_fusion.1, bf16[512,2048]{1,0:T(8,128)(2,1)S(1)} %collective-permute-done, bf16[512,2048]{1,0:T(8,128)(2,1)S(1)} %copy-done.4), kind=kOutput, calls=%fused_computation.26 | convolution fusion | flops 4309647360 | bytes 10486784 | tf_op jit(solution)/shard_map/dot_general | solution.py:93
  205.6 9.3 %fusion.17 = f32[16,128,512]{2,1,0:T(8,128)} fusion(bf16[512,16,128]{0,2,1:T(8,128)(2,1)} %bitcast.161, bf16[512,16,128]{0,2,1:T(8,128)(2,1)} %bitcast.162, bf16[512,16,128]{0,2,1:T(8,128)(2,1)S(1)} %bitcast.159, pred[512,512]{1,0:T(8,128)(4,1)S(1)} %iota_compare_fusion), kind=kOutput, calls=%fused_computation.30 | convolution fusion | flops 2155872256 | bytes 10747904 | tf_op jit(solution)/shard_map/while/body/eval_jaxpr/hbc,che->bhe/dot_general | solution.py:34
  215.0 59.9 %all-gather.3.cloned.1.call-done = bf16[256,128,128]{2,1,0:T(8,128)(2,1)} async-done(((bf16[16,128,128]{2,1,0:T(8,128)(2,1)}), bf16[256,128,128]{2,1,0:T(8,128)(2,1)}) %all-gather.3.cloned.1.call-update) | async-done | bytes 8388624 | tf_op jit(solution)/shard_map/all_gather | solution.py:119
  274.9 8.4 %fusion = f32[1,16,128,128]{3,0,2,1:T(1,128)S(1)} fusion(bf16[16,16,128,128]{3,2,1,0:T(8,128)(2,1)} %bitcast.156, s32[]{:T(128)S(6)} %add.367), kind=kOutput, calls=%fused_computation.1 | convolution fusion | flops 8388624 | bytes 9437188 | tf_op jit(solution)/shard_map/c,chde->hde/dot_general | solution.py:122
  284.8 2.4 copy.68
  (138 shorter events, 49.9 us)
Async XLA Ops:
  6.5 268.4 %all-gather.3.cloned.1.call-start = ((), (), s32[]{:S(2)}) async-start(), calls=%async_computation | async-start | bytes 8912896 | tf_op jit(solution)/shard_map/all_gather | solution.py:119
  7.6 16.6 %collective-permute-start.19 = (bf16[16,2048]{1,0:T(8,128)(2,1)S(1)}, bf16[16,2048]{1,0:T(8,128)(2,1)S(1)}, u32[]{:S(2)}, u32[]{:S(2)}) collective-permute-start(bf16[16,2048]{1,0:T(8,128)(2,1)S(1)} %get-tuple-element.39), channel_id=1, source_target_pairs={{0,32},{32,64},{64,96},{96,0},{1,33},{33,65},{65,97},{97,1},{2,34}... | collective-permute-start | bytes 196616 | tf_op jit(solution)/shard_map/ppermute | solution.py:56
  10.1 15.4 %collective-permute-start.20 = (bf16[16,2048]{1,0:T(8,128)(2,1)S(1)}, bf16[16,2048]{1,0:T(8,128)(2,1)S(1)}, u32[]{:S(2)}, u32[]{:S(2)}) collective-permute-start(bf16[16,2048]{1,0:T(8,128)(2,1)S(1)} %get-tuple-element.39), channel_id=1, source_target_pairs={{0,64},{32,96},{64,0},{96,32},{1,65},{33,97},{65,1},{97,33},{2,66}... | collective-permute-start | bytes 196616 | tf_op jit(solution)/shard_map/ppermute | solution.py:56
  13.4 13.4 %collective-permute-start.21 = (bf16[16,2048]{1,0:T(8,128)(2,1)S(1)}, bf16[16,2048]{1,0:T(8,128)(2,1)S(1)}, u32[]{:S(2)}, u32[]{:S(2)}) collective-permute-start(bf16[16,2048]{1,0:T(8,128)(2,1)S(1)} %get-tuple-element.39), channel_id=1, source_target_pairs={{0,96},{32,0},{64,32},{96,64},{1,97},{33,1},{65,33},{97,65},{2,98}... | collective-permute-start | bytes 196616 | tf_op jit(solution)/shard_map/ppermute | solution.py:56
  14.2 15.6 %collective-permute-start.1 = (bf16[16,2048]{1,0:T(8,128)(2,1)S(1)}, bf16[16,2048]{1,0:T(8,128)(2,1)S(1)}, u32[]{:S(2)}, u32[]{:S(2)}) collective-permute-start(bf16[16,2048]{1,0:T(8,128)(2,1)S(1)} %get-tuple-element.38), channel_id=1, source_target_pairs={{0,1},{1,2},{2,3},{3,0},{4,5},{5,6},{6,7},{7,4},{8,9},{9,10},{10,1... | collective-permute-start | bytes 196616 | tf_op jit(solution)/shard_map/ppermute | solution.py:56
  15.4 15.5 %collective-permute-start.2 = (bf16[16,2048]{1,0:T(8,128)(2,1)S(1)}, bf16[16,2048]{1,0:T(8,128)(2,1)S(1)}, u32[]{:S(2)}, u32[]{:S(2)}) collective-permute-start(bf16[16,2048]{1,0:T(8,128)(2,1)S(1)} %get-tuple-element.38), channel_id=1, source_target_pairs={{0,2},{1,3},{2,0},{3,1},{4,6},{5,7},{6,4},{7,5},{8,10},{9,11},{10,... | collective-permute-start | bytes 196616 | tf_op jit(solution)/shard_map/ppermute | solution.py:56
  30.9 128.8 %collective-permute-start = (bf16[512,2048]{1,0:T(8,128)(2,1)}, bf16[512,2048]{1,0:T(8,128)(2,1)S(1)}, u32[]{:S(2)}, u32[]{:S(2)}) collective-permute-start(bf16[512,2048]{1,0:T(8,128)(2,1)} %fusion.4), channel_id=1, source_target_pairs={{0,16},{16,0},{1,17},{17,1},{2,18},{18,2},{3,19},{19,3},{4,20},{20... | collective-permute-start | bytes 6291464 | tf_op jit(solution)/shard_map/ppermute | solution.py:82
  34.2 14.8 %collective-permute-start.22 = (bf16[4,16,2048]{2,1,0:T(8,128)(2,1)S(1)}, bf16[4,16,2048]{2,1,0:T(8,128)(2,1)S(1)}, u32[]{:S(2)}, u32[]{:S(2)}) collective-permute-start(bf16[4,16,2048]{2,1,0:T(8,128)(2,1)S(1)} %bitcast_dynamic-update-slice_fusion.24), channel_id=1, source_target_pairs={{0,1},{1,2},{2,3},{3,0},{4,5},{5,6},{6,7},{7,4},{8,9},{9,10},{10,1... | collective-permute-start | bytes 786440 | tf_op jit(solution)/shard_map/ppermute | solution.py:56
  34.8 14.3 %collective-permute-start.23 = (bf16[4,16,2048]{2,1,0:T(8,128)(2,1)S(1)}, bf16[4,16,2048]{2,1,0:T(8,128)(2,1)S(1)}, u32[]{:S(2)}, u32[]{:S(2)}) collective-permute-start(bf16[4,16,2048]{2,1,0:T(8,128)(2,1)S(1)} %bitcast_dynamic-update-slice_fusion.24), channel_id=1, source_target_pairs={{0,2},{1,3},{2,0},{3,1},{4,6},{5,7},{6,4},{7,5},{8,10},{9,11},{10,... | collective-permute-start | bytes 786440 | tf_op jit(solution)/shard_map/ppermute | solution.py:56
  35.5 16.5 %collective-permute-start.24 = (bf16[4,16,2048]{2,1,0:T(8,128)(2,1)S(1)}, bf16[4,16,2048]{2,1,0:T(8,128)(2,1)S(1)}, u32[]{:S(2)}, u32[]{:S(2)}) collective-permute-start(bf16[4,16,2048]{2,1,0:T(8,128)(2,1)S(1)} %bitcast_dynamic-update-slice_fusion.24), channel_id=1, source_target_pairs={{0,3},{1,0},{2,1},{3,2},{4,7},{5,4},{6,5},{7,6},{8,11},{9,8},{10,9... | collective-permute-start | bytes 786440 | tf_op jit(solution)/shard_map/ppermute | solution.py:56
  37.4 16.1 %collective-permute-start.4 = (bf16[4,16,2048]{2,1,0:T(8,128)(2,1)S(1)}, bf16[4,16,2048]{2,1,0:T(8,128)(2,1)S(1)}, u32[]{:S(2)}, u32[]{:S(2)}) collective-permute-start(bf16[4,16,2048]{2,1,0:T(8,128)(2,1)S(1)} %bitcast_dynamic-update-slice_fusion.32), channel_id=1, source_target_pairs={{0,4},{4,8},{8,12},{12,0},{1,5},{5,9},{9,13},{13,1},{2,6},{6,10},{... | collective-permute-start | bytes 786440 | tf_op jit(solution)/shard_map/ppermute | solution.py:56
  52.0 12.2 %collective-permute-start.13 = (bf16[4,16,2048]{2,1,0:T(8,128)(2,1)S(1)}, bf16[4,16,2048]{2,1,0:T(8,128)(2,1)S(1)}, u32[]{:S(2)}, u32[]{:S(2)}) collective-permute-start(bf16[4,16,2048]{2,1,0:T(8,128)(2,1)S(1)} %bitcast_dynamic-update-slice_fusion.28), channel_id=1, source_target_pairs={{0,32},{32,64},{64,96},{96,0},{1,33},{33,65},{65,97},{97,1},{2,34}... | collective-permute-start | bytes 786440 | tf_op jit(solution)/shard_map/ppermute | solution.py:56
  53.5 12.7 %collective-permute-start.14 = (bf16[4,16,2048]{2,1,0:T(8,128)(2,1)S(1)}, bf16[4,16,2048]{2,1,0:T(8,128)(2,1)S(1)}, u32[]{:S(2)}, u32[]{:S(2)}) collective-permute-start(bf16[4,16,2048]{2,1,0:T(8,128)(2,1)S(1)} %bitcast_dynamic-update-slice_fusion.28), channel_id=1, source_target_pairs={{0,64},{32,96},{64,0},{96,32},{1,65},{33,97},{65,1},{97,33},{2,66}... | collective-permute-start | bytes 786440 | tf_op jit(solution)/shard_map/ppermute | solution.py:56
  60.8 25.8 %collective-permute-start.25 = (bf16[4,4,16,2048]{3,2,1,0:T(8,128)(2,1)S(1)}, bf16[4,4,16,2048]{3,2,1,0:T(8,128)(2,1)S(1)}, u32[]{:S(2)}, u32[]{:S(2)}) collective-permute-start(bf16[4,4,16,2048]{3,2,1,0:T(8,128)(2,1)S(1)} %bitcast_dynamic-update-slice_fusion.12), channel_id=1, source_target_pairs={{0,4},{4,8},{8,12},{12,0},{1,5},{5,9},{9,13},{13,1},{2,6},{6,10},{... | collective-permute-start | bytes 3145736 | tf_op jit(solution)/shard_map/ppermute | solution.py:56
  64.2 46.4 %collective-permute-start.26 = (bf16[4,4,16,2048]{3,2,1,0:T(8,128)(2,1)S(1)}, bf16[4,4,16,2048]{3,2,1,0:T(8,128)(2,1)S(1)}, u32[]{:S(2)}, u32[]{:S(2)}) collective-permute-start(bf16[4,4,16,2048]{3,2,1,0:T(8,128)(2,1)S(1)} %bitcast_dynamic-update-slice_fusion.12), channel_id=1, source_target_pairs={{0,8},{4,12},{8,0},{12,4},{1,9},{5,13},{9,1},{13,5},{2,10},{6,14},... | collective-permute-start | bytes 3145736 | tf_op jit(solution)/shard_map/ppermute | solution.py:56
  66.2 44.8 %collective-permute-start.27 = (bf16[4,4,16,2048]{3,2,1,0:T(8,128)(2,1)S(1)}, bf16[4,4,16,2048]{3,2,1,0:T(8,128)(2,1)S(1)}, u32[]{:S(2)}, u32[]{:S(2)}) collective-permute-start(bf16[4,4,16,2048]{3,2,1,0:T(8,128)(2,1)S(1)} %bitcast_dynamic-update-slice_fusion.12), channel_id=1, source_target_pairs={{0,12},{4,0},{8,4},{12,8},{1,13},{5,1},{9,5},{13,9},{2,14},{6,2},{... | collective-permute-start | bytes 3145736 | tf_op jit(solution)/shard_map/ppermute | solution.py:56
  67.4 43.8 %collective-permute-start.7 = (bf16[4,4,16,2048]{3,2,1,0:T(8,128)(2,1)S(1)}, bf16[4,4,16,2048]{3,2,1,0:T(8,128)(2,1)S(1)}, u32[]{:S(2)}, u32[]{:S(2)}) collective-permute-start(bf16[4,4,16,2048]{3,2,1,0:T(8,128)(2,1)S(1)} %bitcast_dynamic-update-slice_fusion.20), channel_id=1, source_target_pairs={{0,32},{32,64},{64,96},{96,0},{1,33},{33,65},{65,97},{97,1},{2,34}... | collective-permute-start | bytes 3145736 | tf_op jit(solution)/shard_map/ppermute | solution.py:56
  86.6 30.6 %collective-permute-start.8 = (bf16[4,4,16,2048]{3,2,1,0:T(8,128)(2,1)S(1)}, bf16[4,4,16,2048]{3,2,1,0:T(8,128)(2,1)S(1)}, u32[]{:S(2)}, u32[]{:S(2)}) collective-permute-start(bf16[4,4,16,2048]{3,2,1,0:T(8,128)(2,1)S(1)} %bitcast_dynamic-update-slice_fusion.20), channel_id=1, source_target_pairs={{0,64},{32,96},{64,0},{96,32},{1,65},{33,97},{65,1},{97,33},{2,66}... | collective-permute-start | bytes 3145736 | tf_op jit(solution)/shard_map/ppermute | solution.py:56
  110.6 23.6 %collective-permute-start.9 = (bf16[4,4,16,2048]{3,2,1,0:T(8,128)(2,1)S(1)}, bf16[4,4,16,2048]{3,2,1,0:T(8,128)(2,1)S(1)}, u32[]{:S(2)}, u32[]{:S(2)}) collective-permute-start(bf16[4,4,16,2048]{3,2,1,0:T(8,128)(2,1)S(1)} %bitcast_dynamic-update-slice_fusion.20), channel_id=1, source_target_pairs={{0,96},{32,0},{64,32},{96,64},{1,97},{33,1},{65,33},{97,65},{2,98}... | collective-permute-start | bytes 3145736 | tf_op jit(solution)/shard_map/ppermute | solution.py:56
  111.0 25.6 %collective-permute-start.16 = (bf16[4,4,16,2048]{3,2,1,0:T(8,128)(2,1)S(1)}, bf16[4,4,16,2048]{3,2,1,0:T(8,128)(2,1)S(1)}, u32[]{:S(2)}, u32[]{:S(2)}) collective-permute-start(bf16[4,4,16,2048]{3,2,1,0:T(8,128)(2,1)S(1)} %bitcast_dynamic-update-slice_fusion.16), channel_id=1, source_target_pairs={{0,1},{1,2},{2,3},{3,0},{4,5},{5,6},{6,7},{7,4},{8,9},{9,10},{10,1... | collective-permute-start | bytes 3145736 | tf_op jit(solution)/shard_map/ppermute | solution.py:56
  111.3 45.8 %collective-permute-start.17 = (bf16[4,4,16,2048]{3,2,1,0:T(8,128)(2,1)S(1)}, bf16[4,4,16,2048]{3,2,1,0:T(8,128)(2,1)S(1)}, u32[]{:S(2)}, u32[]{:S(2)}) collective-permute-start(bf16[4,4,16,2048]{3,2,1,0:T(8,128)(2,1)S(1)} %bitcast_dynamic-update-slice_fusion.16), channel_id=1, source_target_pairs={{0,2},{1,3},{2,0},{3,1},{4,6},{5,7},{6,4},{7,5},{8,10},{9,11},{10,... | collective-permute-start | bytes 3145736 | tf_op jit(solution)/shard_map/ppermute | solution.py:56
  117.2 42.4 %collective-permute-start.18 = (bf16[4,4,16,2048]{3,2,1,0:T(8,128)(2,1)S(1)}, bf16[4,4,16,2048]{3,2,1,0:T(8,128)(2,1)S(1)}, u32[]{:S(2)}, u32[]{:S(2)}) collective-permute-start(bf16[4,4,16,2048]{3,2,1,0:T(8,128)(2,1)S(1)} %bitcast_dynamic-update-slice_fusion.16), channel_id=1, source_target_pairs={{0,3},{1,0},{2,1},{3,2},{4,7},{5,4},{6,5},{7,6},{8,11},{9,8},{10,9... | collective-permute-start | bytes 3145736 | tf_op jit(solution)/shard_map/ppermute | solution.py:56
  166.0 28.3 %collective-permute-start.30 = (bf16[512,4,4,4,16]{0,4,2,1,3:T(8,128)(2,1)}, bf16[512,4,4,4,16]{0,4,2,1,3:T(8,128)(2,1)}, u32[]{:S(2)}, u32[]{:S(2)}) collective-permute-start(bf16[512,4,4,4,16]{0,4,2,1,3:T(8,128)(2,1)} %get-tuple-element.37), channel_id=1, source_target_pairs={{0,16},{16,0},{1,17},{17,1},{2,18},{18,2},{3,19},{19,3},{4,20},{20... | collective-permute-start | bytes 3145736 | tf_op jit(solution)/shard_map/ppermute | solution.py:105
  174.5 19.8 %collective-permute-start.28 = (bf16[512,4,4,4,16]{0,4,3,2,1:T(8,128)(2,1)}, bf16[512,4,4,4,16]{0,4,3,2,1:T(8,128)(2,1)}, u32[]{:S(2)}, u32[]{:S(2)}) collective-permute-start(bf16[512,4,4,4,16]{0,4,3,2,1:T(8,128)(2,1)} %get-tuple-element.23), channel_id=1, source_target_pairs={{0,16},{16,0},{1,17},{17,1},{2,18},{18,2},{3,19},{19,3},{4,20},{20... | collective-permute-start | bytes 3145736 | tf_op jit(solution)/shard_map/ppermute | solution.py:105
  (16 other events, 173.1 us)
Sparse Core Ops, SparseCore 0:
  205.6 69.2 all-gather.2

commit v3 on v0

--- a/solution.py
+++ b/solution.py
@@ -1,7 +1,7 @@
 import jax
 import jax.numpy as jnp
 from jax import lax
-from jax.sharding import PartitionSpec as P
+from jax.sharding import Mesh, PartitionSpec as P
 
 D = 2048
 H = 16
@@ -53,28 +53,33 @@
     normed = inputs * lax.rsqrt(jnp.mean(inputs * inputs, axis=-1, keepdims=True) + epsilon)
     normed = (normed * input_gain.astype(jnp.float32)).astype(jnp.bfloat16)
     tok_rows = normed.shape[0]
-    projected = jnp.dot(
-        normed,
-        lax.all_gather(qkv_weight, ("dp", "seq"), axis=1, tiled=True),
-        preferred_element_type=jnp.float32,
-    )
-    queries = feature_map(projected[:, :D]).astype(jnp.bfloat16).reshape(tok_rows, H, DH)
-    key_feats = feature_map(projected[:, D : 2 * D]).astype(jnp.bfloat16).reshape(tok_rows, H, DH)
-    values = projected[:, 2 * D :].astype(jnp.bfloat16).reshape(tok_rows, H, DH)
+    weight = lax.all_gather(qkv_weight, ("dp", "y", "x"), axis=1, tiled=True)
+    kv = jnp.dot(normed, weight[:, D:], preferred_element_type=jnp.float32)
+    key_feats = feature_map(kv[:, :D]).astype(jnp.bfloat16).reshape(tok_rows, H, DH)
+    values = kv[:, D:].astype(jnp.bfloat16).reshape(tok_rows, H, DH)
     local = jnp.einsum(
         "thd,the->hde", key_feats, values, preferred_element_type=jnp.float32
     ).astype(jnp.bfloat16)
-    gathered = lax.all_gather(local[None], "seq", axis=0, tiled=True)
-    my_index = lax.axis_index("seq")
-    earlier = (jnp.arange(gathered.shape[0]) < my_index).astype(jnp.bfloat16)
-    before = jnp.einsum("c,chde->hde", earlier, gathered, preferred_element_type=jnp.float32)
-    memory = prefix_state[0] + before
+    row = lax.all_gather(local, "x", axis=0).astype(jnp.float32)
+    x_here = lax.axis_index("x")
+    y_here = lax.axis_index("y")
+    row_before = jnp.sum(jnp.where((jnp.arange(row.shape[0]) < x_here)[:, None, None, None], row, 0.0), axis=0)
+    row_total = jnp.sum(row, axis=0)
+    totals = lax.all_gather(row_total, "y", axis=0)
+    rows_before = jnp.sum(jnp.where((jnp.arange(totals.shape[0]) < y_here)[:, None, None, None], totals, 0.0), axis=0)
+    memory = prefix_state[0] + (rows_before + row_before)
+    q = jnp.dot(normed, weight[:, :D], preferred_element_type=jnp.float32)
+    queries = feature_map(q).astype(jnp.bfloat16).reshape(tok_rows, H, DH)
     attended = span_attention(queries, key_feats, values, memory, head_gain)
     return attended[None]
 
 
 def solution(mesh):
-    placed = (P("dp", "seq", None), P(), P(None, ("dp", "seq")), P(), P("dp", None, None, None))
+    n_dp, n_seq = mesh.devices.shape
+    n_x = int(round(n_seq ** 0.5))
+    split = Mesh(mesh.devices.reshape(n_dp, n_seq // n_x, n_x), ("dp", "y", "x"))
+    cols = ("y", "x")
+    placed = (P("dp", cols, None), P(), P(None, ("dp", "y", "x")), P(), P("dp", None, None, None))
     return jax.shard_map(
-        body, mesh=mesh, in_specs=placed, out_specs=P("dp", "seq", None), check_vma=False
+        body, mesh=split, in_specs=placed, out_specs=P("dp", cols, None), check_vma=False
     )

time: 236 us -> 237 us (level)
  other arithmetic: 9.23 us -> 13.1 us
    reduce_sum x0 -> x2, other arithmetic: none -> 6.51 us  [the longest x1 3.54 us: body(): jnp.sum(jnp.where((jnp.arange(row.shape[0]) < x_here)[:, None, None, None...]
    unnamed x1 -> x0, other arithmetic: 5.73 us -> none
    convert_element_type x0 -> x1, other arithmetic: none -> 3.1 us  [body(): feature_map(kv[:, :D]).astype(jnp.bfloat16).reshape(tok_rows, H, DH)]
    dot_general x2, matrix products: 28.4 us -> 25.5 us  [the longest x1 15.1 us: body(): kv = jnp.dot(normed, weight[:, D:], preferred_element_type=jnp.float32)]
    all_gather x2 -> x3, waiting for transfers between devices: 157 us -> 155 us  [the longest x1 97 us: body(): weight = lax.all_gather(qkv_weight, ('dp', 'y', 'x'), axis=1, tiled=True)]
  transfers between devices with their start and end apart: 2 -> 3, of which waited for: 2 -> 3; matrix products, arithmetic and copies ran while one was open for 5% -> 10% of each run, Pallas kernels for 0% -> 0%
where the time goes in v3:
time: 237 us
  waiting for transfers between devices  156 us (66%)
  matrix products  40.8 us (17%)
  local copies, waits for them, and re-layouts  13.3 us (6%)
  between operations  13.2 us (6%)
  other arithmetic  13.1 us (6%)
    all_gather x1, waiting for transfers between devices, body(): weight = lax.all_gather(qkv_weight, ('dp', 'y', 'x'), axis=1, tiled=True)  97 us
    all_gather x1, waiting for transfers between devices, body(): row = lax.all_gather(local, 'x', axis=0).astype(jnp.float32)  29.7 us
    all_gather x1, waiting for transfers between devices, body(): totals = lax.all_gather(row_total, 'y', axis=0)  28.5 us
    dot_general x1, matrix products, body(): kv = jnp.dot(normed, weight[:, D:], preferred_element_type=jnp.float32)  15.1 us
    dot_general x1, matrix products, body(): q = jnp.dot(normed, weight[:, :D], preferred_element_type=jnp.float32)  10.4 us
    dot_general x1, matrix products, advance(): jnp.einsum('hbc,che->bhe', scores, value_blk, preferred_element_type=jnp....  9.48 us
  transfers between devices with their start and end apart: 3, of which 3 were waited for; matrix products, arithmetic and copies ran while one was open for 10% of the time, Pallas kernels for 0%

profile of v3, /device:TPU:1, one launch (start us, length us, event | category | flops | bytes accessed | tf_op | source)
XLA Modules:
  0.0 236.6 jit_solution(13438979628427171573)
XLA Ops:
  6.5 0.7 all-gather.6.cloned.1.call-update
  7.3 0.0 all-gather.8.cloned.1.call-start
  7.3 0.7 convert_element_type.40
  8.0 2.1 fusion.4
  10.1 97.0 %all-gather.6.cloned.1.call-done = bf16[2048,6144]{0,1:T(8,128)(2,1)} async-done(((bf16[2048,48]{0,1:T(8,128)(2,1)}), bf16[2048,6144]{0,1:T(8,128)(2,1)}) %all-gather.6.cloned.1.call-update) | async-done | bytes 25165840 | tf_op jit(solution)/shard_map/all_gather | solution.py:56
  107.1 15.1 %fusion = f32[512,4096]{1,0:T(8,128)} fusion(bf16[2048,6144]{0,1:T(8,128)(2,1)} %all-gather.6.cloned.1.call-done, bf16[1,512,2048]{2,1,0:T(8,128)(2,1)} %param.5, f32[2048]{0:T(1024)S(1)} %convert_element_type.40, f32[512]{0:T(512)S(1)} %add_rsqrt_fusion.1), kind=kOutput, calls=%fused_computation | convolution fusion | flops 8594128896 | bytes 27273216 | tf_op jit(solution)/shard_map/dot_general | solution.py:57
  122.2 3.8 %slice.31 = bf16[512,2048]{1,0:T(8,128)(2,1)} slice(f32[512,4096]{1,0:T(8,128)} %fusion), slice={[0:512], [2048:4096]} | slice | bytes 4194304 | tf_op jit(solution)/shard_map/slice | solution.py:59
  126.0 3.1 %select_convert_fusion.2 = bf16[512,2048]{1,0:T(8,128)(2,1)S(1)} fusion(f32[512,4096]{1,0:T(8,128)} %fusion), kind=kLoop, calls=%fused_computation.21 | loop fusion | flops 5242880 | bytes 6291456 | tf_op jit(solution)/shard_map/convert_element_type | solution.py:58
  129.1 2.5 %copy.19 = bf16[512,2048]{0,1:T(8,128)(2,1)} copy(bf16[512,2048]{1,0:T(8,128)(2,1)S(1)} %select_convert_fusion.2) | data formatting | bytes 4194304 | tf_op jit(solution)/shard_map/reshape | solution.py:58
  131.7 4.1 %copy.20 = bf16[512,2048]{0,1:T(8,128)(2,1)} copy(bf16[512,2048]{1,0:T(8,128)(2,1)} %slice.31) | data formatting | bytes 4194304 | tf_op jit(solution)/shard_map/reshape | solution.py:59
  135.8 3.1 %convolution_convert_fusion = bf16[16,128,128]{2,1,0:T(8,128)(2,1)} fusion(bf16[512,16,128]{0,2,1:T(8,128)(2,1)S(1)} %bitcast.45, bf16[512,16,128]{0,2,1:T(8,128)(2,1)} %bitcast.47), kind=kOutput, calls=%fused_computation.29 | convolution fusion | flops 268697600 | bytes 4718592 | tf_op jit(solution)/shard_map/thd,the->hde/dot_general | solution.py:60
  138.9 0.2 all-gather.10.cloned.1.call-start
  139.1 29.7 %all-gather.8.cloned.1.call-done = bf16[64,128,128]{2,1,0:T(8,128)(2,1)} async-done(((bf16[16,128,128]{2,1,0:T(8,128)(2,1)}), bf16[64,128,128]{2,1,0:T(8,128)(2,1)}) %all-gather.8.cloned.1.call-update) | async-done | bytes 2097168 | tf_op jit(solution)/shard_map/all_gather | solution.py:63
  168.8 3.5 %fusion.7 = (f32[16,128,128]{2,1,0:T(8,128)S(1)}, f32[16,128,128]{2,1,0:T(8,128)}) fusion(bf16[4,16,128,128]{3,2,1,0:T(8,128)(2,1)} %bitcast.51, pred[4]{0:T(512)(128)(4,1)S(1)} %iota_compare_fusion.1), kind=kLoop, calls=%fused_computation.12 | loop fusion | flops 3670016 | bytes 4194308 | tf_op jit(solution)/shard_map/reduce_sum | solution.py:66
  172.4 0.0 all-gather.10.cloned.1.call-update
  172.4 0.1 iota_compare_fusion
  172.5 10.4 %fusion.20 = bf16[64,16,8,128]{3,2,1,0:T(8,128)(2,1)} fusion(bf16[2048,6144]{0,1:T(8,128)(2,1)} %all-gather.6.cloned.1.call-done, bf16[1,512,2048]{2,1,0:T(8,128)(2,1)} %param.5, f32[2048]{0:T(1024)S(1)} %convert_element_type.40, f32[512]{0:T(512)S(1)} %add_rsqrt_fusion.1), kind=kOutput, calls=%fused_computation.28 | convolution fusion | flops 4304404480 | bytes 12593152 | tf_op jit(solution)/shard_map/dot_general | solution.py:71
  182.9 9.5 %fusion.13 = f32[16,128,512]{2,1,0:T(8,128)} fusion(bf16[512,16,128]{0,2,1:T(8,128)(2,1)} %bitcast.48, bf16[512,16,128]{0,2,1:T(8,128)(2,1)S(1)} %bitcast.46, pred[512,512]{1,0:T(8,128)(4,1)S(1)} %iota_compare_fusion, bf16[64,16,8,128]{3,2,1,0:T(8,128)(2,1)} %fusion.20), kind=kOutput, calls=%fused_computation.22 | convolution fusion | flops 2155872256 | bytes 10747904 | tf_op jit(solution)/shard_map/while/body/eval_jaxpr/hbc,che->bhe/dot_general | solution.py:34
  192.4 28.5 %all-gather.10.cloned.1.call-done = f32[64,128,128]{2,1,0:T(8,128)} async-done(((f32[16,128,128]{2,1,0:T(8,128)}), f32[64,128,128]{2,1,0:T(8,128)}) %all-gather.10.cloned.1.call-update) | async-done | bytes 4194320 | tf_op jit(solution)/shard_map/all_gather | solution.py:68
  220.9 3.0 %select_reduce_fusion = f32[16,128,128]{2,1,0:T(8,128)S(1)} fusion(f32[4,16,128,128]{3,2,1,0:T(8,128)} %bitcast.50, pred[4]{0:T(512)(128)(4,1)S(1)} %iota_compare_fusion.2), kind=kLoop, calls=%fused_computation.20 | loop fusion | flops 1835008 | bytes 5242884 | tf_op jit(solution)/shard_map/reduce_sum | solution.py:69
  223.9 0.5 copy-done.1
  224.3 2.7 %fusion.8 = (f32[512,16]{0,1:T(8,128)S(1)}, f32[16,128,512]{2,1,0:T(8,128)S(1)}) fusion(f32[16,128,512]{2,1,0:T(8,128)S(1)} %copy-done.1, bf16[64,16,8,128]{3,2,1,0:T(8,128)(2,1)} %fusion.20, f32[1,16,128,128]{3,2,1,0:T(8,128)S(1)} %copy-done.2, f32[16,128,128]{2,1,0:T(8,128)S(1)} %select_reduce_fusion, f32[16,128,128]{2,1,0:T(8,128)S(1)} %get-tuple-element.19), kind=kOutput, calls=%fused_computation.16 | convolution fusion | flops 272359424 | bytes 13664256 | tf_op jit(solution)/shard_map/while/body/eval_jaxpr/bhd,hde->bhe/dot_general | solution.py:26
  227.1 0.6 fusion.10
  227.7 2.4 %copy.17 = bf16[1,512,2048]{2,1,0:T(8,128)(2,1)} copy(bf16[1,512,2048]{1,2,0:T(8,128)(2,1)S(1)} %bitcast.49) | data formatting | bytes 4194304 | tf_op jit(solution)/shard_map/broadcast_in_dim;reshape | solution.py:74
  (14 shorter events, 0.1 us)
Async XLA Ops:
  6.5 100.6 %all-gather.6.cloned.1.call-start = ((), (), s32[]{:S(2)}) async-start(), calls=%async_computation | async-start | bytes 25362432 | tf_op jit(solution)/shard_map/all_gather | solution.py:56
  7.3 161.6 %all-gather.8.cloned.1.call-start = ((), (), s32[]{:S(2)}) async-start(), calls=%async_computation.1 | async-start | bytes 2621440 | tf_op jit(solution)/shard_map/all_gather | solution.py:63
  131.7 4.1 %copy-start = (bf16[512,2048]{0,1:T(8,128)(2,1)S(1)}, bf16[512,2048]{0,1:T(8,128)(2,1)}, u32[]{:S(2)}) copy-start(bf16[512,2048]{0,1:T(8,128)(2,1)} %copy.19) | copy-start | bytes 6291460
  138.8 33.6 %copy-start.3 = (bf16[2048]{0:T(1024)(128)(2,1)S(1)}, bf16[2048]{0:T(1024)(128)(2,1)}, u32[]{:S(2)}) copy-start(bf16[2048]{0:T(1024)(128)(2,1)} %param.8) | copy-start | bytes 12292
  138.9 82.0 %all-gather.10.cloned.1.call-start = ((), (), s32[]{:S(2)}) async-start(), calls=%async_computation.2 | async-start | bytes 5242880 | tf_op jit(solution)/shard_map/all_gather | solution.py:68
  192.4 31.5 %copy-start.2 = (f32[1,16,128,128]{3,2,1,0:T(8,128)S(1)}, f32[1,16,128,128]{3,2,1,0:T(8,128)}, u32[]{:S(2)}) copy-start(f32[1,16,128,128]{3,2,1,0:T(8,128)} %param.9) | copy-start | bytes 3145732
  220.9 3.4 %copy-start.1 = (f32[16,128,512]{2,1,0:T(8,128)S(1)}, f32[16,128,512]{2,1,0:T(8,128)}, u32[]{:S(2)}) copy-start(f32[16,128,512]{2,1,0:T(8,128)} %fusion.13) | copy-start | bytes 12582916
Sparse Core Ops, SparseCore 0:
  10.4 96.6 all-gather.5
  139.0 29.7 all-gather.7
  172.5 48.3 all-gather.9

commit v4 on v3

--- a/solution.py
+++ b/solution.py
@@ -54,20 +54,27 @@
     normed = (normed * input_gain.astype(jnp.float32)).astype(jnp.bfloat16)
     tok_rows = normed.shape[0]
     weight = lax.all_gather(qkv_weight, ("dp", "y", "x"), axis=1, tiled=True)
-    kv = jnp.dot(normed, weight[:, D:], preferred_element_type=jnp.float32)
-    key_feats = feature_map(kv[:, :D]).astype(jnp.bfloat16).reshape(tok_rows, H, DH)
-    values = kv[:, D:].astype(jnp.bfloat16).reshape(tok_rows, H, DH)
-    local = jnp.einsum(
-        "thd,the->hde", key_feats, values, preferred_element_type=jnp.float32
-    ).astype(jnp.bfloat16)
-    row = lax.all_gather(local, "x", axis=0).astype(jnp.float32)
-    x_here = lax.axis_index("x")
-    y_here = lax.axis_index("y")
-    row_before = jnp.sum(jnp.where((jnp.arange(row.shape[0]) < x_here)[:, None, None, None], row, 0.0), axis=0)
-    row_total = jnp.sum(row, axis=0)
-    totals = lax.all_gather(row_total, "y", axis=0)
-    rows_before = jnp.sum(jnp.where((jnp.arange(totals.shape[0]) < y_here)[:, None, None, None], totals, 0.0), axis=0)
-    memory = prefix_state[0] + (rows_before + row_before)
+    n_half = 2
+    per = D // n_half
+    seq_here = lax.axis_index(("y", "x"))
+    keys, vals, mems = [], [], []
+    for g in range(n_half):
+        lo = g * per
+        k_g = jnp.dot(normed, weight[:, D + lo : D + lo + per], preferred_element_type=jnp.float32)
+        v_g = jnp.dot(normed, weight[:, 2 * D + lo : 2 * D + lo + per], preferred_element_type=jnp.float32)
+        k_g = feature_map(k_g).astype(jnp.bfloat16).reshape(tok_rows, per // DH, DH)
+        v_g = v_g.astype(jnp.bfloat16).reshape(tok_rows, per // DH, DH)
+        local = jnp.einsum(
+            "thd,the->hde", k_g, v_g, preferred_element_type=jnp.float32
+        ).astype(jnp.bfloat16)
+        gathered = lax.all_gather(local[None], ("y", "x"), axis=0, tiled=True)
+        earlier = (jnp.arange(gathered.shape[0]) < seq_here).astype(jnp.bfloat16)
+        mems.append(jnp.einsum("c,chde->hde", earlier, gathered, preferred_element_type=jnp.float32))
+        keys.append(k_g)
+        vals.append(v_g)
+    key_feats = jnp.concatenate(keys, axis=1)
+    values = jnp.concatenate(vals, axis=1)
+    memory = prefix_state[0] + jnp.concatenate(mems, axis=0)
     q = jnp.dot(normed, weight[:, :D], preferred_element_type=jnp.float32)
     queries = feature_map(q).astype(jnp.bfloat16).reshape(tok_rows, H, DH)
     attended = span_attention(queries, key_feats, values, memory, head_gain)

time: 237 us -> 240 us (1.013)
  matrix products: 40.8 us -> 56.5 us
  other arithmetic: 13.1 us -> 5.19 us
  local copies, waits for them, and re-layouts: 13.3 us -> 7.49 us
    dot_general x2 -> x8, matrix products: 18.2 us -> 34.7 us  [the longest x2 11.4 us: body(): jnp.dot(normed, weight[:, 2 * D + lo:2 * D + lo + per], preferred_element...]
    reduce_sum x2 -> x0, other arithmetic: 6.51 us -> none  [the longest x1 3.54 us: body(): jnp.sum(jnp.where((jnp.arange(row.shape[0]) < x_here)[:, None, None, None...]
    reshape x2, local copies, waits for them, and re-layouts: 6.61 us -> 2.22 us  [body(): v_g = v_g.astype(jnp.bfloat16).reshape(tok_rows, per // DH, DH)]
    slice x1 -> x0, local copies, waits for them, and re-layouts: 3.83 us -> none  [body(): values = kv[:, D:].astype(jnp.bfloat16).reshape(tok_rows, H, DH)]
    convert_element_type x1 -> x0, other arithmetic: 3.1 us -> none  [body(): feature_map(kv[:, :D]).astype(jnp.bfloat16).reshape(tok_rows, H, DH)]
    unnamed x8 -> x12, local copies, waits for them, and re-layouts: 0.47 us -> 2.9 us
  transfers between devices with their start and end apart: 3 -> 3, of which waited for: 3 -> 3; matrix products, arithmetic and copies ran while one was open for 10% -> 19% of each run, Pallas kernels for 0% -> 0%
where the time goes in v4:
time: 240 us
  waiting for transfers between devices  158 us (66%)
  matrix products  56.5 us (24%)
  between operations  13.2 us (6%)
  local copies, waits for them, and re-layouts  7.49 us (3%)
  other arithmetic  5.19 us (2%)
    all_gather x1, waiting for transfers between devices, body(): weight = lax.all_gather(qkv_weight, ('dp', 'y', 'x'), axis=1, tiled=True)  97 us
    all_gather x2, waiting for transfers between devices, body(): gathered = lax.all_gather(local[None], ('y', 'x'), axis=0, tiled=True)  59.8 us
    dot_general x2, matrix products, body(): jnp.dot(normed, weight[:, 2 * D + lo:2 * D + lo + per], preferred_element...  11.4 us
    dot_general x2, matrix products, body(): jnp.dot(normed, weight[:, D + lo:D + lo + per], preferred_element_type=jn...  11 us
    dot_general x2, matrix products, body(): jnp.einsum('c,chde->hde', earlier, gathered, preferred_element_type=jnp.f...  9.88 us
    dot_general x1, matrix products, body(): q = jnp.dot(normed, weight[:, :D], preferred_element_type=jnp.float32)  9.75 us
    dot_general x1, matrix products, advance(): jnp.einsum('hbc,che->bhe', scores, value_blk, preferred_element_type=jnp....  9.67 us
  transfers between devices with their start and end apart: 3, of which 3 were waited for; matrix products, arithmetic and copies ran while one was open for 19% of the time, Pallas kernels for 0%

profile of v4, /device:TPU:1, one launch (start us, length us, event | category | flops | bytes accessed | tf_op | source)
XLA Modules:
  0.0 240.1 jit_solution(10725810064593640005)
XLA Ops:
  6.5 0.7 all-gather.6.cloned.1.call-update
  7.3 0.7 convert_element_type.50
  8.0 2.1 fusion.2
  10.1 97.0 %all-gather.6.cloned.1.call-done = bf16[2048,6144]{0,1:T(8,128)(2,1)} async-done(((bf16[2048,48]{0,1:T(8,128)(2,1)}), bf16[2048,6144]{0,1:T(8,128)(2,1)}) %all-gather.6.cloned.1.call-update) | async-done | bytes 25165840 | tf_op jit(solution)/shard_map/all_gather | solution.py:56
  107.1 5.2 %fusion.40 = bf16[512,1024]{1,0:T(8,128)(2,1)S(1)} fusion(bf16[2048,6144]{0,1:T(8,128)(2,1)} %all-gather.6.cloned.1.call-done, bf16[1,512,2048]{2,1,0:T(8,128)(2,1)} %param.5, f32[2048]{0:T(1024)S(1)} %convert_element_type.50, f32[512]{0:T(512)S(1)} %add_rsqrt_fusion.1), kind=kOutput, calls=%fused_computation.41 | convolution fusion | flops 2152202240 | bytes 7350272 | tf_op jit(solution)/shard_map/dot_general | solution.py:64
  112.3 0.5 copy.33
  112.9 5.4 %select_convert_fusion.2 = bf16[512,1024]{1,0:T(8,128)(2,1)S(1)} fusion(bf16[2048,6144]{0,1:T(8,128)(2,1)} %all-gather.6.cloned.1.call-done, bf16[1,512,2048]{2,1,0:T(8,128)(2,1)} %param.5, f32[2048]{0:T(1024)S(1)} %convert_element_type.50, f32[512]{0:T(512)S(1)} %add_rsqrt_fusion.1), kind=kOutput, calls=%fused_computation.35 | convolution fusion | flops 2154299392 | bytes 7350272 | tf_op jit(solution)/shard_map/dot_general | solution.py:63
  118.3 1.2 convolution_convert_fusion
  119.6 6.2 %fusion.37 = bf16[512,1024]{1,0:T(8,128)(2,1)} fusion(bf16[2048,6144]{0,1:T(8,128)(2,1)} %all-gather.6.cloned.1.call-done, bf16[1,512,2048]{2,1,0:T(8,128)(2,1)} %param.5, f32[2048]{0:T(1024)S(1)} %convert_element_type.50, f32[512]{0:T(512)S(1)} %add_rsqrt_fusion.1), kind=kOutput, calls=%fused_computation.40 | convolution fusion | flops 2152202240 | bytes 7350272 | tf_op jit(solution)/shard_map/dot_general | solution.py:64
  125.7 1.7 copy.32
  127.4 5.6 %select_convert_fusion.3 = bf16[512,1024]{1,0:T(8,128)(2,1)S(1)} fusion(bf16[2048,6144]{0,1:T(8,128)(2,1)} %all-gather.6.cloned.1.call-done, bf16[1,512,2048]{2,1,0:T(8,128)(2,1)} %param.5, f32[2048]{0:T(1024)S(1)} %convert_element_type.50, f32[512]{0:T(512)S(1)} %add_rsqrt_fusion.1), kind=kOutput, calls=%fused_computation.36 | convolution fusion | flops 2154299392 | bytes 7350272 | tf_op jit(solution)/shard_map/dot_general | solution.py:63
  133.1 1.0 copy-done.1
  134.0 1.2 convolution_convert_fusion.1
  135.4 1.6 copy.37
  137.4 1.7 pad_maximum_fusion
  139.1 9.7 %fusion.34 = bf16[64,16,8,128]{3,2,1,0:T(8,128)(2,1)} fusion(bf16[2048,6144]{0,1:T(8,128)(2,1)} %all-gather.6.cloned.1.call-done, bf16[1,512,2048]{2,1,0:T(8,128)(2,1)S(1)} %copy-done.2, f32[2048]{0:T(1024)S(1)} %convert_element_type.50, f32[512]{0:T(512)S(1)} %add_rsqrt_fusion.1), kind=kOutput, calls=%fused_computation.39 | convolution fusion | flops 4304404480 | bytes 12593152 | tf_op jit(solution)/shard_map/dot_general | solution.py:78
  148.8 9.7 %fusion.22 = f32[16,128,512]{2,1,0:T(8,128)} fusion(pred[512,512]{1,0:T(8,128)(4,1)S(1)} %iota_compare_fusion, bf16[512,8,128]{0,2,1:T(8,128)(2,1)S(1)} %bitcast.78, bf16[512,8,128]{0,2,1:T(8,128)(2,1)S(1)} %bitcast.81, bf16[512,16,128]{2,1,0:T(8,128)(2,1)} %pad_maximum_fusion, bf16[64,16,8,128]{3,2,1,0:T(8,128)(2,1)} %fusion.34), kind=kOutput, calls=%fused_computation.26 | convolution fusion | flops 2156920832 | bytes 10747904 | tf_op jit(solution)/shard_map/while/body/eval_jaxpr/hbc,che->bhe/dot_general | solution.py:34
  158.5 11.6 %all-gather.10.cloned.1.call-done = bf16[128,128,128]{2,1,0:T(8,128)(2,1)} async-done(((bf16[8,128,128]{2,1,0:T(8,128)(2,1)}), bf16[128,128,128]{2,1,0:T(8,128)(2,1)}) %all-gather.10.cloned.1.call-update) | async-done | bytes 4194320 | tf_op jit(solution)/shard_map/all_gather | solution.py:70
  170.1 5.0 %fusion.16 = f32[1,8,128,128]{3,0,2,1:T(1,128)S(1)} fusion(bf16[16,8,128,128]{3,2,1,0:T(8,128)(2,1)} %bitcast.75, s32[]{:T(128)S(6)} %add.49), kind=kOutput, calls=%fused_computation.21 | convolution fusion | flops 4194320 | bytes 4718596 | tf_op jit(solution)/shard_map/c,chde->hde/dot_general | solution.py:72
  175.1 48.2 %all-gather.8.cloned.1.call-done = bf16[128,128,128]{2,1,0:T(8,128)(2,1)} async-done(((bf16[8,128,128]{2,1,0:T(8,128)(2,1)}), bf16[128,128,128]{2,1,0:T(8,128)(2,1)}) %all-gather.8.cloned.1.call-update) | async-done | bytes 4194320 | tf_op jit(solution)/shard_map/all_gather | solution.py:70
  223.3 4.8 %fusion.18 = f32[1,8,128,128]{3,0,2,1:T(1,128)S(1)} fusion(bf16[16,8,128,128]{3,2,1,0:T(8,128)(2,1)} %bitcast.76, s32[]{:T(128)S(6)} %add.49), kind=kOutput, calls=%fused_computation.23 | convolution fusion | flops 4194320 | bytes 4718596 | tf_op jit(solution)/shard_map/c,chde->hde/dot_general | solution.py:72
  228.2 2.3 fusion.13
  230.5 0.6 fusion.15
  231.1 2.4 copy.23
  (19 shorter events, 0.5 us)
Async XLA Ops:
  6.5 100.6 %all-gather.6.cloned.1.call-start = ((), (), s32[]{:S(2)}) async-start(), calls=%async_computation | async-start | bytes 25362432 | tf_op jit(solution)/shard_map/all_gather | solution.py:56
  7.3 162.8 %all-gather.10.cloned.1.call-start = ((), (), s32[]{:S(2)}) async-start(), calls=%async_computation.2 | async-start | bytes 4456448 | tf_op jit(solution)/shard_map/all_gather | solution.py:70
  119.5 103.8 %all-gather.8.cloned.1.call-start = ((), (), s32[]{:S(2)}) async-start(), calls=%async_computation.1 | async-start | bytes 4456448 | tf_op jit(solution)/shard_map/all_gather | solution.py:70
  127.4 8.0 %copy-start.4 = (bf16[2048]{0:T(1024)(128)(2,1)S(1)}, bf16[2048]{0:T(1024)(128)(2,1)}, u32[]{:S(2)}) copy-start(bf16[2048]{0:T(1024)(128)(2,1)} %param.8) | copy-start | bytes 12292
  133.1 1.0 copy-start.1
  135.4 3.6 %copy-start.2 = (bf16[1,512,2048]{2,1,0:T(8,128)(2,1)S(1)}, bf16[1,512,2048]{2,1,0:T(8,128)(2,1)}, u32[]{:S(2)}) copy-start(bf16[1,512,2048]{2,1,0:T(8,128)(2,1)} %param.5) | copy-start | bytes 6291460
  170.0 58.1 %copy-start.3 = (bf16[64,16,8,128]{3,2,1,0:T(8,128)(2,1)S(1)}, bf16[64,16,8,128]{3,2,1,0:T(8,128)(2,1)}, u32[]{:S(2)}) copy-start(bf16[64,16,8,128]{3,2,1,0:T(8,128)(2,1)} %fusion.34) | copy-start | bytes 6291460
  223.3 4.8 %copy-start = (f32[16,128,512]{2,1,0:T(8,128)S(1)}, f32[16,128,512]{2,1,0:T(8,128)}, u32[]{:S(2)}) copy-start(f32[16,128,512]{2,1,0:T(8,128)} %fusion.22) | copy-start | bytes 12582916
Sparse Core Ops, SparseCore 0:
  10.4 96.6 all-gather.5
  119.6 50.3 all-gather.9
  172.2 51.1 all-gather.7

commit v5 on v3

v5 whole, which is shorter than its diff:
```python
import jax
import jax.numpy as jnp
from jax import lax
from jax.sharding import Mesh, PartitionSpec as P

D = 2048
H = 16
DH = 128
BLOCK = 512


epsilon = 1e-05


def feature_map(inputs):
    return jnp.where(inputs > 0, inputs + 1.0, jnp.exp(jnp.minimum(inputs, 0.0)))


def body(tokens, input_gain, qkv_weight, head_gain, prefix_state):
    inputs = tokens[0].astype(jnp.float32)
    normed = inputs * lax.rsqrt(jnp.mean(inputs * inputs, axis=-1, keepdims=True) + epsilon)
    normed = (normed * input_gain.astype(jnp.float32)).astype(jnp.bfloat16)
    tok_rows = normed.shape[0]
    weight = lax.all_gather(qkv_weight, ("dp", "y", "x"), axis=1, tiled=True)
    keys_t = lax.dot_general(
        weight[:, D : 2 * D], normed, (((0,), (1,)), ((), ())), preferred_element_type=jnp.float32
    )
    keys_t = feature_map(keys_t).astype(jnp.bfloat16).reshape(H, DH, tok_rows)
    values = jnp.dot(normed, weight[:, 2 * D :], preferred_element_type=jnp.float32)
    values = values.astype(jnp.bfloat16).reshape(tok_rows, H, DH)
    local = jnp.einsum(
        "hdt,the->hde", keys_t, values, preferred_element_type=jnp.float32
    ).astype(jnp.bfloat16)
    gathered = lax.all_gather(local[None], ("y", "x"), axis=0, tiled=True)
    seq_here = lax.axis_index(("y", "x"))
    earlier = (jnp.arange(gathered.shape[0]) < seq_here).astype(jnp.bfloat16)
    before = jnp.einsum("c,chde->hde", earlier, gathered, preferred_element_type=jnp.float32)
    memory = prefix_state[0] + before
    queries = jnp.dot(normed, weight[:, :D], preferred_element_type=jnp.float32)
    queries = feature_map(queries).astype(jnp.bfloat16).reshape(tok_rows, H, DH)

    causal = jnp.arange(tok_rows)[:, None] >= jnp.arange(tok_rows)[None, :]
    gains = head_gain.astype(jnp.float32).reshape(H, DH)
    scores = jnp.einsum("bhd,hdc->hbc", queries, keys_t, preferred_element_type=jnp.float32)
    scores = jnp.where(causal[None], scores, 0.0).astype(jnp.bfloat16)
    within = jnp.einsum("hbc,che->bhe", scores, values, preferred_element_type=jnp.float32)
    carried = jnp.einsum(
        "bhd,hde->bhe", queries, memory.astype(jnp.bfloat16), preferred_element_type=jnp.float32
    )
    numerator = carried + within
    scale = lax.rsqrt(jnp.mean(numerator * numerator, axis=-1, keepdims=True) + epsilon)
    attended = (numerator * scale * gains).astype(jnp.bfloat16)
    return attended.reshape(1, tok_rows, H * DH)


def solution(mesh):
    n_dp, n_seq = mesh.devices.shape
    n_x = int(round(n_seq ** 0.5))
    split = Mesh(mesh.devices.reshape(n_dp, n_seq // n_x, n_x), ("dp", "y", "x"))
    cols = ("y", "x")
    placed = (P("dp", cols, None), P(), P(None, ("dp", "y", "x")), P(), P("dp", None, None, None))
    return jax.shard_map(
        body, mesh=split, in_specs=placed, out_specs=P("dp", cols, None), check_vma=False
    )
```

time: 237 us -> 227 us (0.958)
  matrix products: 40.8 us -> 52.5 us
  other arithmetic: 13.1 us -> 3.51 us
  waiting for transfers between devices: 156 us -> 148 us
  local copies, waits for them, and re-layouts: 13.3 us -> 9.18 us
    dot_general x5 -> x7, matrix products: 40.8 us -> 52.5 us  [the longest x1 10.4 us: body(): queries = jnp.dot(normed, weight[:, :D], preferred_element_type=jnp.float32)]
    all_gather x2 -> x1, waiting for transfers between devices: 58.2 us -> 50.2 us  [body(): gathered = lax.all_gather(local[None], ('y', 'x'), axis=0, tiled=True)]
    reduce_sum x2 -> x0, other arithmetic: 6.51 us -> none  [the longest x1 3.54 us: body(): jnp.sum(jnp.where((jnp.arange(row.shape[0]) < x_here)[:, None, None, None...]
    slice x1 -> x0, local copies, waits for them, and re-layouts: 3.83 us -> none  [body(): values = kv[:, D:].astype(jnp.bfloat16).reshape(tok_rows, H, DH)]
    convert_element_type x2 -> x1, other arithmetic: 3.71 us -> 0.64 us  [body(): attended = (numerator * scale * gains).astype(jnp.bfloat16)]
    reshape x2 -> x3, local copies, waits for them, and re-layouts: 6.61 us -> 9.17 us  [the longest x1 3.93 us: body(): keys_t = feature_map(keys_t).astype(jnp.bfloat16).reshape(H, DH, tok_rows)]
    another operation x1 -> x0, local copies, waits for them, and re-layouts: 2.38 us -> none  [body(): return attended[None]]
  transfers between devices with their start and end apart: 3 -> 2, of which waited for: 3 -> 2; matrix products, arithmetic and copies ran while one was open for 10% -> 10% of each run, Pallas kernels for 0% -> 0%
where the time goes in v5:
time: 227 us
  waiting for transfers between devices  148 us (65%)
  matrix products  52.5 us (23%)
  between operations  13.5 us (6%)
  local copies, waits for them, and re-layouts  9.18 us (4%)
  other arithmetic  3.51 us (2%)
    all_gather x1, waiting for transfers between devices, body(): weight = lax.all_gather(qkv_weight, ('dp', 'y', 'x'), axis=1, tiled=True)  97 us
    all_gather x1, waiting for transfers between devices, body(): gathered = lax.all_gather(local[None], ('y', 'x'), axis=0, tiled=True)  50.2 us
    dot_general x1, matrix products, body(): queries = jnp.dot(normed, weight[:, :D], preferred_element_type=jnp.float32)  10.4 us
    dot_general x1, matrix products, body(): lax.dot_general(weight[:, D:2 * D], normed, (((0,), (1,)), ((), ())), pre...  10.3 us
    dot_general x1, matrix products, body(): jnp.dot(normed, weight[:, 2 * D:], preferred_element_type=jnp.float32)  9.89 us
    dot_general x1, matrix products, body(): jnp.einsum('hbc,che->bhe', scores, values, preferred_element_type=jnp.flo...  9.16 us
    dot_general x1, matrix products, body(): jnp.einsum('c,chde->hde', earlier, gathered, preferred_element_type=jnp.f...  8.66 us
  transfers between devices with their start and end apart: 2, of which 2 were waited for; matrix products, arithmetic and copies ran while one was open for 10% of the time, Pallas kernels for 0%

profile of v5, /device:TPU:1, one launch (start us, length us, event | category | flops | bytes accessed | tf_op | source)
XLA Modules:
  0.0 226.6 jit_solution(10848702317231720216)
XLA Ops:
  6.5 0.0 all-gather.4.cloned.1.call-start
  6.5 0.7 all-gather.4.cloned.1.call-update
  7.3 0.0 all-gather.6.cloned.1.call-start
  7.3 0.7 convert_element_type.40
  8.0 2.1 fusion.8
  10.1 97.0 %all-gather.4.cloned.1.call-done = bf16[2048,6144]{0,1:T(8,128)(2,1)} async-done(((bf16[2048,48]{0,1:T(8,128)(2,1)}), bf16[2048,6144]{0,1:T(8,128)(2,1)}) %all-gather.4.cloned.1.call-update) | async-done | bytes 25165840 | tf_op jit(solution)/shard_map/all_gather | solution.py:24
  107.1 9.9 %fusion.14 = bf16[512,2048]{1,0:T(8,128)(2,1)} fusion(bf16[2048,6144]{0,1:T(8,128)(2,1)} %all-gather.4.cloned.1.call-done, bf16[1,512,2048]{2,1,0:T(8,128)(2,1)} %param.5, f32[2048]{0:T(1024)S(1)} %convert_element_type.40, f32[512]{0:T(512)S(1)} %add_rsqrt_fusion.1), kind=kOutput, calls=%fused_computation.21 | convolution fusion | flops 4300210176 | bytes 12593152 | tf_op jit(solution)/shard_map/dot_general | solution.py:29
  117.0 2.9 %copy.23 = bf16[512,2048]{0,1:T(8,128)(2,1)S(1)} copy(bf16[512,2048]{1,0:T(8,128)(2,1)} %fusion.14) | data formatting | bytes 4194304 | tf_op jit(solution)/shard_map/reshape | solution.py:30
  119.9 10.3 %fusion.21 = bf16[2048,512]{0,1:T(8,128)(2,1)} fusion(bf16[2048,6144]{0,1:T(8,128)(2,1)} %all-gather.4.cloned.1.call-done, bf16[1,512,2048]{2,1,0:T(8,128)(2,1)} %param.5, f32[2048]{0:T(1024)S(1)} %convert_element_type.40, f32[512]{0:T(512)S(1)} %add_rsqrt_fusion.1), kind=kOutput, calls=%fused_computation.22 | convolution fusion | flops 4304404480 | bytes 12593152 | tf_op jit(solution)/shard_map/dot_general | solution.py:25
  130.1 3.9 %copy.22 = bf16[2048,512]{1,0:T(8,128)(2,1)} copy(bf16[2048,512]{0,1:T(8,128)(2,1)} %fusion.21) | data formatting | bytes 4194304 | tf_op jit(solution)/shard_map/reshape | solution.py:28
  134.1 3.1 %convolution_convert_fusion = bf16[16,128,128]{2,1,0:T(8,128)(2,1)} fusion(bf16[16,128,512]{2,1,0:T(8,128)(2,1)} %bitcast.56, bf16[512,16,128]{0,2,1:T(8,128)(2,1)S(1)} %bitcast.54), kind=kOutput, calls=%fused_computation.30 | convolution fusion | flops 268697600 | bytes 4718592 | tf_op jit(solution)/shard_map/hdt,the->hde/dot_general | solution.py:31
  137.2 0.0 all-gather.6.cloned.1.call-update
  137.2 0.1 iota_compare_fusion
  137.3 0.0 copy-done.3
  137.3 10.4 %fusion.31 = bf16[64,16,8,128]{3,2,1,0:T(8,128)(2,1)} fusion(bf16[2048,6144]{0,1:T(8,128)(2,1)} %all-gather.4.cloned.1.call-done, bf16[1,512,2048]{2,1,0:T(8,128)(2,1)} %param.5, f32[2048]{0:T(1024)S(1)} %convert_element_type.40, f32[512]{0:T(512)S(1)} %add_rsqrt_fusion.1), kind=kOutput, calls=%fused_computation.29 | convolution fusion | flops 4304404480 | bytes 12593152 | tf_op jit(solution)/shard_map/dot_general | solution.py:39
  147.7 9.2 %fusion.24 = f32[16,128,512]{2,1,0:T(8,128)} fusion(bf16[512,16,128]{0,2,1:T(8,128)(2,1)S(1)} %bitcast.55, bf16[16,128,512]{2,1,0:T(8,128)(2,1)} %bitcast.57, pred[512,512]{1,0:T(8,128)(4,1)S(1)} %iota_compare_fusion, bf16[64,16,8,128]{3,2,1,0:T(8,128)(2,1)} %fusion.31), kind=kOutput, calls=%fused_computation.23 | convolution fusion | flops 2155872256 | bytes 10747904 | tf_op jit(solution)/shard_map/hbc,che->bhe/dot_general | solution.py:46
  156.8 50.2 %all-gather.6.cloned.1.call-done = bf16[256,128,128]{2,1,0:T(8,128)(2,1)} async-done(((bf16[16,128,128]{2,1,0:T(8,128)(2,1)}), bf16[256,128,128]{2,1,0:T(8,128)(2,1)}) %all-gather.6.cloned.1.call-update) | async-done | bytes 8388624 | tf_op jit(solution)/shard_map/all_gather | solution.py:34
  207.0 8.7 %fusion.6 = f32[1,16,128,128]{3,0,2,1:T(1,128)S(1)} fusion(bf16[16,16,128,128]{3,2,1,0:T(8,128)(2,1)} %bitcast.53, s32[]{:T(128)S(6)} %add.45), kind=kOutput, calls=%fused_computation.7 | convolution fusion | flops 8388624 | bytes 9437188 | tf_op jit(solution)/shard_map/c,chde->hde/dot_general | solution.py:37
  215.7 0.0 copy-done
  215.7 0.0 copy-done.1
  215.7 0.0 copy-done.2
  215.7 1.0 fusion.11
  216.8 0.6 fusion.13
  217.4 2.4 %copy.17 = bf16[1,512,2048]{2,1,0:T(8,128)(2,1)} copy(bf16[1,512,2048]{1,2,0:T(8,128)(2,1)S(1)} %bitcast.58) | data formatting | bytes 4194304 | tf_op jit(solution)/shard_map/reshape | solution.py:53
  (7 shorter events, 0.0 us)
Async XLA Ops:
  6.5 100.6 %all-gather.4.cloned.1.call-start = ((), (), s32[]{:S(2)}) async-start(), calls=%async_computation | async-start | bytes 25362432 | tf_op jit(solution)/shard_map/all_gather | solution.py:24
  7.3 199.8 %all-gather.6.cloned.1.call-start = ((), (), s32[]{:S(2)}) async-start(), calls=%async_computation.1 | async-start | bytes 8912896 | tf_op jit(solution)/shard_map/all_gather | solution.py:34
  130.1 7.2 %copy-start.3 = (bf16[2048]{0:T(1024)(128)(2,1)S(1)}, bf16[2048]{0:T(1024)(128)(2,1)}, u32[]{:S(2)}) copy-start(bf16[2048]{0:T(1024)(128)(2,1)} %param.8) | copy-start | bytes 12292
  207.0 8.7 %copy-start = (f32[16,128,512]{2,1,0:T(8,128)S(1)}, f32[16,128,512]{2,1,0:T(8,128)}, u32[]{:S(2)}) copy-start(f32[16,128,512]{2,1,0:T(8,128)} %fusion.24) | copy-start | bytes 12582916
  207.0 8.7 %copy-start.1 = (bf16[64,16,8,128]{3,2,1,0:T(8,128)(2,1)S(1)}, bf16[64,16,8,128]{3,2,1,0:T(8,128)(2,1)}, u32[]{:S(2)}) copy-start(bf16[64,16,8,128]{3,2,1,0:T(8,128)(2,1)} %fusion.31) | copy-start | bytes 6291460
  207.0 8.7 %copy-start.2 = (f32[1,16,128,128]{3,2,1,0:T(8,128)S(1)}, f32[1,16,128,128]{3,2,1,0:T(8,128)}, u32[]{:S(2)}) copy-start(f32[1,16,128,128]{3,2,1,0:T(8,128)} %param.9) | copy-start | bytes 3145732
Sparse Core Ops, SparseCore 0:
  10.4 96.6 all-gather.3
  137.3 69.6 all-gather.5

commit v6 on v5

--- a/solution.py
+++ b/solution.py
@@ -1,6 +1,7 @@
 import jax
 import jax.numpy as jnp
 from jax import lax
+from jax.experimental import pallas as pl
 from jax.sharding import Mesh, PartitionSpec as P
 
 D = 2048
@@ -16,21 +17,55 @@
     return jnp.where(inputs > 0, inputs + 1.0, jnp.exp(jnp.minimum(inputs, 0.0)))
 
 
+def kv_memory_kernel(x_ref, wk_ref, wv_ref, k_ref, v_ref, m_ref):
+    x = x_ref[...]
+    dims = (((1,), (1,)), ((), ()))
+    k = lax.dot_general(x, wk_ref[...], dims, preferred_element_type=jnp.float32)
+    k = feature_map(k).astype(jnp.bfloat16)
+    v = lax.dot_general(x, wv_ref[...], dims, preferred_element_type=jnp.float32).astype(jnp.bfloat16)
+    k_ref[...] = k
+    v_ref[...] = v
+    for j in range(m_ref.shape[0]):
+        part = slice(j * DH, (j + 1) * DH)
+        m = lax.dot_general(k[:, part], v[:, part], (((0,), (0,)), ((), ())), preferred_element_type=jnp.float32)
+        m_ref[j] = m.astype(jnp.bfloat16)
+
+
+def kv_memory(normed, weight_t, heads_per_step=2):
+    rows = normed.shape[0]
+    width = heads_per_step * DH
+    k_off = D // width
+    v_off = 2 * D // width
+    return pl.pallas_call(
+        kv_memory_kernel,
+        grid=(H // heads_per_step,),
+        in_specs=[
+            pl.BlockSpec((rows, D), lambda i: (0, 0)),
+            pl.BlockSpec((width, D), lambda i: (k_off + i, 0)),
+            pl.BlockSpec((width, D), lambda i: (v_off + i, 0)),
+        ],
+        out_specs=[
+            pl.BlockSpec((rows, width), lambda i: (0, i)),
+            pl.BlockSpec((rows, width), lambda i: (0, i)),
+            pl.BlockSpec((heads_per_step, DH, DH), lambda i: (i, 0, 0)),
+        ],
+        out_shape=[
+            jax.ShapeDtypeStruct((rows, D), jnp.bfloat16),
+            jax.ShapeDtypeStruct((rows, D), jnp.bfloat16),
+            jax.ShapeDtypeStruct((H, DH, DH), jnp.bfloat16),
+        ],
+    )(normed, weight_t, weight_t)
+
+
 def body(tokens, input_gain, qkv_weight, head_gain, prefix_state):
     inputs = tokens[0].astype(jnp.float32)
     normed = inputs * lax.rsqrt(jnp.mean(inputs * inputs, axis=-1, keepdims=True) + epsilon)
     normed = (normed * input_gain.astype(jnp.float32)).astype(jnp.bfloat16)
     tok_rows = normed.shape[0]
     weight = lax.all_gather(qkv_weight, ("dp", "y", "x"), axis=1, tiled=True)
-    keys_t = lax.dot_general(
-        weight[:, D : 2 * D], normed, (((0,), (1,)), ((), ())), preferred_element_type=jnp.float32
-    )
-    keys_t = feature_map(keys_t).astype(jnp.bfloat16).reshape(H, DH, tok_rows)
-    values = jnp.dot(normed, weight[:, 2 * D :], preferred_element_type=jnp.float32)
-    values = values.astype(jnp.bfloat16).reshape(tok_rows, H, DH)
-    local = jnp.einsum(
-        "hdt,the->hde", keys_t, values, preferred_element_type=jnp.float32
-    ).astype(jnp.bfloat16)
+    key_feats, values, local = kv_memory(normed, weight.T)
+    key_feats = key_feats.reshape(tok_rows, H, DH)
+    values = values.reshape(tok_rows, H, DH)
     gathered = lax.all_gather(local[None], ("y", "x"), axis=0, tiled=True)
     seq_here = lax.axis_index(("y", "x"))
     earlier = (jnp.arange(gathered.shape[0]) < seq_here).astype(jnp.bfloat16)
@@ -41,7 +76,7 @@
 
     causal = jnp.arange(tok_rows)[:, None] >= jnp.arange(tok_rows)[None, :]
     gains = head_gain.astype(jnp.float32).reshape(H, DH)
-    scores = jnp.einsum("bhd,hdc->hbc", queries, keys_t, preferred_element_type=jnp.float32)
+    scores = jnp.einsum("bhd,chd->hbc", queries, key_feats, preferred_element_type=jnp.float32)
     scores = jnp.where(causal[None], scores, 0.0).astype(jnp.bfloat16)
     within = jnp.einsum("hbc,che->bhe", scores, values, preferred_element_type=jnp.float32)
     carried = jnp.einsum(

time: 227 us -> 212 us (0.934)
  matrix products: 52.5 us -> 29.5 us
  Pallas kernels: 0 us -> 15.4 us
  waiting for transfers between devices: 148 us -> 136 us
  other arithmetic: 3.51 us -> 6.97 us
    dot_general x3 -> x0, matrix products: 23.3 us -> none  [the longest x1 10.3 us: body(): lax.dot_general(weight[:, D:2 * D], normed, (((0,), (1,)), ((), ())), pre...]
    pallas_call x0 -> x1, Pallas kernels: none -> 15.4 us  [kv_memory(): pl.pallas_call(kv_memory_kernel, grid=(H // heads_per_step,), in_specs=[p...]
    all_gather x1, waiting for transfers between devices: 50.2 us -> 41.8 us  [body(): gathered = lax.all_gather(local[None], ('y', 'x'), axis=0, tiled=True)]
    all_gather x1, waiting for transfers between devices: 97 us -> 93.6 us  [body(): weight = lax.all_gather(qkv_weight, ('dp', 'y', 'x'), axis=1, tiled=True)]
    convert_element_type x1 -> x2, other arithmetic: 0.69 us -> 4.15 us  [body(): normed = (normed * input_gain.astype(jnp.float32)).astype(jnp.bfloat16)]
  transfers between devices with their start and end apart: 2 -> 2, of which waited for: 2 -> 2; matrix products, arithmetic and copies ran while one was open for 10% -> 16% of each run, Pallas kernels for 0% -> 0%
where the time goes in v6:
time: 212 us
  waiting for transfers between devices  136 us (64%)
  matrix products  29.5 us (14%)
  Pallas kernels  15.4 us (7%)
  between operations  13.5 us (6%)
  local copies, waits for them, and re-layouts  10.4 us (5%)
  other arithmetic  6.97 us (3%)
    all_gather x1, waiting for transfers between devices, body(): weight = lax.all_gather(qkv_weight, ('dp', 'y', 'x'), axis=1, tiled=True)  93.6 us
    all_gather x1, waiting for transfers between devices, body(): gathered = lax.all_gather(local[None], ('y', 'x'), axis=0, tiled=True)  41.8 us
    pallas_call x1, Pallas kernels, kv_memory(): pl.pallas_call(kv_memory_kernel, grid=(H // heads_per_step,), in_specs=[p...  15.4 us
    dot_general x1, matrix products, body(): queries = jnp.dot(normed, weight[:, :D], preferred_element_type=jnp.float32)  10.1 us
    dot_general x1, matrix products, body(): jnp.einsum('hbc,che->bhe', scores, values, preferred_element_type=jnp.flo...  9.88 us
    dot_general x1, matrix products, body(): jnp.einsum('c,chde->hde', earlier, gathered, preferred_element_type=jnp.f...  8.45 us
  transfers between devices with their start and end apart: 2, of which 2 were waited for; matrix products, arithmetic and copies ran while one was open for 16% of the time, Pallas kernels for 0%

profile of v6, /device:TPU:1, one launch (start us, length us, event | category | flops | bytes accessed | tf_op | source)
XLA Modules:
  0.0 211.9 jit_solution(3052334883787599934)
XLA Ops:
  6.5 0.0 all-gather.4.cloned.1.call-start
  6.5 0.7 all-gather.4.cloned.1.call-update
  7.3 0.0 all-gather.6.cloned.1.call-start
  7.3 0.7 convert_element_type.28
  8.0 2.1 fusion.4
  10.1 3.5 %fusion.6.x_ref = bf16[512,2048]{1,0:T(8,128)(2,1)} fusion(bf16[1,512,2048]{2,1,0:T(8,128)(2,1)} %param.5, f32[2048]{0:T(1024)S(1)} %convert_element_type.28, f32[512]{0:T(512)S(1)} %add_rsqrt_fusion.1), kind=kLoop, calls=%fused_computation.9 | loop fusion | flops 4194304 | bytes 4204544 | tf_op jit(solution)/shard_map/convert_element_type | solution.py:63
  13.5 93.6 %all-gather.4.cloned.1.call-done = bf16[2048,6144]{0,1:T(8,128)(2,1)} async-done(((bf16[2048,48]{0,1:T(8,128)(2,1)}), bf16[2048,6144]{0,1:T(8,128)(2,1)}) %all-gather.4.cloned.1.call-update) | async-done | bytes 25165840 | tf_op jit(solution)/shard_map/all_gather | solution.py:65
  107.1 15.4 %shard_map.55 = (bf16[512,2048]{1,0:T(8,128)(2,1)}, bf16[512,2048]{1,0:T(8,128)(2,1)}, bf16[16,128,128]{2,1,0:T(8,128)(2,1)}) custom-call(bf16[512,2048]{1,0:T(8,128)(2,1)} %fusion.6.x_ref, bf16[6144,2048]{1,0:T(8,128)(2,1)} %bitcast.48, bf16[6144,2048]{1,0:T(8,128)(2,1)} %bitcast.49), custom_call_target="tpu_custom_call" | custom-call | tf_op jit(solution)/shard_map/pallas_call | solution.py:39
  122.5 0.0 all-gather.6.cloned.1.call-update
  122.5 0.1 iota_compare_fusion
  122.6 0.0 copy-done.4
  122.6 0.0 copy-start
  122.7 4.1 %copy.20 = bf16[512,2048]{0,1:T(8,128)(2,1)} copy(bf16[512,2048]{1,0:T(8,128)(2,1)} %get-tuple-element.10) | data formatting | bytes 4194304 | tf_op jit(solution)/shard_map/reshape | solution.py:67
  126.8 3.9 %copy.19 = bf16[512,2048]{0,1:T(8,128)(2,1)} copy(bf16[512,2048]{1,0:T(8,128)(2,1)} %get-tuple-element.9) | data formatting | bytes 4194304 | tf_op jit(solution)/shard_map/reshape | solution.py:68
  130.6 0.0 copy-done
  130.7 10.1 %fusion.19 = bf16[64,16,8,128]{3,2,1,0:T(8,128)(2,1)} fusion(bf16[512,2048]{1,0:T(8,128)(2,1)S(1)} %copy-done, bf16[2048,6144]{0,1:T(8,128)(2,1)} %all-gather.4.cloned.1.call-done), kind=kOutput, calls=%fused_computation.22 | convolution fusion | flops 4300210176 | bytes 12582912 | tf_op jit(solution)/shard_map/dot_general | solution.py:74
  140.8 9.9 %fusion.12 = f32[16,128,512]{2,1,0:T(8,128)} fusion(bf16[512,16,128]{0,2,1:T(8,128)(2,1)} %bitcast.54, bf16[512,16,128]{0,2,1:T(8,128)(2,1)} %bitcast.53, pred[512,512]{1,0:T(8,128)(4,1)S(1)} %iota_compare_fusion, bf16[64,16,8,128]{3,2,1,0:T(8,128)(2,1)} %fusion.19), kind=kOutput, calls=%fused_computation.16 | convolution fusion | flops 2155872256 | bytes 10747904 | tf_op jit(solution)/shard_map/hbc,che->bhe/dot_general | solution.py:81
  150.7 41.8 %all-gather.6.cloned.1.call-done = bf16[256,128,128]{2,1,0:T(8,128)(2,1)} async-done(((bf16[16,128,128]{2,1,0:T(8,128)(2,1)}), bf16[256,128,128]{2,1,0:T(8,128)(2,1)}) %all-gather.6.cloned.1.call-update) | async-done | bytes 8388624 | tf_op jit(solution)/shard_map/all_gather | solution.py:69
  192.5 8.4 %fusion.2 = f32[1,16,128,128]{3,0,2,1:T(1,128)S(1)} fusion(bf16[16,16,128,128]{3,2,1,0:T(8,128)(2,1)} %bitcast.50, s32[]{:T(128)S(6)} %add.40), kind=kOutput, calls=%fused_computation.3 | convolution fusion | flops 8388624 | bytes 9437188 | tf_op jit(solution)/shard_map/c,chde->hde/dot_general | solution.py:72
  200.9 0.0 copy-done.1
  200.9 0.0 copy-done.2
  201.0 1.0 fusion.7
  202.0 0.6 fusion.9
  202.7 2.4 %copy.13 = bf16[1,512,2048]{2,1,0:T(8,128)(2,1)} copy(bf16[1,512,2048]{1,2,0:T(8,128)(2,1)S(1)} %bitcast.51) | data formatting | bytes 4194304 | tf_op jit(solution)/shard_map/reshape | solution.py:88
  (8 shorter events, 0.0 us)
Async XLA Ops:
  6.5 100.6 %all-gather.4.cloned.1.call-start = ((), (), s32[]{:S(2)}) async-start(), calls=%async_computation | async-start | bytes 25362432 | tf_op jit(solution)/shard_map/all_gather | solution.py:65
  7.3 185.2 %all-gather.6.cloned.1.call-start = ((), (), s32[]{:S(2)}) async-start(), calls=%async_computation.1 | async-start | bytes 8912896 | tf_op jit(solution)/shard_map/all_gather | solution.py:69
  107.1 15.5 %copy-start.4 = (bf16[2048]{0:T(1024)(128)(2,1)S(1)}, bf16[2048]{0:T(1024)(128)(2,1)}, u32[]{:S(2)}) copy-start(bf16[2048]{0:T(1024)(128)(2,1)} %param.8) | copy-start | bytes 12292
  122.6 8.0 %copy-start = (bf16[512,2048]{1,0:T(8,128)(2,1)S(1)}, bf16[512,2048]{1,0:T(8,128)(2,1)}, u32[]{:S(2)}) copy-start(bf16[512,2048]{1,0:T(8,128)(2,1)} %fusion.6.x_ref) | copy-start | bytes 6291460
  192.5 8.5 %copy-start.1 = (f32[16,128,512]{2,1,0:T(8,128)S(1)}, f32[16,128,512]{2,1,0:T(8,128)}, u32[]{:S(2)}) copy-start(f32[16,128,512]{2,1,0:T(8,128)} %fusion.12) | copy-start | bytes 12582916
  192.5 8.5 %copy-start.2 = (bf16[64,16,8,128]{3,2,1,0:T(8,128)(2,1)S(1)}, bf16[64,16,8,128]{3,2,1,0:T(8,128)(2,1)}, u32[]{:S(2)}) copy-start(bf16[64,16,8,128]{3,2,1,0:T(8,128)(2,1)} %fusion.19) | copy-start | bytes 6291460
  192.5 8.5 %copy-start.3 = (f32[1,16,128,128]{3,2,1,0:T(8,128)S(1)}, f32[1,16,128,128]{3,2,1,0:T(8,128)}, u32[]{:S(2)}) copy-start(f32[1,16,128,128]{3,2,1,0:T(8,128)} %param.9) | copy-start | bytes 3145732
Sparse Core Ops, SparseCore 0:
  10.4 96.6 all-gather.3
  122.7 69.7 all-gather.5

commit v7 on v6

--- a/solution.py
+++ b/solution.py
@@ -2,6 +2,7 @@
 import jax.numpy as jnp
 from jax import lax
 from jax.experimental import pallas as pl
+from jax.experimental.pallas import tpu as pltpu
 from jax.sharding import Mesh, PartitionSpec as P
 
 D = 2048
@@ -57,6 +58,42 @@
     )(normed, weight_t, weight_t)
 
 
+def tail_kernel(here_ref, g_ref, p_ref, q_ref, w_ref, gain_ref, o_ref):
+    here = here_ref[0]
+    for j in range(p_ref.shape[0]):
+        state = p_ref[j]
+        for c in range(g_ref.shape[0]):
+            state = state + jnp.where(c < here, g_ref[c, j].astype(jnp.float32), 0.0)
+        part = slice(j * DH, (j + 1) * DH)
+        carried = jnp.dot(q_ref[:, part], state.astype(jnp.bfloat16), preferred_element_type=jnp.float32)
+        numerator = carried + w_ref[:, part]
+        scale = lax.rsqrt(jnp.mean(numerator * numerator, axis=-1, keepdims=True) + epsilon)
+        o_ref[:, part] = (numerator * scale * gain_ref[:, part]).astype(o_ref.dtype)
+
+
+def attend_tail(here, gathered, prefix, queries, within, gains, heads_per_step=2):
+    rows = queries.shape[0]
+    n_piece = gathered.shape[0]
+    width = heads_per_step * DH
+    grid_spec = pltpu.PrefetchScalarGridSpec(
+        num_scalar_prefetch=1,
+        grid=(H // heads_per_step,),
+        in_specs=[
+            pl.BlockSpec((n_piece, heads_per_step, DH, DH), lambda i, s: (0, i, 0, 0)),
+            pl.BlockSpec((heads_per_step, DH, DH), lambda i, s: (i, 0, 0)),
+            pl.BlockSpec((rows, width), lambda i, s: (0, i)),
+            pl.BlockSpec((rows, width), lambda i, s: (0, i)),
+            pl.BlockSpec((1, width), lambda i, s: (0, i)),
+        ],
+        out_specs=pl.BlockSpec((rows, width), lambda i, s: (0, i)),
+    )
+    return pl.pallas_call(
+        tail_kernel,
+        grid_spec=grid_spec,
+        out_shape=jax.ShapeDtypeStruct((rows, H * DH), jnp.bfloat16),
+    )(here, gathered, prefix, queries, within, gains)
+
+
 def body(tokens, input_gain, qkv_weight, head_gain, prefix_state):
     inputs = tokens[0].astype(jnp.float32)
     normed = inputs * lax.rsqrt(jnp.mean(inputs * inputs, axis=-1, keepdims=True) + epsilon)
@@ -67,24 +104,20 @@
     key_feats = key_feats.reshape(tok_rows, H, DH)
     values = values.reshape(tok_rows, H, DH)
     gathered = lax.all_gather(local[None], ("y", "x"), axis=0, tiled=True)
-    seq_here = lax.axis_index(("y", "x"))
-    earlier = (jnp.arange(gathered.shape[0]) < seq_here).astype(jnp.bfloat16)
-    before = jnp.einsum("c,chde->hde", earlier, gathered, preferred_element_type=jnp.float32)
-    memory = prefix_state[0] + before
+    seq_here = lax.axis_index(("y", "x")).astype(jnp.int32).reshape(1)
     queries = jnp.dot(normed, weight[:, :D], preferred_element_type=jnp.float32)
-    queries = feature_map(queries).astype(jnp.bfloat16).reshape(tok_rows, H, DH)
+    queries = feature_map(queries).astype(jnp.bfloat16)
 
     causal = jnp.arange(tok_rows)[:, None] >= jnp.arange(tok_rows)[None, :]
-    gains = head_gain.astype(jnp.float32).reshape(H, DH)
-    scores = jnp.einsum("bhd,chd->hbc", queries, key_feats, preferred_element_type=jnp.float32)
+    scores = jnp.einsum(
+        "bhd,chd->hbc", queries.reshape(tok_rows, H, DH), key_feats, preferred_element_type=jnp.float32
+    )
     scores = jnp.where(causal[None], scores, 0.0).astype(jnp.bfloat16)
     within = jnp.einsum("hbc,che->bhe", scores, values, preferred_element_type=jnp.float32)
-    carried = jnp.einsum(
-        "bhd,hde->bhe", queries, memory.astype(jnp.bfloat16), preferred_element_type=jnp.float32
+    gains = head_gain.astype(jnp.float32).reshape(1, H * DH)
+    attended = attend_tail(
+        seq_here, gathered, prefix_state[0], queries, within.reshape(tok_rows, H * DH), gains
     )
-    numerator = carried + within
-    scale = lax.rsqrt(jnp.mean(numerator * numerator, axis=-1, keepdims=True) + epsilon)
-    attended = (numerator * scale * gains).astype(jnp.bfloat16)
     return attended.reshape(1, tok_rows, H * DH)
 
 

time: 212 us -> 210 us (level)
  Pallas kernels: 15.4 us -> 25.7 us
  matrix products: 29.5 us -> 19.9 us
  waiting for transfers between devices: 136 us -> 130 us
  local copies, waits for them, and re-layouts: 10.4 us -> 13.4 us
    pallas_call x0 -> x1, Pallas kernels: none -> 10.3 us  [attend_tail(): pl.pallas_call(tail_kernel, grid_spec=grid_spec, out_shape=jax.ShapeDtype...]
    dot_general x2 -> x0, matrix products: 9.47 us -> none  [the longest x1 8.45 us: body(): jnp.einsum('c,chde->hde', earlier, gathered, preferred_element_type=jnp.f...]
    all_gather x1, waiting for transfers between devices: 41.8 us -> 35.7 us  [body(): gathered = lax.all_gather(local[None], ('y', 'x'), axis=0, tiled=True)]
    reshape x1, local copies, waits for them, and re-layouts: 2.38 us -> 5.38 us  [body(): within.reshape(tok_rows, H * DH)]
  transfers between devices with their start and end apart: 2 -> 2, of which waited for: 2 -> 2; matrix products, arithmetic and copies ran while one was open for 16% -> 19% of each run, Pallas kernels for 0% -> 0%
where the time goes in v7:
time: 210 us; the launch traced here: 209 us
  waiting for transfers between devices  130 us (62%)
  Pallas kernels  25.7 us (12%)
  matrix products  19.9 us (9%)
  local copies, waits for them, and re-layouts  13.4 us (6%)
  between operations  13.4 us (6%)
  other arithmetic  6.92 us (3%)
    all_gather x1, waiting for transfers between devices, body(): weight = lax.all_gather(qkv_weight, ('dp', 'y', 'x'), axis=1, tiled=True)  93.6 us
    all_gather x1, waiting for transfers between devices, body(): gathered = lax.all_gather(local[None], ('y', 'x'), axis=0, tiled=True)  35.7 us
    pallas_call x1, Pallas kernels, kv_memory(): pl.pallas_call(kv_memory_kernel, grid=(H // heads_per_step,), in_specs=[p...  15.4 us
    pallas_call x1, Pallas kernels, attend_tail(): pl.pallas_call(tail_kernel, grid_spec=grid_spec, out_shape=jax.ShapeDtype...  10.3 us
    dot_general x1, matrix products, body(): queries = jnp.dot(normed, weight[:, :D], preferred_element_type=jnp.float32)  10 us
    dot_general x1, matrix products, body(): jnp.einsum('hbc,che->bhe', scores, values, preferred_element_type=jnp.flo...  9.91 us
    reshape x1, local copies, waits for them, and re-layouts, body(): within.reshape(tok_rows, H * DH)  5.38 us
  transfers between devices with their start and end apart: 2, of which 2 were waited for; matrix products, arithmetic and copies ran while one was open for 19% of the time, Pallas kernels for 0%

profile of v7, /device:TPU:1, one launch (start us, length us, event | category | flops | bytes accessed | tf_op | source)
XLA Modules:
  0.0 209.4 jit_solution(12605537147700999059)
XLA Ops:
  6.5 0.0 all-gather.4.cloned.1.call-start
  6.5 0.7 all-gather.4.cloned.1.call-update
  7.3 0.0 all-gather.6.cloned.1.call-start
  7.3 0.7 convert_element_type.21
  8.0 2.1 fusion.2
  10.1 3.5 %fusion.4.x_ref = bf16[512,2048]{1,0:T(8,128)(2,1)} fusion(bf16[1,512,2048]{2,1,0:T(8,128)(2,1)} %param.5, f32[2048]{0:T(1024)S(1)} %convert_element_type.21, f32[512]{0:T(512)S(1)} %add_rsqrt_fusion), kind=kLoop, calls=%fused_computation.7 | loop fusion | flops 4194304 | bytes 4204544 | tf_op jit(solution)/shard_map/convert_element_type | solution.py:100
  13.5 93.6 %all-gather.4.cloned.1.call-done = bf16[2048,6144]{0,1:T(8,128)(2,1)} async-done(((bf16[2048,48]{0,1:T(8,128)(2,1)}), bf16[2048,6144]{0,1:T(8,128)(2,1)}) %all-gather.4.cloned.1.call-update) | async-done | bytes 25165840 | tf_op jit(solution)/shard_map/all_gather | solution.py:102
  107.1 0.0 copy-start.1
  107.1 15.4 %shard_map.55 = (bf16[512,2048]{1,0:T(8,128)(2,1)}, bf16[512,2048]{1,0:T(8,128)(2,1)}, bf16[16,128,128]{2,1,0:T(8,128)(2,1)}) custom-call(bf16[512,2048]{1,0:T(8,128)(2,1)} %fusion.4.x_ref, bf16[6144,2048]{1,0:T(8,128)(2,1)} %bitcast.27, bf16[6144,2048]{1,0:T(8,128)(2,1)} %bitcast.28), custom_call_target="tpu_custom_call" | custom-call | tf_op jit(solution)/shard_map/pallas_call | solution.py:40
  122.5 0.0 all-gather.6.cloned.1.call-update
  122.5 0.0 copy-done.1
  122.5 0.6 reshape.55
  123.1 0.1 iota_compare_fusion
  123.2 0.0 copy-start
  123.2 4.1 %copy.12 = bf16[512,2048]{0,1:T(8,128)(2,1)} copy(bf16[512,2048]{1,0:T(8,128)(2,1)} %get-tuple-element.9) | data formatting | bytes 4194304 | tf_op jit(solution)/shard_map/reshape | solution.py:105
  127.3 3.9 %copy.13 = bf16[512,2048]{0,1:T(8,128)(2,1)} copy(bf16[512,2048]{1,0:T(8,128)(2,1)} %get-tuple-element.10) | data formatting | bytes 4194304 | tf_op jit(solution)/shard_map/reshape | solution.py:104
  131.2 0.0 copy-done
  131.2 10.0 %select_convert_fusion.1.q_ref = bf16[512,2048]{1,0:T(8,128)(2,1)} fusion(bf16[512,2048]{1,0:T(8,128)(2,1)S(1)} %copy-done, bf16[2048,6144]{0,1:T(8,128)(2,1)} %all-gather.4.cloned.1.call-done), kind=kOutput, calls=%fused_computation.8 | convolution fusion | flops 4300210176 | bytes 12582912 | tf_op jit(solution)/shard_map/dot_general | solution.py:108
  141.2 9.9 %fusion.7 = f32[16,128,512]{2,1,0:T(8,128)} fusion(bf16[512,16,128]{0,2,1:T(8,128)(2,1)} %bitcast.31, bf16[512,16,128]{0,2,1:T(8,128)(2,1)} %bitcast.32, pred[512,512]{1,0:T(8,128)(4,1)S(1)} %iota_compare_fusion, bf16[512,2048]{1,0:T(8,128)(2,1)} %select_convert_fusion.1.q_ref), kind=kOutput, calls=%fused_computation.9 | convolution fusion | flops 2155872256 | bytes 10747904 | tf_op jit(solution)/shard_map/hbc,che->bhe/dot_general | solution.py:116
  151.1 5.4 %copy.14.w_ref = f32[512,2048]{1,0:T(8,128)} copy(f32[512,2048]{0,1:T(8,128)} %bitcast.30) | data formatting | bytes 8388608 | tf_op jit(solution)/shard_map/reshape | solution.py:119
  156.5 35.7 %all-gather.6.cloned.1.call-done = bf16[256,128,128]{2,1,0:T(8,128)(2,1)} async-done(((bf16[16,128,128]{2,1,0:T(8,128)(2,1)}), bf16[256,128,128]{2,1,0:T(8,128)(2,1)}) %all-gather.6.cloned.1.call-update) | async-done | bytes 8388624 | tf_op jit(solution)/shard_map/all_gather | solution.py:106
  192.3 10.3 %shard_map.56 = bf16[512,2048]{1,0:T(8,128)(2,1)} custom-call(s32[1]{0:T(128)} %bitcast.here_ref, bf16[16,16,128,128]{3,2,1,0:T(8,128)(2,1)} %bitcast.29, f32[16,128,128]{2,1,0:T(8,128)} %bitcast.33, bf16[512,2048]{1,0:T(8,128)(2,1)} %select_convert_fusion.1.q_ref, f32[512,2048]{1,0:T(8,128)} %copy.14.w_ref, f32[1,2048]{1,0:T(1,128)} %bitcast.34), custom_call_target="tpu_custom_call" | custom-call | tf_op jit(solution)/shard_map/pallas_call | solution.py:90
  (1 shorter events, 0.0 us)
Async XLA Ops:
  6.5 100.6 %all-gather.4.cloned.1.call-start = ((), (), s32[]{:S(2)}) async-start(), calls=%async_computation | async-start | bytes 25362432 | tf_op jit(solution)/shard_map/all_gather | solution.py:102
  7.3 185.0 %all-gather.6.cloned.1.call-start = ((), (), s32[]{:S(2)}) async-start(), calls=%async_computation.1 | async-start | bytes 8912896 | tf_op jit(solution)/shard_map/all_gather | solution.py:106
  107.1 15.4 %copy-start.1 = (bf16[2048]{0:T(1024)(128)(2,1)S(1)}, bf16[2048]{0:T(1024)(128)(2,1)}, u32[]{:S(2)}) copy-start(bf16[2048]{0:T(1024)(128)(2,1)} %param.8) | copy-start | bytes 12292
  123.2 8.0 %copy-start = (bf16[512,2048]{1,0:T(8,128)(2,1)S(1)}, bf16[512,2048]{1,0:T(8,128)(2,1)}, u32[]{:S(2)}) copy-start(bf16[512,2048]{1,0:T(8,128)(2,1)} %fusion.4.x_ref) | copy-start | bytes 6291460
Sparse Core Ops, SparseCore 0:
  10.4 96.6 all-gather.3
  122.6 69.5 all-gather.5

commit v8 on v7

--- a/solution.py
+++ b/solution.py
@@ -58,12 +58,10 @@
     )(normed, weight_t, weight_t)
 
 
-def tail_kernel(here_ref, g_ref, p_ref, q_ref, w_ref, gain_ref, o_ref):
-    here = here_ref[0]
+def tail_kernel(sel_ref, g_ref, p_ref, q_ref, w_ref, gain_ref, o_ref):
+    sel = sel_ref[...]
     for j in range(p_ref.shape[0]):
-        state = p_ref[j]
-        for c in range(g_ref.shape[0]):
-            state = state + jnp.where(c < here, g_ref[c, j].astype(jnp.float32), 0.0)
+        state = p_ref[j] + jnp.dot(sel, g_ref[j], preferred_element_type=jnp.float32)
         part = slice(j * DH, (j + 1) * DH)
         carried = jnp.dot(q_ref[:, part], state.astype(jnp.bfloat16), preferred_element_type=jnp.float32)
         numerator = carried + w_ref[:, part]
@@ -71,27 +69,24 @@
         o_ref[:, part] = (numerator * scale * gain_ref[:, part]).astype(o_ref.dtype)
 
 
-def attend_tail(here, gathered, prefix, queries, within, gains, heads_per_step=2):
+def attend_tail(select, gathered, prefix, queries, within, gains, heads_per_step=2):
     rows = queries.shape[0]
-    n_piece = gathered.shape[0]
+    stack = gathered.shape[1]
     width = heads_per_step * DH
-    grid_spec = pltpu.PrefetchScalarGridSpec(
-        num_scalar_prefetch=1,
+    return pl.pallas_call(
+        tail_kernel,
         grid=(H // heads_per_step,),
         in_specs=[
-            pl.BlockSpec((n_piece, heads_per_step, DH, DH), lambda i, s: (0, i, 0, 0)),
-            pl.BlockSpec((heads_per_step, DH, DH), lambda i, s: (i, 0, 0)),
-            pl.BlockSpec((rows, width), lambda i, s: (0, i)),
-            pl.BlockSpec((rows, width), lambda i, s: (0, i)),
-            pl.BlockSpec((1, width), lambda i, s: (0, i)),
+            pl.BlockSpec((DH, stack), lambda i: (0, 0)),
+            pl.BlockSpec((heads_per_step, stack, DH), lambda i: (i, 0, 0)),
+            pl.BlockSpec((heads_per_step, DH, DH), lambda i: (i, 0, 0)),
+            pl.BlockSpec((rows, width), lambda i: (0, i)),
+            pl.BlockSpec((rows, width), lambda i: (0, i)),
+            pl.BlockSpec((1, width), lambda i: (0, i)),
         ],
-        out_specs=pl.BlockSpec((rows, width), lambda i, s: (0, i)),
-    )
-    return pl.pallas_call(
-        tail_kernel,
-        grid_spec=grid_spec,
+        out_specs=pl.BlockSpec((rows, width), lambda i: (0, i)),
         out_shape=jax.ShapeDtypeStruct((rows, H * DH), jnp.bfloat16),
-    )(here, gathered, prefix, queries, within, gains)
+    )(select, gathered, prefix, queries, within, gains)
 
 
 def body(tokens, input_gain, qkv_weight, head_gain, prefix_state):
@@ -103,8 +98,11 @@
     key_feats, values, local = kv_memory(normed, weight.T)
     key_feats = key_feats.reshape(tok_rows, H, DH)
     values = values.reshape(tok_rows, H, DH)
-    gathered = lax.all_gather(local[None], ("y", "x"), axis=0, tiled=True)
-    seq_here = lax.axis_index(("y", "x")).astype(jnp.int32).reshape(1)
+    gathered = lax.all_gather(local, ("y", "x"), axis=1, tiled=True)
+    seq_here = lax.axis_index(("y", "x"))
+    sel_row = jnp.arange(DH)[:, None]
+    sel_col = jnp.arange(gathered.shape[1])[None, :]
+    select = ((sel_col % DH == sel_row) & (sel_col // DH < seq_here)).astype(jnp.bfloat16)
     queries = jnp.dot(normed, weight[:, :D], preferred_element_type=jnp.float32)
     queries = feature_map(queries).astype(jnp.bfloat16)
 
@@ -116,7 +114,7 @@
     within = jnp.einsum("hbc,che->bhe", scores, values, preferred_element_type=jnp.float32)
     gains = head_gain.astype(jnp.float32).reshape(1, H * DH)
     attended = attend_tail(
-        seq_here, gathered, prefix_state[0], queries, within.reshape(tok_rows, H * DH), gains
+        select, gathered, prefix_state[0], queries, within.reshape(tok_rows, H * DH), gains
     )
     return attended.reshape(1, tok_rows, H * DH)
 

time: 210 us -> 212 us (level)
  Pallas kernels: 25.7 us -> 27.9 us
    pallas_call x1, Pallas kernels: 10.3 us -> 12.5 us  [attend_tail(): pl.pallas_call(tail_kernel, grid=(H // heads_per_step,), in_specs=[pl.Blo...]
where the time goes in v8:
time: 212 us
  waiting for transfers between devices  129 us (61%)
  Pallas kernels  27.9 us (13%)
  matrix products  19.7 us (9%)
  local copies, waits for them, and re-layouts  13.4 us (6%)
  between operations  13.4 us (6%)
  other arithmetic  7.9 us (4%)
    all_gather x1, waiting for transfers between devices, body(): weight = lax.all_gather(qkv_weight, ('dp', 'y', 'x'), axis=1, tiled=True)  93.6 us
    all_gather x1, waiting for transfers between devices, body(): gathered = lax.all_gather(local, ('y', 'x'), axis=1, tiled=True)  34.9 us
    pallas_call x1, Pallas kernels, kv_memory(): pl.pallas_call(kv_memory_kernel, grid=(H // heads_per_step,), in_specs=[p...  15.4 us
    pallas_call x1, Pallas kernels, attend_tail(): pl.pallas_call(tail_kernel, grid=(H // heads_per_step,), in_specs=[pl.Blo...  12.5 us
    dot_general x1, matrix products, body(): jnp.einsum('hbc,che->bhe', scores, values, preferred_element_type=jnp.flo...  9.92 us
    dot_general x1, matrix products, body(): queries = jnp.dot(normed, weight[:, :D], preferred_element_type=jnp.float32)  9.83 us
    reshape x1, local copies, waits for them, and re-layouts, body(): within.reshape(tok_rows, H * DH)  5.42 us
  transfers between devices with their start and end apart: 2, of which 2 were waited for; matrix products, arithmetic and copies ran while one was open for 19% of the time, Pallas kernels for 0%

profile of v8, /device:TPU:1, one launch (start us, length us, event | category | flops | bytes accessed | tf_op | source)
XLA Modules:
  0.0 211.7 jit_solution(424597667086150771)
XLA Ops:
  6.5 0.0 all-gather.3.cloned.1.call-start
  6.5 0.7 all-gather.3.cloned.1.call-update
  7.3 0.0 all-gather.5.cloned.1.call-start
  7.3 0.7 convert_element_type.25
  8.0 2.1 fusion.2
  10.1 3.5 %fusion.4.x_ref = bf16[512,2048]{1,0:T(8,128)(2,1)} fusion(bf16[1,512,2048]{2,1,0:T(8,128)(2,1)} %param.5, f32[2048]{0:T(1024)S(1)} %convert_element_type.25, f32[512]{0:T(512)S(1)} %add_rsqrt_fusion), kind=kLoop, calls=%fused_computation.7 | loop fusion | flops 4194304 | bytes 4204544 | tf_op jit(solution)/shard_map/convert_element_type | solution.py:95
  13.5 93.6 %all-gather.3.cloned.1.call-done = bf16[2048,6144]{0,1:T(8,128)(2,1)} async-done(((bf16[2048,48]{0,1:T(8,128)(2,1)}), bf16[2048,6144]{0,1:T(8,128)(2,1)}) %all-gather.3.cloned.1.call-update) | async-done | bytes 25165840 | tf_op jit(solution)/shard_map/all_gather | solution.py:97
  107.1 0.0 copy-start.1
  107.1 15.4 %shard_map.55 = (bf16[512,2048]{1,0:T(8,128)(2,1)}, bf16[512,2048]{1,0:T(8,128)(2,1)}, bf16[16,128,128]{2,1,0:T(8,128)(2,1)}) custom-call(bf16[512,2048]{1,0:T(8,128)(2,1)} %fusion.4.x_ref, bf16[6144,2048]{1,0:T(8,128)(2,1)} %bitcast.25, bf16[6144,2048]{1,0:T(8,128)(2,1)} %bitcast.26), custom_call_target="tpu_custom_call" | custom-call | tf_op jit(solution)/shard_map/pallas_call | solution.py:40
  122.5 0.0 all-gather.5.cloned.1.call-update
  122.5 0.0 copy-done.1
  122.5 0.6 reshape.105
  123.2 0.1 iota_compare_fusion
  123.2 1.0 fusion.13.sel_ref
  124.2 0.0 copy-start
  124.2 4.1 %copy.10 = bf16[512,2048]{0,1:T(8,128)(2,1)} copy(bf16[512,2048]{1,0:T(8,128)(2,1)} %get-tuple-element.9) | data formatting | bytes 4194304 | tf_op jit(solution)/shard_map/reshape | solution.py:100
  128.3 4.0 %copy.11 = bf16[512,2048]{0,1:T(8,128)(2,1)} copy(bf16[512,2048]{1,0:T(8,128)(2,1)} %get-tuple-element.10) | data formatting | bytes 4194304 | tf_op jit(solution)/shard_map/reshape | solution.py:99
  132.2 0.0 copy-done
  132.2 9.8 %select_convert_fusion.1.q_ref = bf16[512,2048]{1,0:T(8,128)(2,1)} fusion(bf16[512,2048]{1,0:T(8,128)(2,1)S(1)} %copy-done, bf16[2048,6144]{0,1:T(8,128)(2,1)} %all-gather.3.cloned.1.call-done), kind=kOutput, calls=%fused_computation.8 | convolution fusion | flops 4300210176 | bytes 12582912 | tf_op jit(solution)/shard_map/dot_general | solution.py:106
  142.1 9.9 %fusion.7 = f32[16,128,512]{2,1,0:T(8,128)} fusion(bf16[512,16,128]{0,2,1:T(8,128)(2,1)} %bitcast.28, bf16[512,16,128]{0,2,1:T(8,128)(2,1)} %bitcast.29, pred[512,512]{1,0:T(8,128)(4,1)S(1)} %iota_compare_fusion, bf16[512,2048]{1,0:T(8,128)(2,1)} %select_convert_fusion.1.q_ref), kind=kOutput, calls=%fused_computation.9 | convolution fusion | flops 2155872256 | bytes 10747904 | tf_op jit(solution)/shard_map/hbc,che->bhe/dot_general | solution.py:114
  152.0 5.4 %copy.12.w_ref = f32[512,2048]{1,0:T(8,128)} copy(f32[512,2048]{0,1:T(8,128)} %bitcast.27) | data formatting | bytes 8388608 | tf_op jit(solution)/shard_map/reshape | solution.py:117
  157.4 34.9 %all-gather.5.cloned.1.call-done.g_ref = bf16[16,2048,128]{2,1,0:T(8,128)(2,1)} async-done(((bf16[16,128,128]{2,1,0:T(8,128)(2,1)}), bf16[16,2048,128]{2,1,0:T(8,128)(2,1)}) %all-gather.5.cloned.1.call-update) | async-done | bytes 8388624 | tf_op jit(solution)/shard_map/all_gather | solution.py:101
  192.3 12.5 %shard_map.56 = bf16[512,2048]{1,0:T(8,128)(2,1)} custom-call(bf16[128,2048]{1,0:T(8,128)(2,1)} %fusion.13.sel_ref, bf16[16,2048,128]{2,1,0:T(8,128)(2,1)} %all-gather.5.cloned.1.call-done.g_ref, f32[16,128,128]{2,1,0:T(8,128)} %bitcast.30, bf16[512,2048]{1,0:T(8,128)(2,1)} %select_convert_fusion.1.q_ref, f32[512,2048]{1,0:T(8,128)} %copy.12.w_ref, ...), custom_call_target="tpu_custom_call" | custom-call | tf_op jit(solution)/shard_map/pallas_call | solution.py:76
  (3 shorter events, 0.0 us)
Async XLA Ops:
  6.5 100.6 %all-gather.3.cloned.1.call-start = ((), (), s32[]{:S(2)}) async-start(), calls=%async_computation | async-start | bytes 25362432 | tf_op jit(solution)/shard_map/all_gather | solution.py:97
  7.3 185.0 %all-gather.5.cloned.1.call-start = ((), (), s32[]{:S(2)}) async-start(), calls=%async_computation.1 | async-start | bytes 8912896 | tf_op jit(solution)/shard_map/all_gather | solution.py:101
  107.1 15.4 %copy-start.1 = (bf16[2048]{0:T(1024)(128)(2,1)S(1)}, bf16[2048]{0:T(1024)(128)(2,1)}, u32[]{:S(2)}) copy-start(bf16[2048]{0:T(1024)(128)(2,1)} %param.8) | copy-start | bytes 12292
  124.2 8.0 %copy-start = (bf16[512,2048]{1,0:T(8,128)(2,1)S(1)}, bf16[512,2048]{1,0:T(8,128)(2,1)}, u32[]{:S(2)}) copy-start(bf16[512,2048]{1,0:T(8,128)(2,1)} %fusion.4.x_ref) | copy-start | bytes 6291460
Sparse Core Ops, SparseCore 0:
  10.4 96.6 all-gather.2
  122.7 69.5 all-gather.4

commit v9 on v6

--- a/solution.py
+++ b/solution.py
@@ -66,10 +66,12 @@
     key_feats, values, local = kv_memory(normed, weight.T)
     key_feats = key_feats.reshape(tok_rows, H, DH)
     values = values.reshape(tok_rows, H, DH)
-    gathered = lax.all_gather(local[None], ("y", "x"), axis=0, tiled=True)
+    gathered = lax.all_gather(local, ("y", "x"), axis=1, tiled=True)
     seq_here = lax.axis_index(("y", "x"))
-    earlier = (jnp.arange(gathered.shape[0]) < seq_here).astype(jnp.bfloat16)
-    before = jnp.einsum("c,chde->hde", earlier, gathered, preferred_element_type=jnp.float32)
+    sel_row = jnp.arange(DH)[:, None]
+    sel_col = jnp.arange(gathered.shape[1])[None, :]
+    select = ((sel_col % DH == sel_row) & (sel_col // DH < seq_here)).astype(jnp.bfloat16)
+    before = jnp.einsum("rc,hce->hre", select, gathered, preferred_element_type=jnp.float32)
     memory = prefix_state[0] + before
     queries = jnp.dot(normed, weight[:, :D], preferred_element_type=jnp.float32)
     queries = feature_map(queries).astype(jnp.bfloat16).reshape(tok_rows, H, DH)

time: 212 us -> 213 us (level)
    dot_general x1 -> x0, matrix products: 8.45 us -> none  [body(): jnp.einsum('c,chde->hde', earlier, gathered, preferred_element_type=jnp.f...]
    dot_general x1, matrix products: 1.02 us -> 8.62 us  [body(): jnp.einsum('bhd,hde->bhe', queries, memory.astype(jnp.bfloat16), preferre...]
where the time goes in v9:
time: 213 us
  waiting for transfers between devices  136 us (64%)
  matrix products  28.8 us (14%)
  Pallas kernels  15.4 us (7%)
  between operations  13.5 us (6%)
  local copies, waits for them, and re-layouts  10.4 us (5%)
  other arithmetic  9.06 us (4%)
    all_gather x1, waiting for transfers between devices, body(): weight = lax.all_gather(qkv_weight, ('dp', 'y', 'x'), axis=1, tiled=True)  93.6 us
    all_gather x1, waiting for transfers between devices, body(): gathered = lax.all_gather(local, ('y', 'x'), axis=1, tiled=True)  41.4 us
    pallas_call x1, Pallas kernels, kv_memory(): pl.pallas_call(kv_memory_kernel, grid=(H // heads_per_step,), in_specs=[p...  15.4 us
    dot_general x1, matrix products, body(): queries = jnp.dot(normed, weight[:, :D], preferred_element_type=jnp.float32)  10.2 us
    dot_general x1, matrix products, body(): jnp.einsum('hbc,che->bhe', scores, values, preferred_element_type=jnp.flo...  10 us
    dot_general x1, matrix products, body(): jnp.einsum('bhd,hde->bhe', queries, memory.astype(jnp.bfloat16), preferre...  8.62 us
  transfers between devices with their start and end apart: 2, of which 2 were waited for; matrix products, arithmetic and copies ran while one was open for 16% of the time, Pallas kernels for 0%

profile of v9, /device:TPU:1, one launch (start us, length us, event | category | flops | bytes accessed | tf_op | source)
XLA Modules:
  0.0 212.9 jit_solution(14480782108374031844)
XLA Ops:
  6.5 0.0 all-gather.3.cloned.1.call-start
  6.5 0.7 all-gather.3.cloned.1.call-update
  7.3 0.0 all-gather.5.cloned.1.call-start
  7.3 0.7 convert_element_type.28
  8.0 2.1 fusion.2
  10.1 3.5 %fusion.4.x_ref = bf16[512,2048]{1,0:T(8,128)(2,1)} fusion(bf16[1,512,2048]{2,1,0:T(8,128)(2,1)} %param.5, f32[2048]{0:T(1024)S(1)} %convert_element_type.28, f32[512]{0:T(512)S(1)} %add_rsqrt_fusion.1), kind=kLoop, calls=%fused_computation.7 | loop fusion | flops 4194304 | bytes 4204544 | tf_op jit(solution)/shard_map/convert_element_type | solution.py:63
  13.5 93.6 %all-gather.3.cloned.1.call-done = bf16[2048,6144]{0,1:T(8,128)(2,1)} async-done(((bf16[2048,48]{0,1:T(8,128)(2,1)}), bf16[2048,6144]{0,1:T(8,128)(2,1)}) %all-gather.3.cloned.1.call-update) | async-done | bytes 25165840 | tf_op jit(solution)/shard_map/all_gather | solution.py:65
  107.1 0.0 copy-start.3
  107.1 15.4 %shard_map.55 = (bf16[512,2048]{1,0:T(8,128)(2,1)}, bf16[512,2048]{1,0:T(8,128)(2,1)}, bf16[16,128,128]{2,1,0:T(8,128)(2,1)}) custom-call(bf16[512,2048]{1,0:T(8,128)(2,1)} %fusion.4.x_ref, bf16[6144,2048]{1,0:T(8,128)(2,1)} %bitcast.57, bf16[6144,2048]{1,0:T(8,128)(2,1)} %bitcast.58), custom_call_target="tpu_custom_call" | custom-call | tf_op jit(solution)/shard_map/pallas_call | solution.py:39
  122.5 0.0 all-gather.5.cloned.1.call-update
  122.6 0.1 iota_compare_fusion
  122.7 0.0 copy-done.3
  122.7 0.0 copy-start
  122.7 4.1 %copy.12 = bf16[512,2048]{0,1:T(8,128)(2,1)} copy(bf16[512,2048]{1,0:T(8,128)(2,1)} %get-tuple-element.9) | data formatting | bytes 4194304 | tf_op jit(solution)/shard_map/reshape | solution.py:68
  126.8 3.9 %copy.13 = bf16[512,2048]{0,1:T(8,128)(2,1)} copy(bf16[512,2048]{1,0:T(8,128)(2,1)} %get-tuple-element.10) | data formatting | bytes 4194304 | tf_op jit(solution)/shard_map/reshape | solution.py:67
  130.7 0.0 copy-done
  130.7 10.2 %fusion.17 = bf16[64,16,8,128]{3,2,1,0:T(8,128)(2,1)} fusion(bf16[512,2048]{1,0:T(8,128)(2,1)S(1)} %copy-done, bf16[2048,6144]{0,1:T(8,128)(2,1)} %all-gather.3.cloned.1.call-done), kind=kOutput, calls=%fused_computation.20 | convolution fusion | flops 4300210176 | bytes 12582912 | tf_op jit(solution)/shard_map/dot_general | solution.py:76
  140.8 10.0 %fusion.10 = f32[16,128,512]{2,1,0:T(8,128)} fusion(bf16[512,16,128]{0,2,1:T(8,128)(2,1)} %bitcast.60, bf16[512,16,128]{0,2,1:T(8,128)(2,1)} %bitcast.61, pred[512,512]{1,0:T(8,128)(4,1)S(1)} %iota_compare_fusion, bf16[64,16,8,128]{3,2,1,0:T(8,128)(2,1)} %fusion.17), kind=kOutput, calls=%fused_computation.14 | convolution fusion | flops 2155872256 | bytes 10747904 | tf_op jit(solution)/shard_map/hbc,che->bhe/dot_general | solution.py:83
  150.9 41.4 %all-gather.5.cloned.1.call-done = bf16[16,2048,128]{2,1,0:T(8,128)(2,1)} async-done(((bf16[16,128,128]{2,1,0:T(8,128)(2,1)}), bf16[16,2048,128]{2,1,0:T(8,128)(2,1)}) %all-gather.5.cloned.1.call-update) | async-done | bytes 8388624 | tf_op jit(solution)/shard_map/all_gather | solution.py:69
  192.3 0.0 copy-done.1
  192.3 0.0 copy-done.2
  192.3 8.6 %fusion.5 = (f32[512,16]{0,1:T(8,128)S(1)}, f32[16,128,512]{2,1,0:T(8,128)}) fusion(f32[16,128,512]{2,1,0:T(8,128)} %fusion.10, bf16[64,16,8,128]{3,2,1,0:T(8,128)(2,1)S(1)} %copy-done.1, bf16[16,2048,128]{2,1,0:T(8,128)(2,1)} %all-gather.5.cloned.1.call-done, f32[1,16,128,128]{3,2,1,0:T(8,128)S(1)} %copy-done.2, s32[2048]{0:T(1024)S(1)} %add_select_fusion.1, ...), kind=kOutput, calls=%fused_computation.10 | convolution fusion | flops 1346363392 | bytes 19965952 | tf_op jit(solution)/shard_map/bhd,hde->bhe/dot_general | solution.py:84
  200.9 2.7 %fusion.7 = bf16[512,16,128]{0,2,1:T(8,128)(2,1)S(1)} fusion(f32[16,128,512]{2,1,0:T(8,128)} %get-tuple-element.12, f32[16,128]{1,0:T(8,128)S(1)} %bitcast_convert_fusion, f32[512,16]{0,1:T(8,128)S(1)} %add_rsqrt_fusion), kind=kLoop, calls=%fused_computation.12 | loop fusion | flops 3145728 | bytes 6332416 | tf_op jit(solution)/shard_map/convert_element_type | solution.py:89
  203.7 2.4 %copy.9 = bf16[1,512,2048]{2,1,0:T(8,128)(2,1)} copy(bf16[1,512,2048]{1,2,0:T(8,128)(2,1)S(1)} %bitcast.59) | data formatting | bytes 4194304 | tf_op jit(solution)/shard_map/reshape | solution.py:90
  (7 shorter events, 0.0 us)
Async XLA Ops:
  6.5 100.6 %all-gather.3.cloned.1.call-start = ((), (), s32[]{:S(2)}) async-start(), calls=%async_computation | async-start | bytes 25362432 | tf_op jit(solution)/shard_map/all_gather | solution.py:65
  7.3 185.0 %all-gather.5.cloned.1.call-start = ((), (), s32[]{:S(2)}) async-start(), calls=%async_computation.1 | async-start | bytes 8912896 | tf_op jit(solution)/shard_map/all_gather | solution.py:69
  107.1 15.6 %copy-start.3 = (bf16[2048]{0:T(1024)(128)(2,1)S(1)}, bf16[2048]{0:T(1024)(128)(2,1)}, u32[]{:S(2)}) copy-start(bf16[2048]{0:T(1024)(128)(2,1)} %param.8) | copy-start | bytes 12292
  122.7 8.0 %copy-start = (bf16[512,2048]{1,0:T(8,128)(2,1)S(1)}, bf16[512,2048]{1,0:T(8,128)(2,1)}, u32[]{:S(2)}) copy-start(bf16[512,2048]{1,0:T(8,128)(2,1)} %fusion.4.x_ref) | copy-start | bytes 6291460
  140.8 51.5 %copy-start.1 = (bf16[64,16,8,128]{3,2,1,0:T(8,128)(2,1)S(1)}, bf16[64,16,8,128]{3,2,1,0:T(8,128)(2,1)}, u32[]{:S(2)}) copy-start(bf16[64,16,8,128]{3,2,1,0:T(8,128)(2,1)} %fusion.17) | copy-start | bytes 6291460
  140.8 51.5 %copy-start.2 = (f32[1,16,128,128]{3,2,1,0:T(8,128)S(1)}, f32[1,16,128,128]{3,2,1,0:T(8,128)}, u32[]{:S(2)}) copy-start(f32[1,16,128,128]{3,2,1,0:T(8,128)} %param.9) | copy-start | bytes 3145732
Sparse Core Ops, SparseCore 0:
  10.4 96.6 all-gather.2
  122.7 69.5 all-gather.4

commit v10 on v7

--- a/solution.py
+++ b/solution.py
@@ -64,15 +64,15 @@
         state = p_ref[j]
         for c in range(g_ref.shape[0]):
             state = state + jnp.where(c < here, g_ref[c, j].astype(jnp.float32), 0.0)
+        carried = jnp.dot(q_ref[j], state.astype(jnp.bfloat16), preferred_element_type=jnp.float32)
+        numerator = carried + w_ref[j]
+        scale = lax.rsqrt(jnp.mean(numerator * numerator, axis=-1, keepdims=True) + epsilon)
         part = slice(j * DH, (j + 1) * DH)
-        carried = jnp.dot(q_ref[:, part], state.astype(jnp.bfloat16), preferred_element_type=jnp.float32)
-        numerator = carried + w_ref[:, part]
-        scale = lax.rsqrt(jnp.mean(numerator * numerator, axis=-1, keepdims=True) + epsilon)
         o_ref[:, part] = (numerator * scale * gain_ref[:, part]).astype(o_ref.dtype)
 
 
-def attend_tail(here, gathered, prefix, queries, within, gains, heads_per_step=2):
-    rows = queries.shape[0]
+def attend_tail(here, gathered, prefix, queries, within, gains, heads_per_step=4):
+    rows = queries.shape[1]
     n_piece = gathered.shape[0]
     width = heads_per_step * DH
     grid_spec = pltpu.PrefetchScalarGridSpec(
@@ -81,8 +81,8 @@
         in_specs=[
             pl.BlockSpec((n_piece, heads_per_step, DH, DH), lambda i, s: (0, i, 0, 0)),
             pl.BlockSpec((heads_per_step, DH, DH), lambda i, s: (i, 0, 0)),
-            pl.BlockSpec((rows, width), lambda i, s: (0, i)),
-            pl.BlockSpec((rows, width), lambda i, s: (0, i)),
+            pl.BlockSpec((heads_per_step, rows, DH), lambda i, s: (i, 0, 0)),
+            pl.BlockSpec((heads_per_step, rows, DH), lambda i, s: (i, 0, 0)),
             pl.BlockSpec((1, width), lambda i, s: (0, i)),
         ],
         out_specs=pl.BlockSpec((rows, width), lambda i, s: (0, i)),
@@ -113,10 +113,10 @@
         "bhd,chd->hbc", queries.reshape(tok_rows, H, DH), key_feats, preferred_element_type=jnp.float32
     )
     scores = jnp.where(causal[None], scores, 0.0).astype(jnp.bfloat16)
-    within = jnp.einsum("hbc,che->bhe", scores, values, preferred_element_type=jnp.float32)
+    within = jnp.einsum("hbc,che->hbe", scores, values, preferred_element_type=jnp.float32)
     gains = head_gain.astype(jnp.float32).reshape(1, H * DH)
     attended = attend_tail(
-        seq_here, gathered, prefix_state[0], queries, within.reshape(tok_rows, H * DH), gains
+        seq_here, gathered, prefix_state[0], jnp.transpose(queries.reshape(tok_rows, H, DH), (1, 0, 2)), within, gains
     )
     return attended.reshape(1, tok_rows, H * DH)
 

time: 210 us -> 208 us (level)
  waiting for transfers between devices: 130 us -> 141 us
  local copies, waits for them, and re-layouts: 13.4 us -> 5.27 us
    reshape x3 -> x1, local copies, waits for them, and re-layouts: 13.4 us -> 2.39 us  [body(): queries.reshape(tok_rows, H, DH)]
    all_gather x1, waiting for transfers between devices: 35.7 us -> 45.3 us  [body(): gathered = lax.all_gather(local[None], ('y', 'x'), axis=0, tiled=True)]
    convert_element_type x0 -> x1, local copies, waits for them, and re-layouts: none -> 2.87 us  [body(): queries = feature_map(queries).astype(jnp.bfloat16)]
  transfers between devices with their start and end apart: 2 -> 2, of which waited for: 2 -> 2; matrix products, arithmetic and copies ran while one was open for 19% -> 14% of each run, Pallas kernels for 0% -> 0%
where the time goes in v10:
time: 208 us; the launch traced here: 207 us
  waiting for transfers between devices  141 us (68%)
  Pallas kernels  23.8 us (11%)
  matrix products  18.4 us (9%)
  between operations  13.4 us (6%)
  other arithmetic  5.32 us (3%)
  local copies, waits for them, and re-layouts  5.27 us (3%)
    all_gather x1, waiting for transfers between devices, body(): weight = lax.all_gather(qkv_weight, ('dp', 'y', 'x'), axis=1, tiled=True)  95.1 us
    all_gather x1, waiting for transfers between devices, body(): gathered = lax.all_gather(local[None], ('y', 'x'), axis=0, tiled=True)  45.3 us
    pallas_call x1, Pallas kernels, kv_memory(): pl.pallas_call(kv_memory_kernel, grid=(H // heads_per_step,), in_specs=[p...  15.5 us
    dot_general x1, matrix products, body(): queries = jnp.dot(normed, weight[:, :D], preferred_element_type=jnp.float32)  9.63 us
    dot_general x1, matrix products, body(): jnp.einsum('hbc,che->hbe', scores, values, preferred_element_type=jnp.flo...  8.82 us
    pallas_call x1, Pallas kernels, attend_tail(): pl.pallas_call(tail_kernel, grid_spec=grid_spec, out_shape=jax.ShapeDtype...  8.23 us
  transfers between devices with their start and end apart: 2, of which 2 were waited for; matrix products, arithmetic and copies ran while one was open for 14% of the time, Pallas kernels for 0%

profile of v10, /device:TPU:1, one launch (start us, length us, event | category | flops | bytes accessed | tf_op | source)
XLA Modules:
  0.0 207.5 jit_solution(8749878013537031418)
XLA Ops:
  6.5 0.0 copy-start.1
  6.5 0.0 all-gather.4.cloned.1.call-start
  6.5 0.7 all-gather.4.cloned.1.call-update
  7.3 0.0 all-gather.6.cloned.1.call-start
  7.3 0.7 convert_element_type.21
  8.0 2.1 fusion.2
  10.1 0.0 copy-done.1
  10.1 1.9 fusion.4.x_ref
  12.0 95.1 %all-gather.4.cloned.1.call-done = bf16[2048,6144]{0,1:T(8,128)(2,1)} async-done(((bf16[2048,48]{0,1:T(8,128)(2,1)}), bf16[2048,6144]{0,1:T(8,128)(2,1)}) %all-gather.4.cloned.1.call-update) | async-done | bytes 25165840 | tf_op jit(solution)/shard_map/all_gather | solution.py:102
  107.1 0.0 copy-start.2
  107.1 0.0 copy-start
  107.1 15.5 %shard_map.55 = (bf16[512,2048]{1,0:T(8,128)(2,1)}, bf16[512,2048]{1,0:T(8,128)(2,1)}, bf16[16,128,128]{2,1,0:T(8,128)(2,1)}) custom-call(bf16[512,2048]{1,0:T(8,128)(2,1)} %fusion.4.x_ref, bf16[6144,2048]{1,0:T(8,128)(2,1)} %bitcast.30, bf16[6144,2048]{1,0:T(8,128)(2,1)} %bitcast.31), custom_call_target="tpu_custom_call" | custom-call | tf_op jit(solution)/shard_map/pallas_call | solution.py:40
  122.6 0.0 all-gather.6.cloned.1.call-update
  122.7 0.0 copy-done.2
  122.7 0.6 reshape.52
  123.3 0.1 iota_compare_fusion
  123.4 0.0 copy-done
  123.4 9.6 %select_convert_fusion.1 = bf16[512,2048]{1,0:T(8,128)(2,1)} fusion(bf16[512,2048]{1,0:T(8,128)(2,1)S(1)} %copy-done, bf16[2048,6144]{0,1:T(8,128)(2,1)} %all-gather.4.cloned.1.call-done), kind=kOutput, calls=%fused_computation.8 | convolution fusion | flops 4300210176 | bytes 12582912 | tf_op jit(solution)/shard_map/dot_general | solution.py:108
  133.0 2.9 %copy.10 = bf16[512,2048]{0,1:T(8,128)(2,1)S(1)} copy(bf16[512,2048]{1,0:T(8,128)(2,1)} %select_convert_fusion.1) | data formatting | bytes 4194304 | tf_op jit(solution)/shard_map/convert_element_type | solution.py:109
  135.9 2.4 %copy.11 = bf16[512,16,128]{2,0,1:T(8,128)(2,1)} copy(bf16[512,16,128]{0,2,1:T(8,128)(2,1)S(1)} %bitcast.34) | data formatting | bytes 4194304 | tf_op jit(solution)/shard_map/reshape | solution.py:119
  138.3 8.8 %fusion.7.w_ref = f32[16,512,128]{2,1,0:T(8,128)} fusion(bf16[512,16,128]{0,2,1:T(8,128)(2,1)S(1)} %bitcast.35, pred[512,512]{1,0:T(8,128)(4,1)S(1)} %iota_compare_fusion, bf16[512,2048]{1,0:T(8,128)(2,1)} %get-tuple-element.10, bf16[512,2048]{1,0:T(8,128)(2,1)} %get-tuple-element.9), kind=kOutput, calls=%fused_computation.9 | convolution fusion | flops 2155872256 | bytes 10747904 | tf_op jit(solution)/shard_map/hbc,che->hbe/dot_general | solution.py:116
  147.1 45.3 %all-gather.6.cloned.1.call-done = bf16[256,128,128]{2,1,0:T(8,128)(2,1)} async-done(((bf16[16,128,128]{2,1,0:T(8,128)(2,1)}), bf16[256,128,128]{2,1,0:T(8,128)(2,1)}) %all-gather.6.cloned.1.call-update) | async-done | bytes 8388624 | tf_op jit(solution)/shard_map/all_gather | solution.py:106
  192.4 8.2 %shard_map.56 = bf16[512,2048]{1,0:T(8,128)(2,1)} custom-call(s32[1]{0:T(128)} %bitcast.here_ref, bf16[16,16,128,128]{3,2,1,0:T(8,128)(2,1)} %bitcast.32, f32[16,128,128]{2,1,0:T(8,128)} %bitcast.36, bf16[16,512,128]{2,1,0:T(8,128)(2,1)} %bitcast.33, f32[16,512,128]{2,1,0:T(8,128)} %fusion.7.w_ref, f32[1,2048]{1,0:T(1,128)} %bitcast.37), custom_call_target="tpu_custom_call" | custom-call | tf_op jit(solution)/shard_map/pallas_call | solution.py:90
  (1 shorter events, 0.0 us)
Async XLA Ops:
  6.5 3.5 %copy-start.1 = (bf16[1,512,2048]{2,1,0:T(8,128)(2,1)S(1)}, bf16[1,512,2048]{2,1,0:T(8,128)(2,1)}, u32[]{:S(2)}) copy-start(bf16[1,512,2048]{2,1,0:T(8,128)(2,1)} %param.5) | copy-start | bytes 6291460
  6.5 100.6 %all-gather.4.cloned.1.call-start = ((), (), s32[]{:S(2)}) async-start(), calls=%async_computation | async-start | bytes 25362432 | tf_op jit(solution)/shard_map/all_gather | solution.py:102
  7.3 185.2 %all-gather.6.cloned.1.call-start = ((), (), s32[]{:S(2)}) async-start(), calls=%async_computation.1 | async-start | bytes 8912896 | tf_op jit(solution)/shard_map/all_gather | solution.py:106
  107.1 15.6 %copy-start.2 = (bf16[2048]{0:T(1024)(128)(2,1)S(1)}, bf16[2048]{0:T(1024)(128)(2,1)}, u32[]{:S(2)}) copy-start(bf16[2048]{0:T(1024)(128)(2,1)} %param.8) | copy-start | bytes 12292
  107.1 16.2 %copy-start = (bf16[512,2048]{1,0:T(8,128)(2,1)S(1)}, bf16[512,2048]{1,0:T(8,128)(2,1)}, u32[]{:S(2)}) copy-start(bf16[512,2048]{1,0:T(8,128)(2,1)} %fusion.4.x_ref) | copy-start | bytes 6291460
Sparse Core Ops, SparseCore 0:
  10.4 96.6 all-gather.3
  122.8 69.5 all-gather.5

commit v11 on v10

--- a/solution.py
+++ b/solution.py
@@ -61,9 +61,9 @@
 def tail_kernel(here_ref, g_ref, p_ref, q_ref, w_ref, gain_ref, o_ref):
     here = here_ref[0]
     for j in range(p_ref.shape[0]):
-        state = p_ref[j]
-        for c in range(g_ref.shape[0]):
-            state = state + jnp.where(c < here, g_ref[c, j].astype(jnp.float32), 0.0)
+        state = lax.fori_loop(
+            0, here, lambda c, acc: acc + g_ref[c, j].astype(jnp.float32), p_ref[j]
+        )
         carried = jnp.dot(q_ref[j], state.astype(jnp.bfloat16), preferred_element_type=jnp.float32)
         numerator = carried + w_ref[j]
         scale = lax.rsqrt(jnp.mean(numerator * numerator, axis=-1, keepdims=True) + epsilon)

time: 208 us -> 209 us (level)
  no operation moved by 1% of the time
where the time goes in v11:
time: 209 us; the launch traced here: 208 us
  waiting for transfers between devices  141 us (67%)
  Pallas kernels  24.5 us (12%)
  matrix products  18.4 us (9%)
  between operations  13.4 us (6%)
  other arithmetic  5.32 us (3%)
  local copies, waits for them, and re-layouts  5.27 us (3%)
    all_gather x1, waiting for transfers between devices, body(): weight = lax.all_gather(qkv_weight, ('dp', 'y', 'x'), axis=1, tiled=True)  95.1 us
    all_gather x1, waiting for transfers between devices, body(): gathered = lax.all_gather(local[None], ('y', 'x'), axis=0, tiled=True)  45.3 us
    pallas_call x1, Pallas kernels, kv_memory(): pl.pallas_call(kv_memory_kernel, grid=(H // heads_per_step,), in_specs=[p...  15.5 us
    dot_general x1, matrix products, body(): queries = jnp.dot(normed, weight[:, :D], preferred_element_type=jnp.float32)  9.63 us
    pallas_call x1, Pallas kernels, attend_tail(): pl.pallas_call(tail_kernel, grid_spec=grid_spec, out_shape=jax.ShapeDtype...  9.01 us
    dot_general x1, matrix products, body(): jnp.einsum('hbc,che->hbe', scores, values, preferred_element_type=jnp.flo...  8.82 us
  transfers between devices with their start and end apart: 2, of which 2 were waited for; matrix products, arithmetic and copies ran while one was open for 14% of the time, Pallas kernels for 0%

profile of v11, /device:TPU:1, one launch (start us, length us, event | category | flops | bytes accessed | tf_op | source)
XLA Modules:
  0.0 208.3 jit_solution(3189242616501805007)
XLA Ops:
  6.5 0.0 copy-start.1
  6.5 0.0 all-gather.4.cloned.1.call-start
  6.5 0.7 all-gather.4.cloned.1.call-update
  7.3 0.0 all-gather.6.cloned.1.call-start
  7.3 0.7 convert_element_type.21
  8.0 2.1 fusion.2
  10.1 0.0 copy-done.1
  10.1 1.9 fusion.4.x_ref
  12.0 95.1 %all-gather.4.cloned.1.call-done = bf16[2048,6144]{0,1:T(8,128)(2,1)} async-done(((bf16[2048,48]{0,1:T(8,128)(2,1)}), bf16[2048,6144]{0,1:T(8,128)(2,1)}) %all-gather.4.cloned.1.call-update) | async-done | bytes 25165840 | tf_op jit(solution)/shard_map/all_gather | solution.py:102
  107.1 0.0 copy-start.2
  107.1 0.0 copy-start
  107.1 15.5 %shard_map.55 = (bf16[512,2048]{1,0:T(8,128)(2,1)}, bf16[512,2048]{1,0:T(8,128)(2,1)}, bf16[16,128,128]{2,1,0:T(8,128)(2,1)}) custom-call(bf16[512,2048]{1,0:T(8,128)(2,1)} %fusion.4.x_ref, bf16[6144,2048]{1,0:T(8,128)(2,1)} %bitcast.30, bf16[6144,2048]{1,0:T(8,128)(2,1)} %bitcast.31), custom_call_target="tpu_custom_call" | custom-call | tf_op jit(solution)/shard_map/pallas_call | solution.py:40
  122.6 0.0 all-gather.6.cloned.1.call-update
  122.7 0.0 copy-done.2
  122.7 0.6 reshape.52
  123.3 0.1 iota_compare_fusion
  123.4 0.0 copy-done
  123.4 9.6 %select_convert_fusion.1 = bf16[512,2048]{1,0:T(8,128)(2,1)} fusion(bf16[512,2048]{1,0:T(8,128)(2,1)S(1)} %copy-done, bf16[2048,6144]{0,1:T(8,128)(2,1)} %all-gather.4.cloned.1.call-done), kind=kOutput, calls=%fused_computation.8 | convolution fusion | flops 4300210176 | bytes 12582912 | tf_op jit(solution)/shard_map/dot_general | solution.py:108
  133.0 2.9 %copy.10 = bf16[512,2048]{0,1:T(8,128)(2,1)S(1)} copy(bf16[512,2048]{1,0:T(8,128)(2,1)} %select_convert_fusion.1) | data formatting | bytes 4194304 | tf_op jit(solution)/shard_map/convert_element_type | solution.py:109
  135.9 2.4 %copy.11 = bf16[512,16,128]{2,0,1:T(8,128)(2,1)} copy(bf16[512,16,128]{0,2,1:T(8,128)(2,1)S(1)} %bitcast.34) | data formatting | bytes 4194304 | tf_op jit(solution)/shard_map/reshape | solution.py:119
  138.3 8.8 %fusion.7.w_ref = f32[16,512,128]{2,1,0:T(8,128)} fusion(bf16[512,16,128]{0,2,1:T(8,128)(2,1)S(1)} %bitcast.35, pred[512,512]{1,0:T(8,128)(4,1)S(1)} %iota_compare_fusion, bf16[512,2048]{1,0:T(8,128)(2,1)} %get-tuple-element.10, bf16[512,2048]{1,0:T(8,128)(2,1)} %get-tuple-element.9), kind=kOutput, calls=%fused_computation.9 | convolution fusion | flops 2155872256 | bytes 10747904 | tf_op jit(solution)/shard_map/hbc,che->hbe/dot_general | solution.py:116
  147.1 45.3 %all-gather.6.cloned.1.call-done = bf16[256,128,128]{2,1,0:T(8,128)(2,1)} async-done(((bf16[16,128,128]{2,1,0:T(8,128)(2,1)}), bf16[256,128,128]{2,1,0:T(8,128)(2,1)}) %all-gather.6.cloned.1.call-update) | async-done | bytes 8388624 | tf_op jit(solution)/shard_map/all_gather | solution.py:106
  192.4 9.0 %shard_map.56 = bf16[512,2048]{1,0:T(8,128)(2,1)} custom-call(s32[1]{0:T(128)} %bitcast.here_ref, bf16[16,16,128,128]{3,2,1,0:T(8,128)(2,1)} %bitcast.32, f32[16,128,128]{2,1,0:T(8,128)} %bitcast.36, bf16[16,512,128]{2,1,0:T(8,128)(2,1)} %bitcast.33, f32[16,512,128]{2,1,0:T(8,128)} %fusion.7.w_ref, f32[1,2048]{1,0:T(1,128)} %bitcast.37), custom_call_target="tpu_custom_call" | custom-call | tf_op jit(solution)/shard_map/pallas_call | solution.py:90
  (1 shorter events, 0.0 us)
Async XLA Ops:
  6.5 3.5 %copy-start.1 = (bf16[1,512,2048]{2,1,0:T(8,128)(2,1)S(1)}, bf16[1,512,2048]{2,1,0:T(8,128)(2,1)}, u32[]{:S(2)}) copy-start(bf16[1,512,2048]{2,1,0:T(8,128)(2,1)} %param.5) | copy-start | bytes 6291460
  6.5 100.6 %all-gather.4.cloned.1.call-start = ((), (), s32[]{:S(2)}) async-start(), calls=%async_computation | async-start | bytes 25362432 | tf_op jit(solution)/shard_map/all_gather | solution.py:102
  7.3 185.2 %all-gather.6.cloned.1.call-start = ((), (), s32[]{:S(2)}) async-start(), calls=%async_computation.1 | async-start | bytes 8912896 | tf_op jit(solution)/shard_map/all_gather | solution.py:106
  107.1 15.6 %copy-start.2 = (bf16[2048]{0:T(1024)(128)(2,1)S(1)}, bf16[2048]{0:T(1024)(128)(2,1)}, u32[]{:S(2)}) copy-start(bf16[2048]{0:T(1024)(128)(2,1)} %param.8) | copy-start | bytes 12292
  107.1 16.2 %copy-start = (bf16[512,2048]{1,0:T(8,128)(2,1)S(1)}, bf16[512,2048]{1,0:T(8,128)(2,1)}, u32[]{:S(2)}) copy-start(bf16[512,2048]{1,0:T(8,128)(2,1)} %fusion.4.x_ref) | copy-start | bytes 6291460
Sparse Core Ops, SparseCore 0:
  10.4 96.6 all-gather.3
  122.8 69.5 all-gather.5

commit v12 on v8

--- a/solution.py
+++ b/solution.py
@@ -2,7 +2,6 @@
 import jax.numpy as jnp
 from jax import lax
 from jax.experimental import pallas as pl
-from jax.experimental.pallas import tpu as pltpu
 from jax.sharding import Mesh, PartitionSpec as P
 
 D = 2048
@@ -58,35 +57,64 @@
     )(normed, weight_t, weight_t)
 
 
-def tail_kernel(sel_ref, g_ref, p_ref, q_ref, w_ref, gain_ref, o_ref):
-    sel = sel_ref[...]
-    for j in range(p_ref.shape[0]):
-        state = p_ref[j] + jnp.dot(sel, g_ref[j], preferred_element_type=jnp.float32)
+def tail_kernel(m_ref, q_ref, w_ref, gain_ref, o_ref):
+    for j in range(m_ref.shape[0]):
+        carried = jnp.dot(q_ref[j], m_ref[j].astype(jnp.bfloat16), preferred_element_type=jnp.float32)
+        numerator = carried + w_ref[j]
+        scale = lax.rsqrt(jnp.mean(numerator * numerator, axis=-1, keepdims=True) + epsilon)
         part = slice(j * DH, (j + 1) * DH)
-        carried = jnp.dot(q_ref[:, part], state.astype(jnp.bfloat16), preferred_element_type=jnp.float32)
-        numerator = carried + w_ref[:, part]
-        scale = lax.rsqrt(jnp.mean(numerator * numerator, axis=-1, keepdims=True) + epsilon)
         o_ref[:, part] = (numerator * scale * gain_ref[:, part]).astype(o_ref.dtype)
 
 
-def attend_tail(select, gathered, prefix, queries, within, gains, heads_per_step=2):
-    rows = queries.shape[0]
-    stack = gathered.shape[1]
+def attend_tail(memory, queries, within, gains, heads_per_step=4):
+    rows = queries.shape[1]
     width = heads_per_step * DH
     return pl.pallas_call(
         tail_kernel,
         grid=(H // heads_per_step,),
         in_specs=[
-            pl.BlockSpec((DH, stack), lambda i: (0, 0)),
-            pl.BlockSpec((heads_per_step, stack, DH), lambda i: (i, 0, 0)),
             pl.BlockSpec((heads_per_step, DH, DH), lambda i: (i, 0, 0)),
-            pl.BlockSpec((rows, width), lambda i: (0, i)),
-            pl.BlockSpec((rows, width), lambda i: (0, i)),
+            pl.BlockSpec((heads_per_step, rows, DH), lambda i: (i, 0, 0)),
+            pl.BlockSpec((heads_per_step, rows, DH), lambda i: (i, 0, 0)),
             pl.BlockSpec((1, width), lambda i: (0, i)),
         ],
         out_specs=pl.BlockSpec((rows, width), lambda i: (0, i)),
         out_shape=jax.ShapeDtypeStruct((rows, H * DH), jnp.bfloat16),
-    )(select, gathered, prefix, queries, within, gains)
+    )(memory, queries, within, gains)
+
+
+def ring_shift(value, axis, shift, size, wrap=True):
+    pairs = [(j, (j + shift) % size) for j in range(size) if wrap or j + shift < size]
+    return lax.ppermute(value, axis, pairs)
+
+
+def memory_before(local):
+    n_x = lax.axis_size("x")
+    n_y = lax.axis_size("y")
+    x_here = lax.axis_index("x")
+    half = local.shape[0] // 2
+    from_left = ring_shift(local, "x", 1, n_x)
+    from_right = ring_shift(local, "x", -1, n_x)
+    far = jnp.concatenate(
+        [ring_shift(from_left[:half], "x", 1, n_x), ring_shift(from_right[half:], "x", -1, n_x)], axis=0
+    )
+    f32 = lambda v: v.astype(jnp.float32)
+    row_total = f32(local) + f32(from_left) + f32(far) + f32(from_right)
+    row_before = (
+        jnp.where(x_here >= 1, f32(from_left), 0.0)
+        + jnp.where(x_here >= 2, f32(far), 0.0)
+        + jnp.where(x_here >= 3, f32(from_right), 0.0)
+    )
+    per = local.shape[0] // n_x
+    quarter = lax.dynamic_slice_in_dim(row_total, x_here * per, per, axis=0)
+    rows_before = quarter * 0.0
+    for shift in range(1, n_y):
+        rows_before = rows_before + ring_shift(quarter, "y", shift, n_y, wrap=False)
+    got = [rows_before] + [ring_shift(rows_before, "x", k, n_x) for k in range(1, n_x)]
+    stacked = jnp.stack(got)
+    order = (x_here - jnp.arange(n_x)) % n_x
+    earlier_rows = jnp.take(stacked, order, axis=0).reshape(local.shape)
+    return earlier_rows + row_before
 
 
 def body(tokens, input_gain, qkv_weight, head_gain, prefix_state):
@@ -98,11 +126,7 @@
     key_feats, values, local = kv_memory(normed, weight.T)
     key_feats = key_feats.reshape(tok_rows, H, DH)
     values = values.reshape(tok_rows, H, DH)
-    gathered = lax.all_gather(local, ("y", "x"), axis=1, tiled=True)
-    seq_here = lax.axis_index(("y", "x"))
-    sel_row = jnp.arange(DH)[:, None]
-    sel_col = jnp.arange(gathered.shape[1])[None, :]
-    select = ((sel_col % DH == sel_row) & (sel_col // DH < seq_here)).astype(jnp.bfloat16)
+    memory = prefix_state[0] + memory_before(local)
     queries = jnp.dot(normed, weight[:, :D], preferred_element_type=jnp.float32)
     queries = feature_map(queries).astype(jnp.bfloat16)
 
@@ -111,10 +135,10 @@
         "bhd,chd->hbc", queries.reshape(tok_rows, H, DH), key_feats, preferred_element_type=jnp.float32
     )
     scores = jnp.where(causal[None], scores, 0.0).astype(jnp.bfloat16)
-    within = jnp.einsum("hbc,che->bhe", scores, values, preferred_element_type=jnp.float32)
+    within = jnp.einsum("hbc,che->hbe", scores, values, preferred_element_type=jnp.float32)
     gains = head_gain.astype(jnp.float32).reshape(1, H * DH)
     attended = attend_tail(
-        select, gathered, prefix_state[0], queries, within.reshape(tok_rows, H * DH), gains
+        memory, jnp.transpose(queries.reshape(tok_rows, H, DH), (1, 0, 2)), within, gains
     )
     return attended.reshape(1, tok_rows, H * DH)
 

time: 212 us -> 211 us (level)
  starting transfers between devices: 0.04 us -> 17.7 us
  waiting for transfers between devices: 129 us -> 115 us
  Pallas kernels: 27.9 us -> 21.2 us
  other arithmetic: 7.9 us -> 13.9 us
  local copies, waits for them, and re-layouts: 13.4 us -> 9.24 us
    all_gather x1 -> x0, waiting for transfers between devices: 34.9 us -> none  [body(): gathered = lax.all_gather(local, ('y', 'x'), axis=1, tiled=True)]
    ppermute x0 -> x10, waiting for transfers between devices: none -> 19.4 us  [ring_shift(): return lax.ppermute(value, axis, pairs)]
    ppermute x0 -> x10, starting transfers between devices: none -> 17.7 us  [ring_shift(): return lax.ppermute(value, axis, pairs)]
    reshape x2 -> x1, local copies, waits for them, and re-layouts: 9.48 us -> 2.4 us  [body(): queries.reshape(tok_rows, H, DH)]
    pallas_call x1, Pallas kernels: 12.5 us -> 5.79 us  [attend_tail(): pl.pallas_call(tail_kernel, grid=(H // heads_per_step,), in_specs=[pl.Blo...]
    add x0 -> x3, other arithmetic: none -> 6.38 us  [the longest x1 2.79 us: body(): memory = prefix_state[0] + memory_before(local)]
    convert_element_type x0 -> x1, local copies, waits for them, and re-layouts: none -> 2.86 us  [body(): queries = feature_map(queries).astype(jnp.bfloat16)]
  transfers between devices with their start and end apart: 2 -> 11, of which waited for: 2 -> 5; matrix products, arithmetic and copies ran while one was open for 19% -> 16% of each run, Pallas kernels for 0% -> 0%
where the time goes in v12:
time: 211 us; the launch traced here: 209 us
  waiting for transfers between devices  115 us (55%)
  Pallas kernels  21.2 us (10%)
  matrix products  18.5 us (9%)
  starting transfers between devices  17.7 us (8%)
  other arithmetic  13.9 us (7%)
  between operations  13.5 us (6%)
  local copies, waits for them, and re-layouts  9.24 us (4%)
    all_gather x1, waiting for transfers between devices, body(): weight = lax.all_gather(qkv_weight, ('dp', 'y', 'x'), axis=1, tiled=True)  95.2 us
    ppermute x10, waiting for transfers between devices, ring_shift(): return lax.ppermute(value, axis, pairs)  19.4 us
    ppermute x10, starting transfers between devices, ring_shift(): return lax.ppermute(value, axis, pairs)  17.7 us
    pallas_call x1, Pallas kernels, kv_memory(): pl.pallas_call(kv_memory_kernel, grid=(H // heads_per_step,), in_specs=[p...  15.4 us
    dot_general x1, matrix products, body(): queries = jnp.dot(normed, weight[:, :D], preferred_element_type=jnp.float32)  9.62 us
    dot_general x1, matrix products, body(): jnp.einsum('hbc,che->hbe', scores, values, preferred_element_type=jnp.flo...  8.84 us
    pallas_call x1, Pallas kernels, attend_tail(): pl.pallas_call(tail_kernel, grid=(H // heads_per_step,), in_specs=[pl.Blo...  5.79 us
  transfers between devices with their start and end apart: 11, of which 5 were waited for; matrix products, arithmetic and copies ran while one was open for 16% of the time, Pallas kernels for 0%

profile of v12, /device:TPU:1, one launch (start us, length us, event | category | flops | bytes accessed | tf_op | source)
XLA Modules:
  0.0 209.4 jit_solution(11825584064865553800)
XLA Ops:
  7.9 2.1 fusion.2
  10.0 1.9 fusion.4.x_ref
  11.9 95.2 %all-gather.2.cloned.1.call-done = bf16[2048,6144]{0,1:T(8,128)(2,1)} async-done(((bf16[2048,48]{0,1:T(8,128)(2,1)}), bf16[2048,6144]{0,1:T(8,128)(2,1)}) %all-gather.2.cloned.1.call-update) | async-done | bytes 25165840 | tf_op jit(solution)/shard_map/all_gather | solution.py:125
  107.1 15.4 %shard_map.55 = (bf16[512,2048]{1,0:T(8,128)(2,1)}, bf16[512,2048]{1,0:T(8,128)(2,1)}, bf16[16,128,128]{2,1,0:T(8,128)(2,1)}) custom-call(bf16[512,2048]{1,0:T(8,128)(2,1)} %fusion.4.x_ref, bf16[6144,2048]{1,0:T(8,128)(2,1)} %bitcast.34, bf16[6144,2048]{1,0:T(8,128)(2,1)} %bitcast.35), custom_call_target="tpu_custom_call" | custom-call | tf_op jit(solution)/shard_map/pallas_call | solution.py:39
  122.5 2.4 %collective-permute-start.2 = (bf16[16,128,128]{2,1,0:T(8,128)(2,1)}, bf16[16,128,128]{2,1,0:T(8,128)(2,1)S(1)}, u32[]{:S(2)}, u32[]{:S(2)}) collective-permute-start(bf16[16,128,128]{2,1,0:T(8,128)(2,1)} %get-tuple-element.8), channel_id=1, source_target_pairs={{0,3},{1,0},{2,1},{3,2},{4,7},{5,4},{6,5},{7,6},{8,11},{9,8},{10,9... | collective-permute-start | bytes 1572872 | tf_op jit(solution)/shard_map/ppermute | solution.py:88
  124.9 11.4 %collective-permute-done.2 = bf16[16,128,128]{2,1,0:T(8,128)(2,1)S(1)} collective-permute-done((bf16[16,128,128]{2,1,0:T(8,128)(2,1)}, bf16[16,128,128]{2,1,0:T(8,128)(2,1)S(1)}, u32[]{:S(2)}, u32[]{:S(2)}) %collective-permute-start.2) | collective-permute-done | bytes 524320 | tf_op jit(solution)/shard_map/ppermute | solution.py:88
  136.4 3.4 %collective-permute-start.3 = (bf16[8,128,128]{2,1,0:T(8,128)(2,1)S(1)}, bf16[8,128,128]{2,1,0:T(8,128)(2,1)S(1)}, u32[]{:S(2)}, u32[]{:S(2)}) collective-permute-start(bf16[8,128,128]{2,1,0:T(8,128)(2,1)S(1)} %slice.15), channel_id=1, source_target_pairs={{0,3},{1,0},{2,1},{3,2},{4,7},{5,4},{6,5},{7,6},{8,11},{9,8},{10,9... | collective-permute-start | bytes 786440 | tf_op jit(solution)/shard_map/ppermute | solution.py:88
  140.6 0.8 iota_compare_fusion
  141.6 2.6 %collective-permute-done.3 = bf16[8,128,128]{2,1,0:T(8,128)(2,1)S(1)} collective-permute-done((bf16[8,128,128]{2,1,0:T(8,128)(2,1)S(1)}, bf16[8,128,128]{2,1,0:T(8,128)(2,1)S(1)}, u32[]{:S(2)}, u32[]{:S(2)}) %collective-permute-start.3) | collective-permute-done | bytes 262176 | tf_op jit(solution)/shard_map/ppermute | solution.py:88
  144.3 3.2 %collective-permute-done.1 = bf16[8,128,128]{2,1,0:T(8,128)(2,1)S(1)} collective-permute-done((bf16[8,128,128]{2,1,0:T(8,128)(2,1)S(1)}, bf16[8,128,128]{2,1,0:T(8,128)(2,1)S(1)}, u32[]{:S(2)}, u32[]{:S(2)}) %collective-permute-start.1) | collective-permute-done | bytes 262176 | tf_op jit(solution)/shard_map/ppermute | solution.py:88
  148.2 1.6 dynamic-slice_add_fusion
  149.9 5.5 %collective-permute-start.5 = (f32[4,128,128]{2,1,0:T(8,128)}, f32[4,128,128]{2,1,0:T(8,128)}, u32[]{:S(2)}, u32[]{:S(2)}) collective-permute-start(f32[4,128,128]{2,1,0:T(8,128)} %dynamic-slice_add_fusion), channel_id=1, source_target_pairs={{0,8},{4,12},{1,9},{5,13},{2,10},{6,14},{3,11},{7,15},{16,24},{20,... | collective-permute-start | bytes 786440 | tf_op jit(solution)/shard_map/ppermute | solution.py:88
  155.3 2.9 %collective-permute-start.4 = (f32[4,128,128]{2,1,0:T(8,128)}, f32[4,128,128]{2,1,0:T(8,128)}, u32[]{:S(2)}, u32[]{:S(2)}) collective-permute-start(f32[4,128,128]{2,1,0:T(8,128)} %dynamic-slice_add_fusion), channel_id=1, source_target_pairs={{0,4},{4,8},{8,12},{1,5},{5,9},{9,13},{2,6},{6,10},{10,14},{3,7},{... | collective-permute-start | bytes 786440 | tf_op jit(solution)/shard_map/ppermute | solution.py:88
  158.2 2.0 collective-permute-start.6
  160.2 9.6 %select_convert_fusion.1 = bf16[512,2048]{1,0:T(8,128)(2,1)} fusion(bf16[512,2048]{1,0:T(8,128)(2,1)S(1)} %copy-done, bf16[2048,6144]{0,1:T(8,128)(2,1)} %all-gather.2.cloned.1.call-done), kind=kOutput, calls=%fused_computation.9 | convolution fusion | flops 4300210176 | bytes 12582912 | tf_op jit(solution)/shard_map/dot_general | solution.py:130
  169.8 2.5 %copy.11 = bf16[512,2048]{0,1:T(8,128)(2,1)} copy(bf16[512,2048]{1,0:T(8,128)(2,1)S(1)} %copy-done.2) | data formatting | bytes 4194304 | tf_op jit(solution)/shard_map/reshape | solution.py:127
  172.3 2.9 %copy.7 = bf16[512,2048]{0,1:T(8,128)(2,1)S(1)} copy(bf16[512,2048]{1,0:T(8,128)(2,1)} %select_convert_fusion.1) | data formatting | bytes 4194304 | tf_op jit(solution)/shard_map/convert_element_type | solution.py:131
  175.2 1.9 add_add_fusion
  178.6 8.8 %fusion.7.w_ref = f32[16,512,128]{2,1,0:T(8,128)} fusion(bf16[512,16,128]{0,2,1:T(8,128)(2,1)S(1)} %bitcast.36, bf16[512,16,128]{0,2,1:T(8,128)(2,1)} %bitcast.39, pred[512,512]{1,0:T(8,128)(4,1)} %iota_compare_fusion, bf16[512,2048]{1,0:T(8,128)(2,1)} %get-tuple-element.10), kind=kOutput, calls=%fused_computation.10 | convolution fusion | flops 2155872256 | bytes 10747904 | tf_op jit(solution)/shard_map/hbc,che->hbe/dot_general | solution.py:138
  187.5 2.4 %copy.8 = bf16[512,16,128]{2,0,1:T(8,128)(2,1)} copy(bf16[512,16,128]{0,2,1:T(8,128)(2,1)S(1)} %bitcast.37) | data formatting | bytes 4194304 | tf_op jit(solution)/shard_map/reshape | solution.py:141
  189.9 2.1 %collective-permute-done.7 = f32[4,128,128]{2,1,0:T(8,128)} collective-permute-done((f32[4,128,128]{2,1,0:T(8,128)}, f32[4,128,128]{2,1,0:T(8,128)}, u32[]{:S(2)}, u32[]{:S(2)}) %collective-permute-start.7) | collective-permute-done | bytes 262176 | tf_op jit(solution)/shard_map/ppermute | solution.py:88
  192.0 1.3 pad_maximum_fusion
  193.9 2.8 %fusion.11.m_ref = f32[16,128,128]{2,1,0:T(8,128)} fusion(f32[4,4,128,128]{3,2,1,0:T(8,128)S(1)} %gather_fusion, f32[1,16,128,128]{3,2,1,0:T(8,128)} %param.9, pred[16]{0:T(512)(128)(4,1)S(1)} %broadcast_in_dim.38, pred[]{:T(512)S(6)} %ge.36, pred[]{:T(512)S(6)} %ge.35, pred[]{:T(512)S(6)} %ge.34, bf16[16,128,128]{2,1,0:T(8,128)(2,1)S(1)} %collective-permute-done.2, ...), kind=kLoop, calls=%fused_computation.16 | loop fusion | flops 3145728 | bytes 4718611 | tf_op jit(solution)/shard_map/add | solution.py:129
  196.7 5.8 %shard_map.56 = bf16[512,2048]{1,0:T(8,128)(2,1)} custom-call(f32[16,128,128]{2,1,0:T(8,128)} %fusion.11.m_ref, bf16[16,512,128]{2,1,0:T(8,128)(2,1)} %bitcast.38, f32[16,512,128]{2,1,0:T(8,128)} %fusion.7.w_ref, f32[1,2048]{1,0:T(1,128)} %bitcast.40), custom_call_target="tpu_custom_call" | custom-call | tf_op jit(solution)/shard_map/pallas_call | solution.py:72
  (37 shorter events, 5.3 us)
Async XLA Ops:
  6.5 3.5 %copy-start.1 = (bf16[1,512,2048]{2,1,0:T(8,128)(2,1)S(1)}, bf16[1,512,2048]{2,1,0:T(8,128)(2,1)}, u32[]{:S(2)}) copy-start(bf16[1,512,2048]{2,1,0:T(8,128)(2,1)} %param.5) | copy-start | bytes 6291460
  6.5 100.6 %all-gather.2.cloned.1.call-start = ((), (), s32[]{:S(2)}) async-start(), calls=%async_computation | async-start | bytes 25362432 | tf_op jit(solution)/shard_map/all_gather | solution.py:125
  107.1 32.9 %copy-start.4 = (bf16[2048]{0:T(1024)(128)(2,1)S(1)}, bf16[2048]{0:T(1024)(128)(2,1)}, u32[]{:S(2)}) copy-start(bf16[2048]{0:T(1024)(128)(2,1)} %param.8) | copy-start | bytes 12292
  122.5 13.8 %collective-permute-start.2 = (bf16[16,128,128]{2,1,0:T(8,128)(2,1)}, bf16[16,128,128]{2,1,0:T(8,128)(2,1)S(1)}, u32[]{:S(2)}, u32[]{:S(2)}) collective-permute-start(bf16[16,128,128]{2,1,0:T(8,128)(2,1)} %get-tuple-element.8), channel_id=1, source_target_pairs={{0,3},{1,0},{2,1},{3,2},{4,7},{5,4},{6,5},{7,6},{8,11},{9,8},{10,9... | collective-permute-start | bytes 1572872 | tf_op jit(solution)/shard_map/ppermute | solution.py:88
  124.9 14.8 %collective-permute-start = (bf16[16,128,128]{2,1,0:T(8,128)(2,1)}, bf16[16,128,128]{2,1,0:T(8,128)(2,1)S(1)}, u32[]{:S(2)}, u32[]{:S(2)}) collective-permute-start(bf16[16,128,128]{2,1,0:T(8,128)(2,1)} %get-tuple-element.8), channel_id=1, source_target_pairs={{0,1},{1,2},{2,3},{3,0},{4,5},{5,6},{6,7},{7,4},{8,9},{9,10},{10,1... | collective-permute-start | bytes 1572872 | tf_op jit(solution)/shard_map/ppermute | solution.py:88
  136.4 7.9 %collective-permute-start.3 = (bf16[8,128,128]{2,1,0:T(8,128)(2,1)S(1)}, bf16[8,128,128]{2,1,0:T(8,128)(2,1)S(1)}, u32[]{:S(2)}, u32[]{:S(2)}) collective-permute-start(bf16[8,128,128]{2,1,0:T(8,128)(2,1)S(1)} %slice.15), channel_id=1, source_target_pairs={{0,3},{1,0},{2,1},{3,2},{4,7},{5,4},{6,5},{7,6},{8,11},{9,8},{10,9... | collective-permute-start | bytes 786440 | tf_op jit(solution)/shard_map/ppermute | solution.py:88
  139.8 7.8 %collective-permute-start.1 = (bf16[8,128,128]{2,1,0:T(8,128)(2,1)S(1)}, bf16[8,128,128]{2,1,0:T(8,128)(2,1)S(1)}, u32[]{:S(2)}, u32[]{:S(2)}) collective-permute-start(bf16[8,128,128]{2,1,0:T(8,128)(2,1)S(1)} %slice.14), channel_id=1, source_target_pairs={{0,1},{1,2},{2,3},{3,0},{4,5},{5,6},{6,7},{7,4},{8,9},{9,10},{10,1... | collective-permute-start | bytes 786440 | tf_op jit(solution)/shard_map/ppermute | solution.py:88
  141.5 18.7 %copy-start = (bf16[512,2048]{1,0:T(8,128)(2,1)S(1)}, bf16[512,2048]{1,0:T(8,128)(2,1)}, u32[]{:S(2)}) copy-start(bf16[512,2048]{1,0:T(8,128)(2,1)} %fusion.4.x_ref) | copy-start | bytes 6291460
  147.5 0.7 copy-start.3
  149.9 19.9 %copy-start.2 = (bf16[512,2048]{1,0:T(8,128)(2,1)S(1)}, bf16[512,2048]{1,0:T(8,128)(2,1)}, u32[]{:S(2)}) copy-start(bf16[512,2048]{1,0:T(8,128)(2,1)} %get-tuple-element.9) | copy-start | bytes 6291460
  149.9 25.3 %collective-permute-start.5 = (f32[4,128,128]{2,1,0:T(8,128)}, f32[4,128,128]{2,1,0:T(8,128)}, u32[]{:S(2)}, u32[]{:S(2)}) collective-permute-start(f32[4,128,128]{2,1,0:T(8,128)} %dynamic-slice_add_fusion), channel_id=1, source_target_pairs={{0,8},{4,12},{1,9},{5,13},{2,10},{6,14},{3,11},{7,15},{16,24},{20,... | collective-permute-start | bytes 786440 | tf_op jit(solution)/shard_map/ppermute | solution.py:88
  155.3 19.9 %collective-permute-start.4 = (f32[4,128,128]{2,1,0:T(8,128)}, f32[4,128,128]{2,1,0:T(8,128)}, u32[]{:S(2)}, u32[]{:S(2)}) collective-permute-start(f32[4,128,128]{2,1,0:T(8,128)} %dynamic-slice_add_fusion), channel_id=1, source_target_pairs={{0,4},{4,8},{8,12},{1,5},{5,9},{9,13},{2,6},{6,10},{10,14},{3,7},{... | collective-permute-start | bytes 786440 | tf_op jit(solution)/shard_map/ppermute | solution.py:88
  158.2 17.0 %collective-permute-start.6 = (f32[4,128,128]{2,1,0:T(8,128)}, f32[4,128,128]{2,1,0:T(8,128)}, u32[]{:S(2)}, u32[]{:S(2)}) collective-permute-start(f32[4,128,128]{2,1,0:T(8,128)} %dynamic-slice_add_fusion), channel_id=1, source_target_pairs={{0,12},{1,13},{2,14},{3,15},{16,28},{17,29},{18,30},{19,31},{32,44... | collective-permute-start | bytes 786440 | tf_op jit(solution)/shard_map/ppermute | solution.py:88
  177.2 12.7 %collective-permute-start.9 = (f32[4,128,128]{2,1,0:T(8,128)}, f32[4,128,128]{2,1,0:T(8,128)}, u32[]{:S(2)}, u32[]{:S(2)}) collective-permute-start(f32[4,128,128]{2,1,0:T(8,128)} %add_add_fusion), channel_id=1, source_target_pairs={{0,3},{1,0},{2,1},{3,2},{4,7},{5,4},{6,5},{7,6},{8,11},{9,8},{10,9... | collective-permute-start | bytes 786440 | tf_op jit(solution)/shard_map/ppermute | solution.py:88
  177.4 12.5 %collective-permute-start.8 = (f32[4,128,128]{2,1,0:T(8,128)}, f32[4,128,128]{2,1,0:T(8,128)}, u32[]{:S(2)}, u32[]{:S(2)}) collective-permute-start(f32[4,128,128]{2,1,0:T(8,128)} %add_add_fusion), channel_id=1, source_target_pairs={{0,2},{1,3},{2,0},{3,1},{4,6},{5,7},{6,4},{7,5},{8,10},{9,11},{10,... | collective-permute-start | bytes 786440 | tf_op jit(solution)/shard_map/ppermute | solution.py:88
  178.0 14.0 %collective-permute-start.7 = (f32[4,128,128]{2,1,0:T(8,128)}, f32[4,128,128]{2,1,0:T(8,128)}, u32[]{:S(2)}, u32[]{:S(2)}) collective-permute-start(f32[4,128,128]{2,1,0:T(8,128)} %add_add_fusion), channel_id=1, source_target_pairs={{0,1},{1,2},{2,3},{3,0},{4,5},{5,6},{6,7},{7,4},{8,9},{9,10},{10,1... | collective-permute-start | bytes 786440 | tf_op jit(solution)/shard_map/ppermute | solution.py:88
Sparse Core Ops, SparseCore 0:
  10.4 96.6 all-gather.1

commit v13 on v12

--- a/solution.py
+++ b/solution.py
@@ -88,7 +88,7 @@
     return lax.ppermute(value, axis, pairs)
 
 
-def memory_before(local):
+def memory_before(local, filler):
     n_x = lax.axis_size("x")
     n_y = lax.axis_size("y")
     x_here = lax.axis_index("x")
@@ -107,6 +107,7 @@
     )
     per = local.shape[0] // n_x
     quarter = lax.dynamic_slice_in_dim(row_total, x_here * per, per, axis=0)
+    quarter, filler = lax.optimization_barrier((quarter, filler))
     rows_before = quarter * 0.0
     for shift in range(1, n_y):
         rows_before = rows_before + ring_shift(quarter, "y", shift, n_y, wrap=False)
@@ -114,7 +115,7 @@
     stacked = jnp.stack(got)
     order = (x_here - jnp.arange(n_x)) % n_x
     earlier_rows = jnp.take(stacked, order, axis=0).reshape(local.shape)
-    return earlier_rows + row_before
+    return earlier_rows + row_before, filler
 
 
 def body(tokens, input_gain, qkv_weight, head_gain, prefix_state):
@@ -126,7 +127,6 @@
     key_feats, values, local = kv_memory(normed, weight.T)
     key_feats = key_feats.reshape(tok_rows, H, DH)
     values = values.reshape(tok_rows, H, DH)
-    memory = prefix_state[0] + memory_before(local)
     queries = jnp.dot(normed, weight[:, :D], preferred_element_type=jnp.float32)
     queries = feature_map(queries).astype(jnp.bfloat16)
 
@@ -136,6 +136,8 @@
     )
     scores = jnp.where(causal[None], scores, 0.0).astype(jnp.bfloat16)
     within = jnp.einsum("hbc,che->hbe", scores, values, preferred_element_type=jnp.float32)
+    before, within = memory_before(local, within)
+    memory = prefix_state[0] + before
     gains = head_gain.astype(jnp.float32).reshape(1, H * DH)
     attended = attend_tail(
         memory, jnp.transpose(queries.reshape(tok_rows, H, DH), (1, 0, 2)), within, gains

time: 211 us -> 211 us (level)
  local copies, waits for them, and re-layouts: 9.24 us -> 11.5 us
  transfers between devices with their start and end apart: 11 -> 11, of which waited for: 5 -> 6; matrix products, arithmetic and copies ran while one was open for 16% -> 17% of each run, Pallas kernels for 0% -> 0%
where the time goes in v13:
time: 211 us; the launch traced here: 208 us
  waiting for transfers between devices  114 us (54%)
  Pallas kernels  21.5 us (10%)
  matrix products  18.4 us (9%)
  starting transfers between devices  16.5 us (8%)
  between operations  13.5 us (6%)
  other arithmetic  13.1 us (6%)
  local copies, waits for them, and re-layouts  11.5 us (5%)
    all_gather x1, waiting for transfers between devices, body(): weight = lax.all_gather(qkv_weight, ('dp', 'y', 'x'), axis=1, tiled=True)  94.4 us
    ppermute x10, waiting for transfers between devices, ring_shift(): return lax.ppermute(value, axis, pairs)  18.6 us
    ppermute x10, starting transfers between devices, ring_shift(): return lax.ppermute(value, axis, pairs)  16.5 us
    pallas_call x1, Pallas kernels, kv_memory(): pl.pallas_call(kv_memory_kernel, grid=(H // heads_per_step,), in_specs=[p...  15.7 us
    dot_general x1, matrix products, body(): queries = jnp.dot(normed, weight[:, :D], preferred_element_type=jnp.float32)  9.61 us
    dot_general x1, matrix products, body(): jnp.einsum('hbc,che->hbe', scores, values, preferred_element_type=jnp.flo...  8.82 us
    pallas_call x1, Pallas kernels, attend_tail(): pl.pallas_call(tail_kernel, grid=(H // heads_per_step,), in_specs=[pl.Blo...  5.79 us
  transfers between devices with their start and end apart: 11, of which 6 were waited for; matrix products, arithmetic and copies ran while one was open for 17% of the time, Pallas kernels for 0%

profile of v13, /device:TPU:1, one launch (start us, length us, event | category | flops | bytes accessed | tf_op | source)
XLA Modules:
  0.0 208.2 jit_solution(17727395581815578216)
XLA Ops:
  8.8 2.1 fusion.2
  10.8 1.9 fusion.4.x_ref
  12.7 94.4 %all-gather.2.cloned.1.call-done = bf16[2048,6144]{0,1:T(8,128)(2,1)} async-done(((bf16[2048,48]{0,1:T(8,128)(2,1)}), bf16[2048,6144]{0,1:T(8,128)(2,1)}) %all-gather.2.cloned.1.call-update) | async-done | bytes 25165840 | tf_op jit(solution)/shard_map/all_gather | solution.py:126
  107.1 15.7 %shard_map.55 = (bf16[512,2048]{1,0:T(8,128)(2,1)}, bf16[512,2048]{1,0:T(8,128)(2,1)}, bf16[16,128,128]{2,1,0:T(8,128)(2,1)}) custom-call(bf16[512,2048]{1,0:T(8,128)(2,1)} %fusion.4.x_ref, bf16[6144,2048]{1,0:T(8,128)(2,1)} %bitcast.34, bf16[6144,2048]{1,0:T(8,128)(2,1)} %bitcast.35), custom_call_target="tpu_custom_call" | custom-call | tf_op jit(solution)/shard_map/pallas_call | solution.py:39
  122.8 2.4 %collective-permute-start.2 = (bf16[16,128,128]{2,1,0:T(8,128)(2,1)}, bf16[16,128,128]{2,1,0:T(8,128)(2,1)S(1)}, u32[]{:S(2)}, u32[]{:S(2)}) collective-permute-start(bf16[16,128,128]{2,1,0:T(8,128)(2,1)} %get-tuple-element.10), channel_id=1, source_target_pairs={{0,3},{1,0},{2,1},{3,2},{4,7},{5,4},{6,5},{7,6},{8,11},{9,8},{10,9... | collective-permute-start | bytes 1572872 | tf_op jit(solution)/shard_map/ppermute | solution.py:88
  125.2 9.6 %select_convert_fusion.1 = bf16[512,2048]{1,0:T(8,128)(2,1)} fusion(bf16[512,2048]{1,0:T(8,128)(2,1)S(1)} %copy-done, bf16[2048,6144]{0,1:T(8,128)(2,1)} %all-gather.2.cloned.1.call-done), kind=kOutput, calls=%fused_computation.9 | convolution fusion | flops 4300210176 | bytes 12582912 | tf_op jit(solution)/shard_map/dot_general | solution.py:130
  134.9 3.9 %copy.11 = bf16[512,2048]{0,1:T(8,128)(2,1)} copy(bf16[512,2048]{1,0:T(8,128)(2,1)} %get-tuple-element.11) | data formatting | bytes 4194304 | tf_op jit(solution)/shard_map/reshape | solution.py:128
  138.8 2.9 %copy.7 = bf16[512,2048]{0,1:T(8,128)(2,1)S(1)} copy(bf16[512,2048]{1,0:T(8,128)(2,1)} %select_convert_fusion.1) | data formatting | bytes 4194304 | tf_op jit(solution)/shard_map/convert_element_type | solution.py:131
  142.4 2.7 %collective-permute-start.3 = (bf16[8,128,128]{2,1,0:T(8,128)(2,1)}, bf16[8,128,128]{2,1,0:T(8,128)(2,1)S(1)}, u32[]{:S(2)}, u32[]{:S(2)}) collective-permute-start(bf16[8,128,128]{2,1,0:T(8,128)(2,1)} %slice.15), channel_id=1, source_target_pairs={{0,3},{1,0},{2,1},{3,2},{4,7},{5,4},{6,5},{7,6},{8,11},{9,8},{10,9... | collective-permute-start | bytes 786440 | tf_op jit(solution)/shard_map/ppermute | solution.py:88
  145.8 8.8 %fusion.7.w_ref = f32[16,512,128]{2,1,0:T(8,128)} fusion(bf16[512,16,128]{0,2,1:T(8,128)(2,1)S(1)} %bitcast.36, bf16[512,16,128]{0,2,1:T(8,128)(2,1)} %bitcast.39, pred[512,512]{1,0:T(8,128)(4,1)} %iota_compare_fusion, bf16[512,2048]{1,0:T(8,128)(2,1)} %get-tuple-element.12), kind=kOutput, calls=%fused_computation.10 | convolution fusion | flops 2155872256 | bytes 10747904 | tf_op jit(solution)/shard_map/hbc,che->hbe/dot_general | solution.py:138
  154.9 1.0 maximum_convert_fusion
  156.9 4.4 %collective-permute-start.6 = (f32[4,128,128]{2,1,0:T(8,128)S(1)}, f32[4,128,128]{2,1,0:T(8,128)S(1)}, u32[]{:S(2)}, u32[]{:S(2)}) collective-permute-start(f32[4,128,128]{2,1,0:T(8,128)S(1)} %dynamic-slice_add_fusion), channel_id=1, source_target_pairs={{0,12},{1,13},{2,14},{3,15},{16,28},{17,29},{18,30},{19,31},{32,44... | collective-permute-start | bytes 786440 | tf_op jit(solution)/shard_map/ppermute | solution.py:88
  161.3 1.3 collective-permute-start.5
  162.6 2.7 %collective-permute-start.4 = (f32[4,128,128]{2,1,0:T(8,128)S(1)}, f32[4,128,128]{2,1,0:T(8,128)S(1)}, u32[]{:S(2)}, u32[]{:S(2)}) collective-permute-start(f32[4,128,128]{2,1,0:T(8,128)S(1)} %dynamic-slice_add_fusion), channel_id=1, source_target_pairs={{0,4},{4,8},{8,12},{1,5},{5,9},{9,13},{2,6},{6,10},{10,14},{3,7},{... | collective-permute-start | bytes 786440 | tf_op jit(solution)/shard_map/ppermute | solution.py:88
  165.2 6.0 %collective-permute-done.6 = f32[4,128,128]{2,1,0:T(8,128)S(1)} collective-permute-done((f32[4,128,128]{2,1,0:T(8,128)S(1)}, f32[4,128,128]{2,1,0:T(8,128)S(1)}, u32[]{:S(2)}, u32[]{:S(2)}) %collective-permute-start.6) | collective-permute-done | bytes 262176 | tf_op jit(solution)/shard_map/ppermute | solution.py:88
  171.3 1.3 collective-permute-done.4
  173.4 2.5 %collective-permute-start.9 = (f32[4,128,128]{2,1,0:T(8,128)}, f32[4,128,128]{2,1,0:T(8,128)}, u32[]{:S(2)}, u32[]{:S(2)}) collective-permute-start(f32[4,128,128]{2,1,0:T(8,128)} %add_add_fusion), channel_id=1, source_target_pairs={{0,3},{1,0},{2,1},{3,2},{4,7},{5,4},{6,5},{7,6},{8,11},{9,8},{10,9... | collective-permute-start | bytes 786440 | tf_op jit(solution)/shard_map/ppermute | solution.py:88
  177.3 2.4 %copy.9 = bf16[512,16,128]{2,0,1:T(8,128)(2,1)} copy(bf16[512,16,128]{0,2,1:T(8,128)(2,1)S(1)} %bitcast.37) | data formatting | bytes 4194304 | tf_op jit(solution)/shard_map/reshape | solution.py:135
  179.7 1.4 collective-permute-done.9
  181.1 1.9 collective-permute-done.8
  183.0 7.9 %collective-permute-done.7 = f32[4,128,128]{2,1,0:T(8,128)} collective-permute-done((f32[4,128,128]{2,1,0:T(8,128)}, f32[4,128,128]{2,1,0:T(8,128)}, u32[]{:S(2)}, u32[]{:S(2)}) %collective-permute-start.7) | collective-permute-done | bytes 262176 | tf_op jit(solution)/shard_map/ppermute | solution.py:88
  190.9 1.3 pad_maximum_fusion
  192.8 2.8 %fusion.11.m_ref = f32[16,128,128]{2,1,0:T(8,128)} fusion(f32[4,4,128,128]{3,2,1,0:T(8,128)S(1)} %gather_fusion, f32[1,16,128,128]{3,2,1,0:T(8,128)} %param.9, pred[16]{0:T(512)(128)(4,1)S(1)} %broadcast_in_dim.38, pred[]{:T(512)S(6)} %ge.39, pred[]{:T(512)S(6)} %ge.38, pred[]{:T(512)S(6)} %ge.37, bf16[16,128,128]{2,1,0:T(8,128)(2,1)S(1)} %collective-permute-done.2, ...), kind=kLoop, calls=%fused_computation.16 | loop fusion | flops 3145728 | bytes 4718611 | tf_op jit(solution)/shard_map/add | solution.py:140
  195.6 5.8 %shard_map.56 = bf16[512,2048]{1,0:T(8,128)(2,1)} custom-call(f32[16,128,128]{2,1,0:T(8,128)} %fusion.11.m_ref, bf16[16,512,128]{2,1,0:T(8,128)(2,1)} %bitcast.38, f32[16,512,128]{2,1,0:T(8,128)} %fusion.7.w_ref, f32[1,2048]{1,0:T(1,128)} %bitcast.40), custom_call_target="tpu_custom_call" | custom-call | tf_op jit(solution)/shard_map/pallas_call | solution.py:72
  (33 shorter events, 7.6 us)
Async XLA Ops:
  6.5 4.3 %copy-start.1 = (bf16[1,512,2048]{2,1,0:T(8,128)(2,1)S(1)}, bf16[1,512,2048]{2,1,0:T(8,128)(2,1)}, u32[]{:S(2)}) copy-start(bf16[1,512,2048]{2,1,0:T(8,128)(2,1)} %param.5) | copy-start | bytes 6291460
  6.5 100.6 %all-gather.2.cloned.1.call-start = ((), (), s32[]{:S(2)}) async-start(), calls=%async_computation | async-start | bytes 25362432 | tf_op jit(solution)/shard_map/all_gather | solution.py:126
  107.1 18.1 %copy-start = (bf16[512,2048]{1,0:T(8,128)(2,1)S(1)}, bf16[512,2048]{1,0:T(8,128)(2,1)}, u32[]{:S(2)}) copy-start(bf16[512,2048]{1,0:T(8,128)(2,1)} %fusion.4.x_ref) | copy-start | bytes 6291460
  122.8 18.8 %collective-permute-start.2 = (bf16[16,128,128]{2,1,0:T(8,128)(2,1)}, bf16[16,128,128]{2,1,0:T(8,128)(2,1)S(1)}, u32[]{:S(2)}, u32[]{:S(2)}) collective-permute-start(bf16[16,128,128]{2,1,0:T(8,128)(2,1)} %get-tuple-element.10), channel_id=1, source_target_pairs={{0,3},{1,0},{2,1},{3,2},{4,7},{5,4},{6,5},{7,6},{8,11},{9,8},{10,9... | collective-permute-start | bytes 1572872 | tf_op jit(solution)/shard_map/ppermute | solution.py:88
  125.2 19.8 %collective-permute-start = (bf16[16,128,128]{2,1,0:T(8,128)(2,1)}, bf16[16,128,128]{2,1,0:T(8,128)(2,1)S(1)}, u32[]{:S(2)}, u32[]{:S(2)}) collective-permute-start(bf16[16,128,128]{2,1,0:T(8,128)(2,1)} %get-tuple-element.10), channel_id=1, source_target_pairs={{0,1},{1,2},{2,3},{3,0},{4,5},{5,6},{6,7},{7,4},{8,9},{9,10},{10,1... | collective-permute-start | bytes 1572872 | tf_op jit(solution)/shard_map/ppermute | solution.py:88
  142.4 12.5 %collective-permute-start.3 = (bf16[8,128,128]{2,1,0:T(8,128)(2,1)}, bf16[8,128,128]{2,1,0:T(8,128)(2,1)S(1)}, u32[]{:S(2)}, u32[]{:S(2)}) collective-permute-start(bf16[8,128,128]{2,1,0:T(8,128)(2,1)} %slice.15), channel_id=1, source_target_pairs={{0,3},{1,0},{2,1},{3,2},{4,7},{5,4},{6,5},{7,6},{8,11},{9,8},{10,9... | collective-permute-start | bytes 786440 | tf_op jit(solution)/shard_map/ppermute | solution.py:88
  145.8 9.1 %collective-permute-start.1 = (bf16[8,128,128]{2,1,0:T(8,128)(2,1)}, bf16[8,128,128]{2,1,0:T(8,128)(2,1)}, u32[]{:S(2)}, u32[]{:S(2)}) collective-permute-start(bf16[8,128,128]{2,1,0:T(8,128)(2,1)} %slice.14), channel_id=1, source_target_pairs={{0,1},{1,2},{2,3},{3,0},{4,5},{5,6},{6,7},{7,4},{8,9},{9,10},{10,1... | collective-permute-start | bytes 786440 | tf_op jit(solution)/shard_map/ppermute | solution.py:88
  154.8 21.8 %copy-start.2 = (bf16[2048]{0:T(1024)(128)(2,1)S(1)}, bf16[2048]{0:T(1024)(128)(2,1)}, u32[]{:S(2)}) copy-start(bf16[2048]{0:T(1024)(128)(2,1)} %param.8) | copy-start | bytes 12292
  156.9 14.4 %collective-permute-start.6 = (f32[4,128,128]{2,1,0:T(8,128)S(1)}, f32[4,128,128]{2,1,0:T(8,128)S(1)}, u32[]{:S(2)}, u32[]{:S(2)}) collective-permute-start(f32[4,128,128]{2,1,0:T(8,128)S(1)} %dynamic-slice_add_fusion), channel_id=1, source_target_pairs={{0,12},{1,13},{2,14},{3,15},{16,28},{17,29},{18,30},{19,31},{32,44... | collective-permute-start | bytes 786440 | tf_op jit(solution)/shard_map/ppermute | solution.py:88
  161.3 10.0 %collective-permute-start.5 = (f32[4,128,128]{2,1,0:T(8,128)S(1)}, f32[4,128,128]{2,1,0:T(8,128)S(1)}, u32[]{:S(2)}, u32[]{:S(2)}) collective-permute-start(f32[4,128,128]{2,1,0:T(8,128)S(1)} %dynamic-slice_add_fusion), channel_id=1, source_target_pairs={{0,8},{4,12},{1,9},{5,13},{2,10},{6,14},{3,11},{7,15},{16,24},{20,... | collective-permute-start | bytes 786440 | tf_op jit(solution)/shard_map/ppermute | solution.py:88
  162.6 10.1 %collective-permute-start.4 = (f32[4,128,128]{2,1,0:T(8,128)S(1)}, f32[4,128,128]{2,1,0:T(8,128)S(1)}, u32[]{:S(2)}, u32[]{:S(2)}) collective-permute-start(f32[4,128,128]{2,1,0:T(8,128)S(1)} %dynamic-slice_add_fusion), channel_id=1, source_target_pairs={{0,4},{4,8},{8,12},{1,5},{5,9},{9,13},{2,6},{6,10},{10,14},{3,7},{... | collective-permute-start | bytes 786440 | tf_op jit(solution)/shard_map/ppermute | solution.py:88
  173.4 7.7 %collective-permute-start.9 = (f32[4,128,128]{2,1,0:T(8,128)}, f32[4,128,128]{2,1,0:T(8,128)}, u32[]{:S(2)}, u32[]{:S(2)}) collective-permute-start(f32[4,128,128]{2,1,0:T(8,128)} %add_add_fusion), channel_id=1, source_target_pairs={{0,3},{1,0},{2,1},{3,2},{4,7},{5,4},{6,5},{7,6},{8,11},{9,8},{10,9... | collective-permute-start | bytes 786440 | tf_op jit(solution)/shard_map/ppermute | solution.py:88
  175.9 7.1 %collective-permute-start.8 = (f32[4,128,128]{2,1,0:T(8,128)}, f32[4,128,128]{2,1,0:T(8,128)}, u32[]{:S(2)}, u32[]{:S(2)}) collective-permute-start(f32[4,128,128]{2,1,0:T(8,128)} %add_add_fusion), channel_id=1, source_target_pairs={{0,2},{1,3},{2,0},{3,1},{4,6},{5,7},{6,4},{7,5},{8,10},{9,11},{10,... | collective-permute-start | bytes 786440 | tf_op jit(solution)/shard_map/ppermute | solution.py:88
  175.9 15.0 %collective-permute-start.7 = (f32[4,128,128]{2,1,0:T(8,128)}, f32[4,128,128]{2,1,0:T(8,128)}, u32[]{:S(2)}, u32[]{:S(2)}) collective-permute-start(f32[4,128,128]{2,1,0:T(8,128)} %add_add_fusion), channel_id=1, source_target_pairs={{0,1},{1,2},{2,3},{3,0},{4,5},{5,6},{6,7},{7,4},{8,9},{9,10},{10,1... | collective-permute-start | bytes 786440 | tf_op jit(solution)/shard_map/ppermute | solution.py:88
Sparse Core Ops, SparseCore 0:
  10.4 96.6 all-gather.1

commit v14 on v10

--- a/solution.py
+++ b/solution.py
@@ -32,7 +32,7 @@
         m_ref[j] = m.astype(jnp.bfloat16)
 
 
-def kv_memory(normed, weight_t, heads_per_step=2):
+def kv_memory(normed, weight_t, heads_per_step=4):
     rows = normed.shape[0]
     width = heads_per_step * DH
     k_off = D // width

time: 208 us -> 207 us (level)
  no operation moved by 1% of the time
where the time goes in v14:
time: 207 us
  waiting for transfers between devices  141 us (68%)
  Pallas kernels  23 us (11%)
  matrix products  18.5 us (9%)
  between operations  13.4 us (6%)
  other arithmetic  5.32 us (3%)
  local copies, waits for them, and re-layouts  5.27 us (3%)
    all_gather x1, waiting for transfers between devices, body(): weight = lax.all_gather(qkv_weight, ('dp', 'y', 'x'), axis=1, tiled=True)  95.1 us
    all_gather x1, waiting for transfers between devices, body(): gathered = lax.all_gather(local[None], ('y', 'x'), axis=0, tiled=True)  45.3 us
    pallas_call x1, Pallas kernels, kv_memory(): pl.pallas_call(kv_memory_kernel, grid=(H // heads_per_step,), in_specs=[p...  14.8 us
    dot_general x1, matrix products, body(): queries = jnp.dot(normed, weight[:, :D], preferred_element_type=jnp.float32)  9.65 us
    dot_general x1, matrix products, body(): jnp.einsum('hbc,che->hbe', scores, values, preferred_element_type=jnp.flo...  8.82 us
    pallas_call x1, Pallas kernels, attend_tail(): pl.pallas_call(tail_kernel, grid_spec=grid_spec, out_shape=jax.ShapeDtype...  8.24 us
  transfers between devices with their start and end apart: 2, of which 2 were waited for; matrix products, arithmetic and copies ran while one was open for 14% of the time, Pallas kernels for 0%

profile of v14, /device:TPU:1, one launch (start us, length us, event | category | flops | bytes accessed | tf_op | source)
XLA Modules:
  0.0 206.7 jit_solution(13501186039937705704)
XLA Ops:
  6.5 0.0 copy-start.1
  6.5 0.0 all-gather.4.cloned.1.call-start
  6.5 0.7 all-gather.4.cloned.1.call-update
  7.3 0.0 all-gather.6.cloned.1.call-start
  7.3 0.7 convert_element_type.21
  8.0 2.1 %fusion.2 = f32[512]{0:T(512)S(1)} fusion(bf16[1,512,2048]{2,1,0:T(8,128)(2,1)} %param.5), kind=kLoop, calls=%fused_computation.5 | loop fusion | flops 3145216 | bytes 2099200 | tf_op jit(solution)/shard_map/reduce_sum | solution.py:99
  10.1 0.0 copy-done.1
  10.1 1.9 fusion.4.x_ref
  12.0 95.1 %all-gather.4.cloned.1.call-done = bf16[2048,6144]{0,1:T(8,128)(2,1)} async-done(((bf16[2048,48]{0,1:T(8,128)(2,1)}), bf16[2048,6144]{0,1:T(8,128)(2,1)}) %all-gather.4.cloned.1.call-update) | async-done | bytes 25165840 | tf_op jit(solution)/shard_map/all_gather | solution.py:102
  107.1 0.0 copy-start.2
  107.1 0.0 copy-start
  107.1 14.8 %shard_map.55 = (bf16[512,2048]{1,0:T(8,128)(2,1)}, bf16[512,2048]{1,0:T(8,128)(2,1)}, bf16[16,128,128]{2,1,0:T(8,128)(2,1)}) custom-call(bf16[512,2048]{1,0:T(8,128)(2,1)} %fusion.4.x_ref, bf16[6144,2048]{1,0:T(8,128)(2,1)} %bitcast.30, bf16[6144,2048]{1,0:T(8,128)(2,1)} %bitcast.31), custom_call_target="tpu_custom_call" | custom-call | tf_op jit(solution)/shard_map/pallas_call | solution.py:40
  121.9 0.0 all-gather.6.cloned.1.call-update
  121.9 0.0 copy-done.2
  121.9 0.6 reshape.52
  122.5 0.1 iota_compare_fusion
  122.6 0.0 copy-done
  122.6 9.6 %select_convert_fusion.1 = bf16[512,2048]{1,0:T(8,128)(2,1)} fusion(bf16[512,2048]{1,0:T(8,128)(2,1)S(1)} %copy-done, bf16[2048,6144]{0,1:T(8,128)(2,1)} %all-gather.4.cloned.1.call-done), kind=kOutput, calls=%fused_computation.8 | convolution fusion | flops 4300210176 | bytes 12582912 | tf_op jit(solution)/shard_map/dot_general | solution.py:108
  132.2 2.9 %copy.10 = bf16[512,2048]{0,1:T(8,128)(2,1)S(1)} copy(bf16[512,2048]{1,0:T(8,128)(2,1)} %select_convert_fusion.1) | data formatting | bytes 4194304 | tf_op jit(solution)/shard_map/convert_element_type | solution.py:109
  135.1 2.4 %copy.11 = bf16[512,16,128]{2,0,1:T(8,128)(2,1)} copy(bf16[512,16,128]{0,2,1:T(8,128)(2,1)S(1)} %bitcast.34) | data formatting | bytes 4194304 | tf_op jit(solution)/shard_map/reshape | solution.py:119
  137.5 8.8 %fusion.7.w_ref = f32[16,512,128]{2,1,0:T(8,128)} fusion(bf16[512,16,128]{0,2,1:T(8,128)(2,1)S(1)} %bitcast.35, pred[512,512]{1,0:T(8,128)(4,1)S(1)} %iota_compare_fusion, bf16[512,2048]{1,0:T(8,128)(2,1)} %get-tuple-element.10, bf16[512,2048]{1,0:T(8,128)(2,1)} %get-tuple-element.9), kind=kOutput, calls=%fused_computation.9 | convolution fusion | flops 2155872256 | bytes 10747904 | tf_op jit(solution)/shard_map/hbc,che->hbe/dot_general | solution.py:116
  146.3 45.3 %all-gather.6.cloned.1.call-done = bf16[256,128,128]{2,1,0:T(8,128)(2,1)} async-done(((bf16[16,128,128]{2,1,0:T(8,128)(2,1)}), bf16[256,128,128]{2,1,0:T(8,128)(2,1)}) %all-gather.6.cloned.1.call-update) | async-done | bytes 8388624 | tf_op jit(solution)/shard_map/all_gather | solution.py:106
  191.6 8.2 %shard_map.56 = bf16[512,2048]{1,0:T(8,128)(2,1)} custom-call(s32[1]{0:T(128)} %bitcast.here_ref, bf16[16,16,128,128]{3,2,1,0:T(8,128)(2,1)} %bitcast.32, f32[16,128,128]{2,1,0:T(8,128)} %bitcast.36, bf16[16,512,128]{2,1,0:T(8,128)(2,1)} %bitcast.33, f32[16,512,128]{2,1,0:T(8,128)} %fusion.7.w_ref, f32[1,2048]{1,0:T(1,128)} %bitcast.37), custom_call_target="tpu_custom_call" | custom-call | tf_op jit(solution)/shard_map/pallas_call | solution.py:90
  (1 shorter events, 0.0 us)
Async XLA Ops:
  6.5 3.5 %copy-start.1 = (bf16[1,512,2048]{2,1,0:T(8,128)(2,1)S(1)}, bf16[1,512,2048]{2,1,0:T(8,128)(2,1)}, u32[]{:S(2)}) copy-start(bf16[1,512,2048]{2,1,0:T(8,128)(2,1)} %param.5) | copy-start | bytes 6291460
  6.5 100.6 %all-gather.4.cloned.1.call-start = ((), (), s32[]{:S(2)}) async-start(), calls=%async_computation | async-start | bytes 25362432 | tf_op jit(solution)/shard_map/all_gather | solution.py:102
  7.3 184.4 %all-gather.6.cloned.1.call-start = ((), (), s32[]{:S(2)}) async-start(), calls=%async_computation.1 | async-start | bytes 8912896 | tf_op jit(solution)/shard_map/all_gather | solution.py:106
  107.1 14.8 %copy-start.2 = (bf16[2048]{0:T(1024)(128)(2,1)S(1)}, bf16[2048]{0:T(1024)(128)(2,1)}, u32[]{:S(2)}) copy-start(bf16[2048]{0:T(1024)(128)(2,1)} %param.8) | copy-start | bytes 12292
  107.1 15.5 %copy-start = (bf16[512,2048]{1,0:T(8,128)(2,1)S(1)}, bf16[512,2048]{1,0:T(8,128)(2,1)}, u32[]{:S(2)}) copy-start(bf16[512,2048]{1,0:T(8,128)(2,1)} %fusion.4.x_ref) | copy-start | bytes 6291460
Sparse Core Ops, SparseCore 0:
  10.4 96.6 all-gather.3
  122.0 69.5 all-gather.5

commit v15 on v13

--- a/solution.py
+++ b/solution.py
@@ -31,7 +31,7 @@
         m_ref[j] = m.astype(jnp.bfloat16)
 
 
-def kv_memory(normed, weight_t, heads_per_step=2):
+def kv_memory(normed, weight_t, heads_per_step=4):
     rows = normed.shape[0]
     width = heads_per_step * DH
     k_off = D // width
@@ -127,6 +127,8 @@
     key_feats, values, local = kv_memory(normed, weight.T)
     key_feats = key_feats.reshape(tok_rows, H, DH)
     values = values.reshape(tok_rows, H, DH)
+    half = H // 2
+    gathered = lax.all_gather(local[None, :half], ("y", "x"), axis=0, tiled=True)
     queries = jnp.dot(normed, weight[:, :D], preferred_element_type=jnp.float32)
     queries = feature_map(queries).astype(jnp.bfloat16)
 
@@ -136,8 +138,11 @@
     )
     scores = jnp.where(causal[None], scores, 0.0).astype(jnp.bfloat16)
     within = jnp.einsum("hbc,che->hbe", scores, values, preferred_element_type=jnp.float32)
-    before, within = memory_before(local, within)
-    memory = prefix_state[0] + before
+    before_late, within = memory_before(local[half:], within)
+    seq_here = lax.axis_index(("y", "x"))
+    earlier = (jnp.arange(gathered.shape[0]) < seq_here)[:, None, None, None]
+    before_early = jnp.sum(jnp.where(earlier, gathered.astype(jnp.float32), 0.0), axis=0)
+    memory = prefix_state[0] + jnp.concatenate([before_early, before_late], axis=0)
     gains = head_gain.astype(jnp.float32).reshape(1, H * DH)
     attended = attend_tail(
         memory, jnp.transpose(queries.reshape(tok_rows, H, DH), (1, 0, 2)), within, gains

time: 211 us -> 201 us (0.953)
  local copies, waits for them, and re-layouts: 11.5 us -> 8.49 us
  other arithmetic: 13.1 us -> 10.1 us
  waiting for transfers between devices: 114 us -> 111 us
    reshape x1 -> x0, local copies, waits for them, and re-layouts: 3.93 us -> none  [body(): key_feats = key_feats.reshape(tok_rows, H, DH)]
    ppermute x10, waiting for transfers between devices: 18.6 us -> 14.9 us  [ring_shift(): return lax.ppermute(value, axis, pairs)]
    reduce_sum x0 -> x1, other arithmetic: none -> 3.27 us  [body(): jnp.sum(jnp.where(earlier, gathered.astype(jnp.float32), 0.0), axis=0)]
  transfers between devices with their start and end apart: 11 -> 12, of which waited for: 6 -> 6; matrix products, arithmetic and copies ran while one was open for 17% -> 15% of each run, Pallas kernels for 0% -> 0%
where the time goes in v15:
time: 201 us; the launch traced here: 200 us
  waiting for transfers between devices  111 us (55%)
  Pallas kernels  21.4 us (11%)
  matrix products  18.4 us (9%)
  starting transfers between devices  16.7 us (8%)
  between operations  13.6 us (7%)
  other arithmetic  10.1 us (5%)
  local copies, waits for them, and re-layouts  8.49 us (4%)
    all_gather x1, waiting for transfers between devices, body(): weight = lax.all_gather(qkv_weight, ('dp', 'y', 'x'), axis=1, tiled=True)  95.1 us
    ppermute x10, starting transfers between devices, ring_shift(): return lax.ppermute(value, axis, pairs)  16.6 us
    pallas_call x1, Pallas kernels, kv_memory(): pl.pallas_call(kv_memory_kernel, grid=(H // heads_per_step,), in_specs=[p...  15.6 us
    ppermute x10, waiting for transfers between devices, ring_shift(): return lax.ppermute(value, axis, pairs)  14.9 us
    dot_general x1, matrix products, body(): queries = jnp.dot(normed, weight[:, :D], preferred_element_type=jnp.float32)  9.62 us
    dot_general x1, matrix products, body(): jnp.einsum('hbc,che->hbe', scores, values, preferred_element_type=jnp.flo...  8.8 us
    pallas_call x1, Pallas kernels, attend_tail(): pl.pallas_call(tail_kernel, grid=(H // heads_per_step,), in_specs=[pl.Blo...  5.79 us
  transfers between devices with their start and end apart: 12, of which 6 were waited for; matrix products, arithmetic and copies ran while one was open for 15% of the time, Pallas kernels for 0%

profile of v15, /device:TPU:1, one launch (start us, length us, event | category | flops | bytes accessed | tf_op | source)
XLA Modules:
  0.0 199.5 jit_solution(2974746019543136890)
XLA Ops:
  6.5 0.7 all-gather.4.cloned.1.call-update
  8.0 2.1 %fusion.3 = f32[512]{0:T(512)S(1)} fusion(bf16[1,512,2048]{2,1,0:T(8,128)(2,1)} %param.5), kind=kLoop, calls=%fused_computation.8 | loop fusion | flops 3145216 | bytes 2099200 | tf_op jit(solution)/shard_map/reduce_sum | solution.py:123
  10.1 1.9 fusion.5.x_ref
  12.0 95.1 %all-gather.4.cloned.1.call-done = bf16[2048,6144]{0,1:T(8,128)(2,1)} async-done(((bf16[2048,48]{0,1:T(8,128)(2,1)}), bf16[2048,6144]{0,1:T(8,128)(2,1)}) %all-gather.4.cloned.1.call-update) | async-done | bytes 25165840 | tf_op jit(solution)/shard_map/all_gather | solution.py:126
  107.1 15.6 %shard_map.55 = (bf16[512,2048]{1,0:T(8,128)(2,1)}, bf16[512,2048]{1,0:T(8,128)(2,1)}, bf16[16,128,128]{2,1,0:T(8,128)(2,1)}) custom-call(bf16[512,2048]{1,0:T(8,128)(2,1)} %fusion.5.x_ref, bf16[6144,2048]{1,0:T(8,128)(2,1)} %bitcast.41, bf16[6144,2048]{1,0:T(8,128)(2,1)} %bitcast.42), custom_call_target="tpu_custom_call" | custom-call | tf_op jit(solution)/shard_map/pallas_call | solution.py:39
  122.7 1.8 fusion.20
  124.6 2.5 %collective-permute-start.2 = (bf16[8,128,128]{2,1,0:T(8,128)(2,1)S(1)}, bf16[8,128,128]{2,1,0:T(8,128)(2,1)S(1)}, u32[]{:S(2)}, u32[]{:S(2)}) collective-permute-start(bf16[8,128,128]{2,1,0:T(8,128)(2,1)S(1)} %get-tuple-element.16), channel_id=1, source_target_pairs={{0,3},{1,0},{2,1},{3,2},{4,7},{5,4},{6,5},{7,6},{8,11},{9,8},{10,9... | collective-permute-start | bytes 786440 | tf_op jit(solution)/shard_map/ppermute | solution.py:88
  127.1 9.6 %select_convert_fusion.1 = bf16[512,2048]{1,0:T(8,128)(2,1)} fusion(bf16[512,2048]{1,0:T(8,128)(2,1)S(1)} %copy-done, bf16[2048,6144]{0,1:T(8,128)(2,1)} %all-gather.4.cloned.1.call-done), kind=kOutput, calls=%fused_computation.11 | convolution fusion | flops 4300210176 | bytes 12582912 | tf_op jit(solution)/shard_map/dot_general | solution.py:132
  136.7 2.9 %copy.10 = bf16[512,2048]{0,1:T(8,128)(2,1)S(1)} copy(bf16[512,2048]{1,0:T(8,128)(2,1)} %select_convert_fusion.1) | data formatting | bytes 4194304 | tf_op jit(solution)/shard_map/convert_element_type | solution.py:133
  139.6 2.7 %collective-permute-start.3 = (bf16[4,128,128]{2,1,0:T(8,128)(2,1)S(1)}, bf16[4,128,128]{2,1,0:T(8,128)(2,1)S(1)}, u32[]{:S(2)}, u32[]{:S(2)}) collective-permute-start(bf16[4,128,128]{2,1,0:T(8,128)(2,1)S(1)} %slice.23), channel_id=1, source_target_pairs={{0,3},{1,0},{2,1},{3,2},{4,7},{5,4},{6,5},{7,6},{8,11},{9,8},{10,9... | collective-permute-start | bytes 393224 | tf_op jit(solution)/shard_map/ppermute | solution.py:88
  143.0 8.8 %fusion.8.w_ref = f32[16,512,128]{2,1,0:T(8,128)} fusion(bf16[512,16,128]{0,2,1:T(8,128)(2,1)S(1)} %bitcast.43, pred[512,512]{1,0:T(8,128)(4,1)S(1)} %iota_compare_fusion, bf16[512,2048]{1,0:T(8,128)(2,1)} %get-tuple-element.12, bf16[512,2048]{1,0:T(8,128)(2,1)} %get-tuple-element.11), kind=kOutput, calls=%fused_computation.12 | convolution fusion | flops 2155872256 | bytes 10747904 | tf_op jit(solution)/shard_map/hbc,che->hbe/dot_general | solution.py:140
  152.0 4.3 %collective-permute-start.6 = (f32[2,128,128]{2,1,0:T(8,128)S(1)}, f32[2,128,128]{2,1,0:T(8,128)S(1)}, u32[]{:S(2)}, u32[]{:S(2)}) collective-permute-start(f32[2,128,128]{2,1,0:T(8,128)S(1)} %dynamic-slice_add_fusion), channel_id=1, source_target_pairs={{0,12},{1,13},{2,14},{3,15},{16,28},{17,29},{18,30},{19,31},{32,44... | collective-permute-start | bytes 393224 | tf_op jit(solution)/shard_map/ppermute | solution.py:88
  156.3 1.3 collective-permute-start.5
  157.6 2.5 %collective-permute-start.4 = (f32[2,128,128]{2,1,0:T(8,128)S(1)}, f32[2,128,128]{2,1,0:T(8,128)S(1)}, u32[]{:S(2)}, u32[]{:S(2)}) collective-permute-start(f32[2,128,128]{2,1,0:T(8,128)S(1)} %dynamic-slice_add_fusion), channel_id=1, source_target_pairs={{0,4},{4,8},{8,12},{1,5},{5,9},{9,13},{2,6},{6,10},{10,14},{3,7},{... | collective-permute-start | bytes 393224 | tf_op jit(solution)/shard_map/ppermute | solution.py:88
  160.2 3.3 %collective-permute-done.6 = f32[2,128,128]{2,1,0:T(8,128)S(1)} collective-permute-done((f32[2,128,128]{2,1,0:T(8,128)S(1)}, f32[2,128,128]{2,1,0:T(8,128)S(1)}, u32[]{:S(2)}, u32[]{:S(2)}) %collective-permute-start.6) | collective-permute-done | bytes 131104 | tf_op jit(solution)/shard_map/ppermute | solution.py:88
  163.4 5.4 %collective-permute-done.4 = f32[2,128,128]{2,1,0:T(8,128)S(1)} collective-permute-done((f32[2,128,128]{2,1,0:T(8,128)S(1)}, f32[2,128,128]{2,1,0:T(8,128)S(1)}, u32[]{:S(2)}, u32[]{:S(2)}) %collective-permute-start.4) | collective-permute-done | bytes 131104 | tf_op jit(solution)/shard_map/ppermute | solution.py:88
  168.8 2.6 %collective-permute-start.9 = (f32[2,128,128]{2,1,0:T(8,128)S(1)}, f32[2,128,128]{2,1,0:T(8,128)S(1)}, u32[]{:S(2)}, u32[]{:S(2)}) collective-permute-start(f32[2,128,128]{2,1,0:T(8,128)S(1)} %add_add_fusion), channel_id=1, source_target_pairs={{0,3},{1,0},{2,1},{3,2},{4,7},{5,4},{6,5},{7,6},{8,11},{9,8},{10,9... | collective-permute-start | bytes 393224 | tf_op jit(solution)/shard_map/ppermute | solution.py:88
  172.9 2.4 %copy.14 = bf16[512,16,128]{2,0,1:T(8,128)(2,1)} copy(bf16[512,16,128]{0,2,1:T(8,128)(2,1)S(1)} %bitcast.44) | data formatting | bytes 4194304 | tf_op jit(solution)/shard_map/reshape | solution.py:137
  175.3 0.9 collective-permute-done.9
  176.3 1.9 collective-permute-done.8
  178.1 3.5 %collective-permute-done.7 = f32[2,128,128]{2,1,0:T(8,128)S(1)} collective-permute-done((f32[2,128,128]{2,1,0:T(8,128)S(1)}, f32[2,128,128]{2,1,0:T(8,128)S(1)}, u32[]{:S(2)}, u32[]{:S(2)}) %collective-permute-start.7) | collective-permute-done | bytes 131104 | tf_op jit(solution)/shard_map/ppermute | solution.py:88
  182.5 3.3 %fusion.2 = f32[8,128,128]{2,1,0:T(8,128)S(1)} fusion(bf16[16,8,128,128]{3,2,1,0:T(8,128)(2,1)} %bitcast.46, pred[16]{0:T(512)(128)(4,1)S(1)} %iota_compare_fusion.1), kind=kLoop, calls=%fused_computation.5 | loop fusion | flops 6160384 | bytes 4718608 | tf_op jit(solution)/shard_map/reduce_sum | solution.py:144
  185.8 1.1 maximum_add_fusion.m_ref
  186.9 5.8 %shard_map.56 = bf16[512,2048]{1,0:T(8,128)(2,1)} custom-call(f32[16,128,128]{2,1,0:T(8,128)} %maximum_add_fusion.m_ref, bf16[16,512,128]{2,1,0:T(8,128)(2,1)} %bitcast.45, f32[16,512,128]{2,1,0:T(8,128)} %fusion.8.w_ref, f32[1,2048]{1,0:T(1,128)} %bitcast.51), custom_call_target="tpu_custom_call" | custom-call | tf_op jit(solution)/shard_map/pallas_call | solution.py:72
  (41 shorter events, 4.0 us)
Async XLA Ops:
  6.5 3.5 %copy-start.1 = (bf16[1,512,2048]{2,1,0:T(8,128)(2,1)S(1)}, bf16[1,512,2048]{2,1,0:T(8,128)(2,1)}, u32[]{:S(2)}) copy-start(bf16[1,512,2048]{2,1,0:T(8,128)(2,1)} %param.5) | copy-start | bytes 6291460
  6.5 100.6 %all-gather.4.cloned.1.call-start = ((), (), s32[]{:S(2)}) async-start(), calls=%async_computation | async-start | bytes 25362432 | tf_op jit(solution)/shard_map/all_gather | solution.py:126
  7.3 175.2 %all-gather.6.cloned.1.call-start = ((), (), s32[]{:S(2)}) async-start(), calls=%async_computation.1 | async-start | bytes 4456448 | tf_op jit(solution)/shard_map/all_gather | solution.py:131
  107.1 20.0 %copy-start = (bf16[512,2048]{1,0:T(8,128)(2,1)S(1)}, bf16[512,2048]{1,0:T(8,128)(2,1)}, u32[]{:S(2)}) copy-start(bf16[512,2048]{1,0:T(8,128)(2,1)} %fusion.5.x_ref) | copy-start | bytes 6291460
  124.6 15.0 %collective-permute-start.2 = (bf16[8,128,128]{2,1,0:T(8,128)(2,1)S(1)}, bf16[8,128,128]{2,1,0:T(8,128)(2,1)S(1)}, u32[]{:S(2)}, u32[]{:S(2)}) collective-permute-start(bf16[8,128,128]{2,1,0:T(8,128)(2,1)S(1)} %get-tuple-element.16), channel_id=1, source_target_pairs={{0,3},{1,0},{2,1},{3,2},{4,7},{5,4},{6,5},{7,6},{8,11},{9,8},{10,9... | collective-permute-start | bytes 786440 | tf_op jit(solution)/shard_map/ppermute | solution.py:88
  127.1 15.3 %collective-permute-start = (bf16[8,128,128]{2,1,0:T(8,128)(2,1)S(1)}, bf16[8,128,128]{2,1,0:T(8,128)(2,1)S(1)}, u32[]{:S(2)}, u32[]{:S(2)}) collective-permute-start(bf16[8,128,128]{2,1,0:T(8,128)(2,1)S(1)} %get-tuple-element.16), channel_id=1, source_target_pairs={{0,1},{1,2},{2,3},{3,0},{4,5},{5,6},{6,7},{7,4},{8,9},{9,10},{10,1... | collective-permute-start | bytes 786440 | tf_op jit(solution)/shard_map/ppermute | solution.py:88
  139.6 12.3 %collective-permute-start.3 = (bf16[4,128,128]{2,1,0:T(8,128)(2,1)S(1)}, bf16[4,128,128]{2,1,0:T(8,128)(2,1)S(1)}, u32[]{:S(2)}, u32[]{:S(2)}) collective-permute-start(bf16[4,128,128]{2,1,0:T(8,128)(2,1)S(1)} %slice.23), channel_id=1, source_target_pairs={{0,3},{1,0},{2,1},{3,2},{4,7},{5,4},{6,5},{7,6},{8,11},{9,8},{10,9... | collective-permute-start | bytes 393224 | tf_op jit(solution)/shard_map/ppermute | solution.py:88
  143.0 8.9 %collective-permute-start.1 = (bf16[4,128,128]{2,1,0:T(8,128)(2,1)}, bf16[4,128,128]{2,1,0:T(8,128)(2,1)S(1)}, u32[]{:S(2)}, u32[]{:S(2)}) collective-permute-start(bf16[4,128,128]{2,1,0:T(8,128)(2,1)} %slice.22), channel_id=1, source_target_pairs={{0,1},{1,2},{2,3},{3,0},{4,5},{5,6},{6,7},{7,4},{8,9},{9,10},{10,1... | collective-permute-start | bytes 393224 | tf_op jit(solution)/shard_map/ppermute | solution.py:88
  151.8 20.5 %copy-start.3 = (bf16[2048]{0:T(1024)(128)(2,1)S(1)}, bf16[2048]{0:T(1024)(128)(2,1)}, u32[]{:S(2)}) copy-start(bf16[2048]{0:T(1024)(128)(2,1)} %param.8) | copy-start | bytes 12292
  152.0 11.4 %collective-permute-start.6 = (f32[2,128,128]{2,1,0:T(8,128)S(1)}, f32[2,128,128]{2,1,0:T(8,128)S(1)}, u32[]{:S(2)}, u32[]{:S(2)}) collective-permute-start(f32[2,128,128]{2,1,0:T(8,128)S(1)} %dynamic-slice_add_fusion), channel_id=1, source_target_pairs={{0,12},{1,13},{2,14},{3,15},{16,28},{17,29},{18,30},{19,31},{32,44... | collective-permute-start | bytes 393224 | tf_op jit(solution)/shard_map/ppermute | solution.py:88
  156.3 7.1 %collective-permute-start.5 = (f32[2,128,128]{2,1,0:T(8,128)S(1)}, f32[2,128,128]{2,1,0:T(8,128)S(1)}, u32[]{:S(2)}, u32[]{:S(2)}) collective-permute-start(f32[2,128,128]{2,1,0:T(8,128)S(1)} %dynamic-slice_add_fusion), channel_id=1, source_target_pairs={{0,8},{4,12},{1,9},{5,13},{2,10},{6,14},{3,11},{7,15},{16,24},{20,... | collective-permute-start | bytes 393224 | tf_op jit(solution)/shard_map/ppermute | solution.py:88
  157.6 11.2 %collective-permute-start.4 = (f32[2,128,128]{2,1,0:T(8,128)S(1)}, f32[2,128,128]{2,1,0:T(8,128)S(1)}, u32[]{:S(2)}, u32[]{:S(2)}) collective-permute-start(f32[2,128,128]{2,1,0:T(8,128)S(1)} %dynamic-slice_add_fusion), channel_id=1, source_target_pairs={{0,4},{4,8},{8,12},{1,5},{5,9},{9,13},{2,6},{6,10},{10,14},{3,7},{... | collective-permute-start | bytes 393224 | tf_op jit(solution)/shard_map/ppermute | solution.py:88
  168.8 7.4 %collective-permute-start.9 = (f32[2,128,128]{2,1,0:T(8,128)S(1)}, f32[2,128,128]{2,1,0:T(8,128)S(1)}, u32[]{:S(2)}, u32[]{:S(2)}) collective-permute-start(f32[2,128,128]{2,1,0:T(8,128)S(1)} %add_add_fusion), channel_id=1, source_target_pairs={{0,3},{1,0},{2,1},{3,2},{4,7},{5,4},{6,5},{7,6},{8,11},{9,8},{10,9... | collective-permute-start | bytes 393224 | tf_op jit(solution)/shard_map/ppermute | solution.py:88
  171.5 6.7 %collective-permute-start.8 = (f32[2,128,128]{2,1,0:T(8,128)S(1)}, f32[2,128,128]{2,1,0:T(8,128)S(1)}, u32[]{:S(2)}, u32[]{:S(2)}) collective-permute-start(f32[2,128,128]{2,1,0:T(8,128)S(1)} %add_add_fusion), channel_id=1, source_target_pairs={{0,2},{1,3},{2,0},{3,1},{4,6},{5,7},{6,4},{7,5},{8,10},{9,11},{10,... | collective-permute-start | bytes 393224 | tf_op jit(solution)/shard_map/ppermute | solution.py:88
  171.5 10.1 %collective-permute-start.7 = (f32[2,128,128]{2,1,0:T(8,128)S(1)}, f32[2,128,128]{2,1,0:T(8,128)S(1)}, u32[]{:S(2)}, u32[]{:S(2)}) collective-permute-start(f32[2,128,128]{2,1,0:T(8,128)S(1)} %add_add_fusion), channel_id=1, source_target_pairs={{0,1},{1,2},{2,3},{3,0},{4,5},{5,6},{6,7},{7,4},{8,9},{9,10},{10,1... | collective-permute-start | bytes 393224 | tf_op jit(solution)/shard_map/ppermute | solution.py:88
  182.5 3.3 %copy-start.2 = (f32[1,16,128,128]{3,2,1,0:T(8,128)S(1)}, f32[1,16,128,128]{3,2,1,0:T(8,128)}, u32[]{:S(2)}) copy-start(f32[1,16,128,128]{3,2,1,0:T(8,128)} %param.9) | copy-start | bytes 3145732
Sparse Core Ops, SparseCore 0:
  10.4 96.6 all-gather.3
  124.6 53.8 all-gather.5

commit v16 on v15

--- a/solution.py
+++ b/solution.py
@@ -2,6 +2,7 @@
 import jax.numpy as jnp
 from jax import lax
 from jax.experimental import pallas as pl
+from jax.experimental.pallas import tpu as pltpu
 from jax.sharding import Mesh, PartitionSpec as P
 
 D = 2048
@@ -81,6 +82,63 @@
         out_specs=pl.BlockSpec((rows, width), lambda i: (0, i)),
         out_shape=jax.ShapeDtypeStruct((rows, H * DH), jnp.bfloat16),
     )(memory, queries, within, gains)
+
+
+def tail_gathered_kernel(here_ref, g_ref, p_ref, q_ref, w_ref, gain_ref, o_ref):
+    here = here_ref[0]
+    for j in range(p_ref.shape[0]):
+        state = p_ref[j]
+        for c in range(g_ref.shape[0]):
+            state = state + jnp.where(c < here, g_ref[c, j].astype(jnp.float32), 0.0)
+        carried = jnp.dot(q_ref[j], state.astype(jnp.bfloat16), preferred_element_type=jnp.float32)
+        numerator = carried + w_ref[j]
+        scale = lax.rsqrt(jnp.mean(numerator * numerator, axis=-1, keepdims=True) + epsilon)
+        part = slice(j * DH, (j + 1) * DH)
+        o_ref[:, part] = (numerator * scale * gain_ref[:, part]).astype(o_ref.dtype)
+
+
+def tail_from_memory_kernel(m_ref, q_ref, w_ref, gain_ref, prior_ref, o_ref):
+    del prior_ref
+    tail_kernel(m_ref, q_ref, w_ref, gain_ref, o_ref)
+
+
+def attend_tail_split(here, gathered, prefix, late_memory, queries, within, gains, heads_per_step=4):
+    rows = queries.shape[1]
+    width = heads_per_step * DH
+    n_piece = gathered.shape[0]
+    early = gathered.shape[1] // heads_per_step
+    late = late_memory.shape[0] // heads_per_step
+    grid_spec = pltpu.PrefetchScalarGridSpec(
+        num_scalar_prefetch=1,
+        grid=(early,),
+        in_specs=[
+            pl.BlockSpec((n_piece, heads_per_step, DH, DH), lambda i, s: (0, i, 0, 0)),
+            pl.BlockSpec((heads_per_step, DH, DH), lambda i, s: (i, 0, 0)),
+            pl.BlockSpec((heads_per_step, rows, DH), lambda i, s: (i, 0, 0)),
+            pl.BlockSpec((heads_per_step, rows, DH), lambda i, s: (i, 0, 0)),
+            pl.BlockSpec((1, width), lambda i, s: (0, i)),
+        ],
+        out_specs=pl.BlockSpec((rows, width), lambda i, s: (0, i)),
+    )
+    first = pl.pallas_call(
+        tail_gathered_kernel,
+        grid_spec=grid_spec,
+        out_shape=jax.ShapeDtypeStruct((rows, H * DH), jnp.bfloat16),
+    )(here, gathered, prefix, queries, within, gains)
+    return pl.pallas_call(
+        tail_from_memory_kernel,
+        grid=(late,),
+        in_specs=[
+            pl.BlockSpec((heads_per_step, DH, DH), lambda i: (i, 0, 0)),
+            pl.BlockSpec((heads_per_step, rows, DH), lambda i: (early + i, 0, 0)),
+            pl.BlockSpec((heads_per_step, rows, DH), lambda i: (early + i, 0, 0)),
+            pl.BlockSpec((1, width), lambda i: (0, early + i)),
+            pl.BlockSpec(memory_space=pl.ANY),
+        ],
+        out_specs=pl.BlockSpec((rows, width), lambda i: (0, early + i)),
+        out_shape=jax.ShapeDtypeStruct((rows, H * DH), jnp.bfloat16),
+        input_output_aliases={4: 0},
+    )(late_memory, queries, within, gains, first)
 
 
 def ring_shift(value, axis, shift, size, wrap=True):
@@ -139,13 +197,12 @@
     scores = jnp.where(causal[None], scores, 0.0).astype(jnp.bfloat16)
     within = jnp.einsum("hbc,che->hbe", scores, values, preferred_element_type=jnp.float32)
     before_late, within = memory_before(local[half:], within)
-    seq_here = lax.axis_index(("y", "x"))
-    earlier = (jnp.arange(gathered.shape[0]) < seq_here)[:, None, None, None]
-    before_early = jnp.sum(jnp.where(earlier, gathered.astype(jnp.float32), 0.0), axis=0)
-    memory = prefix_state[0] + jnp.concatenate([before_early, before_late], axis=0)
+    seq_here = lax.axis_index(("y", "x")).astype(jnp.int32).reshape(1)
+    late_memory = prefix_state[0, half:] + before_late
     gains = head_gain.astype(jnp.float32).reshape(1, H * DH)
-    attended = attend_tail(
-        memory, jnp.transpose(queries.reshape(tok_rows, H, DH), (1, 0, 2)), within, gains
+    attended = attend_tail_split(
+        seq_here, gathered, prefix_state[0], late_memory,
+        jnp.transpose(queries.reshape(tok_rows, H, DH), (1, 0, 2)), within, gains,
     )
     return attended.reshape(1, tok_rows, H * DH)
 

time: 201 us -> 200 us (level)
  other arithmetic: 10.1 us -> 6.58 us
  Pallas kernels: 21.4 us -> 23.7 us
    reduce_sum x1 -> x0, other arithmetic: 3.27 us -> none  [body(): jnp.sum(jnp.where(earlier, gathered.astype(jnp.float32), 0.0), axis=0)]
    pallas_call x1 -> x2, Pallas kernels: 5.79 us -> 8.16 us  [the longest x1 4.81 us: attend_tail_split(): pl.pallas_call(tail_gathered_kernel, grid_spec=grid_spec, out_shape=jax.S...]
  transfers between devices with their start and end apart: 12 -> 12, of which waited for: 6 -> 6; matrix products, arithmetic and copies ran while one was open for 15% -> 16% of each run, Pallas kernels for 0% -> 0%
where the time goes in v16:
time: 200 us; the launch traced here: 198 us
  waiting for transfers between devices  111 us (56%)
  Pallas kernels  23.7 us (12%)
  matrix products  18.4 us (9%)
  starting transfers between devices  16.7 us (8%)
  between operations  13.6 us (7%)
  local copies, waits for them, and re-layouts  8.48 us (4%)
  other arithmetic  6.58 us (3%)
    all_gather x1, waiting for transfers between devices, body(): weight = lax.all_gather(qkv_weight, ('dp', 'y', 'x'), axis=1, tiled=True)  95.1 us
    ppermute x10, starting transfers between devices, ring_shift(): return lax.ppermute(value, axis, pairs)  16.6 us
    pallas_call x1, Pallas kernels, kv_memory(): pl.pallas_call(kv_memory_kernel, grid=(H // heads_per_step,), in_specs=[p...  15.5 us
    ppermute x10, waiting for transfers between devices, ring_shift(): return lax.ppermute(value, axis, pairs)  15 us
    dot_general x1, matrix products, body(): queries = jnp.dot(normed, weight[:, :D], preferred_element_type=jnp.float32)  9.62 us
    dot_general x1, matrix products, body(): jnp.einsum('hbc,che->hbe', scores, values, preferred_element_type=jnp.flo...  8.78 us
    pallas_call x1, Pallas kernels, attend_tail_split(): pl.pallas_call(tail_gathered_kernel, grid_spec=grid_spec, out_shape=jax.S...  4.81 us
  transfers between devices with their start and end apart: 12, of which 6 were waited for; matrix products, arithmetic and copies ran while one was open for 16% of the time, Pallas kernels for 0%

profile of v16, /device:TPU:1, one launch (start us, length us, event | category | flops | bytes accessed | tf_op | source)
XLA Modules:
  0.0 198.2 jit_solution(4600848950792715617)
XLA Ops:
  6.5 0.7 all-gather.4.cloned.1.call-update
  8.0 2.1 %fusion.2 = f32[512]{0:T(512)S(1)} fusion(bf16[1,512,2048]{2,1,0:T(8,128)(2,1)} %param.5), kind=kLoop, calls=%fused_computation.6 | loop fusion | flops 3145216 | bytes 2099200 | tf_op jit(solution)/shard_map/reduce_sum | solution.py:181
  10.1 1.9 fusion.4.x_ref
  12.0 95.1 %all-gather.4.cloned.1.call-done = bf16[2048,6144]{0,1:T(8,128)(2,1)} async-done(((bf16[2048,48]{0,1:T(8,128)(2,1)}), bf16[2048,6144]{0,1:T(8,128)(2,1)}) %all-gather.4.cloned.1.call-update) | async-done | bytes 25165840 | tf_op jit(solution)/shard_map/all_gather | solution.py:184
  107.1 15.5 %shard_map.55 = (bf16[512,2048]{1,0:T(8,128)(2,1)}, bf16[512,2048]{1,0:T(8,128)(2,1)}, bf16[16,128,128]{2,1,0:T(8,128)(2,1)}) custom-call(bf16[512,2048]{1,0:T(8,128)(2,1)} %fusion.4.x_ref, bf16[6144,2048]{1,0:T(8,128)(2,1)} %bitcast.44, bf16[6144,2048]{1,0:T(8,128)(2,1)} %bitcast.45), custom_call_target="tpu_custom_call" | custom-call | tf_op jit(solution)/shard_map/pallas_call | solution.py:40
  122.6 1.8 fusion.20
  124.5 2.5 %collective-permute-start.2 = (bf16[8,128,128]{2,1,0:T(8,128)(2,1)S(1)}, bf16[8,128,128]{2,1,0:T(8,128)(2,1)S(1)}, u32[]{:S(2)}, u32[]{:S(2)}) collective-permute-start(bf16[8,128,128]{2,1,0:T(8,128)(2,1)S(1)} %get-tuple-element.16), channel_id=1, source_target_pairs={{0,3},{1,0},{2,1},{3,2},{4,7},{5,4},{6,5},{7,6},{8,11},{9,8},{10,9... | collective-permute-start | bytes 786440 | tf_op jit(solution)/shard_map/ppermute | solution.py:146
  127.0 9.6 %select_convert_fusion.1 = bf16[512,2048]{1,0:T(8,128)(2,1)} fusion(bf16[512,2048]{1,0:T(8,128)(2,1)S(1)} %copy-done, bf16[2048,6144]{0,1:T(8,128)(2,1)} %all-gather.4.cloned.1.call-done), kind=kOutput, calls=%fused_computation.9 | convolution fusion | flops 4300210176 | bytes 12582912 | tf_op jit(solution)/shard_map/dot_general | solution.py:190
  136.6 2.9 %copy.11 = bf16[512,2048]{0,1:T(8,128)(2,1)S(1)} copy(bf16[512,2048]{1,0:T(8,128)(2,1)} %select_convert_fusion.1) | data formatting | bytes 4194304 | tf_op jit(solution)/shard_map/convert_element_type | solution.py:191
  139.6 2.7 %collective-permute-start.3 = (bf16[4,128,128]{2,1,0:T(8,128)(2,1)S(1)}, bf16[4,128,128]{2,1,0:T(8,128)(2,1)S(1)}, u32[]{:S(2)}, u32[]{:S(2)}) collective-permute-start(bf16[4,128,128]{2,1,0:T(8,128)(2,1)S(1)} %slice.27), channel_id=1, source_target_pairs={{0,3},{1,0},{2,1},{3,2},{4,7},{5,4},{6,5},{7,6},{8,11},{9,8},{10,9... | collective-permute-start | bytes 393224 | tf_op jit(solution)/shard_map/ppermute | solution.py:146
  143.0 8.8 %fusion.7.w_ref = f32[16,512,128]{2,1,0:T(8,128)} fusion(bf16[512,16,128]{0,2,1:T(8,128)(2,1)S(1)} %bitcast.48, pred[512,512]{1,0:T(8,128)(4,1)S(1)} %iota_compare_fusion, bf16[512,2048]{1,0:T(8,128)(2,1)} %get-tuple-element.12, bf16[512,2048]{1,0:T(8,128)(2,1)} %get-tuple-element.11), kind=kOutput, calls=%fused_computation.10 | convolution fusion | flops 2155872256 | bytes 10747904 | tf_op jit(solution)/shard_map/hbc,che->hbe/dot_general | solution.py:198
  151.9 4.3 %collective-permute-start.6 = (f32[2,128,128]{2,1,0:T(8,128)S(1)}, f32[2,128,128]{2,1,0:T(8,128)S(1)}, u32[]{:S(2)}, u32[]{:S(2)}) collective-permute-start(f32[2,128,128]{2,1,0:T(8,128)S(1)} %dynamic-slice_add_fusion), channel_id=1, source_target_pairs={{0,12},{1,13},{2,14},{3,15},{16,28},{17,29},{18,30},{19,31},{32,44... | collective-permute-start | bytes 393224 | tf_op jit(solution)/shard_map/ppermute | solution.py:146
  156.3 1.3 collective-permute-start.5
  157.6 2.5 %collective-permute-start.4 = (f32[2,128,128]{2,1,0:T(8,128)S(1)}, f32[2,128,128]{2,1,0:T(8,128)S(1)}, u32[]{:S(2)}, u32[]{:S(2)}) collective-permute-start(f32[2,128,128]{2,1,0:T(8,128)S(1)} %dynamic-slice_add_fusion), channel_id=1, source_target_pairs={{0,4},{4,8},{8,12},{1,5},{5,9},{9,13},{2,6},{6,10},{10,14},{3,7},{... | collective-permute-start | bytes 393224 | tf_op jit(solution)/shard_map/ppermute | solution.py:146
  160.1 3.3 %collective-permute-done.6 = f32[2,128,128]{2,1,0:T(8,128)S(1)} collective-permute-done((f32[2,128,128]{2,1,0:T(8,128)S(1)}, f32[2,128,128]{2,1,0:T(8,128)S(1)}, u32[]{:S(2)}, u32[]{:S(2)}) %collective-permute-start.6) | collective-permute-done | bytes 131104 | tf_op jit(solution)/shard_map/ppermute | solution.py:146
  163.4 5.4 %collective-permute-done.4 = f32[2,128,128]{2,1,0:T(8,128)S(1)} collective-permute-done((f32[2,128,128]{2,1,0:T(8,128)S(1)}, f32[2,128,128]{2,1,0:T(8,128)S(1)}, u32[]{:S(2)}, u32[]{:S(2)}) %collective-permute-start.4) | collective-permute-done | bytes 131104 | tf_op jit(solution)/shard_map/ppermute | solution.py:146
  168.8 2.6 %collective-permute-start.9 = (f32[2,128,128]{2,1,0:T(8,128)S(1)}, f32[2,128,128]{2,1,0:T(8,128)S(1)}, u32[]{:S(2)}, u32[]{:S(2)}) collective-permute-start(f32[2,128,128]{2,1,0:T(8,128)S(1)} %add_add_fusion), channel_id=1, source_target_pairs={{0,3},{1,0},{2,1},{3,2},{4,7},{5,4},{6,5},{7,6},{8,11},{9,8},{10,9... | collective-permute-start | bytes 393224 | tf_op jit(solution)/shard_map/ppermute | solution.py:146
  172.9 2.4 %copy.15 = bf16[512,16,128]{2,0,1:T(8,128)(2,1)} copy(bf16[512,16,128]{0,2,1:T(8,128)(2,1)S(1)} %bitcast.49) | data formatting | bytes 4194304 | tf_op jit(solution)/shard_map/reshape | solution.py:195
  175.3 0.9 collective-permute-done.9
  176.2 1.9 collective-permute-done.8
  178.1 3.5 %collective-permute-done.7 = f32[2,128,128]{2,1,0:T(8,128)S(1)} collective-permute-done((f32[2,128,128]{2,1,0:T(8,128)S(1)}, f32[2,128,128]{2,1,0:T(8,128)S(1)}, u32[]{:S(2)}, u32[]{:S(2)}) %collective-permute-start.7) | collective-permute-done | bytes 131104 | tf_op jit(solution)/shard_map/ppermute | solution.py:146
  182.2 1.0 fusion.15.m_ref
  183.2 4.8 %shard_map.56.prior_ref = bf16[512,2048]{1,0:T(8,128)(2,1)} custom-call(s32[1]{0:T(128)} %bitcast.13.here_ref, bf16[16,8,128,128]{3,2,1,0:T(8,128)(2,1)} %bitcast.50, f32[16,128,128]{2,1,0:T(8,128)} %bitcast.51, bf16[16,512,128]{2,1,0:T(8,128)(2,1)} %bitcast.46, f32[16,512,128]{2,1,0:T(8,128)} %fusion.7.w_ref, f32[1,2048]{1,0:T(1,128)} %bitcast.56), custom_call_target="tpu_custom_call" | custom-call | tf_op jit(solution)/shard_map/pallas_call | solution.py:123
  188.0 3.4 %shard_map.57 = bf16[512,2048]{1,0:T(8,128)(2,1)} custom-call(f32[8,128,128]{2,1,0:T(8,128)} %fusion.15.m_ref, bf16[16,512,128]{2,1,0:T(8,128)(2,1)} %bitcast.47, f32[16,512,128]{2,1,0:T(8,128)} %fusion.7.w_ref, f32[1,2048]{1,0:T(1,128)} %bitcast.57, bf16[512,2048]{1,0:T(8,128)(2,1)} %shard_map.56.prior_ref), custom_call_target="tpu_custom_call", output_to_operand_aliasing={{}: (4, {})} | custom-call | tf_op jit(solution)/shard_map/pallas_call | solution.py:128
  (39 shorter events, 3.8 us)
Async XLA Ops:
  6.5 3.5 %copy-start.1 = (bf16[1,512,2048]{2,1,0:T(8,128)(2,1)S(1)}, bf16[1,512,2048]{2,1,0:T(8,128)(2,1)}, u32[]{:S(2)}) copy-start(bf16[1,512,2048]{2,1,0:T(8,128)(2,1)} %param.5) | copy-start | bytes 6291460
  6.5 100.6 %all-gather.4.cloned.1.call-start = ((), (), s32[]{:S(2)}) async-start(), calls=%async_computation | async-start | bytes 25362432 | tf_op jit(solution)/shard_map/all_gather | solution.py:184
  7.3 176.0 %all-gather.6.cloned.1.call-start = ((), (), s32[]{:S(2)}) async-start(), calls=%async_computation.1 | async-start | bytes 4456448 | tf_op jit(solution)/shard_map/all_gather | solution.py:189
  107.1 19.9 %copy-start = (bf16[512,2048]{1,0:T(8,128)(2,1)S(1)}, bf16[512,2048]{1,0:T(8,128)(2,1)}, u32[]{:S(2)}) copy-start(bf16[512,2048]{1,0:T(8,128)(2,1)} %fusion.4.x_ref) | copy-start | bytes 6291460
  124.5 15.0 %collective-permute-start.2 = (bf16[8,128,128]{2,1,0:T(8,128)(2,1)S(1)}, bf16[8,128,128]{2,1,0:T(8,128)(2,1)S(1)}, u32[]{:S(2)}, u32[]{:S(2)}) collective-permute-start(bf16[8,128,128]{2,1,0:T(8,128)(2,1)S(1)} %get-tuple-element.16), channel_id=1, source_target_pairs={{0,3},{1,0},{2,1},{3,2},{4,7},{5,4},{6,5},{7,6},{8,11},{9,8},{10,9... | collective-permute-start | bytes 786440 | tf_op jit(solution)/shard_map/ppermute | solution.py:146
  127.0 15.3 %collective-permute-start = (bf16[8,128,128]{2,1,0:T(8,128)(2,1)S(1)}, bf16[8,128,128]{2,1,0:T(8,128)(2,1)S(1)}, u32[]{:S(2)}, u32[]{:S(2)}) collective-permute-start(bf16[8,128,128]{2,1,0:T(8,128)(2,1)S(1)} %get-tuple-element.16), channel_id=1, source_target_pairs={{0,1},{1,2},{2,3},{3,0},{4,5},{5,6},{6,7},{7,4},{8,9},{9,10},{10,1... | collective-permute-start | bytes 786440 | tf_op jit(solution)/shard_map/ppermute | solution.py:146
  139.6 12.3 %collective-permute-start.3 = (bf16[4,128,128]{2,1,0:T(8,128)(2,1)S(1)}, bf16[4,128,128]{2,1,0:T(8,128)(2,1)S(1)}, u32[]{:S(2)}, u32[]{:S(2)}) collective-permute-start(bf16[4,128,128]{2,1,0:T(8,128)(2,1)S(1)} %slice.27), channel_id=1, source_target_pairs={{0,3},{1,0},{2,1},{3,2},{4,7},{5,4},{6,5},{7,6},{8,11},{9,8},{10,9... | collective-permute-start | bytes 393224 | tf_op jit(solution)/shard_map/ppermute | solution.py:146
  143.0 8.9 %collective-permute-start.1 = (bf16[4,128,128]{2,1,0:T(8,128)(2,1)}, bf16[4,128,128]{2,1,0:T(8,128)(2,1)S(1)}, u32[]{:S(2)}, u32[]{:S(2)}) collective-permute-start(bf16[4,128,128]{2,1,0:T(8,128)(2,1)} %slice.26), channel_id=1, source_target_pairs={{0,1},{1,2},{2,3},{3,0},{4,5},{5,6},{6,7},{7,4},{8,9},{9,10},{10,1... | collective-permute-start | bytes 393224 | tf_op jit(solution)/shard_map/ppermute | solution.py:146
  151.8 20.5 %copy-start.3 = (bf16[2048]{0:T(1024)(128)(2,1)S(1)}, bf16[2048]{0:T(1024)(128)(2,1)}, u32[]{:S(2)}) copy-start(bf16[2048]{0:T(1024)(128)(2,1)} %param.8) | copy-start | bytes 12292
  151.9 11.4 %collective-permute-start.6 = (f32[2,128,128]{2,1,0:T(8,128)S(1)}, f32[2,128,128]{2,1,0:T(8,128)S(1)}, u32[]{:S(2)}, u32[]{:S(2)}) collective-permute-start(f32[2,128,128]{2,1,0:T(8,128)S(1)} %dynamic-slice_add_fusion), channel_id=1, source_target_pairs={{0,12},{1,13},{2,14},{3,15},{16,28},{17,29},{18,30},{19,31},{32,44... | collective-permute-start | bytes 393224 | tf_op jit(solution)/shard_map/ppermute | solution.py:146
  156.3 7.1 %collective-permute-start.5 = (f32[2,128,128]{2,1,0:T(8,128)S(1)}, f32[2,128,128]{2,1,0:T(8,128)S(1)}, u32[]{:S(2)}, u32[]{:S(2)}) collective-permute-start(f32[2,128,128]{2,1,0:T(8,128)S(1)} %dynamic-slice_add_fusion), channel_id=1, source_target_pairs={{0,8},{4,12},{1,9},{5,13},{2,10},{6,14},{3,11},{7,15},{16,24},{20,... | collective-permute-start | bytes 393224 | tf_op jit(solution)/shard_map/ppermute | solution.py:146
  157.6 11.2 %collective-permute-start.4 = (f32[2,128,128]{2,1,0:T(8,128)S(1)}, f32[2,128,128]{2,1,0:T(8,128)S(1)}, u32[]{:S(2)}, u32[]{:S(2)}) collective-permute-start(f32[2,128,128]{2,1,0:T(8,128)S(1)} %dynamic-slice_add_fusion), channel_id=1, source_target_pairs={{0,4},{4,8},{8,12},{1,5},{5,9},{9,13},{2,6},{6,10},{10,14},{3,7},{... | collective-permute-start | bytes 393224 | tf_op jit(solution)/shard_map/ppermute | solution.py:146
  168.8 7.4 %collective-permute-start.9 = (f32[2,128,128]{2,1,0:T(8,128)S(1)}, f32[2,128,128]{2,1,0:T(8,128)S(1)}, u32[]{:S(2)}, u32[]{:S(2)}) collective-permute-start(f32[2,128,128]{2,1,0:T(8,128)S(1)} %add_add_fusion), channel_id=1, source_target_pairs={{0,3},{1,0},{2,1},{3,2},{4,7},{5,4},{6,5},{7,6},{8,11},{9,8},{10,9... | collective-permute-start | bytes 393224 | tf_op jit(solution)/shard_map/ppermute | solution.py:146
  171.4 6.7 %collective-permute-start.8 = (f32[2,128,128]{2,1,0:T(8,128)S(1)}, f32[2,128,128]{2,1,0:T(8,128)S(1)}, u32[]{:S(2)}, u32[]{:S(2)}) collective-permute-start(f32[2,128,128]{2,1,0:T(8,128)S(1)} %add_add_fusion), channel_id=1, source_target_pairs={{0,2},{1,3},{2,0},{3,1},{4,6},{5,7},{6,4},{7,5},{8,10},{9,11},{10,... | collective-permute-start | bytes 393224 | tf_op jit(solution)/shard_map/ppermute | solution.py:146
  171.4 10.1 %collective-permute-start.7 = (f32[2,128,128]{2,1,0:T(8,128)S(1)}, f32[2,128,128]{2,1,0:T(8,128)S(1)}, u32[]{:S(2)}, u32[]{:S(2)}) collective-permute-start(f32[2,128,128]{2,1,0:T(8,128)S(1)} %add_add_fusion), channel_id=1, source_target_pairs={{0,1},{1,2},{2,3},{3,0},{4,5},{5,6},{6,7},{7,4},{8,9},{9,10},{10,1... | collective-permute-start | bytes 393224 | tf_op jit(solution)/shard_map/ppermute | solution.py:146
  175.3 6.9 %copy-start.2 = (f32[1,16,128,128]{3,2,1,0:T(8,128)S(1)}, f32[1,16,128,128]{3,2,1,0:T(8,128)}, u32[]{:S(2)}) copy-start(f32[1,16,128,128]{3,2,1,0:T(8,128)} %param.9) | copy-start | bytes 3145732
Sparse Core Ops, SparseCore 0:
  10.4 96.6 all-gather.3
  124.6 53.8 all-gather.5

commit v17 on v16

--- a/solution.py
+++ b/solution.py
@@ -163,16 +163,10 @@
         + jnp.where(x_here >= 2, f32(far), 0.0)
         + jnp.where(x_here >= 3, f32(from_right), 0.0)
     )
-    per = local.shape[0] // n_x
-    quarter = lax.dynamic_slice_in_dim(row_total, x_here * per, per, axis=0)
-    quarter, filler = lax.optimization_barrier((quarter, filler))
-    rows_before = quarter * 0.0
+    row_total, filler = lax.optimization_barrier((row_total, filler))
+    earlier_rows = row_total * 0.0
     for shift in range(1, n_y):
-        rows_before = rows_before + ring_shift(quarter, "y", shift, n_y, wrap=False)
-    got = [rows_before] + [ring_shift(rows_before, "x", k, n_x) for k in range(1, n_x)]
-    stacked = jnp.stack(got)
-    order = (x_here - jnp.arange(n_x)) % n_x
-    earlier_rows = jnp.take(stacked, order, axis=0).reshape(local.shape)
+        earlier_rows = earlier_rows + ring_shift(row_total, "y", shift, n_y, wrap=False)
     return earlier_rows + row_before, filler
 
 

time: 200 us -> 213 us (1.065)
  waiting for transfers between devices: 111 us -> 124 us
  other arithmetic: 6.58 us -> 9.63 us
    ppermute x10 -> x7, waiting for transfers between devices: 15 us -> 27.7 us  [ring_shift(): return lax.ppermute(value, axis, pairs)]
    ppermute x10 -> x7, starting transfers between devices: 16.6 us -> 15.1 us  [ring_shift(): return lax.ppermute(value, axis, pairs)]
  transfers between devices with their start and end apart: 12 -> 9, of which waited for: 6 -> 3; matrix products, arithmetic and copies ran while one was open for 16% -> 16% of each run, Pallas kernels for 0% -> 0%
where the time goes in v17:
time: 213 us; the launch traced here: 212 us
  waiting for transfers between devices  124 us (58%)
  Pallas kernels  23.6 us (11%)
  matrix products  18.5 us (9%)
  starting transfers between devices  15.2 us (7%)
  between operations  13.5 us (6%)
  other arithmetic  9.63 us (5%)
  local copies, waits for them, and re-layouts  7.79 us (4%)
    all_gather x1, waiting for transfers between devices, body(): weight = lax.all_gather(qkv_weight, ('dp', 'y', 'x'), axis=1, tiled=True)  95.1 us
    ppermute x7, waiting for transfers between devices, ring_shift(): return lax.ppermute(value, axis, pairs)  27.7 us
    pallas_call x1, Pallas kernels, kv_memory(): pl.pallas_call(kv_memory_kernel, grid=(H // heads_per_step,), in_specs=[p...  15.5 us
    ppermute x7, starting transfers between devices, ring_shift(): return lax.ppermute(value, axis, pairs)  15.1 us
    dot_general x1, matrix products, body(): queries = jnp.dot(normed, weight[:, :D], preferred_element_type=jnp.float32)  9.63 us
    dot_general x1, matrix products, body(): jnp.einsum('hbc,che->hbe', scores, values, preferred_element_type=jnp.flo...  8.89 us
    pallas_call x1, Pallas kernels, attend_tail_split(): pl.pallas_call(tail_gathered_kernel, grid_spec=grid_spec, out_shape=jax.S...  4.81 us
  transfers between devices with their start and end apart: 9, of which 3 were waited for; matrix products, arithmetic and copies ran while one was open for 16% of the time, Pallas kernels for 0%

profile of v17, /device:TPU:1, one launch (start us, length us, event | category | flops | bytes accessed | tf_op | source)
XLA Modules:
  0.0 211.8 jit_solution(18317420101796939213)
XLA Ops:
  6.5 0.7 all-gather.4.cloned.1.call-update
  8.0 2.1 fusion.2
  10.1 1.9 fusion.4.x_ref
  12.0 95.1 %all-gather.4.cloned.1.call-done = bf16[2048,6144]{0,1:T(8,128)(2,1)} async-done(((bf16[2048,48]{0,1:T(8,128)(2,1)}), bf16[2048,6144]{0,1:T(8,128)(2,1)}) %all-gather.4.cloned.1.call-update) | async-done | bytes 25165840 | tf_op jit(solution)/shard_map/all_gather | solution.py:178
  107.1 15.5 %shard_map.55 = (bf16[512,2048]{1,0:T(8,128)(2,1)}, bf16[512,2048]{1,0:T(8,128)(2,1)}, bf16[16,128,128]{2,1,0:T(8,128)(2,1)}) custom-call(bf16[512,2048]{1,0:T(8,128)(2,1)} %fusion.4.x_ref, bf16[6144,2048]{1,0:T(8,128)(2,1)} %bitcast.32, bf16[6144,2048]{1,0:T(8,128)(2,1)} %bitcast.33), custom_call_target="tpu_custom_call" | custom-call | tf_op jit(solution)/shard_map/pallas_call | solution.py:40
  122.6 1.8 fusion.19
  124.4 0.8 iota_compare_fusion
  125.2 1.2 collective-permute-start
  126.4 1.5 collective-permute-start.2
  127.8 9.6 %select_convert_fusion.1 = bf16[512,2048]{1,0:T(8,128)(2,1)} fusion(bf16[512,2048]{1,0:T(8,128)(2,1)S(1)} %copy-done, bf16[2048,6144]{0,1:T(8,128)(2,1)} %all-gather.4.cloned.1.call-done), kind=kOutput, calls=%fused_computation.8 | convolution fusion | flops 4300210176 | bytes 12582912 | tf_op jit(solution)/shard_map/dot_general | solution.py:184
  137.5 2.9 %copy.11 = bf16[512,2048]{0,1:T(8,128)(2,1)S(1)} copy(bf16[512,2048]{1,0:T(8,128)(2,1)} %select_convert_fusion.1) | data formatting | bytes 4194304 | tf_op jit(solution)/shard_map/convert_element_type | solution.py:185
  140.5 0.7 slice.25
  141.2 2.6 %collective-permute-start.3 = (bf16[4,128,128]{2,1,0:T(8,128)(2,1)}, bf16[4,128,128]{2,1,0:T(8,128)(2,1)S(1)}, u32[]{:S(2)}, u32[]{:S(2)}) collective-permute-start(bf16[4,128,128]{2,1,0:T(8,128)(2,1)} %slice.25), channel_id=1, source_target_pairs={{0,3},{1,0},{2,1},{3,2},{4,7},{5,4},{6,5},{7,6},{8,11},{9,8},{10,9... | collective-permute-start | bytes 393224 | tf_op jit(solution)/shard_map/ppermute | solution.py:146
  143.9 8.9 %fusion.7.w_ref = f32[16,512,128]{2,1,0:T(8,128)} fusion(bf16[512,16,128]{0,2,1:T(8,128)(2,1)S(1)} %bitcast.36, pred[512,512]{1,0:T(8,128)(4,1)} %iota_compare_fusion, bf16[512,2048]{1,0:T(8,128)(2,1)} %get-tuple-element.12, bf16[512,2048]{1,0:T(8,128)(2,1)} %get-tuple-element.11), kind=kOutput, calls=%fused_computation.9 | convolution fusion | flops 2155872256 | bytes 10747904 | tf_op jit(solution)/shard_map/hbc,che->hbe/dot_general | solution.py:192
  152.8 0.9 convert_add_fusion
  153.7 5.1 %collective-permute-start.6 = (f32[8,128,128]{2,1,0:T(8,128)}, f32[8,128,128]{2,1,0:T(8,128)}, u32[]{:S(2)}, u32[]{:S(2)}) collective-permute-start(f32[8,128,128]{2,1,0:T(8,128)} %convert_add_fusion), channel_id=1, source_target_pairs={{0,12},{1,13},{2,14},{3,15},{16,28},{17,29},{18,30},{19,31},{32,44... | collective-permute-start | bytes 1572872 | tf_op jit(solution)/shard_map/ppermute | solution.py:146
  158.8 2.1 collective-permute-start.5
  160.9 2.5 %collective-permute-start.4 = (f32[8,128,128]{2,1,0:T(8,128)}, f32[8,128,128]{2,1,0:T(8,128)}, u32[]{:S(2)}, u32[]{:S(2)}) collective-permute-start(f32[8,128,128]{2,1,0:T(8,128)} %convert_add_fusion), channel_id=1, source_target_pairs={{0,4},{4,8},{8,12},{1,5},{5,9},{9,13},{2,6},{6,10},{10,14},{3,7},{... | collective-permute-start | bytes 1572872 | tf_op jit(solution)/shard_map/ppermute | solution.py:146
  164.1 2.4 %copy.15 = bf16[512,16,128]{2,0,1:T(8,128)(2,1)} copy(bf16[512,16,128]{0,2,1:T(8,128)(2,1)S(1)} %bitcast.37) | data formatting | bytes 4194304 | tf_op jit(solution)/shard_map/reshape | solution.py:189
  166.4 25.5 %collective-permute-done.6 = f32[8,128,128]{2,1,0:T(8,128)} collective-permute-done((f32[8,128,128]{2,1,0:T(8,128)}, f32[8,128,128]{2,1,0:T(8,128)}, u32[]{:S(2)}, u32[]{:S(2)}) %collective-permute-start.6) | collective-permute-done | bytes 524320 | tf_op jit(solution)/shard_map/ppermute | solution.py:146
  191.9 2.2 %collective-permute-done.4 = f32[8,128,128]{2,1,0:T(8,128)} collective-permute-done((f32[8,128,128]{2,1,0:T(8,128)}, f32[8,128,128]{2,1,0:T(8,128)}, u32[]{:S(2)}, u32[]{:S(2)}) %collective-permute-start.4) | collective-permute-done | bytes 524320 | tf_op jit(solution)/shard_map/ppermute | solution.py:146
  194.1 2.7 %fusion.17.m_ref = f32[8,128,128]{2,1,0:T(8,128)} fusion(bf16[8,128,128]{2,1,0:T(8,128)(2,1)S(1)} %collective-permute-done, bf16[8,128,128]{2,1,0:T(8,128)(2,1)} %copy-done.3, f32[8,128,128]{2,1,0:T(8,128)} %collective-permute-done.6, f32[8,128,128]{2,1,0:T(8,128)} %collective-permute-done.5, f32[8,128,128]{2,1,0:T(8,128)} %collective-permute-done.4, ...), kind=kLoop, calls=%fused_computation.24 | loop fusion | flops 1966080 | bytes 3932163 | tf_op jit(solution)/shard_map/add | solution.py:195
  196.8 4.8 %shard_map.56.prior_ref = bf16[512,2048]{1,0:T(8,128)(2,1)} custom-call(s32[1]{0:T(128)} %bitcast.7.here_ref, bf16[16,8,128,128]{3,2,1,0:T(8,128)(2,1)} %bitcast.38, f32[16,128,128]{2,1,0:T(8,128)} %bitcast.39, bf16[16,512,128]{2,1,0:T(8,128)(2,1)} %bitcast.34, f32[16,512,128]{2,1,0:T(8,128)} %fusion.7.w_ref, f32[1,2048]{1,0:T(1,128)} %bitcast.40), custom_call_target="tpu_custom_call" | custom-call | tf_op jit(solution)/shard_map/pallas_call | solution.py:123
  201.6 3.3 %shard_map.57 = bf16[512,2048]{1,0:T(8,128)(2,1)} custom-call(f32[8,128,128]{2,1,0:T(8,128)} %fusion.17.m_ref, bf16[16,512,128]{2,1,0:T(8,128)(2,1)} %bitcast.35, f32[16,512,128]{2,1,0:T(8,128)} %fusion.7.w_ref, f32[1,2048]{1,0:T(1,128)} %bitcast.41, bf16[512,2048]{1,0:T(8,128)(2,1)} %shard_map.56.prior_ref), custom_call_target="tpu_custom_call", output_to_operand_aliasing={{}: (4, {})} | custom-call | tf_op jit(solution)/shard_map/pallas_call | solution.py:128
  (28 shorter events, 1.5 us)
Async XLA Ops:
  6.5 3.5 %copy-start.1 = (bf16[1,512,2048]{2,1,0:T(8,128)(2,1)S(1)}, bf16[1,512,2048]{2,1,0:T(8,128)(2,1)}, u32[]{:S(2)}) copy-start(bf16[1,512,2048]{2,1,0:T(8,128)(2,1)} %param.5) | copy-start | bytes 6291460
  6.5 100.6 %all-gather.4.cloned.1.call-start = ((), (), s32[]{:S(2)}) async-start(), calls=%async_computation | async-start | bytes 25362432 | tf_op jit(solution)/shard_map/all_gather | solution.py:178
  7.3 189.6 %all-gather.6.cloned.1.call-start = ((), (), s32[]{:S(2)}) async-start(), calls=%async_computation.1 | async-start | bytes 4456448 | tf_op jit(solution)/shard_map/all_gather | solution.py:183
  107.1 20.7 %copy-start = (bf16[512,2048]{1,0:T(8,128)(2,1)S(1)}, bf16[512,2048]{1,0:T(8,128)(2,1)}, u32[]{:S(2)}) copy-start(bf16[512,2048]{1,0:T(8,128)(2,1)} %fusion.4.x_ref) | copy-start | bytes 6291460
  125.2 15.2 %collective-permute-start = (bf16[8,128,128]{2,1,0:T(8,128)(2,1)S(1)}, bf16[8,128,128]{2,1,0:T(8,128)(2,1)S(1)}, u32[]{:S(2)}, u32[]{:S(2)}) collective-permute-start(bf16[8,128,128]{2,1,0:T(8,128)(2,1)S(1)} %get-tuple-element.16), channel_id=1, source_target_pairs={{0,1},{1,2},{2,3},{3,0},{4,5},{5,6},{6,7},{7,4},{8,9},{9,10},{10,1... | collective-permute-start | bytes 786440 | tf_op jit(solution)/shard_map/ppermute | solution.py:146
  126.4 14.1 %collective-permute-start.2 = (bf16[8,128,128]{2,1,0:T(8,128)(2,1)S(1)}, bf16[8,128,128]{2,1,0:T(8,128)(2,1)S(1)}, u32[]{:S(2)}, u32[]{:S(2)}) collective-permute-start(bf16[8,128,128]{2,1,0:T(8,128)(2,1)S(1)} %get-tuple-element.16), channel_id=1, source_target_pairs={{0,3},{1,0},{2,1},{3,2},{4,7},{5,4},{6,5},{7,6},{8,11},{9,8},{10,9... | collective-permute-start | bytes 786440 | tf_op jit(solution)/shard_map/ppermute | solution.py:146
  140.4 12.4 %collective-permute-start.1 = (bf16[4,128,128]{2,1,0:T(8,128)(2,1)S(1)}, bf16[4,128,128]{2,1,0:T(8,128)(2,1)S(1)}, u32[]{:S(2)}, u32[]{:S(2)}) collective-permute-start(bf16[4,128,128]{2,1,0:T(8,128)(2,1)S(1)} %slice.24), channel_id=1, source_target_pairs={{0,1},{1,2},{2,3},{3,0},{4,5},{5,6},{6,7},{7,4},{8,9},{9,10},{10,1... | collective-permute-start | bytes 393224 | tf_op jit(solution)/shard_map/ppermute | solution.py:146
  140.5 12.3 %copy-start.3 = (bf16[8,128,128]{2,1,0:T(8,128)(2,1)}, bf16[8,128,128]{2,1,0:T(8,128)(2,1)S(1)}, u32[]{:S(2)}) copy-start(bf16[8,128,128]{2,1,0:T(8,128)(2,1)S(1)} %collective-permute-done.2) | copy-start | bytes 786436
  141.2 11.5 %collective-permute-start.3 = (bf16[4,128,128]{2,1,0:T(8,128)(2,1)}, bf16[4,128,128]{2,1,0:T(8,128)(2,1)S(1)}, u32[]{:S(2)}, u32[]{:S(2)}) collective-permute-start(bf16[4,128,128]{2,1,0:T(8,128)(2,1)} %slice.25), channel_id=1, source_target_pairs={{0,3},{1,0},{2,1},{3,2},{4,7},{5,4},{6,5},{7,6},{8,11},{9,8},{10,9... | collective-permute-start | bytes 393224 | tf_op jit(solution)/shard_map/ppermute | solution.py:146
  143.9 8.9 %copy-start.4 = (bf16[16,128,128]{2,1,0:T(8,128)(2,1)S(1)}, bf16[16,128,128]{2,1,0:T(8,128)(2,1)}, u32[]{:S(2)}) copy-start(bf16[16,128,128]{2,1,0:T(8,128)(2,1)} %get-tuple-element.10) | copy-start | bytes 1572868
  143.9 19.6 %copy-start.6 = (bf16[2048]{0:T(1024)(128)(2,1)S(1)}, bf16[2048]{0:T(1024)(128)(2,1)}, u32[]{:S(2)}) copy-start(bf16[2048]{0:T(1024)(128)(2,1)} %param.8) | copy-start | bytes 12292
  152.8 10.7 %copy-start.5 = (bf16[4,128,128]{2,1,0:T(8,128)(2,1)}, bf16[4,128,128]{2,1,0:T(8,128)(2,1)S(1)}, u32[]{:S(2)}) copy-start(bf16[4,128,128]{2,1,0:T(8,128)(2,1)S(1)} %collective-permute-done.3) | copy-start | bytes 393220
  153.7 38.2 %collective-permute-start.6 = (f32[8,128,128]{2,1,0:T(8,128)}, f32[8,128,128]{2,1,0:T(8,128)}, u32[]{:S(2)}, u32[]{:S(2)}) collective-permute-start(f32[8,128,128]{2,1,0:T(8,128)} %convert_add_fusion), channel_id=1, source_target_pairs={{0,12},{1,13},{2,14},{3,15},{16,28},{17,29},{18,30},{19,31},{32,44... | collective-permute-start | bytes 1572872 | tf_op jit(solution)/shard_map/ppermute | solution.py:146
  158.8 33.1 %collective-permute-start.5 = (f32[8,128,128]{2,1,0:T(8,128)}, f32[8,128,128]{2,1,0:T(8,128)}, u32[]{:S(2)}, u32[]{:S(2)}) collective-permute-start(f32[8,128,128]{2,1,0:T(8,128)} %convert_add_fusion), channel_id=1, source_target_pairs={{0,8},{4,12},{1,9},{5,13},{2,10},{6,14},{3,11},{7,15},{16,24},{20,... | collective-permute-start | bytes 1572872 | tf_op jit(solution)/shard_map/ppermute | solution.py:146
  160.9 33.2 %collective-permute-start.4 = (f32[8,128,128]{2,1,0:T(8,128)}, f32[8,128,128]{2,1,0:T(8,128)}, u32[]{:S(2)}, u32[]{:S(2)}) collective-permute-start(f32[8,128,128]{2,1,0:T(8,128)} %convert_add_fusion), channel_id=1, source_target_pairs={{0,4},{4,8},{8,12},{1,5},{5,9},{9,13},{2,6},{6,10},{10,14},{3,7},{... | collective-permute-start | bytes 1572872 | tf_op jit(solution)/shard_map/ppermute | solution.py:146
  164.1 30.1 %copy-start.2 = (f32[1,16,128,128]{3,2,1,0:T(8,128)S(1)}, f32[1,16,128,128]{3,2,1,0:T(8,128)}, u32[]{:S(2)}) copy-start(f32[1,16,128,128]{3,2,1,0:T(8,128)} %param.9) | copy-start | bytes 3145732
Sparse Core Ops, SparseCore 0:
  10.4 96.6 all-gather.3
  124.5 69.8 all-gather.5

commit v18 on v16

--- a/solution.py
+++ b/solution.py
@@ -32,14 +32,14 @@
         m_ref[j] = m.astype(jnp.bfloat16)
 
 
-def kv_memory(normed, weight_t, heads_per_step=4):
+def kv_memory(normed, weight_t, first_head, n_heads, heads_per_step=4):
     rows = normed.shape[0]
     width = heads_per_step * DH
-    k_off = D // width
-    v_off = 2 * D // width
+    k_off = (D + first_head * DH) // width
+    v_off = (2 * D + first_head * DH) // width
     return pl.pallas_call(
         kv_memory_kernel,
-        grid=(H // heads_per_step,),
+        grid=(n_heads // heads_per_step,),
         in_specs=[
             pl.BlockSpec((rows, D), lambda i: (0, 0)),
             pl.BlockSpec((width, D), lambda i: (k_off + i, 0)),
@@ -51,9 +51,9 @@
             pl.BlockSpec((heads_per_step, DH, DH), lambda i: (i, 0, 0)),
         ],
         out_shape=[
-            jax.ShapeDtypeStruct((rows, D), jnp.bfloat16),
-            jax.ShapeDtypeStruct((rows, D), jnp.bfloat16),
-            jax.ShapeDtypeStruct((H, DH, DH), jnp.bfloat16),
+            jax.ShapeDtypeStruct((rows, n_heads * DH), jnp.bfloat16),
+            jax.ShapeDtypeStruct((rows, n_heads * DH), jnp.bfloat16),
+            jax.ShapeDtypeStruct((n_heads, DH, DH), jnp.bfloat16),
         ],
     )(normed, weight_t, weight_t)
 
@@ -182,11 +182,12 @@
     normed = (normed * input_gain.astype(jnp.float32)).astype(jnp.bfloat16)
     tok_rows = normed.shape[0]
     weight = lax.all_gather(qkv_weight, ("dp", "y", "x"), axis=1, tiled=True)
-    key_feats, values, local = kv_memory(normed, weight.T)
-    key_feats = key_feats.reshape(tok_rows, H, DH)
-    values = values.reshape(tok_rows, H, DH)
     half = H // 2
-    gathered = lax.all_gather(local[None, :half], ("y", "x"), axis=0, tiled=True)
+    k_early, v_early, local_early = kv_memory(normed, weight.T, 0, half)
+    gathered = lax.all_gather(local_early[None], ("y", "x"), axis=0, tiled=True)
+    k_late, v_late, local_late = kv_memory(normed, weight.T, half, H - half)
+    key_feats = jnp.concatenate([k_early, k_late], axis=1).reshape(tok_rows, H, DH)
+    values = jnp.concatenate([v_early, v_late], axis=1).reshape(tok_rows, H, DH)
     queries = jnp.dot(normed, weight[:, :D], preferred_element_type=jnp.float32)
     queries = feature_map(queries).astype(jnp.bfloat16)
 
@@ -196,7 +197,7 @@
     )
     scores = jnp.where(causal[None], scores, 0.0).astype(jnp.bfloat16)
     within = jnp.einsum("hbc,che->hbe", scores, values, preferred_element_type=jnp.float32)
-    before_late, within = memory_before(local[half:], within)
+    before_late, within = memory_before(local_late, within)
     seq_here = lax.axis_index(("y", "x")).astype(jnp.int32).reshape(1)
     late_memory = prefix_state[0, half:] + before_late
     gains = head_gain.astype(jnp.float32).reshape(1, H * DH)

time: 200 us -> 199 us (level)
  waiting for transfers between devices: 111 us -> 105 us
  other arithmetic: 6.58 us -> 12.1 us
  Pallas kernels: 23.7 us -> 26.6 us
  local copies, waits for them, and re-layouts: 8.48 us -> 6.02 us
    ppermute x10, waiting for transfers between devices: 15 us -> 8.83 us  [ring_shift(): return lax.ppermute(value, axis, pairs)]
    unnamed x0 -> x1, other arithmetic: none -> 4.74 us
    pallas_call x1 -> x2, Pallas kernels: 15.5 us -> 18.4 us  [kv_memory(): pl.pallas_call(kv_memory_kernel, grid=(n_heads // heads_per_step,), in_sp...]
  transfers between devices with their start and end apart: 12 -> 12, of which waited for: 6 -> 5; matrix products, arithmetic and copies ran while one was open for 16% -> 18% of each run, Pallas kernels for 0% -> 5%
where the time goes in v18:
time: 199 us; the launch traced here: 198 us
  waiting for transfers between devices  105 us (53%)
  Pallas kernels  26.6 us (13%)
  matrix products  18.4 us (9%)
  starting transfers between devices  16.4 us (8%)
  between operations  13.6 us (7%)
  other arithmetic  12.1 us (6%)
  local copies, waits for them, and re-layouts  6.02 us (3%)
    all_gather x1, waiting for transfers between devices, body(): weight = lax.all_gather(qkv_weight, ('dp', 'y', 'x'), axis=1, tiled=True)  95.1 us
    pallas_call x2, Pallas kernels, kv_memory(): pl.pallas_call(kv_memory_kernel, grid=(n_heads // heads_per_step,), in_sp...  18.4 us
    ppermute x10, starting transfers between devices, ring_shift(): return lax.ppermute(value, axis, pairs)  16.3 us
    dot_general x1, matrix products, body(): queries = jnp.dot(normed, weight[:, :D], preferred_element_type=jnp.float32)  9.66 us
    ppermute x10, waiting for transfers between devices, ring_shift(): return lax.ppermute(value, axis, pairs)  8.83 us
    dot_general x1, matrix products, body(): jnp.einsum('hbc,che->hbe', scores, values, preferred_element_type=jnp.flo...  8.75 us
    pallas_call x1, Pallas kernels, attend_tail_split(): pl.pallas_call(tail_gathered_kernel, grid_spec=grid_spec, out_shape=jax.S...  4.81 us
    unnamed x1, other arithmetic  4.74 us
  transfers between devices with their start and end apart: 12, of which 5 were waited for; matrix products, arithmetic and copies ran while one was open for 18% of the time, Pallas kernels for 5%

profile of v18, /device:TPU:1, one launch (start us, length us, event | category | flops | bytes accessed | tf_op | source)
XLA Modules:
  0.0 197.7 jit_solution(4213259976965938007)
XLA Ops:
  8.0 2.1 %fusion.2 = f32[512]{0:T(512)S(1)} fusion(bf16[1,512,2048]{2,1,0:T(8,128)(2,1)} %param.5), kind=kLoop, calls=%fused_computation.6 | loop fusion | flops 3145216 | bytes 2099200 | tf_op jit(solution)/shard_map/reduce_sum | solution.py:181
  10.1 1.9 fusion.4.x_ref
  12.0 95.1 %all-gather.4.cloned.1.call-done = bf16[2048,6144]{0,1:T(8,128)(2,1)} async-done(((bf16[2048,48]{0,1:T(8,128)(2,1)}), bf16[2048,6144]{0,1:T(8,128)(2,1)}) %all-gather.4.cloned.1.call-update) | async-done | bytes 25165840 | tf_op jit(solution)/shard_map/all_gather | solution.py:184
  107.1 9.1 %shard_map.56 = (bf16[512,1024]{1,0:T(8,128)(2,1)}, bf16[512,1024]{1,0:T(8,128)(2,1)}, bf16[8,128,128]{2,1,0:T(8,128)(2,1)}) custom-call(bf16[512,2048]{1,0:T(8,128)(2,1)} %fusion.4.x_ref, bf16[6144,2048]{1,0:T(8,128)(2,1)} %bitcast.39, bf16[6144,2048]{1,0:T(8,128)(2,1)} %bitcast.40), custom_call_target="tpu_custom_call" | custom-call | tf_op jit(solution)/shard_map/pallas_call | solution.py:40
  116.4 9.3 %shard_map.55 = (bf16[512,1024]{1,0:T(8,128)(2,1)}, bf16[512,1024]{1,0:T(8,128)(2,1)}, bf16[8,128,128]{2,1,0:T(8,128)(2,1)}) custom-call(bf16[512,2048]{1,0:T(8,128)(2,1)} %fusion.4.x_ref, bf16[6144,2048]{1,0:T(8,128)(2,1)} %bitcast.41, bf16[6144,2048]{1,0:T(8,128)(2,1)} %bitcast.42), custom_call_target="tpu_custom_call" | custom-call | tf_op jit(solution)/shard_map/pallas_call | solution.py:40
  125.6 2.4 %collective-permute-start.2 = (bf16[8,128,128]{2,1,0:T(8,128)(2,1)}, bf16[8,128,128]{2,1,0:T(8,128)(2,1)S(1)}, u32[]{:S(2)}, u32[]{:S(2)}) collective-permute-start(bf16[8,128,128]{2,1,0:T(8,128)(2,1)} %get-tuple-element.13), channel_id=1, source_target_pairs={{0,3},{1,0},{2,1},{3,2},{4,7},{5,4},{6,5},{7,6},{8,11},{9,8},{10,9... | collective-permute-start | bytes 786440 | tf_op jit(solution)/shard_map/ppermute | solution.py:146
  128.1 9.7 %select_convert_fusion.1 = bf16[512,2048]{1,0:T(8,128)(2,1)} fusion(bf16[512,2048]{1,0:T(8,128)(2,1)S(1)} %copy-done, bf16[2048,6144]{0,1:T(8,128)(2,1)} %all-gather.4.cloned.1.call-done), kind=kOutput, calls=%fused_computation.9 | convolution fusion | flops 4300210176 | bytes 12582912 | tf_op jit(solution)/shard_map/dot_general | solution.py:191
  137.7 2.9 %copy.11 = bf16[512,2048]{0,1:T(8,128)(2,1)S(1)} copy(bf16[512,2048]{1,0:T(8,128)(2,1)} %select_convert_fusion.1) | data formatting | bytes 4194304 | tf_op jit(solution)/shard_map/convert_element_type | solution.py:192
  140.6 4.7 %maximum_bitcast_fusion = (bf16[64,16,8,128]{3,2,1,0:T(8,128)(2,1)}, bf16[64,16,8,128]{3,2,1,0:T(8,128)(2,1)}) fusion(bf16[512,1024]{1,0:T(8,128)(2,1)} %get-tuple-element.15, bf16[512,1024]{1,0:T(8,128)(2,1)} %get-tuple-element.14, bf16[512,1024]{1,0:T(8,128)(2,1)} %get-tuple-element.17, bf16[512,1024]{1,0:T(8,128)(2,1)} %get-tuple-element.16), kind=kLoop, calls=%fused_computation.15 | loop fusion | flops 8388608 | bytes 8388608
  145.3 2.8 %collective-permute-start.3 = (bf16[4,128,128]{2,1,0:T(8,128)(2,1)S(1)}, bf16[4,128,128]{2,1,0:T(8,128)(2,1)S(1)}, u32[]{:S(2)}, u32[]{:S(2)}) collective-permute-start(bf16[4,128,128]{2,1,0:T(8,128)(2,1)S(1)} %slice.19), channel_id=1, source_target_pairs={{0,3},{1,0},{2,1},{3,2},{4,7},{5,4},{6,5},{7,6},{8,11},{9,8},{10,9... | collective-permute-start | bytes 393224 | tf_op jit(solution)/shard_map/ppermute | solution.py:146
  148.4 8.7 %fusion.7.w_ref = f32[16,512,128]{2,1,0:T(8,128)} fusion(bf16[512,16,128]{0,2,1:T(8,128)(2,1)S(1)} %bitcast.45, pred[512,512]{1,0:T(8,128)(4,1)S(1)} %iota_compare_fusion, bf16[64,16,8,128]{3,2,1,0:T(8,128)(2,1)} %get-tuple-element.22, bf16[64,16,8,128]{3,2,1,0:T(8,128)(2,1)} %get-tuple-element.21), kind=kOutput, calls=%fused_computation.10 | convolution fusion | flops 2155872256 | bytes 10747904 | tf_op jit(solution)/shard_map/hbc,che->hbe/dot_general | solution.py:199
  157.3 0.9 dynamic-slice_add_fusion
  158.1 4.4 %collective-permute-start.6 = (f32[2,128,128]{2,1,0:T(8,128)S(1)}, f32[2,128,128]{2,1,0:T(8,128)S(1)}, u32[]{:S(2)}, u32[]{:S(2)}) collective-permute-start(f32[2,128,128]{2,1,0:T(8,128)S(1)} %dynamic-slice_add_fusion), channel_id=1, source_target_pairs={{0,12},{1,13},{2,14},{3,15},{16,28},{17,29},{18,30},{19,31},{32,44... | collective-permute-start | bytes 393224 | tf_op jit(solution)/shard_map/ppermute | solution.py:146
  162.6 1.3 collective-permute-start.5
  163.9 2.5 %collective-permute-start.4 = (f32[2,128,128]{2,1,0:T(8,128)S(1)}, f32[2,128,128]{2,1,0:T(8,128)S(1)}, u32[]{:S(2)}, u32[]{:S(2)}) collective-permute-start(f32[2,128,128]{2,1,0:T(8,128)S(1)} %dynamic-slice_add_fusion), channel_id=1, source_target_pairs={{0,4},{4,8},{8,12},{1,5},{5,9},{9,13},{2,6},{6,10},{10,14},{3,7},{... | collective-permute-start | bytes 393224 | tf_op jit(solution)/shard_map/ppermute | solution.py:146
  166.4 2.8 %collective-permute-done.6 = f32[2,128,128]{2,1,0:T(8,128)S(1)} collective-permute-done((f32[2,128,128]{2,1,0:T(8,128)S(1)}, f32[2,128,128]{2,1,0:T(8,128)S(1)}, u32[]{:S(2)}, u32[]{:S(2)}) %collective-permute-start.6) | collective-permute-done | bytes 131104 | tf_op jit(solution)/shard_map/ppermute | solution.py:146
  169.2 1.7 collective-permute-done.4
  170.9 1.3 collective-permute-start.9
  174.4 2.4 %copy.15 = bf16[512,16,128]{2,0,1:T(8,128)(2,1)} copy(bf16[512,16,128]{0,2,1:T(8,128)(2,1)S(1)} %bitcast.46) | data formatting | bytes 4194304 | tf_op jit(solution)/shard_map/reshape | solution.py:196
  176.8 0.8 collective-permute-done.8
  177.7 3.4 %collective-permute-done.7 = f32[2,128,128]{2,1,0:T(8,128)S(1)} collective-permute-done((f32[2,128,128]{2,1,0:T(8,128)S(1)}, f32[2,128,128]{2,1,0:T(8,128)S(1)}, u32[]{:S(2)}, u32[]{:S(2)}) %collective-permute-start.7) | collective-permute-done | bytes 131104 | tf_op jit(solution)/shard_map/ppermute | solution.py:146
  181.7 1.0 fusion.15.m_ref
  182.7 4.8 %shard_map.57.prior_ref = bf16[512,2048]{1,0:T(8,128)(2,1)} custom-call(s32[1]{0:T(128)} %bitcast.13.here_ref, bf16[16,8,128,128]{3,2,1,0:T(8,128)(2,1)} %bitcast.47, f32[16,128,128]{2,1,0:T(8,128)} %bitcast.48, bf16[16,512,128]{2,1,0:T(8,128)(2,1)} %bitcast.43, f32[16,512,128]{2,1,0:T(8,128)} %fusion.7.w_ref, f32[1,2048]{1,0:T(1,128)} %bitcast.53), custom_call_target="tpu_custom_call" | custom-call | tf_op jit(solution)/shard_map/pallas_call | solution.py:123
  187.6 3.3 %shard_map.58 = bf16[512,2048]{1,0:T(8,128)(2,1)} custom-call(f32[8,128,128]{2,1,0:T(8,128)} %fusion.15.m_ref, bf16[16,512,128]{2,1,0:T(8,128)(2,1)} %bitcast.44, f32[16,512,128]{2,1,0:T(8,128)} %fusion.7.w_ref, f32[1,2048]{1,0:T(1,128)} %bitcast.54, bf16[512,2048]{1,0:T(8,128)(2,1)} %shard_map.57.prior_ref), custom_call_target="tpu_custom_call", output_to_operand_aliasing={{}: (4, {})} | custom-call | tf_op jit(solution)/shard_map/pallas_call | solution.py:128
  (40 shorter events, 4.8 us)
Async XLA Ops:
  6.5 3.5 %copy-start.1 = (bf16[1,512,2048]{2,1,0:T(8,128)(2,1)S(1)}, bf16[1,512,2048]{2,1,0:T(8,128)(2,1)}, u32[]{:S(2)}) copy-start(bf16[1,512,2048]{2,1,0:T(8,128)(2,1)} %param.5) | copy-start | bytes 6291460
  6.5 100.6 %all-gather.4.cloned.1.call-start = ((), (), s32[]{:S(2)}) async-start(), calls=%async_computation | async-start | bytes 25362432 | tf_op jit(solution)/shard_map/all_gather | solution.py:184
  7.3 175.5 %all-gather.6.cloned.1.call-start = ((), (), s32[]{:S(2)}) async-start(), calls=%async_computation.1 | async-start | bytes 4456448 | tf_op jit(solution)/shard_map/all_gather | solution.py:187
  116.3 11.7 %copy-start = (bf16[512,2048]{1,0:T(8,128)(2,1)S(1)}, bf16[512,2048]{1,0:T(8,128)(2,1)}, u32[]{:S(2)}) copy-start(bf16[512,2048]{1,0:T(8,128)(2,1)} %fusion.4.x_ref) | copy-start | bytes 6291460
  125.6 19.7 %collective-permute-start.2 = (bf16[8,128,128]{2,1,0:T(8,128)(2,1)}, bf16[8,128,128]{2,1,0:T(8,128)(2,1)S(1)}, u32[]{:S(2)}, u32[]{:S(2)}) collective-permute-start(bf16[8,128,128]{2,1,0:T(8,128)(2,1)} %get-tuple-element.13), channel_id=1, source_target_pairs={{0,3},{1,0},{2,1},{3,2},{4,7},{5,4},{6,5},{7,6},{8,11},{9,8},{10,9... | collective-permute-start | bytes 786440 | tf_op jit(solution)/shard_map/ppermute | solution.py:146
  128.0 20.0 %collective-permute-start = (bf16[8,128,128]{2,1,0:T(8,128)(2,1)}, bf16[8,128,128]{2,1,0:T(8,128)(2,1)S(1)}, u32[]{:S(2)}, u32[]{:S(2)}) collective-permute-start(bf16[8,128,128]{2,1,0:T(8,128)(2,1)} %get-tuple-element.13), channel_id=1, source_target_pairs={{0,1},{1,2},{2,3},{3,0},{4,5},{5,6},{6,7},{7,4},{8,9},{9,10},{10,1... | collective-permute-start | bytes 786440 | tf_op jit(solution)/shard_map/ppermute | solution.py:146
  145.3 11.9 %collective-permute-start.3 = (bf16[4,128,128]{2,1,0:T(8,128)(2,1)S(1)}, bf16[4,128,128]{2,1,0:T(8,128)(2,1)S(1)}, u32[]{:S(2)}, u32[]{:S(2)}) collective-permute-start(bf16[4,128,128]{2,1,0:T(8,128)(2,1)S(1)} %slice.19), channel_id=1, source_target_pairs={{0,3},{1,0},{2,1},{3,2},{4,7},{5,4},{6,5},{7,6},{8,11},{9,8},{10,9... | collective-permute-start | bytes 393224 | tf_op jit(solution)/shard_map/ppermute | solution.py:146
  148.1 9.1 %collective-permute-start.1 = (bf16[4,128,128]{2,1,0:T(8,128)(2,1)S(1)}, bf16[4,128,128]{2,1,0:T(8,128)(2,1)S(1)}, u32[]{:S(2)}, u32[]{:S(2)}) collective-permute-start(bf16[4,128,128]{2,1,0:T(8,128)(2,1)S(1)} %slice.18), channel_id=1, source_target_pairs={{0,1},{1,2},{2,3},{3,0},{4,5},{5,6},{6,7},{7,4},{8,9},{9,10},{10,1... | collective-permute-start | bytes 393224 | tf_op jit(solution)/shard_map/ppermute | solution.py:146
  157.1 16.7 %copy-start.3 = (bf16[2048]{0:T(1024)(128)(2,1)S(1)}, bf16[2048]{0:T(1024)(128)(2,1)}, u32[]{:S(2)}) copy-start(bf16[2048]{0:T(1024)(128)(2,1)} %param.8) | copy-start | bytes 12292
  158.1 11.0 %collective-permute-start.6 = (f32[2,128,128]{2,1,0:T(8,128)S(1)}, f32[2,128,128]{2,1,0:T(8,128)S(1)}, u32[]{:S(2)}, u32[]{:S(2)}) collective-permute-start(f32[2,128,128]{2,1,0:T(8,128)S(1)} %dynamic-slice_add_fusion), channel_id=1, source_target_pairs={{0,12},{1,13},{2,14},{3,15},{16,28},{17,29},{18,30},{19,31},{32,44... | collective-permute-start | bytes 393224 | tf_op jit(solution)/shard_map/ppermute | solution.py:146
  162.6 6.6 %collective-permute-start.5 = (f32[2,128,128]{2,1,0:T(8,128)S(1)}, f32[2,128,128]{2,1,0:T(8,128)S(1)}, u32[]{:S(2)}, u32[]{:S(2)}) collective-permute-start(f32[2,128,128]{2,1,0:T(8,128)S(1)} %dynamic-slice_add_fusion), channel_id=1, source_target_pairs={{0,8},{4,12},{1,9},{5,13},{2,10},{6,14},{3,11},{7,15},{16,24},{20,... | collective-permute-start | bytes 393224 | tf_op jit(solution)/shard_map/ppermute | solution.py:146
  163.9 7.0 %collective-permute-start.4 = (f32[2,128,128]{2,1,0:T(8,128)S(1)}, f32[2,128,128]{2,1,0:T(8,128)S(1)}, u32[]{:S(2)}, u32[]{:S(2)}) collective-permute-start(f32[2,128,128]{2,1,0:T(8,128)S(1)} %dynamic-slice_add_fusion), channel_id=1, source_target_pairs={{0,4},{4,8},{8,12},{1,5},{5,9},{9,13},{2,6},{6,10},{10,14},{3,7},{... | collective-permute-start | bytes 393224 | tf_op jit(solution)/shard_map/ppermute | solution.py:146
  170.9 5.9 %collective-permute-start.9 = (f32[2,128,128]{2,1,0:T(8,128)S(1)}, f32[2,128,128]{2,1,0:T(8,128)S(1)}, u32[]{:S(2)}, u32[]{:S(2)}) collective-permute-start(f32[2,128,128]{2,1,0:T(8,128)S(1)} %add_add_fusion), channel_id=1, source_target_pairs={{0,3},{1,0},{2,1},{3,2},{4,7},{5,4},{6,5},{7,6},{8,11},{9,8},{10,9... | collective-permute-start | bytes 393224 | tf_op jit(solution)/shard_map/ppermute | solution.py:146
  172.2 5.4 %collective-permute-start.8 = (f32[2,128,128]{2,1,0:T(8,128)S(1)}, f32[2,128,128]{2,1,0:T(8,128)S(1)}, u32[]{:S(2)}, u32[]{:S(2)}) collective-permute-start(f32[2,128,128]{2,1,0:T(8,128)S(1)} %add_add_fusion), channel_id=1, source_target_pairs={{0,2},{1,3},{2,0},{3,1},{4,6},{5,7},{6,4},{7,5},{8,10},{9,11},{10,... | collective-permute-start | bytes 393224 | tf_op jit(solution)/shard_map/ppermute | solution.py:146
  172.9 8.2 %collective-permute-start.7 = (f32[2,128,128]{2,1,0:T(8,128)S(1)}, f32[2,128,128]{2,1,0:T(8,128)S(1)}, u32[]{:S(2)}, u32[]{:S(2)}) collective-permute-start(f32[2,128,128]{2,1,0:T(8,128)S(1)} %add_add_fusion), channel_id=1, source_target_pairs={{0,1},{1,2},{2,3},{3,0},{4,5},{5,6},{6,7},{7,4},{8,9},{9,10},{10,1... | collective-permute-start | bytes 393224 | tf_op jit(solution)/shard_map/ppermute | solution.py:146
  176.8 4.9 %copy-start.2 = (f32[1,16,128,128]{3,2,1,0:T(8,128)S(1)}, f32[1,16,128,128]{3,2,1,0:T(8,128)}, u32[]{:S(2)}) copy-start(f32[1,16,128,128]{3,2,1,0:T(8,128)} %param.9) | copy-start | bytes 3145732
Sparse Core Ops, SparseCore 0:
  10.4 96.6 all-gather.3
  116.4 54.6 all-gather.5

commit v19 on v18

--- a/solution.py
+++ b/solution.py
@@ -97,9 +97,9 @@
         o_ref[:, part] = (numerator * scale * gain_ref[:, part]).astype(o_ref.dtype)
 
 
-def tail_from_memory_kernel(m_ref, q_ref, w_ref, gain_ref, prior_ref, o_ref):
+def tail_gathered_after_kernel(here_ref, g_ref, p_ref, q_ref, w_ref, gain_ref, prior_ref, o_ref):
     del prior_ref
-    tail_kernel(m_ref, q_ref, w_ref, gain_ref, o_ref)
+    tail_gathered_kernel(here_ref, g_ref, p_ref, q_ref, w_ref, gain_ref, o_ref)
 
 
 def attend_tail_split(here, gathered, prefix, late_memory, queries, within, gains, heads_per_step=4):
@@ -121,24 +121,36 @@
         out_specs=pl.BlockSpec((rows, width), lambda i, s: (0, i)),
     )
     first = pl.pallas_call(
-        tail_gathered_kernel,
-        grid_spec=grid_spec,
-        out_shape=jax.ShapeDtypeStruct((rows, H * DH), jnp.bfloat16),
-    )(here, gathered, prefix, queries, within, gains)
-    return pl.pallas_call(
-        tail_from_memory_kernel,
+        tail_kernel,
         grid=(late,),
         in_specs=[
             pl.BlockSpec((heads_per_step, DH, DH), lambda i: (i, 0, 0)),
             pl.BlockSpec((heads_per_step, rows, DH), lambda i: (early + i, 0, 0)),
             pl.BlockSpec((heads_per_step, rows, DH), lambda i: (early + i, 0, 0)),
             pl.BlockSpec((1, width), lambda i: (0, early + i)),
-            pl.BlockSpec(memory_space=pl.ANY),
         ],
         out_specs=pl.BlockSpec((rows, width), lambda i: (0, early + i)),
         out_shape=jax.ShapeDtypeStruct((rows, H * DH), jnp.bfloat16),
-        input_output_aliases={4: 0},
-    )(late_memory, queries, within, gains, first)
+    )(late_memory, queries, within, gains)
+    grid_spec = pltpu.PrefetchScalarGridSpec(
+        num_scalar_prefetch=1,
+        grid=(early,),
+        in_specs=[
+            pl.BlockSpec((n_piece, heads_per_step, DH, DH), lambda i, s: (0, i, 0, 0)),
+            pl.BlockSpec((heads_per_step, DH, DH), lambda i, s: (i, 0, 0)),
+            pl.BlockSpec((heads_per_step, rows, DH), lambda i, s: (i, 0, 0)),
+            pl.BlockSpec((heads_per_step, rows, DH), lambda i, s: (i, 0, 0)),
+            pl.BlockSpec((1, width), lambda i, s: (0, i)),
+            pl.BlockSpec(memory_space=pl.ANY),
+        ],
+        out_specs=pl.BlockSpec((rows, width), lambda i, s: (0, i)),
+    )
+    return pl.pallas_call(
+        tail_gathered_after_kernel,
+        grid_spec=grid_spec,
+        out_shape=jax.ShapeDtypeStruct((rows, H * DH), jnp.bfloat16),
+        input_output_aliases={6: 0},
+    )(here, gathered, prefix, queries, within, gains, first)
 
 
 def ring_shift(value, axis, shift, size, wrap=True):

time: 199 us -> 199 us (level)
  transfers between devices with their start and end apart: 12 -> 12, of which waited for: 5 -> 5; matrix products, arithmetic and copies ran while one was open for 18% -> 18% of each run, Pallas kernels for 5% -> 6%
where the time goes in v19:
time: 199 us; the launch traced here: 198 us
  waiting for transfers between devices  105 us (53%)
  Pallas kernels  26.5 us (13%)
  matrix products  18.4 us (9%)
  starting transfers between devices  16.4 us (8%)
  between operations  13.6 us (7%)
  other arithmetic  12.1 us (6%)
  local copies, waits for them, and re-layouts  6.02 us (3%)
    all_gather x1, waiting for transfers between devices, body(): weight = lax.all_gather(qkv_weight, ('dp', 'y', 'x'), axis=1, tiled=True)  95.1 us
    pallas_call x2, Pallas kernels, kv_memory(): pl.pallas_call(kv_memory_kernel, grid=(n_heads // heads_per_step,), in_sp...  18.4 us
    ppermute x10, starting transfers between devices, ring_shift(): return lax.ppermute(value, axis, pairs)  16.3 us
    dot_general x1, matrix products, body(): queries = jnp.dot(normed, weight[:, :D], preferred_element_type=jnp.float32)  9.66 us
    ppermute x10, waiting for transfers between devices, ring_shift(): return lax.ppermute(value, axis, pairs)  8.82 us
    dot_general x1, matrix products, body(): jnp.einsum('hbc,che->hbe', scores, values, preferred_element_type=jnp.flo...  8.75 us
    pallas_call x1, Pallas kernels, attend_tail_split(): pl.pallas_call(tail_gathered_after_kernel, grid_spec=grid_spec, out_shape...  4.81 us
    unnamed x1, other arithmetic  4.74 us
  transfers between devices with their start and end apart: 12, of which 5 were waited for; matrix products, arithmetic and copies ran while one was open for 18% of the time, Pallas kernels for 6%

profile of v19, /device:TPU:1, one launch (start us, length us, event | category | flops | bytes accessed | tf_op | source)
XLA Modules:
  0.0 197.7 jit_solution(15255807111070312352)
XLA Ops:
  8.0 2.1 %fusion.2 = f32[512]{0:T(512)S(1)} fusion(bf16[1,512,2048]{2,1,0:T(8,128)(2,1)} %param.5), kind=kLoop, calls=%fused_computation.6 | loop fusion | flops 3145216 | bytes 2099200 | tf_op jit(solution)/shard_map/reduce_sum | solution.py:193
  10.1 1.9 fusion.4.x_ref
  12.0 95.1 %all-gather.4.cloned.1.call-done = bf16[2048,6144]{0,1:T(8,128)(2,1)} async-done(((bf16[2048,48]{0,1:T(8,128)(2,1)}), bf16[2048,6144]{0,1:T(8,128)(2,1)}) %all-gather.4.cloned.1.call-update) | async-done | bytes 25165840 | tf_op jit(solution)/shard_map/all_gather | solution.py:196
  107.1 9.1 %shard_map.55 = (bf16[512,1024]{1,0:T(8,128)(2,1)}, bf16[512,1024]{1,0:T(8,128)(2,1)}, bf16[8,128,128]{2,1,0:T(8,128)(2,1)}) custom-call(bf16[512,2048]{1,0:T(8,128)(2,1)} %fusion.4.x_ref, bf16[6144,2048]{1,0:T(8,128)(2,1)} %bitcast.39, bf16[6144,2048]{1,0:T(8,128)(2,1)} %bitcast.40), custom_call_target="tpu_custom_call" | custom-call | tf_op jit(solution)/shard_map/pallas_call | solution.py:40
  116.4 9.3 %shard_map.56 = (bf16[512,1024]{1,0:T(8,128)(2,1)}, bf16[512,1024]{1,0:T(8,128)(2,1)}, bf16[8,128,128]{2,1,0:T(8,128)(2,1)}) custom-call(bf16[512,2048]{1,0:T(8,128)(2,1)} %fusion.4.x_ref, bf16[6144,2048]{1,0:T(8,128)(2,1)} %bitcast.41, bf16[6144,2048]{1,0:T(8,128)(2,1)} %bitcast.42), custom_call_target="tpu_custom_call" | custom-call | tf_op jit(solution)/shard_map/pallas_call | solution.py:40
  125.6 2.4 %collective-permute-start.2 = (bf16[8,128,128]{2,1,0:T(8,128)(2,1)}, bf16[8,128,128]{2,1,0:T(8,128)(2,1)S(1)}, u32[]{:S(2)}, u32[]{:S(2)}) collective-permute-start(bf16[8,128,128]{2,1,0:T(8,128)(2,1)} %get-tuple-element.14), channel_id=1, source_target_pairs={{0,3},{1,0},{2,1},{3,2},{4,7},{5,4},{6,5},{7,6},{8,11},{9,8},{10,9... | collective-permute-start | bytes 786440 | tf_op jit(solution)/shard_map/ppermute | solution.py:158
  128.1 9.7 %select_convert_fusion.1 = bf16[512,2048]{1,0:T(8,128)(2,1)} fusion(bf16[512,2048]{1,0:T(8,128)(2,1)S(1)} %copy-done, bf16[2048,6144]{0,1:T(8,128)(2,1)} %all-gather.4.cloned.1.call-done), kind=kOutput, calls=%fused_computation.9 | convolution fusion | flops 4300210176 | bytes 12582912 | tf_op jit(solution)/shard_map/dot_general | solution.py:203
  137.7 2.9 %copy.11 = bf16[512,2048]{0,1:T(8,128)(2,1)S(1)} copy(bf16[512,2048]{1,0:T(8,128)(2,1)} %select_convert_fusion.1) | data formatting | bytes 4194304 | tf_op jit(solution)/shard_map/convert_element_type | solution.py:204
  140.6 4.7 %maximum_bitcast_fusion = (bf16[64,16,8,128]{3,2,1,0:T(8,128)(2,1)}, bf16[64,16,8,128]{3,2,1,0:T(8,128)(2,1)}) fusion(bf16[512,1024]{1,0:T(8,128)(2,1)} %get-tuple-element.16, bf16[512,1024]{1,0:T(8,128)(2,1)} %get-tuple-element.15, bf16[512,1024]{1,0:T(8,128)(2,1)} %get-tuple-element.18, bf16[512,1024]{1,0:T(8,128)(2,1)} %get-tuple-element.17), kind=kLoop, calls=%fused_computation.15 | loop fusion | flops 8388608 | bytes 8388608
  145.3 2.8 %collective-permute-start.3 = (bf16[4,128,128]{2,1,0:T(8,128)(2,1)S(1)}, bf16[4,128,128]{2,1,0:T(8,128)(2,1)S(1)}, u32[]{:S(2)}, u32[]{:S(2)}) collective-permute-start(bf16[4,128,128]{2,1,0:T(8,128)(2,1)S(1)} %slice.20), channel_id=1, source_target_pairs={{0,3},{1,0},{2,1},{3,2},{4,7},{5,4},{6,5},{7,6},{8,11},{9,8},{10,9... | collective-permute-start | bytes 393224 | tf_op jit(solution)/shard_map/ppermute | solution.py:158
  148.4 8.7 %fusion.7.w_ref = f32[16,512,128]{2,1,0:T(8,128)} fusion(bf16[512,16,128]{0,2,1:T(8,128)(2,1)S(1)} %bitcast.45, pred[512,512]{1,0:T(8,128)(4,1)S(1)} %iota_compare_fusion, bf16[64,16,8,128]{3,2,1,0:T(8,128)(2,1)} %get-tuple-element.22, bf16[64,16,8,128]{3,2,1,0:T(8,128)(2,1)} %get-tuple-element.21), kind=kOutput, calls=%fused_computation.10 | convolution fusion | flops 2155872256 | bytes 10747904 | tf_op jit(solution)/shard_map/hbc,che->hbe/dot_general | solution.py:211
  157.3 0.9 dynamic-slice_add_fusion
  158.1 4.4 %collective-permute-start.6 = (f32[2,128,128]{2,1,0:T(8,128)S(1)}, f32[2,128,128]{2,1,0:T(8,128)S(1)}, u32[]{:S(2)}, u32[]{:S(2)}) collective-permute-start(f32[2,128,128]{2,1,0:T(8,128)S(1)} %dynamic-slice_add_fusion), channel_id=1, source_target_pairs={{0,12},{1,13},{2,14},{3,15},{16,28},{17,29},{18,30},{19,31},{32,44... | collective-permute-start | bytes 393224 | tf_op jit(solution)/shard_map/ppermute | solution.py:158
  162.6 1.3 collective-permute-start.5
  163.9 2.5 %collective-permute-start.4 = (f32[2,128,128]{2,1,0:T(8,128)S(1)}, f32[2,128,128]{2,1,0:T(8,128)S(1)}, u32[]{:S(2)}, u32[]{:S(2)}) collective-permute-start(f32[2,128,128]{2,1,0:T(8,128)S(1)} %dynamic-slice_add_fusion), channel_id=1, source_target_pairs={{0,4},{4,8},{8,12},{1,5},{5,9},{9,13},{2,6},{6,10},{10,14},{3,7},{... | collective-permute-start | bytes 393224 | tf_op jit(solution)/shard_map/ppermute | solution.py:158
  166.4 2.8 %collective-permute-done.6 = f32[2,128,128]{2,1,0:T(8,128)S(1)} collective-permute-done((f32[2,128,128]{2,1,0:T(8,128)S(1)}, f32[2,128,128]{2,1,0:T(8,128)S(1)}, u32[]{:S(2)}, u32[]{:S(2)}) %collective-permute-start.6) | collective-permute-done | bytes 131104 | tf_op jit(solution)/shard_map/ppermute | solution.py:158
  169.2 1.7 collective-permute-done.4
  170.9 1.3 collective-permute-start.9
  174.4 2.4 %copy.12 = bf16[512,16,128]{2,0,1:T(8,128)(2,1)} copy(bf16[512,16,128]{0,2,1:T(8,128)(2,1)S(1)} %bitcast.46) | data formatting | bytes 4194304 | tf_op jit(solution)/shard_map/reshape | solution.py:218
  176.8 0.8 collective-permute-done.8
  177.7 3.4 %collective-permute-done.7 = f32[2,128,128]{2,1,0:T(8,128)S(1)} collective-permute-done((f32[2,128,128]{2,1,0:T(8,128)S(1)}, f32[2,128,128]{2,1,0:T(8,128)S(1)}, u32[]{:S(2)}, u32[]{:S(2)}) %collective-permute-start.7) | collective-permute-done | bytes 131104 | tf_op jit(solution)/shard_map/ppermute | solution.py:158
  181.7 1.0 fusion.15.m_ref
  182.7 3.3 %shard_map.57.prior_ref = bf16[512,2048]{1,0:T(8,128)(2,1)} custom-call(f32[8,128,128]{2,1,0:T(8,128)} %fusion.15.m_ref, bf16[16,512,128]{2,1,0:T(8,128)(2,1)} %bitcast.43, f32[16,512,128]{2,1,0:T(8,128)} %fusion.7.w_ref, f32[1,2048]{1,0:T(1,128)} %bitcast.53), custom_call_target="tpu_custom_call" | custom-call | tf_op jit(solution)/shard_map/pallas_call | solution.py:123
  186.1 4.8 %shard_map.58 = bf16[512,2048]{1,0:T(8,128)(2,1)} custom-call(s32[1]{0:T(128)} %bitcast.here_ref, bf16[16,8,128,128]{3,2,1,0:T(8,128)(2,1)} %bitcast.47, f32[16,128,128]{2,1,0:T(8,128)} %bitcast.48, bf16[16,512,128]{2,1,0:T(8,128)(2,1)} %bitcast.44, f32[16,512,128]{2,1,0:T(8,128)} %fusion.7.w_ref, ...), custom_call_target="tpu_custom_call", output_to_operand_aliasing={{}: (6, {})} | custom-call | tf_op jit(solution)/shard_map/pallas_call | solution.py:148
  (40 shorter events, 4.8 us)
Async XLA Ops:
  6.5 3.5 %copy-start.1 = (bf16[1,512,2048]{2,1,0:T(8,128)(2,1)S(1)}, bf16[1,512,2048]{2,1,0:T(8,128)(2,1)}, u32[]{:S(2)}) copy-start(bf16[1,512,2048]{2,1,0:T(8,128)(2,1)} %param.5) | copy-start | bytes 6291460
  6.5 100.6 %all-gather.4.cloned.1.call-start = ((), (), s32[]{:S(2)}) async-start(), calls=%async_computation | async-start | bytes 25362432 | tf_op jit(solution)/shard_map/all_gather | solution.py:196
  7.3 178.8 %all-gather.6.cloned.1.call-start = ((), (), s32[]{:S(2)}) async-start(), calls=%async_computation.1 | async-start | bytes 4456448 | tf_op jit(solution)/shard_map/all_gather | solution.py:199
  116.3 11.7 %copy-start = (bf16[512,2048]{1,0:T(8,128)(2,1)S(1)}, bf16[512,2048]{1,0:T(8,128)(2,1)}, u32[]{:S(2)}) copy-start(bf16[512,2048]{1,0:T(8,128)(2,1)} %fusion.4.x_ref) | copy-start | bytes 6291460
  125.6 19.7 %collective-permute-start.2 = (bf16[8,128,128]{2,1,0:T(8,128)(2,1)}, bf16[8,128,128]{2,1,0:T(8,128)(2,1)S(1)}, u32[]{:S(2)}, u32[]{:S(2)}) collective-permute-start(bf16[8,128,128]{2,1,0:T(8,128)(2,1)} %get-tuple-element.14), channel_id=1, source_target_pairs={{0,3},{1,0},{2,1},{3,2},{4,7},{5,4},{6,5},{7,6},{8,11},{9,8},{10,9... | collective-permute-start | bytes 786440 | tf_op jit(solution)/shard_map/ppermute | solution.py:158
  128.0 20.0 %collective-permute-start = (bf16[8,128,128]{2,1,0:T(8,128)(2,1)}, bf16[8,128,128]{2,1,0:T(8,128)(2,1)S(1)}, u32[]{:S(2)}, u32[]{:S(2)}) collective-permute-start(bf16[8,128,128]{2,1,0:T(8,128)(2,1)} %get-tuple-element.14), channel_id=1, source_target_pairs={{0,1},{1,2},{2,3},{3,0},{4,5},{5,6},{6,7},{7,4},{8,9},{9,10},{10,1... | collective-permute-start | bytes 786440 | tf_op jit(solution)/shard_map/ppermute | solution.py:158
  145.3 11.9 %collective-permute-start.3 = (bf16[4,128,128]{2,1,0:T(8,128)(2,1)S(1)}, bf16[4,128,128]{2,1,0:T(8,128)(2,1)S(1)}, u32[]{:S(2)}, u32[]{:S(2)}) collective-permute-start(bf16[4,128,128]{2,1,0:T(8,128)(2,1)S(1)} %slice.20), channel_id=1, source_target_pairs={{0,3},{1,0},{2,1},{3,2},{4,7},{5,4},{6,5},{7,6},{8,11},{9,8},{10,9... | collective-permute-start | bytes 393224 | tf_op jit(solution)/shard_map/ppermute | solution.py:158
  148.1 9.1 %collective-permute-start.1 = (bf16[4,128,128]{2,1,0:T(8,128)(2,1)S(1)}, bf16[4,128,128]{2,1,0:T(8,128)(2,1)S(1)}, u32[]{:S(2)}, u32[]{:S(2)}) collective-permute-start(bf16[4,128,128]{2,1,0:T(8,128)(2,1)S(1)} %slice.19), channel_id=1, source_target_pairs={{0,1},{1,2},{2,3},{3,0},{4,5},{5,6},{6,7},{7,4},{8,9},{9,10},{10,1... | collective-permute-start | bytes 393224 | tf_op jit(solution)/shard_map/ppermute | solution.py:158
  157.1 16.7 %copy-start.3 = (bf16[2048]{0:T(1024)(128)(2,1)S(1)}, bf16[2048]{0:T(1024)(128)(2,1)}, u32[]{:S(2)}) copy-start(bf16[2048]{0:T(1024)(128)(2,1)} %param.8) | copy-start | bytes 12292
  158.1 11.0 %collective-permute-start.6 = (f32[2,128,128]{2,1,0:T(8,128)S(1)}, f32[2,128,128]{2,1,0:T(8,128)S(1)}, u32[]{:S(2)}, u32[]{:S(2)}) collective-permute-start(f32[2,128,128]{2,1,0:T(8,128)S(1)} %dynamic-slice_add_fusion), channel_id=1, source_target_pairs={{0,12},{1,13},{2,14},{3,15},{16,28},{17,29},{18,30},{19,31},{32,44... | collective-permute-start | bytes 393224 | tf_op jit(solution)/shard_map/ppermute | solution.py:158
  162.6 6.6 %collective-permute-start.5 = (f32[2,128,128]{2,1,0:T(8,128)S(1)}, f32[2,128,128]{2,1,0:T(8,128)S(1)}, u32[]{:S(2)}, u32[]{:S(2)}) collective-permute-start(f32[2,128,128]{2,1,0:T(8,128)S(1)} %dynamic-slice_add_fusion), channel_id=1, source_target_pairs={{0,8},{4,12},{1,9},{5,13},{2,10},{6,14},{3,11},{7,15},{16,24},{20,... | collective-permute-start | bytes 393224 | tf_op jit(solution)/shard_map/ppermute | solution.py:158
  163.9 7.0 %collective-permute-start.4 = (f32[2,128,128]{2,1,0:T(8,128)S(1)}, f32[2,128,128]{2,1,0:T(8,128)S(1)}, u32[]{:S(2)}, u32[]{:S(2)}) collective-permute-start(f32[2,128,128]{2,1,0:T(8,128)S(1)} %dynamic-slice_add_fusion), channel_id=1, source_target_pairs={{0,4},{4,8},{8,12},{1,5},{5,9},{9,13},{2,6},{6,10},{10,14},{3,7},{... | collective-permute-start | bytes 393224 | tf_op jit(solution)/shard_map/ppermute | solution.py:158
  170.9 5.9 %collective-permute-start.9 = (f32[2,128,128]{2,1,0:T(8,128)S(1)}, f32[2,128,128]{2,1,0:T(8,128)S(1)}, u32[]{:S(2)}, u32[]{:S(2)}) collective-permute-start(f32[2,128,128]{2,1,0:T(8,128)S(1)} %add_add_fusion), channel_id=1, source_target_pairs={{0,3},{1,0},{2,1},{3,2},{4,7},{5,4},{6,5},{7,6},{8,11},{9,8},{10,9... | collective-permute-start | bytes 393224 | tf_op jit(solution)/shard_map/ppermute | solution.py:158
  172.2 5.4 %collective-permute-start.8 = (f32[2,128,128]{2,1,0:T(8,128)S(1)}, f32[2,128,128]{2,1,0:T(8,128)S(1)}, u32[]{:S(2)}, u32[]{:S(2)}) collective-permute-start(f32[2,128,128]{2,1,0:T(8,128)S(1)} %add_add_fusion), channel_id=1, source_target_pairs={{0,2},{1,3},{2,0},{3,1},{4,6},{5,7},{6,4},{7,5},{8,10},{9,11},{10,... | collective-permute-start | bytes 393224 | tf_op jit(solution)/shard_map/ppermute | solution.py:158
  172.9 8.2 %collective-permute-start.7 = (f32[2,128,128]{2,1,0:T(8,128)S(1)}, f32[2,128,128]{2,1,0:T(8,128)S(1)}, u32[]{:S(2)}, u32[]{:S(2)}) collective-permute-start(f32[2,128,128]{2,1,0:T(8,128)S(1)} %add_add_fusion), channel_id=1, source_target_pairs={{0,1},{1,2},{2,3},{3,0},{4,5},{5,6},{6,7},{7,4},{8,9},{9,10},{10,1... | collective-permute-start | bytes 393224 | tf_op jit(solution)/shard_map/ppermute | solution.py:158
  176.8 4.9 %copy-start.2 = (f32[1,16,128,128]{3,2,1,0:T(8,128)S(1)}, f32[1,16,128,128]{3,2,1,0:T(8,128)}, u32[]{:S(2)}) copy-start(f32[1,16,128,128]{3,2,1,0:T(8,128)} %param.9) | copy-start | bytes 3145732
Sparse Core Ops, SparseCore 0:
  10.4 96.6 all-gather.3
  116.4 54.6 all-gather.5

commit v20 on v19

--- a/solution.py
+++ b/solution.py
@@ -165,9 +165,7 @@
     half = local.shape[0] // 2
     from_left = ring_shift(local, "x", 1, n_x)
     from_right = ring_shift(local, "x", -1, n_x)
-    far = jnp.concatenate(
-        [ring_shift(from_left[:half], "x", 1, n_x), ring_shift(from_right[half:], "x", -1, n_x)], axis=0
-    )
+    far = ring_shift(local, "x", 2, n_x)
     f32 = lambda v: v.astype(jnp.float32)
     row_total = f32(local) + f32(from_left) + f32(far) + f32(from_right)
     row_before = (
@@ -202,6 +200,7 @@
     values = jnp.concatenate([v_early, v_late], axis=1).reshape(tok_rows, H, DH)
     queries = jnp.dot(normed, weight[:, :D], preferred_element_type=jnp.float32)
     queries = feature_map(queries).astype(jnp.bfloat16)
+    before_late, queries = memory_before(local_late, queries)
 
     causal = jnp.arange(tok_rows)[:, None] >= jnp.arange(tok_rows)[None, :]
     scores = jnp.einsum(
@@ -209,7 +208,7 @@
     )
     scores = jnp.where(causal[None], scores, 0.0).astype(jnp.bfloat16)
     within = jnp.einsum("hbc,che->hbe", scores, values, preferred_element_type=jnp.float32)
-    before_late, within = memory_before(local_late, within)
+
     seq_here = lax.axis_index(("y", "x")).astype(jnp.int32).reshape(1)
     late_memory = prefix_state[0, half:] + before_late
     gains = head_gain.astype(jnp.float32).reshape(1, H * DH)

time: 199 us -> 197 us (0.990)
  waiting for transfers between devices: 105 us -> 99.8 us
  starting transfers between devices: 16.4 us -> 18.5 us
    ppermute x10 -> x9, waiting for transfers between devices: 8.82 us -> 3.96 us  [ring_shift(): return lax.ppermute(value, axis, pairs)]
    optimization_barrier x0 -> x1, local copies, waits for them, and re-layouts: none -> 2.9 us  [memory_before(): quarter, filler = lax.optimization_barrier((quarter, filler))]
    convert_element_type x1 -> x0, local copies, waits for them, and re-layouts: 2.86 us -> none  [body(): queries = feature_map(queries).astype(jnp.bfloat16)]
    unnamed x1, other arithmetic: 4.74 us -> 2.36 us
    ppermute x10 -> x9, starting transfers between devices: 16.3 us -> 18.5 us  [ring_shift(): return lax.ppermute(value, axis, pairs)]
  transfers between devices with their start and end apart: 12 -> 11, of which waited for: 5 -> 2; matrix products, arithmetic and copies ran while one was open for 18% -> 19% of each run, Pallas kernels for 6% -> 6%
where the time goes in v20:
time: 197 us; the launch traced here: 196 us
  waiting for transfers between devices  99.8 us (51%)
  Pallas kernels  26.6 us (14%)
  matrix products  18.6 us (9%)
  starting transfers between devices  18.5 us (9%)
  between operations  13.6 us (7%)
  other arithmetic  11.8 us (6%)
  local copies, waits for them, and re-layouts  6.7 us (3%)
    all_gather x1, waiting for transfers between devices, body(): weight = lax.all_gather(qkv_weight, ('dp', 'y', 'x'), axis=1, tiled=True)  95.1 us
    ppermute x9, starting transfers between devices, ring_shift(): return lax.ppermute(value, axis, pairs)  18.5 us
    pallas_call x2, Pallas kernels, kv_memory(): pl.pallas_call(kv_memory_kernel, grid=(n_heads // heads_per_step,), in_sp...  18.4 us
    dot_general x1, matrix products, body(): queries = jnp.dot(normed, weight[:, :D], preferred_element_type=jnp.float32)  9.82 us
    dot_general x1, matrix products, body(): jnp.einsum('hbc,che->hbe', scores, values, preferred_element_type=jnp.flo...  8.8 us
    pallas_call x1, Pallas kernels, attend_tail_split(): pl.pallas_call(tail_gathered_after_kernel, grid_spec=grid_spec, out_shape...  4.81 us
    ppermute x9, waiting for transfers between devices, ring_shift(): return lax.ppermute(value, axis, pairs)  3.96 us
  transfers between devices with their start and end apart: 11, of which 2 were waited for; matrix products, arithmetic and copies ran while one was open for 19% of the time, Pallas kernels for 6%

profile of v20, /device:TPU:1, one launch (start us, length us, event | category | flops | bytes accessed | tf_op | source)
XLA Modules:
  0.0 195.6 jit_solution(11986741948318695700)
XLA Ops:
  8.0 2.1 %fusion.2 = f32[512]{0:T(512)S(1)} fusion(bf16[1,512,2048]{2,1,0:T(8,128)(2,1)} %param.5), kind=kLoop, calls=%fused_computation.6 | loop fusion | flops 3145216 | bytes 2099200 | tf_op jit(solution)/shard_map/reduce_sum | solution.py:191
  10.1 1.9 fusion.4.x_ref
  12.0 95.1 %all-gather.4.cloned.1.call-done = bf16[2048,6144]{0,1:T(8,128)(2,1)} async-done(((bf16[2048,48]{0,1:T(8,128)(2,1)}), bf16[2048,6144]{0,1:T(8,128)(2,1)}) %all-gather.4.cloned.1.call-update) | async-done | bytes 25165840 | tf_op jit(solution)/shard_map/all_gather | solution.py:194
  107.1 9.1 %shard_map.55 = (bf16[512,1024]{1,0:T(8,128)(2,1)}, bf16[512,1024]{1,0:T(8,128)(2,1)}, bf16[8,128,128]{2,1,0:T(8,128)(2,1)}) custom-call(bf16[512,2048]{1,0:T(8,128)(2,1)} %fusion.4.x_ref, bf16[6144,2048]{1,0:T(8,128)(2,1)} %bitcast.39, bf16[6144,2048]{1,0:T(8,128)(2,1)} %bitcast.40), custom_call_target="tpu_custom_call" | custom-call | tf_op jit(solution)/shard_map/pallas_call | solution.py:40
  117.2 9.3 %shard_map.56 = (bf16[512,1024]{1,0:T(8,128)(2,1)}, bf16[512,1024]{1,0:T(8,128)(2,1)}, bf16[8,128,128]{2,1,0:T(8,128)(2,1)}) custom-call(bf16[512,2048]{1,0:T(8,128)(2,1)} %fusion.4.x_ref, bf16[6144,2048]{1,0:T(8,128)(2,1)} %bitcast.41, bf16[6144,2048]{1,0:T(8,128)(2,1)} %bitcast.42), custom_call_target="tpu_custom_call" | custom-call | tf_op jit(solution)/shard_map/pallas_call | solution.py:40
  126.5 1.2 collective-permute-start
  127.7 2.4 %collective-permute-start.1 = (bf16[8,128,128]{2,1,0:T(8,128)(2,1)}, bf16[8,128,128]{2,1,0:T(8,128)(2,1)S(1)}, u32[]{:S(2)}, u32[]{:S(2)}) collective-permute-start(bf16[8,128,128]{2,1,0:T(8,128)(2,1)} %get-tuple-element.14), channel_id=1, source_target_pairs={{0,2},{1,3},{2,0},{3,1},{4,6},{5,7},{6,4},{7,5},{8,10},{9,11},{10,... | collective-permute-start | bytes 786440 | tf_op jit(solution)/shard_map/ppermute | solution.py:158
  130.1 1.2 collective-permute-start.2
  131.2 9.8 %select_convert_fusion.1 = bf16[512,2048]{1,0:T(8,128)(2,1)} fusion(bf16[512,2048]{1,0:T(8,128)(2,1)S(1)} %copy-done, bf16[2048,6144]{0,1:T(8,128)(2,1)} %all-gather.4.cloned.1.call-done), kind=kOutput, calls=%fused_computation.9 | convolution fusion | flops 4300210176 | bytes 12582912 | tf_op jit(solution)/shard_map/dot_general | solution.py:201
  141.1 3.9 %collective-permute-done.1 = bf16[8,128,128]{2,1,0:T(8,128)(2,1)S(1)} collective-permute-done((bf16[8,128,128]{2,1,0:T(8,128)(2,1)}, bf16[8,128,128]{2,1,0:T(8,128)(2,1)S(1)}, u32[]{:S(2)}, u32[]{:S(2)}) %collective-permute-start.1) | collective-permute-done | bytes 262176 | tf_op jit(solution)/shard_map/ppermute | solution.py:158
  145.1 0.9 dynamic-slice_add_fusion
  146.0 3.1 %collective-permute-start.3 = (f32[2,128,128]{2,1,0:T(8,128)S(1)}, f32[2,128,128]{2,1,0:T(8,128)S(1)}, u32[]{:S(2)}, u32[]{:S(2)}) collective-permute-start(f32[2,128,128]{2,1,0:T(8,128)S(1)} %dynamic-slice_add_fusion), channel_id=1, source_target_pairs={{0,4},{4,8},{8,12},{1,5},{5,9},{9,13},{2,6},{6,10},{10,14},{3,7},{... | collective-permute-start | bytes 393224 | tf_op jit(solution)/shard_map/ppermute | solution.py:158
  149.1 4.4 %collective-permute-start.4 = (f32[2,128,128]{2,1,0:T(8,128)S(1)}, f32[2,128,128]{2,1,0:T(8,128)S(1)}, u32[]{:S(2)}, u32[]{:S(2)}) collective-permute-start(f32[2,128,128]{2,1,0:T(8,128)S(1)} %dynamic-slice_add_fusion), channel_id=1, source_target_pairs={{0,8},{4,12},{1,9},{5,13},{2,10},{6,14},{3,11},{7,15},{16,24},{20,... | collective-permute-start | bytes 393224 | tf_op jit(solution)/shard_map/ppermute | solution.py:158
  153.6 1.9 collective-permute-start.5
  155.5 2.4 %maximum_bitcast_fusion = (bf16[64,16,8,128]{3,2,1,0:T(8,128)(2,1)}, bf16[64,16,8,128]{3,2,1,0:T(8,128)(2,1)}) fusion(bf16[512,1024]{1,0:T(8,128)(2,1)S(1)} %copy-done.5, bf16[512,1024]{1,0:T(8,128)(2,1)S(1)} %copy-done.3, bf16[512,1024]{1,0:T(8,128)(2,1)S(1)} %copy-done.6, bf16[512,1024]{1,0:T(8,128)(2,1)S(1)} %copy-done.4), kind=kLoop, calls=%fused_computation.15 | loop fusion | flops 8388608 | bytes 8388608
  157.9 2.9 %copy.11 = bf16[512,2048]{0,1:T(8,128)(2,1)S(1)} copy(bf16[512,2048]{1,0:T(8,128)(2,1)} %select_convert_fusion.1) | data formatting | bytes 4194304 | tf_op jit(solution)/shard_map/optimization_barrier | solution.py:178
  161.5 1.0 add_add_fusion
  163.3 2.8 %collective-permute-start.7 = (f32[2,128,128]{2,1,0:T(8,128)S(1)}, f32[2,128,128]{2,1,0:T(8,128)S(1)}, u32[]{:S(2)}, u32[]{:S(2)}) collective-permute-start(f32[2,128,128]{2,1,0:T(8,128)S(1)} %add_add_fusion), channel_id=1, source_target_pairs={{0,2},{1,3},{2,0},{3,1},{4,6},{5,7},{6,4},{7,5},{8,10},{9,11},{10,... | collective-permute-start | bytes 393224 | tf_op jit(solution)/shard_map/ppermute | solution.py:158
  166.7 8.8 %fusion.7.w_ref = f32[16,512,128]{2,1,0:T(8,128)} fusion(bf16[512,16,128]{0,2,1:T(8,128)(2,1)S(1)} %bitcast.45, pred[512,512]{1,0:T(8,128)(4,1)S(1)} %iota_compare_fusion, bf16[64,16,8,128]{3,2,1,0:T(8,128)(2,1)} %get-tuple-element.22, bf16[64,16,8,128]{3,2,1,0:T(8,128)(2,1)} %get-tuple-element.21), kind=kOutput, calls=%fused_computation.10 | convolution fusion | flops 2155872256 | bytes 10747904 | tf_op jit(solution)/shard_map/hbc,che->hbe/dot_general | solution.py:210
  175.5 2.4 %copy.12 = bf16[512,16,128]{2,0,1:T(8,128)(2,1)} copy(bf16[512,16,128]{0,2,1:T(8,128)(2,1)S(1)} %bitcast.46) | data formatting | bytes 4194304 | tf_op jit(solution)/shard_map/reshape | solution.py:217
  177.9 1.0 pad_maximum_fusion
  179.6 1.0 fusion.15.m_ref
  180.6 3.3 %shard_map.57.prior_ref = bf16[512,2048]{1,0:T(8,128)(2,1)} custom-call(f32[8,128,128]{2,1,0:T(8,128)} %fusion.15.m_ref, bf16[16,512,128]{2,1,0:T(8,128)(2,1)} %bitcast.43, f32[16,512,128]{2,1,0:T(8,128)} %fusion.7.w_ref, f32[1,2048]{1,0:T(1,128)} %bitcast.52), custom_call_target="tpu_custom_call" | custom-call | tf_op jit(solution)/shard_map/pallas_call | solution.py:123
  183.9 4.8 %shard_map.58 = bf16[512,2048]{1,0:T(8,128)(2,1)} custom-call(s32[1]{0:T(128)} %bitcast.here_ref, bf16[16,8,128,128]{3,2,1,0:T(8,128)(2,1)} %bitcast.47, f32[16,128,128]{2,1,0:T(8,128)} %bitcast.48, bf16[16,512,128]{2,1,0:T(8,128)(2,1)} %bitcast.44, f32[16,512,128]{2,1,0:T(8,128)} %fusion.7.w_ref, ...), custom_call_target="tpu_custom_call", output_to_operand_aliasing={{}: (6, {})} | custom-call | tf_op jit(solution)/shard_map/pallas_call | solution.py:148
  (46 shorter events, 5.2 us)
Async XLA Ops:
  6.5 3.5 %copy-start.1 = (bf16[1,512,2048]{2,1,0:T(8,128)(2,1)S(1)}, bf16[1,512,2048]{2,1,0:T(8,128)(2,1)}, u32[]{:S(2)}) copy-start(bf16[1,512,2048]{2,1,0:T(8,128)(2,1)} %param.5) | copy-start | bytes 6291460
  6.5 100.6 %all-gather.4.cloned.1.call-start = ((), (), s32[]{:S(2)}) async-start(), calls=%async_computation | async-start | bytes 25362432 | tf_op jit(solution)/shard_map/all_gather | solution.py:194
  7.3 176.7 %all-gather.6.cloned.1.call-start = ((), (), s32[]{:S(2)}) async-start(), calls=%async_computation.1 | async-start | bytes 4456448 | tf_op jit(solution)/shard_map/all_gather | solution.py:197
  107.1 9.3 %copy-start.8 = (bf16[2048]{0:T(1024)(128)(2,1)S(1)}, bf16[2048]{0:T(1024)(128)(2,1)}, u32[]{:S(2)}) copy-start(bf16[2048]{0:T(1024)(128)(2,1)} %param.8) | copy-start | bytes 12292
  117.2 14.1 %copy-start = (bf16[512,2048]{1,0:T(8,128)(2,1)S(1)}, bf16[512,2048]{1,0:T(8,128)(2,1)}, u32[]{:S(2)}) copy-start(bf16[512,2048]{1,0:T(8,128)(2,1)} %fusion.4.x_ref) | copy-start | bytes 6291460
  126.5 14.6 %collective-permute-start = (bf16[8,128,128]{2,1,0:T(8,128)(2,1)}, bf16[8,128,128]{2,1,0:T(8,128)(2,1)S(1)}, u32[]{:S(2)}, u32[]{:S(2)}) collective-permute-start(bf16[8,128,128]{2,1,0:T(8,128)(2,1)} %get-tuple-element.14), channel_id=1, source_target_pairs={{0,1},{1,2},{2,3},{3,0},{4,5},{5,6},{6,7},{7,4},{8,9},{9,10},{10,1... | collective-permute-start | bytes 786440 | tf_op jit(solution)/shard_map/ppermute | solution.py:158
  127.7 17.4 %collective-permute-start.1 = (bf16[8,128,128]{2,1,0:T(8,128)(2,1)}, bf16[8,128,128]{2,1,0:T(8,128)(2,1)S(1)}, u32[]{:S(2)}, u32[]{:S(2)}) collective-permute-start(bf16[8,128,128]{2,1,0:T(8,128)(2,1)} %get-tuple-element.14), channel_id=1, source_target_pairs={{0,2},{1,3},{2,0},{3,1},{4,6},{5,7},{6,4},{7,5},{8,10},{9,11},{10,... | collective-permute-start | bytes 786440 | tf_op jit(solution)/shard_map/ppermute | solution.py:158
  130.1 15.0 %collective-permute-start.2 = (bf16[8,128,128]{2,1,0:T(8,128)(2,1)}, bf16[8,128,128]{2,1,0:T(8,128)(2,1)S(1)}, u32[]{:S(2)}, u32[]{:S(2)}) collective-permute-start(bf16[8,128,128]{2,1,0:T(8,128)(2,1)} %get-tuple-element.14), channel_id=1, source_target_pairs={{0,3},{1,0},{2,1},{3,2},{4,7},{5,4},{6,5},{7,6},{8,11},{9,8},{10,9... | collective-permute-start | bytes 786440 | tf_op jit(solution)/shard_map/ppermute | solution.py:158
  131.2 24.3 %copy-start.5 = (bf16[512,1024]{1,0:T(8,128)(2,1)S(1)}, bf16[512,1024]{1,0:T(8,128)(2,1)}, u32[]{:S(2)}) copy-start(bf16[512,1024]{1,0:T(8,128)(2,1)} %get-tuple-element.17) | copy-start | bytes 3145732
  131.2 24.3 %copy-start.6 = (bf16[512,1024]{1,0:T(8,128)(2,1)S(1)}, bf16[512,1024]{1,0:T(8,128)(2,1)}, u32[]{:S(2)}) copy-start(bf16[512,1024]{1,0:T(8,128)(2,1)} %get-tuple-element.19) | copy-start | bytes 3145732
  141.1 14.4 %copy-start.3 = (bf16[512,1024]{1,0:T(8,128)(2,1)S(1)}, bf16[512,1024]{1,0:T(8,128)(2,1)}, u32[]{:S(2)}) copy-start(bf16[512,1024]{1,0:T(8,128)(2,1)} %get-tuple-element.16) | copy-start | bytes 3145732
  141.1 14.4 %copy-start.4 = (bf16[512,1024]{1,0:T(8,128)(2,1)S(1)}, bf16[512,1024]{1,0:T(8,128)(2,1)}, u32[]{:S(2)}) copy-start(bf16[512,1024]{1,0:T(8,128)(2,1)} %get-tuple-element.18) | copy-start | bytes 3145732
  146.0 14.8 %collective-permute-start.3 = (f32[2,128,128]{2,1,0:T(8,128)S(1)}, f32[2,128,128]{2,1,0:T(8,128)S(1)}, u32[]{:S(2)}, u32[]{:S(2)}) collective-permute-start(f32[2,128,128]{2,1,0:T(8,128)S(1)} %dynamic-slice_add_fusion), channel_id=1, source_target_pairs={{0,4},{4,8},{8,12},{1,5},{5,9},{9,13},{2,6},{6,10},{10,14},{3,7},{... | collective-permute-start | bytes 393224 | tf_op jit(solution)/shard_map/ppermute | solution.py:158
  149.1 11.7 %collective-permute-start.4 = (f32[2,128,128]{2,1,0:T(8,128)S(1)}, f32[2,128,128]{2,1,0:T(8,128)S(1)}, u32[]{:S(2)}, u32[]{:S(2)}) collective-permute-start(f32[2,128,128]{2,1,0:T(8,128)S(1)} %dynamic-slice_add_fusion), channel_id=1, source_target_pairs={{0,8},{4,12},{1,9},{5,13},{2,10},{6,14},{3,11},{7,15},{16,24},{20,... | collective-permute-start | bytes 393224 | tf_op jit(solution)/shard_map/ppermute | solution.py:158
  153.6 7.9 %collective-permute-start.5 = (f32[2,128,128]{2,1,0:T(8,128)S(1)}, f32[2,128,128]{2,1,0:T(8,128)}, u32[]{:S(2)}, u32[]{:S(2)}) collective-permute-start(f32[2,128,128]{2,1,0:T(8,128)S(1)} %dynamic-slice_add_fusion), channel_id=1, source_target_pairs={{0,12},{1,13},{2,14},{3,15},{16,28},{17,29},{18,30},{19,31},{32,44... | collective-permute-start | bytes 393224 | tf_op jit(solution)/shard_map/ppermute | solution.py:158
  160.8 0.7 copy-start.7
  162.5 15.4 %collective-permute-start.6 = (f32[2,128,128]{2,1,0:T(8,128)S(1)}, f32[2,128,128]{2,1,0:T(8,128)S(1)}, u32[]{:S(2)}, u32[]{:S(2)}) collective-permute-start(f32[2,128,128]{2,1,0:T(8,128)S(1)} %add_add_fusion), channel_id=1, source_target_pairs={{0,1},{1,2},{2,3},{3,0},{4,5},{5,6},{6,7},{7,4},{8,9},{9,10},{10,1... | collective-permute-start | bytes 393224 | tf_op jit(solution)/shard_map/ppermute | solution.py:158
  163.3 14.6 %collective-permute-start.7 = (f32[2,128,128]{2,1,0:T(8,128)S(1)}, f32[2,128,128]{2,1,0:T(8,128)S(1)}, u32[]{:S(2)}, u32[]{:S(2)}) collective-permute-start(f32[2,128,128]{2,1,0:T(8,128)S(1)} %add_add_fusion), channel_id=1, source_target_pairs={{0,2},{1,3},{2,0},{3,1},{4,6},{5,7},{6,4},{7,5},{8,10},{9,11},{10,... | collective-permute-start | bytes 393224 | tf_op jit(solution)/shard_map/ppermute | solution.py:158
  166.2 11.8 %collective-permute-start.8 = (f32[2,128,128]{2,1,0:T(8,128)S(1)}, f32[2,128,128]{2,1,0:T(8,128)}, u32[]{:S(2)}, u32[]{:S(2)}) collective-permute-start(f32[2,128,128]{2,1,0:T(8,128)S(1)} %add_add_fusion), channel_id=1, source_target_pairs={{0,3},{1,0},{2,1},{3,2},{4,7},{5,4},{6,5},{7,6},{8,11},{9,8},{10,9... | collective-permute-start | bytes 393224 | tf_op jit(solution)/shard_map/ppermute | solution.py:158
  177.9 1.6 copy-start.2
Sparse Core Ops, SparseCore 0:
  10.4 96.6 all-gather.3
  116.4 61.8 all-gather.5

commit v21 on v20

--- a/solution.py
+++ b/solution.py
@@ -102,7 +102,7 @@
     tail_gathered_kernel(here_ref, g_ref, p_ref, q_ref, w_ref, gain_ref, o_ref)
 
 
-def attend_tail_split(here, gathered, prefix, late_memory, queries, within, gains, heads_per_step=4):
+def attend_tail_split(here, gathered, prefix, late_memory, queries, within, gains, heads_per_step=2):
     rows = queries.shape[1]
     width = heads_per_step * DH
     n_piece = gathered.shape[0]

time: 197 us -> 200 us (1.015)
  Pallas kernels: 26.6 us -> 28.7 us
  transfers between devices with their start and end apart: 11 -> 11, of which waited for: 2 -> 2; matrix products, arithmetic and copies ran while one was open for 19% -> 18% of each run, Pallas kernels for 6% -> 7%
where the time goes in v21:
time: 200 us; the launch traced here: 198 us
  waiting for transfers between devices  99.8 us (50%)
  Pallas kernels  28.7 us (14%)
  matrix products  18.6 us (9%)
  starting transfers between devices  18.5 us (9%)
  between operations  13.6 us (7%)
  other arithmetic  11.8 us (6%)
  local copies, waits for them, and re-layouts  6.7 us (3%)
    all_gather x1, waiting for transfers between devices, body(): weight = lax.all_gather(qkv_weight, ('dp', 'y', 'x'), axis=1, tiled=True)  95.1 us
    ppermute x9, starting transfers between devices, ring_shift(): return lax.ppermute(value, axis, pairs)  18.5 us
    pallas_call x2, Pallas kernels, kv_memory(): pl.pallas_call(kv_memory_kernel, grid=(n_heads // heads_per_step,), in_sp...  18.4 us
    dot_general x1, matrix products, body(): queries = jnp.dot(normed, weight[:, :D], preferred_element_type=jnp.float32)  9.82 us
    dot_general x1, matrix products, body(): jnp.einsum('hbc,che->hbe', scores, values, preferred_element_type=jnp.flo...  8.8 us
    pallas_call x1, Pallas kernels, attend_tail_split(): pl.pallas_call(tail_gathered_after_kernel, grid_spec=grid_spec, out_shape...  5.7 us
    pallas_call x1, Pallas kernels, attend_tail_split(): pl.pallas_call(tail_kernel, grid=(late,), in_specs=[pl.BlockSpec((heads_p...  4.56 us
  transfers between devices with their start and end apart: 11, of which 2 were waited for; matrix products, arithmetic and copies ran while one was open for 18% of the time, Pallas kernels for 7%

profile of v21, /device:TPU:1, one launch (start us, length us, event | category | flops | bytes accessed | tf_op | source)
XLA Modules:
  0.0 197.7 jit_solution(5471690233014601507)
XLA Ops:
  8.0 2.1 %fusion.2 = f32[512]{0:T(512)S(1)} fusion(bf16[1,512,2048]{2,1,0:T(8,128)(2,1)} %param.5), kind=kLoop, calls=%fused_computation.6 | loop fusion | flops 3145216 | bytes 2099200 | tf_op jit(solution)/shard_map/reduce_sum | solution.py:191
  10.1 1.9 fusion.4.x_ref
  12.0 95.1 %all-gather.4.cloned.1.call-done = bf16[2048,6144]{0,1:T(8,128)(2,1)} async-done(((bf16[2048,48]{0,1:T(8,128)(2,1)}), bf16[2048,6144]{0,1:T(8,128)(2,1)}) %all-gather.4.cloned.1.call-update) | async-done | bytes 25165840 | tf_op jit(solution)/shard_map/all_gather | solution.py:194
  107.1 9.1 %shard_map.55 = (bf16[512,1024]{1,0:T(8,128)(2,1)}, bf16[512,1024]{1,0:T(8,128)(2,1)}, bf16[8,128,128]{2,1,0:T(8,128)(2,1)}) custom-call(bf16[512,2048]{1,0:T(8,128)(2,1)} %fusion.4.x_ref, bf16[6144,2048]{1,0:T(8,128)(2,1)} %bitcast.39, bf16[6144,2048]{1,0:T(8,128)(2,1)} %bitcast.40), custom_call_target="tpu_custom_call" | custom-call | tf_op jit(solution)/shard_map/pallas_call | solution.py:40
  117.2 9.3 %shard_map.56 = (bf16[512,1024]{1,0:T(8,128)(2,1)}, bf16[512,1024]{1,0:T(8,128)(2,1)}, bf16[8,128,128]{2,1,0:T(8,128)(2,1)}) custom-call(bf16[512,2048]{1,0:T(8,128)(2,1)} %fusion.4.x_ref, bf16[6144,2048]{1,0:T(8,128)(2,1)} %bitcast.41, bf16[6144,2048]{1,0:T(8,128)(2,1)} %bitcast.42), custom_call_target="tpu_custom_call" | custom-call | tf_op jit(solution)/shard_map/pallas_call | solution.py:40
  126.5 1.2 collective-permute-start
  127.7 2.4 %collective-permute-start.1 = (bf16[8,128,128]{2,1,0:T(8,128)(2,1)}, bf16[8,128,128]{2,1,0:T(8,128)(2,1)S(1)}, u32[]{:S(2)}, u32[]{:S(2)}) collective-permute-start(bf16[8,128,128]{2,1,0:T(8,128)(2,1)} %get-tuple-element.14), channel_id=1, source_target_pairs={{0,2},{1,3},{2,0},{3,1},{4,6},{5,7},{6,4},{7,5},{8,10},{9,11},{10,... | collective-permute-start | bytes 786440 | tf_op jit(solution)/shard_map/ppermute | solution.py:158
  130.1 1.2 collective-permute-start.2
  131.2 9.8 %select_convert_fusion.1 = bf16[512,2048]{1,0:T(8,128)(2,1)} fusion(bf16[512,2048]{1,0:T(8,128)(2,1)S(1)} %copy-done, bf16[2048,6144]{0,1:T(8,128)(2,1)} %all-gather.4.cloned.1.call-done), kind=kOutput, calls=%fused_computation.9 | convolution fusion | flops 4300210176 | bytes 12582912 | tf_op jit(solution)/shard_map/dot_general | solution.py:201
  141.1 3.9 %collective-permute-done.1 = bf16[8,128,128]{2,1,0:T(8,128)(2,1)S(1)} collective-permute-done((bf16[8,128,128]{2,1,0:T(8,128)(2,1)}, bf16[8,128,128]{2,1,0:T(8,128)(2,1)S(1)}, u32[]{:S(2)}, u32[]{:S(2)}) %collective-permute-start.1) | collective-permute-done | bytes 262176 | tf_op jit(solution)/shard_map/ppermute | solution.py:158
  145.1 0.9 dynamic-slice_add_fusion
  146.0 3.1 %collective-permute-start.3 = (f32[2,128,128]{2,1,0:T(8,128)S(1)}, f32[2,128,128]{2,1,0:T(8,128)S(1)}, u32[]{:S(2)}, u32[]{:S(2)}) collective-permute-start(f32[2,128,128]{2,1,0:T(8,128)S(1)} %dynamic-slice_add_fusion), channel_id=1, source_target_pairs={{0,4},{4,8},{8,12},{1,5},{5,9},{9,13},{2,6},{6,10},{10,14},{3,7},{... | collective-permute-start | bytes 393224 | tf_op jit(solution)/shard_map/ppermute | solution.py:158
  149.1 4.4 %collective-permute-start.4 = (f32[2,128,128]{2,1,0:T(8,128)S(1)}, f32[2,128,128]{2,1,0:T(8,128)S(1)}, u32[]{:S(2)}, u32[]{:S(2)}) collective-permute-start(f32[2,128,128]{2,1,0:T(8,128)S(1)} %dynamic-slice_add_fusion), channel_id=1, source_target_pairs={{0,8},{4,12},{1,9},{5,13},{2,10},{6,14},{3,11},{7,15},{16,24},{20,... | collective-permute-start | bytes 393224 | tf_op jit(solution)/shard_map/ppermute | solution.py:158
  153.6 1.9 collective-permute-start.5
  155.5 2.4 %maximum_bitcast_fusion = (bf16[64,16,8,128]{3,2,1,0:T(8,128)(2,1)}, bf16[64,16,8,128]{3,2,1,0:T(8,128)(2,1)}) fusion(bf16[512,1024]{1,0:T(8,128)(2,1)S(1)} %copy-done.5, bf16[512,1024]{1,0:T(8,128)(2,1)S(1)} %copy-done.3, bf16[512,1024]{1,0:T(8,128)(2,1)S(1)} %copy-done.6, bf16[512,1024]{1,0:T(8,128)(2,1)S(1)} %copy-done.4), kind=kLoop, calls=%fused_computation.15 | loop fusion | flops 8388608 | bytes 8388608
  157.9 2.9 %copy.11 = bf16[512,2048]{0,1:T(8,128)(2,1)S(1)} copy(bf16[512,2048]{1,0:T(8,128)(2,1)} %select_convert_fusion.1) | data formatting | bytes 4194304 | tf_op jit(solution)/shard_map/optimization_barrier | solution.py:178
  161.5 1.0 add_add_fusion
  163.3 2.8 %collective-permute-start.7 = (f32[2,128,128]{2,1,0:T(8,128)S(1)}, f32[2,128,128]{2,1,0:T(8,128)S(1)}, u32[]{:S(2)}, u32[]{:S(2)}) collective-permute-start(f32[2,128,128]{2,1,0:T(8,128)S(1)} %add_add_fusion), channel_id=1, source_target_pairs={{0,2},{1,3},{2,0},{3,1},{4,6},{5,7},{6,4},{7,5},{8,10},{9,11},{10,... | collective-permute-start | bytes 393224 | tf_op jit(solution)/shard_map/ppermute | solution.py:158
  166.7 8.8 %fusion.7.w_ref = f32[16,512,128]{2,1,0:T(8,128)} fusion(bf16[512,16,128]{0,2,1:T(8,128)(2,1)S(1)} %bitcast.45, pred[512,512]{1,0:T(8,128)(4,1)S(1)} %iota_compare_fusion, bf16[64,16,8,128]{3,2,1,0:T(8,128)(2,1)} %get-tuple-element.22, bf16[64,16,8,128]{3,2,1,0:T(8,128)(2,1)} %get-tuple-element.21), kind=kOutput, calls=%fused_computation.10 | convolution fusion | flops 2155872256 | bytes 10747904 | tf_op jit(solution)/shard_map/hbc,che->hbe/dot_general | solution.py:210
  175.5 2.4 %copy.12 = bf16[512,16,128]{2,0,1:T(8,128)(2,1)} copy(bf16[512,16,128]{0,2,1:T(8,128)(2,1)S(1)} %bitcast.46) | data formatting | bytes 4194304 | tf_op jit(solution)/shard_map/reshape | solution.py:217
  177.9 1.0 pad_maximum_fusion
  179.6 1.0 fusion.15.m_ref
  180.6 4.6 %shard_map.57.prior_ref = bf16[512,2048]{1,0:T(8,128)(2,1)} custom-call(f32[8,128,128]{2,1,0:T(8,128)} %fusion.15.m_ref, bf16[16,512,128]{2,1,0:T(8,128)(2,1)} %bitcast.43, f32[16,512,128]{2,1,0:T(8,128)} %fusion.7.w_ref, f32[1,2048]{1,0:T(1,128)} %bitcast.52), custom_call_target="tpu_custom_call" | custom-call | tf_op jit(solution)/shard_map/pallas_call | solution.py:123
  185.2 5.7 %shard_map.58 = bf16[512,2048]{1,0:T(8,128)(2,1)} custom-call(s32[1]{0:T(128)} %bitcast.here_ref, bf16[16,8,128,128]{3,2,1,0:T(8,128)(2,1)} %bitcast.47, f32[16,128,128]{2,1,0:T(8,128)} %bitcast.48, bf16[16,512,128]{2,1,0:T(8,128)(2,1)} %bitcast.44, f32[16,512,128]{2,1,0:T(8,128)} %fusion.7.w_ref, ...), custom_call_target="tpu_custom_call", output_to_operand_aliasing={{}: (6, {})} | custom-call | tf_op jit(solution)/shard_map/pallas_call | solution.py:148
  (46 shorter events, 5.2 us)
Async XLA Ops:
  6.5 3.5 %copy-start.1 = (bf16[1,512,2048]{2,1,0:T(8,128)(2,1)S(1)}, bf16[1,512,2048]{2,1,0:T(8,128)(2,1)}, u32[]{:S(2)}) copy-start(bf16[1,512,2048]{2,1,0:T(8,128)(2,1)} %param.5) | copy-start | bytes 6291460
  6.5 100.6 %all-gather.4.cloned.1.call-start = ((), (), s32[]{:S(2)}) async-start(), calls=%async_computation | async-start | bytes 25362432 | tf_op jit(solution)/shard_map/all_gather | solution.py:194
  7.3 177.9 %all-gather.6.cloned.1.call-start = ((), (), s32[]{:S(2)}) async-start(), calls=%async_computation.1 | async-start | bytes 4456448 | tf_op jit(solution)/shard_map/all_gather | solution.py:197
  107.1 9.3 %copy-start.8 = (bf16[2048]{0:T(1024)(128)(2,1)S(1)}, bf16[2048]{0:T(1024)(128)(2,1)}, u32[]{:S(2)}) copy-start(bf16[2048]{0:T(1024)(128)(2,1)} %param.8) | copy-start | bytes 12292
  117.2 14.1 %copy-start = (bf16[512,2048]{1,0:T(8,128)(2,1)S(1)}, bf16[512,2048]{1,0:T(8,128)(2,1)}, u32[]{:S(2)}) copy-start(bf16[512,2048]{1,0:T(8,128)(2,1)} %fusion.4.x_ref) | copy-start | bytes 6291460
  126.5 14.6 %collective-permute-start = (bf16[8,128,128]{2,1,0:T(8,128)(2,1)}, bf16[8,128,128]{2,1,0:T(8,128)(2,1)S(1)}, u32[]{:S(2)}, u32[]{:S(2)}) collective-permute-start(bf16[8,128,128]{2,1,0:T(8,128)(2,1)} %get-tuple-element.14), channel_id=1, source_target_pairs={{0,1},{1,2},{2,3},{3,0},{4,5},{5,6},{6,7},{7,4},{8,9},{9,10},{10,1... | collective-permute-start | bytes 786440 | tf_op jit(solution)/shard_map/ppermute | solution.py:158
  127.7 17.4 %collective-permute-start.1 = (bf16[8,128,128]{2,1,0:T(8,128)(2,1)}, bf16[8,128,128]{2,1,0:T(8,128)(2,1)S(1)}, u32[]{:S(2)}, u32[]{:S(2)}) collective-permute-start(bf16[8,128,128]{2,1,0:T(8,128)(2,1)} %get-tuple-element.14), channel_id=1, source_target_pairs={{0,2},{1,3},{2,0},{3,1},{4,6},{5,7},{6,4},{7,5},{8,10},{9,11},{10,... | collective-permute-start | bytes 786440 | tf_op jit(solution)/shard_map/ppermute | solution.py:158
  130.1 15.0 %collective-permute-start.2 = (bf16[8,128,128]{2,1,0:T(8,128)(2,1)}, bf16[8,128,128]{2,1,0:T(8,128)(2,1)S(1)}, u32[]{:S(2)}, u32[]{:S(2)}) collective-permute-start(bf16[8,128,128]{2,1,0:T(8,128)(2,1)} %get-tuple-element.14), channel_id=1, source_target_pairs={{0,3},{1,0},{2,1},{3,2},{4,7},{5,4},{6,5},{7,6},{8,11},{9,8},{10,9... | collective-permute-start | bytes 786440 | tf_op jit(solution)/shard_map/ppermute | solution.py:158
  131.2 24.3 %copy-start.5 = (bf16[512,1024]{1,0:T(8,128)(2,1)S(1)}, bf16[512,1024]{1,0:T(8,128)(2,1)}, u32[]{:S(2)}) copy-start(bf16[512,1024]{1,0:T(8,128)(2,1)} %get-tuple-element.17) | copy-start | bytes 3145732
  131.2 24.3 %copy-start.6 = (bf16[512,1024]{1,0:T(8,128)(2,1)S(1)}, bf16[512,1024]{1,0:T(8,128)(2,1)}, u32[]{:S(2)}) copy-start(bf16[512,1024]{1,0:T(8,128)(2,1)} %get-tuple-element.19) | copy-start | bytes 3145732
  141.1 14.4 %copy-start.3 = (bf16[512,1024]{1,0:T(8,128)(2,1)S(1)}, bf16[512,1024]{1,0:T(8,128)(2,1)}, u32[]{:S(2)}) copy-start(bf16[512,1024]{1,0:T(8,128)(2,1)} %get-tuple-element.16) | copy-start | bytes 3145732
  141.1 14.4 %copy-start.4 = (bf16[512,1024]{1,0:T(8,128)(2,1)S(1)}, bf16[512,1024]{1,0:T(8,128)(2,1)}, u32[]{:S(2)}) copy-start(bf16[512,1024]{1,0:T(8,128)(2,1)} %get-tuple-element.18) | copy-start | bytes 3145732
  146.0 14.8 %collective-permute-start.3 = (f32[2,128,128]{2,1,0:T(8,128)S(1)}, f32[2,128,128]{2,1,0:T(8,128)S(1)}, u32[]{:S(2)}, u32[]{:S(2)}) collective-permute-start(f32[2,128,128]{2,1,0:T(8,128)S(1)} %dynamic-slice_add_fusion), channel_id=1, source_target_pairs={{0,4},{4,8},{8,12},{1,5},{5,9},{9,13},{2,6},{6,10},{10,14},{3,7},{... | collective-permute-start | bytes 393224 | tf_op jit(solution)/shard_map/ppermute | solution.py:158
  149.1 11.7 %collective-permute-start.4 = (f32[2,128,128]{2,1,0:T(8,128)S(1)}, f32[2,128,128]{2,1,0:T(8,128)S(1)}, u32[]{:S(2)}, u32[]{:S(2)}) collective-permute-start(f32[2,128,128]{2,1,0:T(8,128)S(1)} %dynamic-slice_add_fusion), channel_id=1, source_target_pairs={{0,8},{4,12},{1,9},{5,13},{2,10},{6,14},{3,11},{7,15},{16,24},{20,... | collective-permute-start | bytes 393224 | tf_op jit(solution)/shard_map/ppermute | solution.py:158
  153.6 7.9 %collective-permute-start.5 = (f32[2,128,128]{2,1,0:T(8,128)S(1)}, f32[2,128,128]{2,1,0:T(8,128)}, u32[]{:S(2)}, u32[]{:S(2)}) collective-permute-start(f32[2,128,128]{2,1,0:T(8,128)S(1)} %dynamic-slice_add_fusion), channel_id=1, source_target_pairs={{0,12},{1,13},{2,14},{3,15},{16,28},{17,29},{18,30},{19,31},{32,44... | collective-permute-start | bytes 393224 | tf_op jit(solution)/shard_map/ppermute | solution.py:158
  160.8 0.7 copy-start.7
  162.5 15.4 %collective-permute-start.6 = (f32[2,128,128]{2,1,0:T(8,128)S(1)}, f32[2,128,128]{2,1,0:T(8,128)S(1)}, u32[]{:S(2)}, u32[]{:S(2)}) collective-permute-start(f32[2,128,128]{2,1,0:T(8,128)S(1)} %add_add_fusion), channel_id=1, source_target_pairs={{0,1},{1,2},{2,3},{3,0},{4,5},{5,6},{6,7},{7,4},{8,9},{9,10},{10,1... | collective-permute-start | bytes 393224 | tf_op jit(solution)/shard_map/ppermute | solution.py:158
  163.3 14.6 %collective-permute-start.7 = (f32[2,128,128]{2,1,0:T(8,128)S(1)}, f32[2,128,128]{2,1,0:T(8,128)S(1)}, u32[]{:S(2)}, u32[]{:S(2)}) collective-permute-start(f32[2,128,128]{2,1,0:T(8,128)S(1)} %add_add_fusion), channel_id=1, source_target_pairs={{0,2},{1,3},{2,0},{3,1},{4,6},{5,7},{6,4},{7,5},{8,10},{9,11},{10,... | collective-permute-start | bytes 393224 | tf_op jit(solution)/shard_map/ppermute | solution.py:158
  166.2 11.8 %collective-permute-start.8 = (f32[2,128,128]{2,1,0:T(8,128)S(1)}, f32[2,128,128]{2,1,0:T(8,128)}, u32[]{:S(2)}, u32[]{:S(2)}) collective-permute-start(f32[2,128,128]{2,1,0:T(8,128)S(1)} %add_add_fusion), channel_id=1, source_target_pairs={{0,3},{1,0},{2,1},{3,2},{4,7},{5,4},{6,5},{7,6},{8,11},{9,8},{10,9... | collective-permute-start | bytes 393224 | tf_op jit(solution)/shard_map/ppermute | solution.py:158
  177.9 1.6 copy-start.2
Sparse Core Ops, SparseCore 0:
  10.4 96.6 all-gather.3
  116.4 61.8 all-gather.5

commit v22 on v21

--- a/solution.py
+++ b/solution.py
@@ -102,7 +102,7 @@
     tail_gathered_kernel(here_ref, g_ref, p_ref, q_ref, w_ref, gain_ref, o_ref)
 
 
-def attend_tail_split(here, gathered, prefix, late_memory, queries, within, gains, heads_per_step=2):
+def attend_tail_split(here, gathered, prefix, late_memory, queries, within, gains, heads_per_step=8):
     rows = queries.shape[1]
     width = heads_per_step * DH
     n_piece = gathered.shape[0]

time: 200 us -> 199 us (level)
  no operation moved by 1% of the time
where the time goes in v22:
time: 199 us; the launch traced here: 197 us
  waiting for transfers between devices  99.8 us (50%)
  Pallas kernels  27.9 us (14%)
  matrix products  18.6 us (9%)
  starting transfers between devices  18.5 us (9%)
  between operations  13.6 us (7%)
  other arithmetic  11.8 us (6%)
  local copies, waits for them, and re-layouts  6.7 us (3%)
    all_gather x1, waiting for transfers between devices, body(): weight = lax.all_gather(qkv_weight, ('dp', 'y', 'x'), axis=1, tiled=True)  95.1 us
    ppermute x9, starting transfers between devices, ring_shift(): return lax.ppermute(value, axis, pairs)  18.5 us
    pallas_call x2, Pallas kernels, kv_memory(): pl.pallas_call(kv_memory_kernel, grid=(n_heads // heads_per_step,), in_sp...  18.4 us
    dot_general x1, matrix products, body(): queries = jnp.dot(normed, weight[:, :D], preferred_element_type=jnp.float32)  9.82 us
    dot_general x1, matrix products, body(): jnp.einsum('hbc,che->hbe', scores, values, preferred_element_type=jnp.flo...  8.8 us
    pallas_call x1, Pallas kernels, attend_tail_split(): pl.pallas_call(tail_gathered_after_kernel, grid_spec=grid_spec, out_shape...  5.65 us
  transfers between devices with their start and end apart: 11, of which 2 were waited for; matrix products, arithmetic and copies ran while one was open for 18% of the time, Pallas kernels for 7%

profile of v22, /device:TPU:1, one launch (start us, length us, event | category | flops | bytes accessed | tf_op | source)
XLA Modules:
  0.0 196.9 jit_solution(11103017791965086249)
XLA Ops:
  8.0 2.1 %fusion.2 = f32[512]{0:T(512)S(1)} fusion(bf16[1,512,2048]{2,1,0:T(8,128)(2,1)} %param.5), kind=kLoop, calls=%fused_computation.6 | loop fusion | flops 3145216 | bytes 2099200 | tf_op jit(solution)/shard_map/reduce_sum | solution.py:191
  10.1 1.9 fusion.4.x_ref
  12.0 95.1 %all-gather.4.cloned.1.call-done = bf16[2048,6144]{0,1:T(8,128)(2,1)} async-done(((bf16[2048,48]{0,1:T(8,128)(2,1)}), bf16[2048,6144]{0,1:T(8,128)(2,1)}) %all-gather.4.cloned.1.call-update) | async-done | bytes 25165840 | tf_op jit(solution)/shard_map/all_gather | solution.py:194
  107.1 9.1 %shard_map.55 = (bf16[512,1024]{1,0:T(8,128)(2,1)}, bf16[512,1024]{1,0:T(8,128)(2,1)}, bf16[8,128,128]{2,1,0:T(8,128)(2,1)}) custom-call(bf16[512,2048]{1,0:T(8,128)(2,1)} %fusion.4.x_ref, bf16[6144,2048]{1,0:T(8,128)(2,1)} %bitcast.39, bf16[6144,2048]{1,0:T(8,128)(2,1)} %bitcast.40), custom_call_target="tpu_custom_call" | custom-call | tf_op jit(solution)/shard_map/pallas_call | solution.py:40
  117.2 9.3 %shard_map.56 = (bf16[512,1024]{1,0:T(8,128)(2,1)}, bf16[512,1024]{1,0:T(8,128)(2,1)}, bf16[8,128,128]{2,1,0:T(8,128)(2,1)}) custom-call(bf16[512,2048]{1,0:T(8,128)(2,1)} %fusion.4.x_ref, bf16[6144,2048]{1,0:T(8,128)(2,1)} %bitcast.41, bf16[6144,2048]{1,0:T(8,128)(2,1)} %bitcast.42), custom_call_target="tpu_custom_call" | custom-call | tf_op jit(solution)/shard_map/pallas_call | solution.py:40
  126.5 1.2 collective-permute-start
  127.7 2.4 %collective-permute-start.1 = (bf16[8,128,128]{2,1,0:T(8,128)(2,1)}, bf16[8,128,128]{2,1,0:T(8,128)(2,1)S(1)}, u32[]{:S(2)}, u32[]{:S(2)}) collective-permute-start(bf16[8,128,128]{2,1,0:T(8,128)(2,1)} %get-tuple-element.14), channel_id=1, source_target_pairs={{0,2},{1,3},{2,0},{3,1},{4,6},{5,7},{6,4},{7,5},{8,10},{9,11},{10,... | collective-permute-start | bytes 786440 | tf_op jit(solution)/shard_map/ppermute | solution.py:158
  130.1 1.2 collective-permute-start.2
  131.2 9.8 %select_convert_fusion.1 = bf16[512,2048]{1,0:T(8,128)(2,1)} fusion(bf16[512,2048]{1,0:T(8,128)(2,1)S(1)} %copy-done, bf16[2048,6144]{0,1:T(8,128)(2,1)} %all-gather.4.cloned.1.call-done), kind=kOutput, calls=%fused_computation.9 | convolution fusion | flops 4300210176 | bytes 12582912 | tf_op jit(solution)/shard_map/dot_general | solution.py:201
  141.1 3.9 %collective-permute-done.1 = bf16[8,128,128]{2,1,0:T(8,128)(2,1)S(1)} collective-permute-done((bf16[8,128,128]{2,1,0:T(8,128)(2,1)}, bf16[8,128,128]{2,1,0:T(8,128)(2,1)S(1)}, u32[]{:S(2)}, u32[]{:S(2)}) %collective-permute-start.1) | collective-permute-done | bytes 262176 | tf_op jit(solution)/shard_map/ppermute | solution.py:158
  145.1 0.9 dynamic-slice_add_fusion
  146.0 3.1 %collective-permute-start.3 = (f32[2,128,128]{2,1,0:T(8,128)S(1)}, f32[2,128,128]{2,1,0:T(8,128)S(1)}, u32[]{:S(2)}, u32[]{:S(2)}) collective-permute-start(f32[2,128,128]{2,1,0:T(8,128)S(1)} %dynamic-slice_add_fusion), channel_id=1, source_target_pairs={{0,4},{4,8},{8,12},{1,5},{5,9},{9,13},{2,6},{6,10},{10,14},{3,7},{... | collective-permute-start | bytes 393224 | tf_op jit(solution)/shard_map/ppermute | solution.py:158
  149.1 4.4 %collective-permute-start.4 = (f32[2,128,128]{2,1,0:T(8,128)S(1)}, f32[2,128,128]{2,1,0:T(8,128)S(1)}, u32[]{:S(2)}, u32[]{:S(2)}) collective-permute-start(f32[2,128,128]{2,1,0:T(8,128)S(1)} %dynamic-slice_add_fusion), channel_id=1, source_target_pairs={{0,8},{4,12},{1,9},{5,13},{2,10},{6,14},{3,11},{7,15},{16,24},{20,... | collective-permute-start | bytes 393224 | tf_op jit(solution)/shard_map/ppermute | solution.py:158
  153.6 1.9 collective-permute-start.5
  155.5 2.4 %maximum_bitcast_fusion = (bf16[64,16,8,128]{3,2,1,0:T(8,128)(2,1)}, bf16[64,16,8,128]{3,2,1,0:T(8,128)(2,1)}) fusion(bf16[512,1024]{1,0:T(8,128)(2,1)S(1)} %copy-done.5, bf16[512,1024]{1,0:T(8,128)(2,1)S(1)} %copy-done.3, bf16[512,1024]{1,0:T(8,128)(2,1)S(1)} %copy-done.6, bf16[512,1024]{1,0:T(8,128)(2,1)S(1)} %copy-done.4), kind=kLoop, calls=%fused_computation.15 | loop fusion | flops 8388608 | bytes 8388608
  157.9 2.9 %copy.11 = bf16[512,2048]{0,1:T(8,128)(2,1)S(1)} copy(bf16[512,2048]{1,0:T(8,128)(2,1)} %select_convert_fusion.1) | data formatting | bytes 4194304 | tf_op jit(solution)/shard_map/optimization_barrier | solution.py:178
  161.5 1.0 add_add_fusion
  163.3 2.8 %collective-permute-start.7 = (f32[2,128,128]{2,1,0:T(8,128)S(1)}, f32[2,128,128]{2,1,0:T(8,128)S(1)}, u32[]{:S(2)}, u32[]{:S(2)}) collective-permute-start(f32[2,128,128]{2,1,0:T(8,128)S(1)} %add_add_fusion), channel_id=1, source_target_pairs={{0,2},{1,3},{2,0},{3,1},{4,6},{5,7},{6,4},{7,5},{8,10},{9,11},{10,... | collective-permute-start | bytes 393224 | tf_op jit(solution)/shard_map/ppermute | solution.py:158
  166.7 8.8 %fusion.7.w_ref = f32[16,512,128]{2,1,0:T(8,128)} fusion(bf16[512,16,128]{0,2,1:T(8,128)(2,1)S(1)} %bitcast.45, pred[512,512]{1,0:T(8,128)(4,1)S(1)} %iota_compare_fusion, bf16[64,16,8,128]{3,2,1,0:T(8,128)(2,1)} %get-tuple-element.22, bf16[64,16,8,128]{3,2,1,0:T(8,128)(2,1)} %get-tuple-element.21), kind=kOutput, calls=%fused_computation.10 | convolution fusion | flops 2155872256 | bytes 10747904 | tf_op jit(solution)/shard_map/hbc,che->hbe/dot_general | solution.py:210
  175.5 2.4 %copy.12 = bf16[512,16,128]{2,0,1:T(8,128)(2,1)} copy(bf16[512,16,128]{0,2,1:T(8,128)(2,1)S(1)} %bitcast.46) | data formatting | bytes 4194304 | tf_op jit(solution)/shard_map/reshape | solution.py:217
  177.9 1.0 pad_maximum_fusion
  179.6 1.0 fusion.15.m_ref
  180.6 3.8 %shard_map.57.prior_ref = bf16[512,2048]{1,0:T(8,128)(2,1)} custom-call(f32[8,128,128]{2,1,0:T(8,128)} %fusion.15.m_ref, bf16[16,512,128]{2,1,0:T(8,128)(2,1)} %bitcast.43, f32[16,512,128]{2,1,0:T(8,128)} %fusion.7.w_ref, f32[1,2048]{1,0:T(1,128)} %bitcast.52), custom_call_target="tpu_custom_call" | custom-call | tf_op jit(solution)/shard_map/pallas_call | solution.py:123
  184.4 5.6 %shard_map.58 = bf16[512,2048]{1,0:T(8,128)(2,1)} custom-call(s32[1]{0:T(128)} %bitcast.here_ref, bf16[16,8,128,128]{3,2,1,0:T(8,128)(2,1)} %bitcast.47, f32[16,128,128]{2,1,0:T(8,128)} %bitcast.48, bf16[16,512,128]{2,1,0:T(8,128)(2,1)} %bitcast.44, f32[16,512,128]{2,1,0:T(8,128)} %fusion.7.w_ref, ...), custom_call_target="tpu_custom_call", output_to_operand_aliasing={{}: (6, {})} | custom-call | tf_op jit(solution)/shard_map/pallas_call | solution.py:148
  (46 shorter events, 5.2 us)
Async XLA Ops:
  6.5 3.5 %copy-start.1 = (bf16[1,512,2048]{2,1,0:T(8,128)(2,1)S(1)}, bf16[1,512,2048]{2,1,0:T(8,128)(2,1)}, u32[]{:S(2)}) copy-start(bf16[1,512,2048]{2,1,0:T(8,128)(2,1)} %param.5) | copy-start | bytes 6291460
  6.5 100.6 %all-gather.4.cloned.1.call-start = ((), (), s32[]{:S(2)}) async-start(), calls=%async_computation | async-start | bytes 25362432 | tf_op jit(solution)/shard_map/all_gather | solution.py:194
  7.3 177.2 %all-gather.6.cloned.1.call-start = ((), (), s32[]{:S(2)}) async-start(), calls=%async_computation.1 | async-start | bytes 4456448 | tf_op jit(solution)/shard_map/all_gather | solution.py:197
  107.1 9.3 %copy-start.8 = (bf16[2048]{0:T(1024)(128)(2,1)S(1)}, bf16[2048]{0:T(1024)(128)(2,1)}, u32[]{:S(2)}) copy-start(bf16[2048]{0:T(1024)(128)(2,1)} %param.8) | copy-start | bytes 12292
  117.2 14.1 %copy-start = (bf16[512,2048]{1,0:T(8,128)(2,1)S(1)}, bf16[512,2048]{1,0:T(8,128)(2,1)}, u32[]{:S(2)}) copy-start(bf16[512,2048]{1,0:T(8,128)(2,1)} %fusion.4.x_ref) | copy-start | bytes 6291460
  126.5 14.6 %collective-permute-start = (bf16[8,128,128]{2,1,0:T(8,128)(2,1)}, bf16[8,128,128]{2,1,0:T(8,128)(2,1)S(1)}, u32[]{:S(2)}, u32[]{:S(2)}) collective-permute-start(bf16[8,128,128]{2,1,0:T(8,128)(2,1)} %get-tuple-element.14), channel_id=1, source_target_pairs={{0,1},{1,2},{2,3},{3,0},{4,5},{5,6},{6,7},{7,4},{8,9},{9,10},{10,1... | collective-permute-start | bytes 786440 | tf_op jit(solution)/shard_map/ppermute | solution.py:158
  127.7 17.4 %collective-permute-start.1 = (bf16[8,128,128]{2,1,0:T(8,128)(2,1)}, bf16[8,128,128]{2,1,0:T(8,128)(2,1)S(1)}, u32[]{:S(2)}, u32[]{:S(2)}) collective-permute-start(bf16[8,128,128]{2,1,0:T(8,128)(2,1)} %get-tuple-element.14), channel_id=1, source_target_pairs={{0,2},{1,3},{2,0},{3,1},{4,6},{5,7},{6,4},{7,5},{8,10},{9,11},{10,... | collective-permute-start | bytes 786440 | tf_op jit(solution)/shard_map/ppermute | solution.py:158
  130.1 15.0 %collective-permute-start.2 = (bf16[8,128,128]{2,1,0:T(8,128)(2,1)}, bf16[8,128,128]{2,1,0:T(8,128)(2,1)S(1)}, u32[]{:S(2)}, u32[]{:S(2)}) collective-permute-start(bf16[8,128,128]{2,1,0:T(8,128)(2,1)} %get-tuple-element.14), channel_id=1, source_target_pairs={{0,3},{1,0},{2,1},{3,2},{4,7},{5,4},{6,5},{7,6},{8,11},{9,8},{10,9... | collective-permute-start | bytes 786440 | tf_op jit(solution)/shard_map/ppermute | solution.py:158
  131.2 24.3 %copy-start.5 = (bf16[512,1024]{1,0:T(8,128)(2,1)S(1)}, bf16[512,1024]{1,0:T(8,128)(2,1)}, u32[]{:S(2)}) copy-start(bf16[512,1024]{1,0:T(8,128)(2,1)} %get-tuple-element.17) | copy-start | bytes 3145732
  131.2 24.3 %copy-start.6 = (bf16[512,1024]{1,0:T(8,128)(2,1)S(1)}, bf16[512,1024]{1,0:T(8,128)(2,1)}, u32[]{:S(2)}) copy-start(bf16[512,1024]{1,0:T(8,128)(2,1)} %get-tuple-element.19) | copy-start | bytes 3145732
  141.1 14.4 %copy-start.3 = (bf16[512,1024]{1,0:T(8,128)(2,1)S(1)}, bf16[512,1024]{1,0:T(8,128)(2,1)}, u32[]{:S(2)}) copy-start(bf16[512,1024]{1,0:T(8,128)(2,1)} %get-tuple-element.16) | copy-start | bytes 3145732
  141.1 14.4 %copy-start.4 = (bf16[512,1024]{1,0:T(8,128)(2,1)S(1)}, bf16[512,1024]{1,0:T(8,128)(2,1)}, u32[]{:S(2)}) copy-start(bf16[512,1024]{1,0:T(8,128)(2,1)} %get-tuple-element.18) | copy-start | bytes 3145732
  146.0 14.8 %collective-permute-start.3 = (f32[2,128,128]{2,1,0:T(8,128)S(1)}, f32[2,128,128]{2,1,0:T(8,128)S(1)}, u32[]{:S(2)}, u32[]{:S(2)}) collective-permute-start(f32[2,128,128]{2,1,0:T(8,128)S(1)} %dynamic-slice_add_fusion), channel_id=1, source_target_pairs={{0,4},{4,8},{8,12},{1,5},{5,9},{9,13},{2,6},{6,10},{10,14},{3,7},{... | collective-permute-start | bytes 393224 | tf_op jit(solution)/shard_map/ppermute | solution.py:158
  149.1 11.7 %collective-permute-start.4 = (f32[2,128,128]{2,1,0:T(8,128)S(1)}, f32[2,128,128]{2,1,0:T(8,128)S(1)}, u32[]{:S(2)}, u32[]{:S(2)}) collective-permute-start(f32[2,128,128]{2,1,0:T(8,128)S(1)} %dynamic-slice_add_fusion), channel_id=1, source_target_pairs={{0,8},{4,12},{1,9},{5,13},{2,10},{6,14},{3,11},{7,15},{16,24},{20,... | collective-permute-start | bytes 393224 | tf_op jit(solution)/shard_map/ppermute | solution.py:158
  153.6 7.9 %collective-permute-start.5 = (f32[2,128,128]{2,1,0:T(8,128)S(1)}, f32[2,128,128]{2,1,0:T(8,128)}, u32[]{:S(2)}, u32[]{:S(2)}) collective-permute-start(f32[2,128,128]{2,1,0:T(8,128)S(1)} %dynamic-slice_add_fusion), channel_id=1, source_target_pairs={{0,12},{1,13},{2,14},{3,15},{16,28},{17,29},{18,30},{19,31},{32,44... | collective-permute-start | bytes 393224 | tf_op jit(solution)/shard_map/ppermute | solution.py:158
  160.8 0.7 copy-start.7
  162.5 15.4 %collective-permute-start.6 = (f32[2,128,128]{2,1,0:T(8,128)S(1)}, f32[2,128,128]{2,1,0:T(8,128)S(1)}, u32[]{:S(2)}, u32[]{:S(2)}) collective-permute-start(f32[2,128,128]{2,1,0:T(8,128)S(1)} %add_add_fusion), channel_id=1, source_target_pairs={{0,1},{1,2},{2,3},{3,0},{4,5},{5,6},{6,7},{7,4},{8,9},{9,10},{10,1... | collective-permute-start | bytes 393224 | tf_op jit(solution)/shard_map/ppermute | solution.py:158
  163.3 14.6 %collective-permute-start.7 = (f32[2,128,128]{2,1,0:T(8,128)S(1)}, f32[2,128,128]{2,1,0:T(8,128)S(1)}, u32[]{:S(2)}, u32[]{:S(2)}) collective-permute-start(f32[2,128,128]{2,1,0:T(8,128)S(1)} %add_add_fusion), channel_id=1, source_target_pairs={{0,2},{1,3},{2,0},{3,1},{4,6},{5,7},{6,4},{7,5},{8,10},{9,11},{10,... | collective-permute-start | bytes 393224 | tf_op jit(solution)/shard_map/ppermute | solution.py:158
  166.2 11.8 %collective-permute-start.8 = (f32[2,128,128]{2,1,0:T(8,128)S(1)}, f32[2,128,128]{2,1,0:T(8,128)}, u32[]{:S(2)}, u32[]{:S(2)}) collective-permute-start(f32[2,128,128]{2,1,0:T(8,128)S(1)} %add_add_fusion), channel_id=1, source_target_pairs={{0,3},{1,0},{2,1},{3,2},{4,7},{5,4},{6,5},{7,6},{8,11},{9,8},{10,9... | collective-permute-start | bytes 393224 | tf_op jit(solution)/shard_map/ppermute | solution.py:158
  177.9 1.6 copy-start.2
Sparse Core Ops, SparseCore 0:
  10.4 96.6 all-gather.3
  116.4 61.8 all-gather.5

commit v23 on v20

--- a/solution.py
+++ b/solution.py
@@ -32,7 +32,7 @@
         m_ref[j] = m.astype(jnp.bfloat16)
 
 
-def kv_memory(normed, weight_t, first_head, n_heads, heads_per_step=4):
+def kv_memory(normed, weight_t, first_head, n_heads, heads_per_step=8):
     rows = normed.shape[0]
     width = heads_per_step * DH
     k_off = (D + first_head * DH) // width

time: 197 us -> 198 us (level)
  transfers between devices with their start and end apart: 11 -> 11, of which waited for: 2 -> 4; matrix products, arithmetic and copies ran while one was open for 19% -> 19% of each run, Pallas kernels for 6% -> 7%
where the time goes in v23:
time: 198 us; the launch traced here: 196 us
  waiting for transfers between devices  99.8 us (50%)
  Pallas kernels  27.7 us (14%)
  matrix products  18.6 us (9%)
  starting transfers between devices  18.1 us (9%)
  between operations  13.6 us (7%)
  other arithmetic  11.7 us (6%)
  local copies, waits for them, and re-layouts  6.7 us (3%)
    all_gather x1, waiting for transfers between devices, body(): weight = lax.all_gather(qkv_weight, ('dp', 'y', 'x'), axis=1, tiled=True)  95.1 us
    pallas_call x2, Pallas kernels, kv_memory(): pl.pallas_call(kv_memory_kernel, grid=(n_heads // heads_per_step,), in_sp...  19.5 us
    ppermute x9, starting transfers between devices, ring_shift(): return lax.ppermute(value, axis, pairs)  18 us
    dot_general x1, matrix products, body(): queries = jnp.dot(normed, weight[:, :D], preferred_element_type=jnp.float32)  9.79 us
    dot_general x1, matrix products, body(): jnp.einsum('hbc,che->hbe', scores, values, preferred_element_type=jnp.flo...  8.82 us
    pallas_call x1, Pallas kernels, attend_tail_split(): pl.pallas_call(tail_gathered_after_kernel, grid_spec=grid_spec, out_shape...  4.81 us
  transfers between devices with their start and end apart: 11, of which 4 were waited for; matrix products, arithmetic and copies ran while one was open for 19% of the time, Pallas kernels for 7%

profile of v23, /device:TPU:1, one launch (start us, length us, event | category | flops | bytes accessed | tf_op | source)
XLA Modules:
  0.0 196.1 jit_solution(9222869165769939263)
XLA Ops:
  8.0 2.1 %fusion.2 = f32[512]{0:T(512)S(1)} fusion(bf16[1,512,2048]{2,1,0:T(8,128)(2,1)} %param.5), kind=kLoop, calls=%fused_computation.6 | loop fusion | flops 3145216 | bytes 2099200 | tf_op jit(solution)/shard_map/reduce_sum | solution.py:191
  10.1 1.9 fusion.4.x_ref
  12.0 95.1 %all-gather.4.cloned.1.call-done = bf16[2048,6144]{0,1:T(8,128)(2,1)} async-done(((bf16[2048,48]{0,1:T(8,128)(2,1)}), bf16[2048,6144]{0,1:T(8,128)(2,1)}) %all-gather.4.cloned.1.call-update) | async-done | bytes 25165840 | tf_op jit(solution)/shard_map/all_gather | solution.py:194
  107.1 9.7 %shard_map.55 = (bf16[512,1024]{1,0:T(8,128)(2,1)}, bf16[512,1024]{1,0:T(8,128)(2,1)}, bf16[8,128,128]{2,1,0:T(8,128)(2,1)}) custom-call(bf16[512,2048]{1,0:T(8,128)(2,1)} %fusion.4.x_ref, bf16[6144,2048]{1,0:T(8,128)(2,1)} %bitcast.39, bf16[6144,2048]{1,0:T(8,128)(2,1)} %bitcast.40), custom_call_target="tpu_custom_call" | custom-call | tf_op jit(solution)/shard_map/pallas_call | solution.py:40
  117.7 9.8 %shard_map.56 = (bf16[512,1024]{1,0:T(8,128)(2,1)}, bf16[512,1024]{1,0:T(8,128)(2,1)}, bf16[8,128,128]{2,1,0:T(8,128)(2,1)}) custom-call(bf16[512,2048]{1,0:T(8,128)(2,1)} %fusion.4.x_ref, bf16[6144,2048]{1,0:T(8,128)(2,1)} %bitcast.41, bf16[6144,2048]{1,0:T(8,128)(2,1)} %bitcast.42), custom_call_target="tpu_custom_call" | custom-call | tf_op jit(solution)/shard_map/pallas_call | solution.py:40
  127.6 1.2 collective-permute-start
  128.8 2.4 %collective-permute-start.1 = (bf16[8,128,128]{2,1,0:T(8,128)(2,1)}, bf16[8,128,128]{2,1,0:T(8,128)(2,1)S(1)}, u32[]{:S(2)}, u32[]{:S(2)}) collective-permute-start(bf16[8,128,128]{2,1,0:T(8,128)(2,1)} %get-tuple-element.14), channel_id=1, source_target_pairs={{0,2},{1,3},{2,0},{3,1},{4,6},{5,7},{6,4},{7,5},{8,10},{9,11},{10,... | collective-permute-start | bytes 786440 | tf_op jit(solution)/shard_map/ppermute | solution.py:158
  131.2 1.2 collective-permute-start.2
  132.3 9.8 %select_convert_fusion.1 = bf16[512,2048]{1,0:T(8,128)(2,1)} fusion(bf16[512,2048]{1,0:T(8,128)(2,1)S(1)} %copy-done, bf16[2048,6144]{0,1:T(8,128)(2,1)} %all-gather.4.cloned.1.call-done), kind=kOutput, calls=%fused_computation.9 | convolution fusion | flops 4300210176 | bytes 12582912 | tf_op jit(solution)/shard_map/dot_general | solution.py:201
  142.2 3.7 %collective-permute-done.1 = bf16[8,128,128]{2,1,0:T(8,128)(2,1)S(1)} collective-permute-done((bf16[8,128,128]{2,1,0:T(8,128)(2,1)}, bf16[8,128,128]{2,1,0:T(8,128)(2,1)S(1)}, u32[]{:S(2)}, u32[]{:S(2)}) %collective-permute-start.1) | collective-permute-done | bytes 262176 | tf_op jit(solution)/shard_map/ppermute | solution.py:158
  146.0 0.9 dynamic-slice_add_fusion
  146.9 3.1 %collective-permute-start.3 = (f32[2,128,128]{2,1,0:T(8,128)S(1)}, f32[2,128,128]{2,1,0:T(8,128)S(1)}, u32[]{:S(2)}, u32[]{:S(2)}) collective-permute-start(f32[2,128,128]{2,1,0:T(8,128)S(1)} %dynamic-slice_add_fusion), channel_id=1, source_target_pairs={{0,4},{4,8},{8,12},{1,5},{5,9},{9,13},{2,6},{6,10},{10,14},{3,7},{... | collective-permute-start | bytes 393224 | tf_op jit(solution)/shard_map/ppermute | solution.py:158
  150.0 4.5 %collective-permute-start.4 = (f32[2,128,128]{2,1,0:T(8,128)S(1)}, f32[2,128,128]{2,1,0:T(8,128)S(1)}, u32[]{:S(2)}, u32[]{:S(2)}) collective-permute-start(f32[2,128,128]{2,1,0:T(8,128)S(1)} %dynamic-slice_add_fusion), channel_id=1, source_target_pairs={{0,8},{4,12},{1,9},{5,13},{2,10},{6,14},{3,11},{7,15},{16,24},{20,... | collective-permute-start | bytes 393224 | tf_op jit(solution)/shard_map/ppermute | solution.py:158
  154.5 1.9 collective-permute-start.5
  156.5 2.4 %maximum_bitcast_fusion = (bf16[64,16,8,128]{3,2,1,0:T(8,128)(2,1)}, bf16[64,16,8,128]{3,2,1,0:T(8,128)(2,1)}) fusion(bf16[512,1024]{1,0:T(8,128)(2,1)S(1)} %copy-done.5, bf16[512,1024]{1,0:T(8,128)(2,1)S(1)} %copy-done.3, bf16[512,1024]{1,0:T(8,128)(2,1)S(1)} %copy-done.6, bf16[512,1024]{1,0:T(8,128)(2,1)S(1)} %copy-done.4), kind=kLoop, calls=%fused_computation.15 | loop fusion | flops 8388608 | bytes 8388608
  158.9 2.9 %copy.11 = bf16[512,2048]{0,1:T(8,128)(2,1)S(1)} copy(bf16[512,2048]{1,0:T(8,128)(2,1)} %select_convert_fusion.1) | data formatting | bytes 4194304 | tf_op jit(solution)/shard_map/optimization_barrier | solution.py:178
  162.5 1.0 add_add_fusion
  164.3 2.9 %collective-permute-start.7 = (f32[2,128,128]{2,1,0:T(8,128)S(1)}, f32[2,128,128]{2,1,0:T(8,128)S(1)}, u32[]{:S(2)}, u32[]{:S(2)}) collective-permute-start(f32[2,128,128]{2,1,0:T(8,128)S(1)} %add_add_fusion), channel_id=1, source_target_pairs={{0,2},{1,3},{2,0},{3,1},{4,6},{5,7},{6,4},{7,5},{8,10},{9,11},{10,... | collective-permute-start | bytes 393224 | tf_op jit(solution)/shard_map/ppermute | solution.py:158
  167.2 8.8 %fusion.7.w_ref = f32[16,512,128]{2,1,0:T(8,128)} fusion(bf16[512,16,128]{0,2,1:T(8,128)(2,1)S(1)} %bitcast.45, pred[512,512]{1,0:T(8,128)(4,1)S(1)} %iota_compare_fusion, bf16[64,16,8,128]{3,2,1,0:T(8,128)(2,1)} %get-tuple-element.22, bf16[64,16,8,128]{3,2,1,0:T(8,128)(2,1)} %get-tuple-element.21), kind=kOutput, calls=%fused_computation.10 | convolution fusion | flops 2155872256 | bytes 10747904 | tf_op jit(solution)/shard_map/hbc,che->hbe/dot_general | solution.py:210
  176.0 2.4 %copy.12 = bf16[512,16,128]{2,0,1:T(8,128)(2,1)} copy(bf16[512,16,128]{0,2,1:T(8,128)(2,1)S(1)} %bitcast.46) | data formatting | bytes 4194304 | tf_op jit(solution)/shard_map/reshape | solution.py:217
  178.5 1.0 pad_maximum_fusion
  180.1 1.0 fusion.15.m_ref
  181.1 3.3 %shard_map.57.prior_ref = bf16[512,2048]{1,0:T(8,128)(2,1)} custom-call(f32[8,128,128]{2,1,0:T(8,128)} %fusion.15.m_ref, bf16[16,512,128]{2,1,0:T(8,128)(2,1)} %bitcast.43, f32[16,512,128]{2,1,0:T(8,128)} %fusion.7.w_ref, f32[1,2048]{1,0:T(1,128)} %bitcast.52), custom_call_target="tpu_custom_call" | custom-call | tf_op jit(solution)/shard_map/pallas_call | solution.py:123
  184.4 4.8 %shard_map.58 = bf16[512,2048]{1,0:T(8,128)(2,1)} custom-call(s32[1]{0:T(128)} %bitcast.here_ref, bf16[16,8,128,128]{3,2,1,0:T(8,128)(2,1)} %bitcast.47, f32[16,128,128]{2,1,0:T(8,128)} %bitcast.48, bf16[16,512,128]{2,1,0:T(8,128)(2,1)} %bitcast.44, f32[16,512,128]{2,1,0:T(8,128)} %fusion.7.w_ref, ...), custom_call_target="tpu_custom_call", output_to_operand_aliasing={{}: (6, {})} | custom-call | tf_op jit(solution)/shard_map/pallas_call | solution.py:148
  (46 shorter events, 4.7 us)
Async XLA Ops:
  6.5 3.5 %copy-start.1 = (bf16[1,512,2048]{2,1,0:T(8,128)(2,1)S(1)}, bf16[1,512,2048]{2,1,0:T(8,128)(2,1)}, u32[]{:S(2)}) copy-start(bf16[1,512,2048]{2,1,0:T(8,128)(2,1)} %param.5) | copy-start | bytes 6291460
  6.5 100.6 %all-gather.4.cloned.1.call-start = ((), (), s32[]{:S(2)}) async-start(), calls=%async_computation | async-start | bytes 25362432 | tf_op jit(solution)/shard_map/all_gather | solution.py:194
  7.3 177.2 %all-gather.6.cloned.1.call-start = ((), (), s32[]{:S(2)}) async-start(), calls=%async_computation.1 | async-start | bytes 4456448 | tf_op jit(solution)/shard_map/all_gather | solution.py:197
  107.1 9.9 %copy-start.8 = (bf16[2048]{0:T(1024)(128)(2,1)S(1)}, bf16[2048]{0:T(1024)(128)(2,1)}, u32[]{:S(2)}) copy-start(bf16[2048]{0:T(1024)(128)(2,1)} %param.8) | copy-start | bytes 12292
  117.7 14.6 %copy-start = (bf16[512,2048]{1,0:T(8,128)(2,1)S(1)}, bf16[512,2048]{1,0:T(8,128)(2,1)}, u32[]{:S(2)}) copy-start(bf16[512,2048]{1,0:T(8,128)(2,1)} %fusion.4.x_ref) | copy-start | bytes 6291460
  127.6 14.6 %collective-permute-start = (bf16[8,128,128]{2,1,0:T(8,128)(2,1)}, bf16[8,128,128]{2,1,0:T(8,128)(2,1)S(1)}, u32[]{:S(2)}, u32[]{:S(2)}) collective-permute-start(bf16[8,128,128]{2,1,0:T(8,128)(2,1)} %get-tuple-element.14), channel_id=1, source_target_pairs={{0,1},{1,2},{2,3},{3,0},{4,5},{5,6},{6,7},{7,4},{8,9},{9,10},{10,1... | collective-permute-start | bytes 786440 | tf_op jit(solution)/shard_map/ppermute | solution.py:158
  128.8 17.1 %collective-permute-start.1 = (bf16[8,128,128]{2,1,0:T(8,128)(2,1)}, bf16[8,128,128]{2,1,0:T(8,128)(2,1)S(1)}, u32[]{:S(2)}, u32[]{:S(2)}) collective-permute-start(bf16[8,128,128]{2,1,0:T(8,128)(2,1)} %get-tuple-element.14), channel_id=1, source_target_pairs={{0,2},{1,3},{2,0},{3,1},{4,6},{5,7},{6,4},{7,5},{8,10},{9,11},{10,... | collective-permute-start | bytes 786440 | tf_op jit(solution)/shard_map/ppermute | solution.py:158
  131.2 14.8 %collective-permute-start.2 = (bf16[8,128,128]{2,1,0:T(8,128)(2,1)}, bf16[8,128,128]{2,1,0:T(8,128)(2,1)S(1)}, u32[]{:S(2)}, u32[]{:S(2)}) collective-permute-start(bf16[8,128,128]{2,1,0:T(8,128)(2,1)} %get-tuple-element.14), channel_id=1, source_target_pairs={{0,3},{1,0},{2,1},{3,2},{4,7},{5,4},{6,5},{7,6},{8,11},{9,8},{10,9... | collective-permute-start | bytes 786440 | tf_op jit(solution)/shard_map/ppermute | solution.py:158
  132.3 24.1 %copy-start.5 = (bf16[512,1024]{1,0:T(8,128)(2,1)S(1)}, bf16[512,1024]{1,0:T(8,128)(2,1)}, u32[]{:S(2)}) copy-start(bf16[512,1024]{1,0:T(8,128)(2,1)} %get-tuple-element.17) | copy-start | bytes 3145732
  132.3 24.1 %copy-start.6 = (bf16[512,1024]{1,0:T(8,128)(2,1)S(1)}, bf16[512,1024]{1,0:T(8,128)(2,1)}, u32[]{:S(2)}) copy-start(bf16[512,1024]{1,0:T(8,128)(2,1)} %get-tuple-element.19) | copy-start | bytes 3145732
  142.1 14.3 %copy-start.3 = (bf16[512,1024]{1,0:T(8,128)(2,1)S(1)}, bf16[512,1024]{1,0:T(8,128)(2,1)}, u32[]{:S(2)}) copy-start(bf16[512,1024]{1,0:T(8,128)(2,1)} %get-tuple-element.16) | copy-start | bytes 3145732
  142.1 14.3 %copy-start.4 = (bf16[512,1024]{1,0:T(8,128)(2,1)S(1)}, bf16[512,1024]{1,0:T(8,128)(2,1)}, u32[]{:S(2)}) copy-start(bf16[512,1024]{1,0:T(8,128)(2,1)} %get-tuple-element.18) | copy-start | bytes 3145732
  146.9 14.9 %collective-permute-start.3 = (f32[2,128,128]{2,1,0:T(8,128)S(1)}, f32[2,128,128]{2,1,0:T(8,128)S(1)}, u32[]{:S(2)}, u32[]{:S(2)}) collective-permute-start(f32[2,128,128]{2,1,0:T(8,128)S(1)} %dynamic-slice_add_fusion), channel_id=1, source_target_pairs={{0,4},{4,8},{8,12},{1,5},{5,9},{9,13},{2,6},{6,10},{10,14},{3,7},{... | collective-permute-start | bytes 393224 | tf_op jit(solution)/shard_map/ppermute | solution.py:158
  150.0 11.8 %collective-permute-start.4 = (f32[2,128,128]{2,1,0:T(8,128)S(1)}, f32[2,128,128]{2,1,0:T(8,128)S(1)}, u32[]{:S(2)}, u32[]{:S(2)}) collective-permute-start(f32[2,128,128]{2,1,0:T(8,128)S(1)} %dynamic-slice_add_fusion), channel_id=1, source_target_pairs={{0,8},{4,12},{1,9},{5,13},{2,10},{6,14},{3,11},{7,15},{16,24},{20,... | collective-permute-start | bytes 393224 | tf_op jit(solution)/shard_map/ppermute | solution.py:158
  154.5 8.0 %collective-permute-start.5 = (f32[2,128,128]{2,1,0:T(8,128)S(1)}, f32[2,128,128]{2,1,0:T(8,128)}, u32[]{:S(2)}, u32[]{:S(2)}) collective-permute-start(f32[2,128,128]{2,1,0:T(8,128)S(1)} %dynamic-slice_add_fusion), channel_id=1, source_target_pairs={{0,12},{1,13},{2,14},{3,15},{16,28},{17,29},{18,30},{19,31},{32,44... | collective-permute-start | bytes 393224 | tf_op jit(solution)/shard_map/ppermute | solution.py:158
  161.8 0.7 copy-start.7
  163.5 14.9 %collective-permute-start.6 = (f32[2,128,128]{2,1,0:T(8,128)S(1)}, f32[2,128,128]{2,1,0:T(8,128)S(1)}, u32[]{:S(2)}, u32[]{:S(2)}) collective-permute-start(f32[2,128,128]{2,1,0:T(8,128)S(1)} %add_add_fusion), channel_id=1, source_target_pairs={{0,1},{1,2},{2,3},{3,0},{4,5},{5,6},{6,7},{7,4},{8,9},{9,10},{10,1... | collective-permute-start | bytes 393224 | tf_op jit(solution)/shard_map/ppermute | solution.py:158
  164.3 14.2 %collective-permute-start.7 = (f32[2,128,128]{2,1,0:T(8,128)S(1)}, f32[2,128,128]{2,1,0:T(8,128)S(1)}, u32[]{:S(2)}, u32[]{:S(2)}) collective-permute-start(f32[2,128,128]{2,1,0:T(8,128)S(1)} %add_add_fusion), channel_id=1, source_target_pairs={{0,2},{1,3},{2,0},{3,1},{4,6},{5,7},{6,4},{7,5},{8,10},{9,11},{10,... | collective-permute-start | bytes 393224 | tf_op jit(solution)/shard_map/ppermute | solution.py:158
  167.2 11.3 %collective-permute-start.8 = (f32[2,128,128]{2,1,0:T(8,128)S(1)}, f32[2,128,128]{2,1,0:T(8,128)}, u32[]{:S(2)}, u32[]{:S(2)}) collective-permute-start(f32[2,128,128]{2,1,0:T(8,128)S(1)} %add_add_fusion), channel_id=1, source_target_pairs={{0,3},{1,0},{2,1},{3,2},{4,7},{5,4},{6,5},{7,6},{8,11},{9,8},{10,9... | collective-permute-start | bytes 393224 | tf_op jit(solution)/shard_map/ppermute | solution.py:158
  178.4 1.7 copy-start.2
Sparse Core Ops, SparseCore 0:
  10.4 96.6 all-gather.3
  116.9 61.8 all-gather.5
